TPU v7x, 128 devices: a whole 4x4x4 slice. The times are simulated.
128 devices in a mesh: seq: 32 (over x, y, core), fsdp: 4 (over z).
Axes of the slice: x: 4, y: 4, z: 4, core: 2. Of those that a mesh axis runs over, the one named last changes fastest.
Arguments:
- patches: bfloat16 [32768, 1280], P(('seq', 'fsdp')), may hold values from -6 to 6
- vis_index: int32 [32768], P(('seq', 'fsdp')), may hold values from 0 to 131071, as said below
- kv_list: int32 [256, 16], P(('seq', 'fsdp')), may hold values from 0 to 255, as said below
- kv_count: int32 [256], P(('seq', 'fsdp')), may hold values from 1 to 16, as said below
- global_tiles: int32 [2], replicated, may hold values from 0 to 255
- frame_table: bfloat16 [256, 1280], replicated, may hold values from -3 to 3
- space_table: bfloat16 [512, 1280], replicated, may hold values from -3 to 3
- ln_gain: bfloat16 [1280], replicated, may hold values from 0.25 to 1.75
- ln_bias: bfloat16 [1280], replicated, may hold values from -3 to 3
- w_qkv: bfloat16 [1280, 3840], P('fsdp')
- w_out: bfloat16 [1280, 1280], P('fsdp'), may hold values from -1.25 to 1.25
Outputs:
- attended: bfloat16 [32768, 1280], P(('seq', 'fsdp'))
Inputs may be any that keep to these rules, and one draw needn't show every extreme that they name: `vis_index`: exactly one visible position in each aligned group of four; strictly increasing. `kv_list`: the first entry of query tile i is i itself; entries may repeat; every entry t satisfies |t // 8 - i // 8| <= 2. Over all entries of an aligned run of 2 query tiles, the tiles that lie in any one group other than the run's own group (group = tile // 8) number at most 3 distinct ones, and exactly 3 for every such group within two of the run's own. On every device at least one query tile has kv_count = 16.
All inputs are finite; a program needn't handle non-finite values.
Results may differ from a plain program's by a relative error of at most 0.0065.
Values may be sent and summed in bfloat16 or wider, within the bound.
No kernel may reach another device: no remote copies, remote signals or barrier semaphores. Data moves between devices by JAX's collectives and lax.ppermute only.
A program may use at most 192 MiB of HBM per device.

v0:
```python
import jax
import jax.numpy as jnp
from jax import lax
from jax.sharding import PartitionSpec as P

HEADS = 16
TILE = 128
KT = 16
GLOBAL = 2
PATCHES = 512


def passed_along(block, axis, distance):
    devices = range(lax.axis_size(axis))
    route = [(i - distance, i) for i in devices if i - distance in devices]
    return lax.ppermute(block, axis, route)


def broadcast(shard, axis, root):
    mine = lax.axis_index(axis) == root
    return lax.psum(jnp.where(mine, shard, jnp.zeros_like(shard)), axis)


def layer_norm(stream, ln_gain, ln_bias):
    stream32 = stream.astype(jnp.float32)
    mean_val = jnp.mean(stream32, axis=-1, keepdims=True)
    centred = stream32 - mean_val
    variance = jnp.mean(centred * centred, axis=-1, keepdims=True)
    scaled = centred * lax.rsqrt(variance + 1e-06)
    return (scaled * ln_gain.astype(jnp.float32) + ln_bias.astype(jnp.float32)).astype(jnp.bfloat16)


def project(inputs, weight):
    return jnp.dot(
        inputs,
        lax.all_gather(weight, "fsdp", axis=0, tiled=True),
        preferred_element_type=jnp.float32,
    )


def attend_tile(query_tile, key_values, key_live, feat_width):
    head_size = feat_width // HEADS
    key_rows = key_values.shape[0]
    queries_h = query_tile.reshape(TILE, HEADS, head_size)
    keys_h = key_values[:, :feat_width].reshape(key_rows, HEADS, head_size)
    values_h = key_values[:, feat_width:].reshape(key_rows, HEADS, head_size)
    scores = jnp.einsum(
        "qhd,khd->hqk", queries_h, keys_h, preferred_element_type=jnp.float32
    ) * head_size ** (-0.5)
    scores = jnp.where(key_live[None, None, :], scores, -jnp.inf)
    row_max = jnp.max(scores, axis=-1, keepdims=True)
    weights_raw = jnp.exp(scores - row_max)
    probs = (weights_raw / jnp.sum(weights_raw, axis=-1, keepdims=True)).astype(jnp.bfloat16)
    mixed_h = jnp.einsum("hqk,khd->qhd", probs, values_h, preferred_element_type=jnp.float32)
    return mixed_h.reshape(TILE, feat_width).astype(jnp.bfloat16)


def local(
    patches,
    vis_index,
    kv_list,
    kv_count,
    global_tiles,
    frame_table,
    space_table,
    ln_gain,
    ln_bias,
    w_qkv,
    w_out,
):
    tok_rows = patches.shape[0]
    feat_width = patches.shape[1]
    tile_count = tok_rows // TILE
    frame_ids = vis_index // PATCHES
    patch_ids = vis_index % PATCHES
    stream = (
        patches.astype(jnp.float32)
        + frame_table[frame_ids].astype(jnp.float32)
        + space_table[patch_ids].astype(jnp.float32)
    ).astype(jnp.bfloat16)
    normed = layer_norm(stream, ln_gain, ln_bias)
    qkv = project(normed, w_qkv).astype(jnp.bfloat16)
    query = qkv[:, :feat_width]
    keyval = qkv[:, feat_width:]
    group_block = lax.all_gather(keyval, "fsdp", axis=0, tiled=True)
    group_tiles = group_block.shape[0] // TILE
    blocks = []
    for offset in (2, 1, 0, -1, -2):
        if offset == 0:
            blocks.append(group_block)
        else:
            blocks.append(passed_along(group_block, "seq", offset))
    window = jnp.concatenate(blocks, axis=0)
    tile_source = window.reshape(5 * group_tiles, TILE, 2 * feat_width)
    local_lists = kv_list - (lax.axis_index("seq") - 2) * group_tiles
    global_list = []
    for slot_no in range(GLOBAL):
        tile_id = global_tiles[slot_no]
        owner_index = tile_id // tile_count
        tile_piece = lax.dynamic_slice_in_dim(keyval, tile_id % tile_count * TILE, TILE, 0)
        global_list.append(broadcast(tile_piece, ("seq", "fsdp"), owner_index))
    global_kv = jnp.stack(global_list, axis=0)
    query_tiles = query.reshape(tile_count, TILE, feat_width)

    def per_tile(tile_args):
        query_tile, local_ids, live_count = tile_args
        slot_live_row = jnp.concatenate(
            [jnp.arange(KT) < live_count, jnp.ones((GLOBAL,), dtype=bool)]
        )
        key_live = jnp.repeat(slot_live_row, TILE)
        key_values = jnp.concatenate([tile_source[local_ids], global_kv], axis=0).reshape(
            (KT + GLOBAL) * TILE, 2 * feat_width
        )
        return attend_tile(query_tile, key_values, key_live, feat_width)

    heads_out = lax.map(per_tile, (query_tiles, local_lists, kv_count)).reshape(
        tok_rows, feat_width
    )
    return project(heads_out, w_out).astype(jnp.bfloat16)


def solution(mesh):
    return jax.shard_map(
        local,
        mesh=mesh,
        in_specs=(
            P(("seq", "fsdp"), None),
            P(("seq", "fsdp")),
            P(("seq", "fsdp"), None),
            P(("seq", "fsdp")),
            P(),
            P(),
            P(),
            P(),
            P(),
            P("fsdp", None),
            P("fsdp", None),
        ),
        out_specs=P(("seq", "fsdp"), None),
        check_vma=False,
    )
```

profile of v0, /device:TPU:24, one launch (start us, length us, event | category | flops | bytes accessed | tf_op | source)
XLA Modules:
  0.0 663.1 jit_solution(8370119231040135235)
XLA Ops:
  6.5 0.7 all-gather.4.cloned.1.call-update
  7.3 0.7 convert_element_type.54
  8.0 0.7 convert_element_type.55
  8.7 0.7 compare_select_fusion.2
  9.4 1.3 gather_fusion.1
  10.7 1.2 gather_fusion.2
  12.6 93.8 %all-gather.4.cloned.1.call-done = bf16[1280,3840]{1,0:T(8,128)(2,1)} async-done(((bf16[320,3840]{1,0:T(8,128)(2,1)}), bf16[1280,3840]{1,0:T(8,128)(2,1)}) %all-gather.4.cloned.1.call-update) | async-done | bytes 9830416 | tf_op jit(solution)/shard_map/all_gather | solution.py:36
  106.5 6.6 %convolution_convert_fusion = bf16[256,3840]{1,0:T(8,128)(2,1)S(1)} fusion(bf16[1280,3840]{1,0:T(8,128)(2,1)} %all-gather.4.cloned.1.call-done, bf16[256,1280]{1,0:T(8,128)(2,1)S(1)} %get-tuple-element.83, f32[1280]{0:T(1024)S(1)} %convert_element_type.55, f32[1280]{0:T(1024)S(1)} %convert_element_type.54, f32[256]{0:T(256)S(1)} %add_rsqrt_fusion, ...), kind=kOutput, calls=%fused_computation.26 | convolution fusion | flops 2519531520 | bytes 12464128 | tf_op jit(solution)/shard_map/dot_general | solution.py:34
  113.1 1.3 slice.30
  114.4 58.2 %all-gather.6.cloned.1.call-done = bf16[1024,2560]{1,0:T(8,128)(2,1)} async-done(((bf16[256,2560]{1,0:T(8,128)(2,1)}), bf16[1024,2560]{1,0:T(8,128)(2,1)}) %all-gather.6.cloned.1.call-update) | async-done | bytes 5242896 | tf_op jit(solution)/shard_map/all_gather | solution.py:85
  172.7 3.3 collective-permute-start
  176.0 1.9 collective-permute-start.1
  177.9 3.6 collective-permute-start.2
  181.6 2.5 collective-permute-start.3
  189.8 2.6 select_bitcast_fusion
  193.0 282.7 %all-reduce.4.cloned.1.call-done = (bf16[1,128,2560]{2,1,0:T(8,128)(2,1)}, bf16[1,128,2560]{2,1,0:T(8,128)(2,1)}) async-done(((bf16[1,128,2560]{2,1,0:T(8,128)(2,1)}, bf16[1,128,2560]{2,1,0:T(8,128)(2,1)}), (bf16[1,128,2560]{2,1,0:T(8,128)(2,1)}, bf16[1,128,2560]{2,1,0:T(8,128)(2,1)})) %all-reduce.4.cloned.1.call-update) | async-done | bytes 1310736 | tf_op jit(solution)/shard_map/psum | solution.py:21
  475.7 2.5 copy.23
  478.3 3.8 copy.24
  482.0 5.3 constant_dynamic-update-slice_fusion.5
  487.3 5.5 constant_dynamic-update-slice_fusion.4
  492.8 2.7 constant_dynamic-update-slice_fusion.3
  495.5 5.2 constant_dynamic-update-slice_fusion.2
  500.7 5.3 constant_dynamic-update-slice_fusion.1
  506.0 146.5 %while.10 = (s32[]{:T(128)}, bf16[2,128,1280]{2,1,0:T(8,128)(2,1)}, s32[2,16]{1,0:T(2,128)S(1)}, bf16[40,128,2560]{2,1,0:T(8,128)(2,1)}, bf16[1,128,2560]{1,0,2:...) while((s32[]{:T(128)}, bf16[2,128,1280]{2,1,0:T(8,128)(2,1)}, ...), condition=%wide.region_7.8_spmd, body=%wide.region_4.7_spmd.sunk | while | flops 1550224640 | bytes 152462336 | solution.py:116
  506.0 14.2 %gather_fusion = bf16[16,128,2560]{2,1,0:T(8,128)(2,1)} fusion(bf16[40,128,2560]{2,1,0:T(8,128)(2,1)} %get-tuple-element.176, s32[1024]{0:T(1024)S(1)} %pad_clamp_fusion.4), kind=kCustom, calls=%fused_computation.clone.1 | custom fusion | bytes 20971584 | tf_op jit(solution)/shard_map/while/body/eval_jaxpr/gather | solution.py:111
  520.2 2.5 copy.38
  522.8 0.9 copy.39
  523.6 7.8 %pad_maximum_fusion.2 = bf16[18,128,2560]{2,1,0:T(8,128)(2,1)S(1)} fusion(bf16[1,128,2560]{2,1,0:T(8,128)(2,1)S(1)} %copy.38, bf16[1,128,2560]{2,1,0:T(8,128)(2,1)S(1)} %copy.39, bf16[16,128,2560]{2,1,0:T(8,128)(2,1)} %gather_fusion), kind=kLoop, calls=%fused_computation.8.clone.1 | loop fusion | flops 11796480 | bytes 23592960 | tf_op jit(solution)/shard_map/while/body/eval_jaxpr/concatenate | solution.py:111
  531.4 4.7 fusion.46
  536.1 8.9 %copy.42 = bf16[2304,1280]{0,1:T(8,128)(2,1)} copy(bf16[2304,1280]{1,0:T(8,128)(2,1)} %get-tuple-element.150) | data formatting | bytes 11796480 | tf_op jit(solution)/shard_map/while
  545.2 0.6 dynamic_slice.35
  545.8 0.6 iota_compare_fusion.2
  546.5 11.2 %fusion.47 = (f32[16,128]{1,0:T(8,128)S(1)}, f32[16,128,2304]{2,1,0:T(8,128)}) fusion(pred[2304]{0:T(1024)(128)(4,1)S(1)} %broadcast_bitcast_fusion.2, bf16[128,16,80]{0,2,1:T(8,128)(2,1)S(1)} %bitcast.63, bf16[2304,16,80]{0,2,1:T(8,128)(2,1)} %bitcast.60), kind=kOutput, calls=%fused_computation.63.clone.1 | convolution fusion | flops 773851392 | bytes 25110784 | tf_op jit(solution)/shard_map/while/body/eval_jaxpr/sub | solution.py:52
  557.7 8.9 %copy.40 = bf16[2304,1280]{0,1:T(8,128)(2,1)} copy(bf16[2304,1280]{1,0:T(8,128)(2,1)} %get-tuple-element.149) | data formatting | bytes 11796480 | tf_op jit(solution)/shard_map/while
  566.6 11.6 %fusion.48 = bf16[16,80,128]{2,1,0:T(8,128)(2,1)S(1)} fusion(bf16[2304,16,80]{0,2,1:T(8,128)(2,1)} %bitcast.61, f32[16,128,2304]{2,1,0:T(8,128)} %get-tuple-element.151, f32[16,128]{1,0:T(8,128)S(1)} %get-tuple-element.152), kind=kOutput, calls=%fused_computation.14.clone.1 | convolution fusion | flops 764575744 | bytes 25108480 | tf_op jit(solution)/shard_map/while/body/eval_jaxpr/hqk,khd->qhd/dot_general | solution.py:54
  578.4 0.8 copy-done.8
  579.3 14.1 %gather_fusion = bf16[16,128,2560]{2,1,0:T(8,128)(2,1)} fusion(bf16[40,128,2560]{2,1,0:T(8,128)(2,1)} %get-tuple-element.176, s32[1024]{0:T(1024)S(1)} %pad_clamp_fusion.4), kind=kCustom, calls=%fused_computation.clone.1 | custom fusion | bytes 20971584 | tf_op jit(solution)/shard_map/while/body/eval_jaxpr/gather | solution.py:111
  593.4 2.5 copy.38
  595.9 0.9 copy.39
  596.8 7.8 %pad_maximum_fusion.2 = bf16[18,128,2560]{2,1,0:T(8,128)(2,1)S(1)} fusion(bf16[1,128,2560]{2,1,0:T(8,128)(2,1)S(1)} %copy.38, bf16[1,128,2560]{2,1,0:T(8,128)(2,1)S(1)} %copy.39, bf16[16,128,2560]{2,1,0:T(8,128)(2,1)} %gather_fusion), kind=kLoop, calls=%fused_computation.8.clone.1 | loop fusion | flops 11796480 | bytes 23592960 | tf_op jit(solution)/shard_map/while/body/eval_jaxpr/concatenate | solution.py:111
  604.6 4.7 fusion.46
  609.3 8.9 %copy.42 = bf16[2304,1280]{0,1:T(8,128)(2,1)} copy(bf16[2304,1280]{1,0:T(8,128)(2,1)} %get-tuple-element.150) | data formatting | bytes 11796480 | tf_op jit(solution)/shard_map/while
  619.0 0.6 iota_compare_fusion.2
  619.7 11.2 %fusion.47 = (f32[16,128]{1,0:T(8,128)S(1)}, f32[16,128,2304]{2,1,0:T(8,128)}) fusion(pred[2304]{0:T(1024)(128)(4,1)S(1)} %broadcast_bitcast_fusion.2, bf16[128,16,80]{0,2,1:T(8,128)(2,1)S(1)} %bitcast.63, bf16[2304,16,80]{0,2,1:T(8,128)(2,1)} %bitcast.60), kind=kOutput, calls=%fused_computation.63.clone.1 | convolution fusion | flops 773851392 | bytes 25110784 | tf_op jit(solution)/shard_map/while/body/eval_jaxpr/sub | solution.py:52
  630.9 8.9 %copy.40 = bf16[2304,1280]{0,1:T(8,128)(2,1)} copy(bf16[2304,1280]{1,0:T(8,128)(2,1)} %get-tuple-element.149) | data formatting | bytes 11796480 | tf_op jit(solution)/shard_map/while
  639.8 11.6 %fusion.48 = bf16[16,80,128]{2,1,0:T(8,128)(2,1)S(1)} fusion(bf16[2304,16,80]{0,2,1:T(8,128)(2,1)} %bitcast.61, f32[16,128,2304]{2,1,0:T(8,128)} %get-tuple-element.151, f32[16,128]{1,0:T(8,128)S(1)} %get-tuple-element.152), kind=kOutput, calls=%fused_computation.14.clone.1 | convolution fusion | flops 764575744 | bytes 25108480 | tf_op jit(solution)/shard_map/while/body/eval_jaxpr/hqk,khd->qhd/dot_general | solution.py:54
  651.6 0.8 copy-done.8
  652.5 4.1 convolution_convert_fusion.1
  (66 shorter events, 3.7 us)
Async XLA Ops:
  6.5 4.1 copy-start
  6.5 2.8 copy-start.2
  6.5 99.9 %all-gather.4.cloned.1.call-start = ((), (), s32[]{:S(2)}) async-start(), calls=%async_computation | async-start | bytes 12288000 | tf_op jit(solution)/shard_map/all_gather | solution.py:36
  7.3 165.4 %all-gather.6.cloned.1.call-start = ((), (), s32[]{:S(2)}) async-start(), calls=%async_computation.1 | async-start | bytes 6553600 | tf_op jit(solution)/shard_map/all_gather | solution.py:85
  9.4 2.5 copy-start.4
  12.6 171.5 %copy-start.5 = (s32[2]{0:T(128)S(1)}, s32[2]{0:T(128)}, u32[]{:S(2)}) copy-start(s32[2]{0:T(128)} %param.17) | copy-start | bytes 28
  113.1 362.6 %copy-start.3 = (bf16[256,3840]{1,0:T(8,128)(2,1)}, bf16[256,3840]{1,0:T(8,128)(2,1)S(1)}, u32[]{:S(2)}) copy-start(bf16[256,3840]{1,0:T(8,128)(2,1)S(1)} %convolution_convert_fusion) | copy-start | bytes 5898244
  113.1 79.9 %copy-start.6 = (s32[2,16]{1,0:T(2,128)S(1)}, s32[2,16]{1,0:T(2,128)}, u32[]{:S(2)}) copy-start(s32[2,16]{1,0:T(2,128)} %param.15) | copy-start | bytes 388
  114.4 361.3 %all-reduce.4.cloned.1.call-start = ((), (), s32[]{:S(2)}) async-start(), calls=%async_computation.3 | async-start | bytes 2621440 | tf_op jit(solution)/shard_map/psum | solution.py:21
  172.7 309.3 %collective-permute-start = (bf16[1024,2560]{1,0:T(8,128)(2,1)}, bf16[1024,2560]{1,0:T(8,128)(2,1)}, u32[]{:S(2)}, u32[]{:S(2)}) collective-permute-start(bf16[1024,2560]{1,0:T(8,128)(2,1)} %all-gather.6.cloned.1.call-done), channel_id=1, source_target_pairs={{0,8},{4,12},{8,16},{12,20},{16,24},{20,28},{24,32},{28,36},{32,40... | collective-permute-start | bytes 15728648 | tf_op jit(solution)/shard_map/ppermute | solution.py:16
  176.0 311.4 %collective-permute-start.1 = (bf16[1024,2560]{1,0:T(8,128)(2,1)}, bf16[1024,2560]{1,0:T(8,128)(2,1)}, u32[]{:S(2)}, u32[]{:S(2)}) collective-permute-start(bf16[1024,2560]{1,0:T(8,128)(2,1)} %all-gather.6.cloned.1.call-done), channel_id=1, source_target_pairs={{0,4},{4,8},{8,12},{12,16},{16,20},{20,24},{24,28},{28,32},{32,36}... | collective-permute-start | bytes 15728648 | tf_op jit(solution)/shard_map/ppermute | solution.py:16
  177.9 317.6 %collective-permute-start.2 = (bf16[1024,2560]{1,0:T(8,128)(2,1)}, bf16[1024,2560]{1,0:T(8,128)(2,1)}, u32[]{:S(2)}, u32[]{:S(2)}) collective-permute-start(bf16[1024,2560]{1,0:T(8,128)(2,1)} %all-gather.6.cloned.1.call-done), channel_id=1, source_target_pairs={{4,0},{8,4},{12,8},{16,12},{20,16},{24,20},{28,24},{32,28},{36,32}... | collective-permute-start | bytes 15728648 | tf_op jit(solution)/shard_map/ppermute | solution.py:16
  181.6 319.1 %collective-permute-start.3 = (bf16[1024,2560]{1,0:T(8,128)(2,1)}, bf16[1024,2560]{1,0:T(8,128)(2,1)}, u32[]{:S(2)}, u32[]{:S(2)}) collective-permute-start(bf16[1024,2560]{1,0:T(8,128)(2,1)} %all-gather.6.cloned.1.call-done), channel_id=1, source_target_pairs={{8,0},{12,4},{16,8},{20,12},{24,16},{28,20},{32,24},{36,28},{40,32... | collective-permute-start | bytes 15728648 | tf_op jit(solution)/shard_map/ppermute | solution.py:16
  192.4 460.0 %all-gather.8.cloned.1.call-start = ((), (), s32[]{:S(2)}) async-start(), calls=%async_computation.2 | async-start | bytes 4096000 | tf_op jit(solution)/shard_map/all_gather | solution.py:36
  482.0 10.8 %slice-start.1 = ((s8[5242880]{0:T(1024)(128)(4,1)}), s8[4194304]{0:T(1024)(128)(4,1)S(1)}, s32[]{:S(2)}) async-start(s8[5242880]{0:T(1024)(128)(4,1)} %bitcast.66), calls=%async_computation.5 | async-start | bytes 8388608
  487.3 5.5 slice-start.2
  500.7 5.3 slice-start
  500.7 5.3 copy-start.9
  566.6 11.8 %copy-start.7 = (bf16[2,128,1280]{2,1,0:T(8,128)(2,1)S(1)}, bf16[2,128,1280]{2,1,0:T(8,128)(2,1)}, u32[]{:S(2)}) copy-start(bf16[2,128,1280]{2,1,0:T(8,128)(2,1)} %get-tuple-element.164) | copy-start | bytes 1966084 | tf_op jit(solution)/shard_map/while
  578.4 0.8 copy-start.8
  639.8 11.8 %copy-start.7 = (bf16[2,128,1280]{2,1,0:T(8,128)(2,1)S(1)}, bf16[2,128,1280]{2,1,0:T(8,128)(2,1)}, u32[]{:S(2)}) copy-start(bf16[2,128,1280]{2,1,0:T(8,128)(2,1)} %get-tuple-element.164) | copy-start | bytes 1966084 | tf_op jit(solution)/shard_map/while
  651.6 0.8 copy-start.8
  652.5 4.1 copy-start.1
Sparse Core Ops, SparseCore 0:
  9.0 97.4 all-gather.3
  114.5 58.1 all-gather.5
  192.6 283.1 all-reduce.3
  477.3 40.0 all-gather.7
where the time goes:
time: 666 us; the launch traced here: 663 us
  waiting for transfers between devices  436 us (65%)
  local copies, waits for them, and re-layouts  118 us (18%)
  matrix products  56.3 us (8%)
  other arithmetic  22.2 us (3%)
  between operations  18.4 us (3%)
  starting transfers between devices  11.7 us (2%)
    psum x1, waiting for transfers between devices, broadcast(): return lax.psum(jnp.where(mine, shard, jnp.zeros_like(shard)), axis)  283 us
    all_gather x2, waiting for transfers between devices, project(): lax.all_gather(weight, 'fsdp', axis=0, tiled=True)  93.8 us
    all_gather x1, waiting for transfers between devices, local(): group_block = lax.all_gather(keyval, 'fsdp', axis=0, tiled=True)  58.2 us
    while x12, local copies, waits for them, and re-layouts  37.1 us
    gather x2, local copies, waits for them, and re-layouts, per_tile(): tile_source[local_ids]  28.3 us
    dot_general x2, matrix products, attend_tile(): jnp.einsum('hqk,khd->qhd', probs, values_h, preferred_element_type=jnp.fl...  23.2 us
    sub x2, matrix products, attend_tile(): weights_raw = jnp.exp(scores - row_max)  22.4 us
    unnamed x24, local copies, waits for them, and re-layouts  18.7 us
  transfers between devices with their start and end apart: 8, of which 3 were waited for; matrix products, arithmetic and copies ran while one was open for 28% of the time, Pallas kernels for 0%

commit v1 on v0

v1 whole, which is shorter than its diff:
```python
import jax
import jax.numpy as jnp
from jax import lax
from jax.sharding import PartitionSpec as P

HEADS = 16
TILE = 128
KT = 16
GLOBAL = 2
PATCHES = 512
NEAR = 3
REACH = (-2, -1, 1, 2)


def passed_along(block, axis, distance):
    devices = range(lax.axis_size(axis))
    route = [(i - distance, i) for i in devices if i - distance in devices]
    return lax.ppermute(block, axis, route)


def layer_norm(stream, ln_gain, ln_bias):
    stream32 = stream.astype(jnp.float32)
    mean_val = jnp.mean(stream32, axis=-1, keepdims=True)
    centred = stream32 - mean_val
    variance = jnp.mean(centred * centred, axis=-1, keepdims=True)
    scaled = centred * lax.rsqrt(variance + 1e-06)
    return (scaled * ln_gain.astype(jnp.float32) + ln_bias.astype(jnp.float32)).astype(jnp.bfloat16)


def embed(patches, vis_index, frame_table, space_table):
    frame_ids = vis_index // PATCHES
    patch_ids = vis_index % PATCHES
    return (
        patches.astype(jnp.float32)
        + frame_table[frame_ids].astype(jnp.float32)
        + space_table[patch_ids].astype(jnp.float32)
    ).astype(jnp.bfloat16)


def near_tiles(entries, group, group_tiles):
    cand = group * group_tiles + jnp.arange(group_tiles, dtype=jnp.int32)
    named = jnp.any(entries.reshape(-1, 1) == cand[None, :], axis=0)
    rank = jnp.cumsum(named.astype(jnp.int32)) - 1
    local_ids = jnp.arange(group_tiles, dtype=jnp.int32)
    picks = jnp.stack(
        [jnp.sum(jnp.where(named & (rank == j), local_ids, 0)) for j in range(NEAR)]
    )
    return picks, rank


def attend_tile(query_tile, key_values, key_live, feat_width):
    head_size = feat_width // HEADS
    key_rows = key_values.shape[0]
    queries_h = query_tile.reshape(TILE, HEADS, head_size)
    keys_h = key_values[:, :feat_width].reshape(key_rows, HEADS, head_size)
    values_h = key_values[:, feat_width:].reshape(key_rows, HEADS, head_size)
    scores = jnp.einsum(
        "qhd,khd->hqk", queries_h, keys_h, preferred_element_type=jnp.float32
    ) * head_size ** (-0.5)
    scores = jnp.where(key_live[None, None, :], scores, -jnp.inf)
    row_max = jnp.max(scores, axis=-1, keepdims=True)
    weights_raw = jnp.exp(scores - row_max)
    probs = (weights_raw / jnp.sum(weights_raw, axis=-1, keepdims=True)).astype(jnp.bfloat16)
    mixed_h = jnp.einsum("hqk,khd->qhd", probs, values_h, preferred_element_type=jnp.float32)
    return mixed_h.reshape(TILE, feat_width).astype(jnp.bfloat16)


def local(
    patches,
    vis_index,
    kv_list,
    kv_count,
    global_tiles,
    frame_table,
    space_table,
    ln_gain,
    ln_bias,
    w_qkv,
    w_out,
):
    tok_rows = patches.shape[0]
    feat_width = patches.shape[1]
    tile_count = tok_rows // TILE
    fsdp_size = lax.axis_size("fsdp")
    seq_size = lax.axis_size("seq")
    seq_at = lax.axis_index("seq")
    dev_at = seq_at * fsdp_size + lax.axis_index("fsdp")
    group_tiles = tile_count * fsdp_size

    stream = embed(patches, vis_index, frame_table, space_table)

    global_rows = []
    for slot_no in range(GLOBAL):
        tile_id = global_tiles[slot_no]
        mine = tile_id // tile_count == dev_at
        rows = lax.dynamic_slice_in_dim(stream, tile_id % tile_count * TILE, TILE, 0)
        global_rows.append(jnp.where(mine, rows, jnp.zeros_like(rows)))
    global_stream = lax.psum(jnp.concatenate(global_rows, axis=0), ("seq", "fsdp"))

    w_full = lax.all_gather(w_qkv, "fsdp", axis=0, tiled=True)
    normed = layer_norm(stream, ln_gain, ln_bias)
    qkv = jnp.dot(normed, w_full, preferred_element_type=jnp.float32).astype(jnp.bfloat16)
    query = qkv[:, :feat_width]
    keyval = qkv[:, feat_width:]
    global_normed = layer_norm(global_stream, ln_gain, ln_bias)
    global_kv = jnp.dot(
        global_normed, w_full[:, feat_width:], preferred_element_type=jnp.float32
    ).astype(jnp.bfloat16).reshape(GLOBAL, TILE, 2 * feat_width)

    group_block = lax.all_gather(keyval, "fsdp", axis=0, tiled=True).reshape(
        group_tiles, TILE, 2 * feat_width
    )
    seq_lists = lax.all_gather(kv_list, "seq", axis=0, tiled=True)

    near_blocks = []
    near_rank = []
    for reach in REACH:
        distance = -reach
        dest = jnp.clip(seq_at + distance, 0, seq_size - 1)
        dest_lists = lax.dynamic_slice_in_dim(seq_lists, dest * tile_count, tile_count, 0)
        send_ids, unused = near_tiles(dest_lists, seq_at, group_tiles)
        sent = passed_along(group_block[send_ids], "seq", distance)
        near_blocks.append(sent)
        unused2, rank = near_tiles(kv_list, seq_at + reach, group_tiles)
        near_rank.append(rank)
    window = jnp.concatenate([group_block] + near_blocks + [global_kv], axis=0)
    near_rank = jnp.stack(near_rank)

    entry_group = kv_list // group_tiles
    entry_local = kv_list % group_tiles
    reach_of = entry_group - seq_at
    reach_slot = jnp.where(reach_of < 0, reach_of + 2, reach_of + 1)
    reach_slot = jnp.clip(reach_slot, 0, len(REACH) - 1)
    entry_rank = near_rank[reach_slot, entry_local]
    local_lists = jnp.where(
        reach_of == 0, entry_local, group_tiles + NEAR * reach_slot + entry_rank
    )
    global_slots = group_tiles + NEAR * len(REACH) + jnp.arange(GLOBAL, dtype=jnp.int32)

    query_tiles = query.reshape(tile_count, TILE, feat_width)

    def per_tile(tile_args):
        query_tile, local_ids, live_count = tile_args
        slot_live_row = jnp.concatenate(
            [jnp.arange(KT) < live_count, jnp.ones((GLOBAL,), dtype=bool)]
        )
        key_live = jnp.repeat(slot_live_row, TILE)
        key_values = window[jnp.concatenate([local_ids, global_slots])].reshape(
            (KT + GLOBAL) * TILE, 2 * feat_width
        )
        return attend_tile(query_tile, key_values, key_live, feat_width)

    heads_out = lax.map(per_tile, (query_tiles, local_lists, kv_count)).reshape(
        tok_rows, feat_width
    )
    return jnp.dot(
        heads_out,
        lax.all_gather(w_out, "fsdp", axis=0, tiled=True),
        preferred_element_type=jnp.float32,
    ).astype(jnp.bfloat16)


def solution(mesh):
    return jax.shard_map(
        local,
        mesh=mesh,
        in_specs=(
            P(("seq", "fsdp"), None),
            P(("seq", "fsdp")),
            P(("seq", "fsdp"), None),
            P(("seq", "fsdp")),
            P(),
            P(),
            P(),
            P(),
            P(),
            P("fsdp", None),
            P("fsdp", None),
        ),
        out_specs=P(("seq", "fsdp"), None),
        check_vma=False,
    )
```

time: 666 us -> 550 us (0.83)
  waiting for transfers between devices: 436 us -> 296 us
  blocking collectives: 0 us -> 23.9 us
    psum x1, waiting for transfers between devices: 283 us -> 138 us  [local(): lax.psum(jnp.concatenate(global_rows, axis=0), ('seq', 'fsdp'))]
    ppermute x4, waiting for transfers between devices: 0.01 us -> 50.2 us  [passed_along(): return lax.ppermute(block, axis, route)]
    all_gather x3, waiting for transfers between devices: 152 us -> 107 us  [the longest x1 93.8 us: local(): w_full = lax.all_gather(w_qkv, 'fsdp', axis=0, tiled=True)]
    all_gather x0 -> x1, blocking collectives: none -> 23.9 us  [local(): seq_lists = lax.all_gather(kv_list, 'seq', axis=0, tiled=True)]
    concatenate x2 -> x4, other arithmetic: 15.6 us -> 0.91 us  [the longest x1 0.88 us: local(): jnp.concatenate(global_rows, axis=0)]
    gather x4 -> x10, local copies, waits for them, and re-layouts: 30.8 us -> 44.2 us  [the longest x2 22.5 us: per_tile(): window[jnp.concatenate([local_ids, global_slots])]]
    slice x2, local copies, waits for them, and re-layouts: 9.37 us -> 19.3 us  [attend_tile(): keys_h = key_values[:, :feat_width].reshape(key_rows, HEADS, head_size)]
    while x14 -> x4, local copies, waits for them, and re-layouts: 43.4 us -> 35.4 us
  transfers between devices with their start and end apart: 8 -> 8, of which waited for: 3 -> 6; matrix products, arithmetic and copies ran while one was open for 28% -> 32% of each run, Pallas kernels for 0% -> 0%
where the time goes in v1:
time: 550 us; the launch traced here: 548 us
  waiting for transfers between devices  296 us (54%)
  local copies, waits for them, and re-layouts  115 us (21%)
  matrix products  61 us (11%)
  blocking collectives  23.9 us (4%)
  between operations  20.2 us (4%)
  other arithmetic  19.5 us (4%)
  starting transfers between devices  11.8 us (2%)
    psum x1, waiting for transfers between devices, local(): lax.psum(jnp.concatenate(global_rows, axis=0), ('seq', 'fsdp'))  138 us
    all_gather x1, waiting for transfers between devices, local(): w_full = lax.all_gather(w_qkv, 'fsdp', axis=0, tiled=True)  93.8 us
    ppermute x4, waiting for transfers between devices, passed_along(): return lax.ppermute(block, axis, route)  50.2 us
    while x4, local copies, waits for them, and re-layouts  35.4 us
    all_gather x1, blocking collectives, local(): seq_lists = lax.all_gather(kv_list, 'seq', axis=0, tiled=True)  23.9 us
    dot_general x2, matrix products, attend_tile(): jnp.einsum('hqk,khd->qhd', probs, values_h, preferred_element_type=jnp.fl...  23.1 us
    sub x2, matrix products, attend_tile(): weights_raw = jnp.exp(scores - row_max)  22.6 us
    gather x2, local copies, waits for them, and re-layouts, per_tile(): window[jnp.concatenate([local_ids, global_slots])]  22.5 us
  transfers between devices with their start and end apart: 8, of which 6 were waited for; matrix products, arithmetic and copies ran while one was open for 32% of the time, Pallas kernels for 0%

profile of v1, /device:TPU:24, one launch (start us, length us, event | category | flops | bytes accessed | tf_op | source)
XLA Modules:
  0.0 548.3 jit_solution(2590682510310247328)
XLA Ops:
  10.2 1.3 gather_fusion.2
  11.5 1.2 gather_fusion.3
  13.5 93.8 %all-gather.5.cloned.1.call-done = bf16[1280,3840]{1,0:T(8,128)(2,1)} async-done(((bf16[320,3840]{1,0:T(8,128)(2,1)}), bf16[1280,3840]{1,0:T(8,128)(2,1)}) %all-gather.5.cloned.1.call-update) | async-done | bytes 9830416 | tf_op jit(solution)/shard_map/all_gather | solution.py:100
  107.3 6.6 %convolution_convert_fusion = bf16[256,3840]{1,0:T(8,128)(2,1)S(1)} fusion(bf16[1280,3840]{1,0:T(8,128)(2,1)} %all-gather.5.cloned.1.call-done, bf16[256,1280]{1,0:T(8,128)(2,1)S(1)} %get-tuple-element.114, f32[1280]{0:T(1024)S(1)} %convert_element_type.182, f32[1280]{0:T(1024)S(1)} %convert_element_type.181, f32[256]{0:T(256)S(1)} %add_rsqrt_fusion.1, ...), kind=kOutput, calls=%fused_computation.34 | convolution fusion | flops 2519531520 | bytes 12464128 | tf_op jit(solution)/shard_map/dot_general | solution.py:102
  113.9 1.2 copy-done.4
  115.2 1.2 slice.46
  122.4 0.9 pad_maximum_fusion
  124.2 23.9 %all-gather = s32[32,2,16]{2,1,0:T(2,128)S(1)} all-gather(s32[1,2,16]{2,1,0:T(2,128)S(1)} %bitcast.181), channel_id=1, replica_groups=mesh['seq'=32,'fsdp'=4] {'seq'}, dimensions={0}, use_global_device_ids=true | all-gather | bytes 4224 | tf_op jit(solution)/shard_map/all_gather | solution.py:113
  148.8 0.7 fusion.65
  149.7 0.7 fusion.68
  150.5 3.8 fusion.61
  154.5 0.7 fusion.71
  155.4 0.7 fusion.74
  156.1 3.8 fusion.63
  161.1 0.8 gather_fusion.1
  162.0 13.0 %all-gather.7.cloned.1.call-done = bf16[1024,2560]{1,0:T(8,128)(2,1)} async-done(((bf16[256,2560]{1,0:T(8,128)(2,1)}), bf16[1024,2560]{1,0:T(8,128)(2,1)}) %all-gather.7.cloned.1.call-update) | async-done | bytes 5242896 | tf_op jit(solution)/shard_map/all_gather | solution.py:110
  175.0 4.6 gather_fusion.4
  179.5 3.3 collective-permute-start
  182.9 138.0 %all-reduce.3.cloned.1.call-done = bf16[256,1280]{1,0:T(8,128)(2,1)} async-done(((bf16[256,1280]{1,0:T(8,128)(2,1)}), bf16[256,1280]{1,0:T(8,128)(2,1)}) %all-reduce.3.cloned.1.call-update) | async-done | bytes 655376 | tf_op jit(solution)/shard_map/psum | solution.py:98
  320.8 1.3 convert_reduce_fusion
  322.2 4.5 gather_fusion.5
  326.7 2.4 collective-permute-start.1
  329.5 4.6 gather_fusion.6
  334.0 3.1 collective-permute-start.2
  337.2 4.7 gather_fusion.7
  341.9 2.9 collective-permute-start.3
  344.8 4.8 fusion.17
  350.0 1.7 constant_dynamic-update-slice_fusion.5
  351.7 1.3 collective-permute-done.1
  353.0 1.7 constant_dynamic-update-slice_fusion.4
  354.6 19.7 %collective-permute-done.2 = bf16[3,128,2560]{2,1,0:T(8,128)(2,1)} collective-permute-done((bf16[3,128,2560]{2,1,0:T(8,128)(2,1)}, bf16[3,128,2560]{2,1,0:T(8,128)(2,1)}, u32[]{:S(2)}, u32[]{:S(2)}) %collective-permute-start.2) | collective-permute-done | bytes 1966112 | tf_op jit(solution)/shard_map/ppermute | solution.py:18
  374.4 1.7 constant_dynamic-update-slice_fusion.3
  376.1 29.2 %collective-permute-done.3 = bf16[3,128,2560]{2,1,0:T(8,128)(2,1)S(1)} collective-permute-done((bf16[3,128,2560]{2,1,0:T(8,128)(2,1)}, bf16[3,128,2560]{2,1,0:T(8,128)(2,1)S(1)}, u32[]{:S(2)}, u32[]{:S(2)}) %collective-permute-start.3) | collective-permute-done | bytes 1966112 | tf_op jit(solution)/shard_map/ppermute | solution.py:18
  405.5 5.0 copy-done.2
  410.5 126.8 %while.11 = (s32[]{:T(128)}, bf16[2,128,1280]{2,1,0:T(8,128)(2,1)S(1)}, s32[2,16]{1,0:T(2,128)S(1)}, bf16[22,128,2560]{2,1,0:T(8,128)(2,1)}, s32[2]{0:T(128)S(1)...) while((s32[]{:T(128)}, bf16[2,128,1280]{2,1,0:T(8,128)(2,1)S(1)}, ...), condition=%wide.region_36.37_spmd.clone, body=%wide.region_33.36_spmd.clone.sunk | while | flops 1538428160 | bytes 123626584 | solution.py:153
  410.6 11.3 %gather_fusion = bf16[18,128,2560]{2,1,0:T(8,128)(2,1)} fusion(bf16[22,128,2560]{2,1,0:T(8,128)(2,1)} %get-tuple-element.205, s32[1024]{0:T(1024)S(1)} %pad_clamp_fusion.8), kind=kCustom, calls=%fused_computation.clone.clone.1 | custom fusion | bytes 23593032 | tf_op jit(solution)/shard_map/while/body/eval_jaxpr/gather | solution.py:148
  421.9 9.7 %fusion.102 = (bf16[2304,1280]{1,0:T(8,128)(2,1)}, bf16[2304,1280]{1,0:T(8,128)(2,1)}) fusion(bf16[2304,2560]{1,0:T(8,128)(2,1)} %bitcast.166), kind=kLoop, calls=%fused_computation.186.clone.1 | loop fusion | bytes 23592960 | tf_op jit(solution)/shard_map/while/body/eval_jaxpr/slice | solution.py:55
  431.6 8.9 %copy.38 = bf16[2304,1280]{0,1:T(8,128)(2,1)} copy(bf16[2304,1280]{1,0:T(8,128)(2,1)} %get-tuple-element.183) | data formatting | bytes 11796480 | tf_op jit(solution)/shard_map/while
  442.0 11.3 %fusion.103 = (f32[16,128]{1,0:T(8,128)S(1)}, f32[16,128,2304]{2,1,0:T(8,128)}) fusion(pred[2304]{0:T(1024)(128)(4,1)S(1)} %broadcast_bitcast_fusion.2, bf16[128,16,80]{0,2,1:T(8,128)(2,1)S(1)} %bitcast.176, bf16[2304,16,80]{0,2,1:T(8,128)(2,1)} %bitcast.167), kind=kOutput, calls=%fused_computation.187.clone.1 | convolution fusion | flops 773851392 | bytes 25110784 | tf_op jit(solution)/shard_map/while/body/eval_jaxpr/sub | solution.py:62
  453.3 8.9 %copy.36 = bf16[2304,1280]{0,1:T(8,128)(2,1)} copy(bf16[2304,1280]{1,0:T(8,128)(2,1)} %get-tuple-element.182) | data formatting | bytes 11796480 | tf_op jit(solution)/shard_map/while
  462.1 11.5 %fusion.104 = bf16[16,80,128]{2,1,0:T(8,128)(2,1)S(1)} fusion(bf16[2304,16,80]{0,2,1:T(8,128)(2,1)} %bitcast.168, f32[16,128,2304]{2,1,0:T(8,128)} %get-tuple-element.184, f32[16,128]{1,0:T(8,128)S(1)} %get-tuple-element.185), kind=kOutput, calls=%fused_computation.19.clone.1 | convolution fusion | flops 764575744 | bytes 25108480 | tf_op jit(solution)/shard_map/while/body/eval_jaxpr/hqk,khd->qhd/dot_general | solution.py:64
  474.0 11.3 %gather_fusion = bf16[18,128,2560]{2,1,0:T(8,128)(2,1)} fusion(bf16[22,128,2560]{2,1,0:T(8,128)(2,1)} %get-tuple-element.205, s32[1024]{0:T(1024)S(1)} %pad_clamp_fusion.8), kind=kCustom, calls=%fused_computation.clone.clone.1 | custom fusion | bytes 23593032 | tf_op jit(solution)/shard_map/while/body/eval_jaxpr/gather | solution.py:148
  485.3 9.7 %fusion.102 = (bf16[2304,1280]{1,0:T(8,128)(2,1)}, bf16[2304,1280]{1,0:T(8,128)(2,1)}) fusion(bf16[2304,2560]{1,0:T(8,128)(2,1)} %bitcast.166), kind=kLoop, calls=%fused_computation.186.clone.1 | loop fusion | bytes 23592960 | tf_op jit(solution)/shard_map/while/body/eval_jaxpr/slice | solution.py:55
  494.9 8.9 %copy.38 = bf16[2304,1280]{0,1:T(8,128)(2,1)} copy(bf16[2304,1280]{1,0:T(8,128)(2,1)} %get-tuple-element.183) | data formatting | bytes 11796480 | tf_op jit(solution)/shard_map/while
  505.4 11.3 %fusion.103 = (f32[16,128]{1,0:T(8,128)S(1)}, f32[16,128,2304]{2,1,0:T(8,128)}) fusion(pred[2304]{0:T(1024)(128)(4,1)S(1)} %broadcast_bitcast_fusion.2, bf16[128,16,80]{0,2,1:T(8,128)(2,1)S(1)} %bitcast.176, bf16[2304,16,80]{0,2,1:T(8,128)(2,1)} %bitcast.167), kind=kOutput, calls=%fused_computation.187.clone.1 | convolution fusion | flops 773851392 | bytes 25110784 | tf_op jit(solution)/shard_map/while/body/eval_jaxpr/sub | solution.py:62
  516.7 8.9 %copy.36 = bf16[2304,1280]{0,1:T(8,128)(2,1)} copy(bf16[2304,1280]{1,0:T(8,128)(2,1)} %get-tuple-element.182) | data formatting | bytes 11796480 | tf_op jit(solution)/shard_map/while
  525.5 11.5 %fusion.104 = bf16[16,80,128]{2,1,0:T(8,128)(2,1)S(1)} fusion(bf16[2304,16,80]{0,2,1:T(8,128)(2,1)} %bitcast.168, f32[16,128,2304]{2,1,0:T(8,128)} %get-tuple-element.184, f32[16,128]{1,0:T(8,128)S(1)} %get-tuple-element.185), kind=kOutput, calls=%fused_computation.19.clone.1 | convolution fusion | flops 764575744 | bytes 25108480 | tf_op jit(solution)/shard_map/while/body/eval_jaxpr/hqk,khd->qhd/dot_general | solution.py:64
  537.3 3.9 convolution_convert_fusion.1
  (116 shorter events, 12.4 us)
Async XLA Ops:
  7.4 4.1 copy-start
  7.4 2.8 copy-start.3
  7.4 99.9 %all-gather.5.cloned.1.call-start = ((), (), s32[]{:S(2)}) async-start(), calls=%async_computation | async-start | bytes 12288000 | tf_op jit(solution)/shard_map/all_gather | solution.py:100
  8.1 166.9 %all-gather.7.cloned.1.call-start = ((), (), s32[]{:S(2)}) async-start(), calls=%async_computation.1 | async-start | bytes 6553600 | tf_op jit(solution)/shard_map/all_gather | solution.py:110
  11.5 1.3 copy-start.6
  113.9 1.3 copy-start.4
  115.2 1.2 copy-start.8
  116.3 7.7 %copy-start.7 = (s32[2,16]{1,0:T(2,128)S(1)}, s32[2,16]{1,0:T(2,128)}, u32[]{:S(2)}) copy-start(s32[2,16]{1,0:T(2,128)} %param.15) | copy-start | bytes 388
  116.4 204.5 %all-reduce.3.cloned.1.call-start = ((), (), s32[]{:S(2)}) async-start(), calls=%async_computation.2 | async-start | bytes 1310720 | tf_op jit(solution)/shard_map/psum | solution.py:98
  123.3 414.0 %all-gather.9.cloned.1.call-start = ((), (), s32[]{:S(2)}) async-start(), calls=%async_computation.3 | async-start | bytes 4096000 | tf_op jit(solution)/shard_map/all_gather | solution.py:158
  179.5 170.4 %collective-permute-start = (bf16[3,128,2560]{2,1,0:T(8,128)(2,1)}, bf16[3,128,2560]{2,1,0:T(8,128)(2,1)}, u32[]{:S(2)}, u32[]{:S(2)}) collective-permute-start(bf16[3,128,2560]{2,1,0:T(8,128)(2,1)} %gather_fusion.4), channel_id=1, source_target_pairs={{0,8},{4,12},{8,16},{12,20},{16,24},{20,28},{24,32},{28,36},{32,40... | collective-permute-start | bytes 5898248 | tf_op jit(solution)/shard_map/ppermute | solution.py:18
  320.8 8.3 %copy-start.5 = (bf16[256,1280]{1,0:T(8,128)(2,1)S(1)}, bf16[256,1280]{1,0:T(8,128)(2,1)}, u32[]{:S(2)}) copy-start(bf16[256,1280]{1,0:T(8,128)(2,1)} %all-reduce.3.cloned.1.call-done) | copy-start | bytes 1966084
  326.7 26.3 %collective-permute-start.1 = (bf16[3,128,2560]{2,1,0:T(8,128)(2,1)}, bf16[3,128,2560]{2,1,0:T(8,128)(2,1)}, u32[]{:S(2)}, u32[]{:S(2)}) collective-permute-start(bf16[3,128,2560]{2,1,0:T(8,128)(2,1)} %gather_fusion.5), channel_id=1, source_target_pairs={{0,4},{4,8},{8,12},{12,16},{16,20},{20,24},{24,28},{28,32},{32,36}... | collective-permute-start | bytes 5898248 | tf_op jit(solution)/shard_map/ppermute | solution.py:18
  334.0 40.3 %collective-permute-start.2 = (bf16[3,128,2560]{2,1,0:T(8,128)(2,1)}, bf16[3,128,2560]{2,1,0:T(8,128)(2,1)}, u32[]{:S(2)}, u32[]{:S(2)}) collective-permute-start(bf16[3,128,2560]{2,1,0:T(8,128)(2,1)} %gather_fusion.6), channel_id=1, source_target_pairs={{4,0},{8,4},{12,8},{16,12},{20,16},{24,20},{28,24},{32,28},{36,32}... | collective-permute-start | bytes 5898248 | tf_op jit(solution)/shard_map/ppermute | solution.py:18
  337.2 12.4 %slice-start = ((s8[5242880]{0:T(1024)(128)(4,1)}), s8[1048576]{0:T(1024)(128)(4,1)S(1)}, s32[]{:S(2)}) async-start(s8[5242880]{0:T(1024)(128)(4,1)} %bitcast.173), calls=%async_computation.4 | async-start | bytes 2097152
  341.9 7.7 %slice-start.1 = ((s8[5242880]{0:T(1024)(128)(4,1)}), s8[4194304]{0:T(1024)(128)(4,1)S(1)}, s32[]{:S(2)}) async-start(s8[5242880]{0:T(1024)(128)(4,1)} %bitcast.173), calls=%async_computation.5 | async-start | bytes 8388608
  341.9 63.3 %collective-permute-start.3 = (bf16[3,128,2560]{2,1,0:T(8,128)(2,1)}, bf16[3,128,2560]{2,1,0:T(8,128)(2,1)S(1)}, u32[]{:S(2)}, u32[]{:S(2)}) collective-permute-start(bf16[3,128,2560]{2,1,0:T(8,128)(2,1)} %gather_fusion.7), channel_id=1, source_target_pairs={{8,0},{12,4},{16,8},{20,12},{24,16},{28,20},{32,24},{36,28},{40,32... | collective-permute-start | bytes 5898248 | tf_op jit(solution)/shard_map/ppermute | solution.py:18
  376.0 34.5 %slice-start.2 = ((bf16[256,3840]{1,0:T(8,128)(2,1)}), bf16[256,1280]{1,0:T(8,128)(2,1)S(1)}, s32[]{:S(2)}) async-start(bf16[256,3840]{1,0:T(8,128)(2,1)} %copy-done.4), calls=%async_computation.6 | async-start | bytes 1310720 | tf_op jit(solution)/shard_map/slice | solution.py:103
  376.1 34.5 %copy-start.9 = (s32[2]{0:T(128)S(1)}, s32[2]{0:T(128)}, u32[]{:S(2)}) copy-start(s32[2]{0:T(128)} %param.16) | copy-start | bytes 28
  405.5 5.0 copy-start.2
  537.3 3.9 copy-start.1
Sparse Core Ops, SparseCore 0:
  9.8 97.4 all-gather.4
  116.5 58.4 all-gather.6
  176.6 41.3 all-gather.8
Sparse Core Ops, SparseCore 1:
  123.4 197.4 all-reduce.2

commit v2 on v1

--- a/solution.py
+++ b/solution.py
@@ -89,13 +89,28 @@
 
     stream = embed(patches, vis_index, frame_table, space_table)
 
+    dev_count = seq_size * fsdp_size
     global_rows = []
+    owners = []
     for slot_no in range(GLOBAL):
         tile_id = global_tiles[slot_no]
-        mine = tile_id // tile_count == dev_at
-        rows = lax.dynamic_slice_in_dim(stream, tile_id % tile_count * TILE, TILE, 0)
-        global_rows.append(jnp.where(mine, rows, jnp.zeros_like(rows)))
-    global_stream = lax.psum(jnp.concatenate(global_rows, axis=0), ("seq", "fsdp"))
+        owners.append(tile_id // tile_count)
+        global_rows.append(
+            lax.dynamic_slice_in_dim(stream, tile_id % tile_count * TILE, TILE, 0)
+        )
+    global_stream = jnp.stack(global_rows)
+    owners = jnp.stack(owners)
+    bit_order = sorted(range(dev_count.bit_length() - 1), key=lambda b: -b)
+    done_bits = 0
+    for bit in bit_order:
+        step = 1 << bit
+        held = ((dev_at ^ owners) & ~done_bits) == 0
+        got = lax.ppermute(
+            global_stream, ("seq", "fsdp"), [(i, i ^ step) for i in range(dev_count)]
+        )
+        global_stream = jnp.where(held[:, None, None], global_stream, got)
+        done_bits |= step
+    global_stream = global_stream.reshape(GLOBAL * TILE, feat_width)
 
     w_full = lax.all_gather(w_qkv, "fsdp", axis=0, tiled=True)
     normed = layer_norm(stream, ln_gain, ln_bias)
@@ -110,18 +125,12 @@
     group_block = lax.all_gather(keyval, "fsdp", axis=0, tiled=True).reshape(
         group_tiles, TILE, 2 * feat_width
     )
-    seq_lists = lax.all_gather(kv_list, "seq", axis=0, tiled=True)
-
     near_blocks = []
     near_rank = []
     for reach in REACH:
-        distance = -reach
-        dest = jnp.clip(seq_at + distance, 0, seq_size - 1)
-        dest_lists = lax.dynamic_slice_in_dim(seq_lists, dest * tile_count, tile_count, 0)
-        send_ids, unused = near_tiles(dest_lists, seq_at, group_tiles)
-        sent = passed_along(group_block[send_ids], "seq", distance)
-        near_blocks.append(sent)
-        unused2, rank = near_tiles(kv_list, seq_at + reach, group_tiles)
+        picks, rank = near_tiles(kv_list, seq_at + reach, group_tiles)
+        asked = passed_along(picks, "seq", reach)
+        near_blocks.append(passed_along(group_block[asked], "seq", -reach))
         near_rank.append(rank)
     window = jnp.concatenate([group_block] + near_blocks + [global_kv], axis=0)
     near_rank = jnp.stack(near_rank)

time: 550 us -> 481 us (0.87)
  waiting for transfers between devices: 296 us -> 235 us
  blocking collectives: 23.9 us -> 0 us
  starting transfers between devices: 11.8 us -> 31.8 us
    psum x1 -> x0, waiting for transfers between devices: 138 us -> none  [local(): lax.psum(jnp.concatenate(global_rows, axis=0), ('seq', 'fsdp'))]
    ppermute x0 -> x7, waiting for transfers between devices: none -> 91 us  [local(): lax.ppermute(global_stream, ('seq', 'fsdp'), [(i, i ^ step) for i in rang...]
    all_gather x1 -> x0, blocking collectives: 23.9 us -> none  [local(): seq_lists = lax.all_gather(kv_list, 'seq', axis=0, tiled=True)]
    all_gather x1, waiting for transfers between devices: 13 us -> 0.02 us  [local(): lax.all_gather(keyval, 'fsdp', axis=0, tiled=True)]
    ppermute x0 -> x7, starting transfers between devices: none -> 10.3 us  [local(): lax.ppermute(global_stream, ('seq', 'fsdp'), [(i, i ^ step) for i in rang...]
    ppermute x4 -> x8, starting transfers between devices: 11.7 us -> 21.4 us  [passed_along(): return lax.ppermute(block, axis, route)]
    another operation x8 -> x9, other arithmetic: 1.46 us -> 8.64 us  [the longest x4 7.85 us: near_tiles(): jnp.stack([jnp.sum(jnp.where(named & (rank == j), local_ids, 0)) for j in...]
    select_n x3 -> x8, other arithmetic: 7.73 us -> 0.83 us  [the longest x6 0.82 us: local(): global_stream = jnp.where(held[:, None, None], global_stream, got)]
  transfers between devices with their start and end apart: 8 -> 18, of which waited for: 6 -> 10; matrix products, arithmetic and copies ran while one was open for 32% -> 37% of each run, Pallas kernels for 0% -> 0%
where the time goes in v2:
time: 481 us; the launch traced here: 480 us
  waiting for transfers between devices  235 us (49%)
  local copies, waits for them, and re-layouts  115 us (24%)
  matrix products  60.9 us (13%)
  starting transfers between devices  31.8 us (7%)
  between operations  18.8 us (4%)
  other arithmetic  17.9 us (4%)
    all_gather x1, waiting for transfers between devices, local(): w_full = lax.all_gather(w_qkv, 'fsdp', axis=0, tiled=True)  93.8 us
    ppermute x7, waiting for transfers between devices, local(): lax.ppermute(global_stream, ('seq', 'fsdp'), [(i, i ^ step) for i in rang...  91 us
    ppermute x8, waiting for transfers between devices, passed_along(): return lax.ppermute(block, axis, route)  49.3 us
    while x4, local copies, waits for them, and re-layouts  35.4 us
    dot_general x2, matrix products, attend_tile(): jnp.einsum('hqk,khd->qhd', probs, values_h, preferred_element_type=jnp.fl...  23.1 us
    sub x2, matrix products, attend_tile(): weights_raw = jnp.exp(scores - row_max)  22.6 us
    gather x2, local copies, waits for them, and re-layouts, per_tile(): window[jnp.concatenate([local_ids, global_slots])]  22.5 us
    ppermute x8, starting transfers between devices, passed_along(): return lax.ppermute(block, axis, route)  21.4 us
  transfers between devices with their start and end apart: 18, of which 10 were waited for; matrix products, arithmetic and copies ran while one was open for 37% of the time, Pallas kernels for 0%

profile of v2, /device:TPU:24, one launch (start us, length us, event | category | flops | bytes accessed | tf_op | source)
XLA Modules:
  0.0 479.6 jit_solution(12287502584570003710)
XLA Ops:
  12.6 93.8 %all-gather.4.cloned.1.call-done = bf16[1280,3840]{1,0:T(8,128)(2,1)} async-done(((bf16[320,3840]{1,0:T(8,128)(2,1)}), bf16[1280,3840]{1,0:T(8,128)(2,1)}) %all-gather.4.cloned.1.call-update) | async-done | bytes 9830416 | tf_op jit(solution)/shard_map/all_gather | solution.py:115
  106.5 6.6 %convolution_convert_fusion = bf16[256,3840]{1,0:T(8,128)(2,1)S(1)} fusion(bf16[1280,3840]{1,0:T(8,128)(2,1)} %all-gather.4.cloned.1.call-done, bf16[256,1280]{1,0:T(8,128)(2,1)S(1)} %get-tuple-element.108, f32[1280]{0:T(1024)S(1)} %convert_element_type.133, f32[1280]{0:T(1024)S(1)} %convert_element_type.132, f32[256]{0:T(256)S(1)} %add_rsqrt_fusion, ...), kind=kOutput, calls=%fused_computation.34 | convolution fusion | flops 2519531520 | bytes 12464128 | tf_op jit(solution)/shard_map/dot_general | solution.py:117
  120.3 3.1 collective-permute-start.8
  124.8 13.3 %collective-permute-done.8 = bf16[2,128,1280]{2,1,0:T(8,128)(2,1)S(1)} collective-permute-done((bf16[2,128,1280]{2,1,0:T(8,128)(2,1)S(1)}, bf16[2,128,1280]{2,1,0:T(8,128)(2,1)S(1)}, u32[]{:S(2)}, u32[]{:S(2)}) %collective-permute-start.8) | collective-permute-done | bytes 655392 | tf_op jit(solution)/shard_map/ppermute | solution.py:108
  140.3 13.6 %collective-permute-done.9 = bf16[2,128,1280]{2,1,0:T(8,128)(2,1)S(1)} collective-permute-done((bf16[2,128,1280]{2,1,0:T(8,128)(2,1)S(1)}, bf16[2,128,1280]{2,1,0:T(8,128)(2,1)S(1)}, u32[]{:S(2)}, u32[]{:S(2)}) %collective-permute-start.9) | collective-permute-done | bytes 655392 | tf_op jit(solution)/shard_map/ppermute | solution.py:108
  156.2 2.0 pad_add_fusion.1
  158.1 1.9 collective-permute-start
  161.0 2.0 pad_add_fusion.2
  162.9 1.9 collective-permute-start.2
  164.8 5.5 %collective-permute-done.10 = bf16[2,128,1280]{2,1,0:T(8,128)(2,1)S(1)} collective-permute-done((bf16[2,128,1280]{2,1,0:T(8,128)(2,1)S(1)}, bf16[2,128,1280]{2,1,0:T(8,128)(2,1)S(1)}, u32[]{:S(2)}, u32[]{:S(2)}) %collective-permute-start.10) | collective-permute-done | bytes 655392 | tf_op jit(solution)/shard_map/ppermute | solution.py:108
  172.2 2.0 pad_add_fusion.3
  174.2 1.9 collective-permute-start.4
  176.3 8.0 %collective-permute-done.11 = bf16[2,128,1280]{2,1,0:T(8,128)(2,1)S(1)} collective-permute-done((bf16[2,128,1280]{2,1,0:T(8,128)(2,1)S(1)}, bf16[2,128,1280]{2,1,0:T(8,128)(2,1)S(1)}, u32[]{:S(2)}, u32[]{:S(2)}) %collective-permute-start.11) | collective-permute-done | bytes 655392 | tf_op jit(solution)/shard_map/ppermute | solution.py:108
  185.3 2.0 pad_add_fusion.4
  187.2 3.9 collective-permute-start.6
  191.3 2.9 collective-permute-start.13
  195.3 20.4 %collective-permute-done.13 = bf16[2,128,1280]{2,1,0:T(8,128)(2,1)S(1)} collective-permute-done((bf16[2,128,1280]{2,1,0:T(8,128)(2,1)S(1)}, bf16[2,128,1280]{2,1,0:T(8,128)(2,1)S(1)}, u32[]{:S(2)}, u32[]{:S(2)}) %collective-permute-start.13) | collective-permute-done | bytes 655392 | tf_op jit(solution)/shard_map/ppermute | solution.py:108
  216.2 30.2 %collective-permute-done.14 = bf16[2,128,1280]{2,1,0:T(8,128)(2,1)S(1)} collective-permute-done((bf16[2,128,1280]{2,1,0:T(8,128)(2,1)S(1)}, bf16[2,128,1280]{2,1,0:T(8,128)(2,1)S(1)}, u32[]{:S(2)}, u32[]{:S(2)}) %collective-permute-start.14) | collective-permute-done | bytes 655392 | tf_op jit(solution)/shard_map/ppermute | solution.py:108
  246.8 4.5 gather_fusion.4
  251.3 2.3 collective-permute-start.1
  254.0 4.5 gather_fusion.5
  258.5 1.9 collective-permute-start.3
  260.4 4.6 gather_fusion.6
  265.0 3.6 collective-permute-start.5
  269.0 4.7 gather_fusion.7
  273.6 4.0 collective-permute-start.7
  277.6 4.7 fusion.17
  282.7 16.5 %collective-permute-done.1 = bf16[3,128,2560]{2,1,0:T(8,128)(2,1)} collective-permute-done((bf16[3,128,2560]{2,1,0:T(8,128)(2,1)}, bf16[3,128,2560]{2,1,0:T(8,128)(2,1)}, u32[]{:S(2)}, u32[]{:S(2)}) %collective-permute-start.1) | collective-permute-done | bytes 1966112 | tf_op jit(solution)/shard_map/ppermute | solution.py:18
  299.2 1.7 constant_dynamic-update-slice_fusion.5
  300.9 15.2 %collective-permute-done.3 = bf16[3,128,2560]{2,1,0:T(8,128)(2,1)} collective-permute-done((bf16[3,128,2560]{2,1,0:T(8,128)(2,1)}, bf16[3,128,2560]{2,1,0:T(8,128)(2,1)}, u32[]{:S(2)}, u32[]{:S(2)}) %collective-permute-start.3) | collective-permute-done | bytes 1966112 | tf_op jit(solution)/shard_map/ppermute | solution.py:18
  316.2 1.7 constant_dynamic-update-slice_fusion.4
  317.8 1.7 constant_dynamic-update-slice_fusion.3
  319.5 17.5 %collective-permute-done.7 = bf16[3,128,2560]{2,1,0:T(8,128)(2,1)S(1)} collective-permute-done((bf16[3,128,2560]{2,1,0:T(8,128)(2,1)}, bf16[3,128,2560]{2,1,0:T(8,128)(2,1)S(1)}, u32[]{:S(2)}, u32[]{:S(2)}) %collective-permute-start.7) | collective-permute-done | bytes 1966112 | tf_op jit(solution)/shard_map/ppermute | solution.py:18
  337.4 5.0 %copy-done.2 = bf16[22,128,2560]{2,1,0:T(8,128)(2,1)} copy-done((bf16[22,128,2560]{2,1,0:T(8,128)(2,1)}, bf16[22,128,2560]{2,1,0:T(8,128)(2,1)S(1)}, u32[]{:S(2)}) %copy-start.2) | copy-done | bytes 14417944
  342.4 126.8 %while.11 = (s32[]{:T(128)}, bf16[2,128,1280]{2,1,0:T(8,128)(2,1)S(1)}, s32[2,16]{1,0:T(2,128)S(1)}, bf16[22,128,2560]{2,1,0:T(8,128)(2,1)}, s32[2]{0:T(128)S(1)...) while((s32[]{:T(128)}, bf16[2,128,1280]{2,1,0:T(8,128)(2,1)S(1)}, ...), condition=%wide.region_27.28_spmd.clone, body=%wide.region_24.27_spmd.clone.sunk | while | flops 1538428160 | bytes 123626584 | solution.py:162
  342.5 11.3 %gather_fusion = bf16[18,128,2560]{2,1,0:T(8,128)(2,1)} fusion(bf16[22,128,2560]{2,1,0:T(8,128)(2,1)} %get-tuple-element.203, s32[1024]{0:T(1024)S(1)} %pad_clamp_fusion.8), kind=kCustom, calls=%fused_computation.clone.clone.1 | custom fusion | bytes 23593032 | tf_op jit(solution)/shard_map/while/body/eval_jaxpr/gather | solution.py:157
  353.8 9.7 %fusion.97 = (bf16[2304,1280]{1,0:T(8,128)(2,1)}, bf16[2304,1280]{1,0:T(8,128)(2,1)}) fusion(bf16[2304,2560]{1,0:T(8,128)(2,1)} %bitcast.177), kind=kLoop, calls=%fused_computation.184.clone.1 | loop fusion | bytes 23592960 | tf_op jit(solution)/shard_map/while/body/eval_jaxpr/slice | solution.py:55
  363.4 8.9 %copy.34 = bf16[2304,1280]{0,1:T(8,128)(2,1)} copy(bf16[2304,1280]{1,0:T(8,128)(2,1)} %get-tuple-element.181) | data formatting | bytes 11796480 | tf_op jit(solution)/shard_map/while
  373.9 11.3 %fusion.98 = (f32[16,128]{1,0:T(8,128)S(1)}, f32[16,128,2304]{2,1,0:T(8,128)}) fusion(pred[2304]{0:T(1024)(128)(4,1)S(1)} %broadcast_bitcast_fusion.2, bf16[128,16,80]{0,2,1:T(8,128)(2,1)S(1)} %bitcast.187, bf16[2304,16,80]{0,2,1:T(8,128)(2,1)} %bitcast.178), kind=kOutput, calls=%fused_computation.185.clone.1 | convolution fusion | flops 773851392 | bytes 25110784 | tf_op jit(solution)/shard_map/while/body/eval_jaxpr/sub | solution.py:62
  385.1 8.9 %copy.32 = bf16[2304,1280]{0,1:T(8,128)(2,1)} copy(bf16[2304,1280]{1,0:T(8,128)(2,1)} %get-tuple-element.180) | data formatting | bytes 11796480 | tf_op jit(solution)/shard_map/while
  394.0 11.5 %fusion.99 = bf16[16,80,128]{2,1,0:T(8,128)(2,1)S(1)} fusion(bf16[2304,16,80]{0,2,1:T(8,128)(2,1)} %bitcast.179, f32[16,128,2304]{2,1,0:T(8,128)} %get-tuple-element.182, f32[16,128]{1,0:T(8,128)S(1)} %get-tuple-element.183), kind=kOutput, calls=%fused_computation.19.clone.1 | convolution fusion | flops 764575744 | bytes 25108480 | tf_op jit(solution)/shard_map/while/body/eval_jaxpr/hqk,khd->qhd/dot_general | solution.py:64
  405.9 11.3 %gather_fusion = bf16[18,128,2560]{2,1,0:T(8,128)(2,1)} fusion(bf16[22,128,2560]{2,1,0:T(8,128)(2,1)} %get-tuple-element.203, s32[1024]{0:T(1024)S(1)} %pad_clamp_fusion.8), kind=kCustom, calls=%fused_computation.clone.clone.1 | custom fusion | bytes 23593032 | tf_op jit(solution)/shard_map/while/body/eval_jaxpr/gather | solution.py:157
  417.2 9.7 %fusion.97 = (bf16[2304,1280]{1,0:T(8,128)(2,1)}, bf16[2304,1280]{1,0:T(8,128)(2,1)}) fusion(bf16[2304,2560]{1,0:T(8,128)(2,1)} %bitcast.177), kind=kLoop, calls=%fused_computation.184.clone.1 | loop fusion | bytes 23592960 | tf_op jit(solution)/shard_map/while/body/eval_jaxpr/slice | solution.py:55
  426.8 8.9 %copy.34 = bf16[2304,1280]{0,1:T(8,128)(2,1)} copy(bf16[2304,1280]{1,0:T(8,128)(2,1)} %get-tuple-element.181) | data formatting | bytes 11796480 | tf_op jit(solution)/shard_map/while
  437.2 11.3 %fusion.98 = (f32[16,128]{1,0:T(8,128)S(1)}, f32[16,128,2304]{2,1,0:T(8,128)}) fusion(pred[2304]{0:T(1024)(128)(4,1)S(1)} %broadcast_bitcast_fusion.2, bf16[128,16,80]{0,2,1:T(8,128)(2,1)S(1)} %bitcast.187, bf16[2304,16,80]{0,2,1:T(8,128)(2,1)} %bitcast.178), kind=kOutput, calls=%fused_computation.185.clone.1 | convolution fusion | flops 773851392 | bytes 25110784 | tf_op jit(solution)/shard_map/while/body/eval_jaxpr/sub | solution.py:62
  448.5 8.9 %copy.32 = bf16[2304,1280]{0,1:T(8,128)(2,1)} copy(bf16[2304,1280]{1,0:T(8,128)(2,1)} %get-tuple-element.180) | data formatting | bytes 11796480 | tf_op jit(solution)/shard_map/while
  457.4 11.5 %fusion.99 = bf16[16,80,128]{2,1,0:T(8,128)(2,1)S(1)} fusion(bf16[2304,16,80]{0,2,1:T(8,128)(2,1)} %bitcast.179, f32[16,128,2304]{2,1,0:T(8,128)} %get-tuple-element.182, f32[16,128]{1,0:T(8,128)S(1)} %get-tuple-element.183), kind=kOutput, calls=%fused_computation.19.clone.1 | convolution fusion | flops 764575744 | bytes 25108480 | tf_op jit(solution)/shard_map/while/body/eval_jaxpr/hqk,khd->qhd/dot_general | solution.py:64
  469.2 3.9 convolution_convert_fusion.1
  (132 shorter events, 24.7 us)
Async XLA Ops:
  6.5 4.1 copy-start
  6.5 2.8 copy-start.3
  6.5 99.9 %all-gather.4.cloned.1.call-start = ((), (), s32[]{:S(2)}) async-start(), calls=%async_computation | async-start | bytes 12288000 | tf_op jit(solution)/shard_map/all_gather | solution.py:115
  7.3 239.5 %all-gather.6.cloned.1.call-start = ((), (), s32[]{:S(2)}) async-start(), calls=%async_computation.1 | async-start | bytes 6553600 | tf_op jit(solution)/shard_map/all_gather | solution.py:125
  10.6 1.3 copy-start.5
  113.1 1.3 copy-start.4
  114.4 1.2 copy-start.7
  114.4 10.3 %copy-start.6 = (s32[2,16]{1,0:T(2,128)S(1)}, s32[2,16]{1,0:T(2,128)}, u32[]{:S(2)}) copy-start(s32[2,16]{1,0:T(2,128)} %param.15) | copy-start | bytes 388
  115.5 353.7 %all-gather.8.cloned.1.call-start = ((), (), s32[]{:S(2)}) async-start(), calls=%async_computation.2 | async-start | bytes 4096000 | tf_op jit(solution)/shard_map/all_gather | solution.py:167
  120.3 17.9 %collective-permute-start.8 = (bf16[2,128,1280]{2,1,0:T(8,128)(2,1)S(1)}, bf16[2,128,1280]{2,1,0:T(8,128)(2,1)S(1)}, u32[]{:S(2)}, u32[]{:S(2)}) collective-permute-start(bf16[2,128,1280]{2,1,0:T(8,128)(2,1)S(1)} %pad_maximum_fusion), channel_id=1, source_target_pairs={{0,64},{1,65},{2,66},{3,67},{4,68},{5,69},{6,70},{7,71},{8,72},{9,... | collective-permute-start | bytes 1966088 | tf_op jit(solution)/shard_map/ppermute | solution.py:108
  138.3 15.5 %collective-permute-start.9 = (bf16[2,128,1280]{2,1,0:T(8,128)(2,1)S(1)}, bf16[2,128,1280]{2,1,0:T(8,128)(2,1)S(1)}, u32[]{:S(2)}, u32[]{:S(2)}) collective-permute-start(bf16[2,128,1280]{2,1,0:T(8,128)(2,1)S(1)} %broadcast_select_fusion), channel_id=1, source_target_pairs={{0,32},{1,33},{2,34},{3,35},{4,36},{5,37},{6,38},{7,39},{8,40},{9,... | collective-permute-start | bytes 1966088 | tf_op jit(solution)/shard_map/ppermute | solution.py:108
  154.0 16.3 %collective-permute-start.10 = (bf16[2,128,1280]{2,1,0:T(8,128)(2,1)S(1)}, bf16[2,128,1280]{2,1,0:T(8,128)(2,1)S(1)}, u32[]{:S(2)}, u32[]{:S(2)}) collective-permute-start(bf16[2,128,1280]{2,1,0:T(8,128)(2,1)S(1)} %broadcast_select_fusion.1), channel_id=1, source_target_pairs={{0,16},{1,17},{2,18},{3,19},{4,20},{5,21},{6,22},{7,23},{8,24},{9,... | collective-permute-start | bytes 1966088 | tf_op jit(solution)/shard_map/ppermute | solution.py:108
  158.1 37.1 %collective-permute-start = (s32[3]{0:T(128)S(1)}, s32[3]{0:T(128)S(1)}, u32[]{:S(2)}, u32[]{:S(2)}) collective-permute-start(s32[3]{0:T(128)S(1)} %pad_add_fusion.1), channel_id=1, source_target_pairs={{8,0},{12,4},{16,8},{20,12},{24,16},{28,20},{32,24},{36,28},{40,32... | collective-permute-start | bytes 44 | tf_op jit(solution)/shard_map/ppermute | solution.py:18
  162.9 32.3 %collective-permute-start.2 = (s32[3]{0:T(128)S(1)}, s32[3]{0:T(128)S(1)}, u32[]{:S(2)}, u32[]{:S(2)}) collective-permute-start(s32[3]{0:T(128)S(1)} %pad_add_fusion.2), channel_id=1, source_target_pairs={{4,0},{8,4},{12,8},{16,12},{20,16},{24,20},{28,24},{32,28},{36,32}... | collective-permute-start | bytes 44 | tf_op jit(solution)/shard_map/ppermute | solution.py:18
  170.5 13.9 %collective-permute-start.11 = (bf16[2,128,1280]{2,1,0:T(8,128)(2,1)S(1)}, bf16[2,128,1280]{2,1,0:T(8,128)(2,1)S(1)}, u32[]{:S(2)}, u32[]{:S(2)}) collective-permute-start(bf16[2,128,1280]{2,1,0:T(8,128)(2,1)S(1)} %broadcast_select_fusion.2), channel_id=1, source_target_pairs={{0,8},{1,9},{2,10},{3,11},{4,12},{5,13},{6,14},{7,15},{8,0},{9,1},... | collective-permute-start | bytes 1966088 | tf_op jit(solution)/shard_map/ppermute | solution.py:108
  174.2 42.0 %collective-permute-start.4 = (s32[3]{0:T(128)S(1)}, s32[3]{0:T(128)S(1)}, u32[]{:S(2)}, u32[]{:S(2)}) collective-permute-start(s32[3]{0:T(128)S(1)} %pad_add_fusion.3), channel_id=1, source_target_pairs={{0,4},{4,8},{8,12},{12,16},{16,20},{20,24},{24,28},{28,32},{32,36}... | collective-permute-start | bytes 44 | tf_op jit(solution)/shard_map/ppermute | solution.py:18
  184.5 6.7 %collective-permute-start.12 = (bf16[2,128,1280]{2,1,0:T(8,128)(2,1)S(1)}, bf16[2,128,1280]{2,1,0:T(8,128)(2,1)S(1)}, u32[]{:S(2)}, u32[]{:S(2)}) collective-permute-start(bf16[2,128,1280]{2,1,0:T(8,128)(2,1)S(1)} %broadcast_select_fusion.3), channel_id=1, source_target_pairs={{0,4},{1,5},{2,6},{3,7},{4,0},{5,1},{6,2},{7,3},{8,12},{9,13},{10,... | collective-permute-start | bytes 1966088 | tf_op jit(solution)/shard_map/ppermute | solution.py:108
  187.2 28.9 %collective-permute-start.6 = (s32[3]{0:T(128)S(1)}, s32[3]{0:T(128)S(1)}, u32[]{:S(2)}, u32[]{:S(2)}) collective-permute-start(s32[3]{0:T(128)S(1)} %pad_add_fusion.4), channel_id=1, source_target_pairs={{0,8},{4,12},{8,16},{12,20},{16,24},{20,28},{24,32},{28,36},{32,40... | collective-permute-start | bytes 44 | tf_op jit(solution)/shard_map/ppermute | solution.py:18
  191.3 24.4 %collective-permute-start.13 = (bf16[2,128,1280]{2,1,0:T(8,128)(2,1)S(1)}, bf16[2,128,1280]{2,1,0:T(8,128)(2,1)S(1)}, u32[]{:S(2)}, u32[]{:S(2)}) collective-permute-start(bf16[2,128,1280]{2,1,0:T(8,128)(2,1)S(1)} %broadcast_select_fusion.4), channel_id=1, source_target_pairs={{0,2},{1,3},{2,0},{3,1},{4,6},{5,7},{6,4},{7,5},{8,10},{9,11},{10,... | collective-permute-start | bytes 1966088 | tf_op jit(solution)/shard_map/ppermute | solution.py:108
  215.8 30.6 %collective-permute-start.14 = (bf16[2,128,1280]{2,1,0:T(8,128)(2,1)S(1)}, bf16[2,128,1280]{2,1,0:T(8,128)(2,1)S(1)}, u32[]{:S(2)}, u32[]{:S(2)}) collective-permute-start(bf16[2,128,1280]{2,1,0:T(8,128)(2,1)S(1)} %broadcast_select_fusion.5), channel_id=1, source_target_pairs={{0,1},{1,0},{2,3},{3,2},{4,5},{5,4},{6,7},{7,6},{8,9},{9,8},{10,11... | collective-permute-start | bytes 1966088 | tf_op jit(solution)/shard_map/ppermute | solution.py:108
  251.3 47.9 %collective-permute-start.1 = (bf16[3,128,2560]{2,1,0:T(8,128)(2,1)}, bf16[3,128,2560]{2,1,0:T(8,128)(2,1)}, u32[]{:S(2)}, u32[]{:S(2)}) collective-permute-start(bf16[3,128,2560]{2,1,0:T(8,128)(2,1)} %gather_fusion.4), channel_id=1, source_target_pairs={{0,8},{4,12},{8,16},{12,20},{16,24},{20,28},{24,32},{28,36},{32,40... | collective-permute-start | bytes 5898248 | tf_op jit(solution)/shard_map/ppermute | solution.py:18
  258.5 57.7 %collective-permute-start.3 = (bf16[3,128,2560]{2,1,0:T(8,128)(2,1)}, bf16[3,128,2560]{2,1,0:T(8,128)(2,1)}, u32[]{:S(2)}, u32[]{:S(2)}) collective-permute-start(bf16[3,128,2560]{2,1,0:T(8,128)(2,1)} %gather_fusion.5), channel_id=1, source_target_pairs={{0,4},{4,8},{8,12},{12,16},{16,20},{20,24},{24,28},{28,32},{32,36}... | collective-permute-start | bytes 5898248 | tf_op jit(solution)/shard_map/ppermute | solution.py:18
  265.0 52.9 %collective-permute-start.5 = (bf16[3,128,2560]{2,1,0:T(8,128)(2,1)}, bf16[3,128,2560]{2,1,0:T(8,128)(2,1)}, u32[]{:S(2)}, u32[]{:S(2)}) collective-permute-start(bf16[3,128,2560]{2,1,0:T(8,128)(2,1)} %gather_fusion.6), channel_id=1, source_target_pairs={{4,0},{8,4},{12,8},{16,12},{20,16},{24,20},{28,24},{32,28},{36,32}... | collective-permute-start | bytes 5898248 | tf_op jit(solution)/shard_map/ppermute | solution.py:18
  268.9 13.4 %slice-start = ((s8[5242880]{0:T(1024)(128)(4,1)}), s8[1048576]{0:T(1024)(128)(4,1)S(1)}, s32[]{:S(2)}) async-start(s8[5242880]{0:T(1024)(128)(4,1)} %bitcast.184), calls=%async_computation.3 | async-start | bytes 2097152
  273.6 8.7 %slice-start.1 = ((s8[5242880]{0:T(1024)(128)(4,1)}), s8[4194304]{0:T(1024)(128)(4,1)S(1)}, s32[]{:S(2)}) async-start(s8[5242880]{0:T(1024)(128)(4,1)} %bitcast.184), calls=%async_computation.4 | async-start | bytes 8388608
  273.6 63.5 %collective-permute-start.7 = (bf16[3,128,2560]{2,1,0:T(8,128)(2,1)}, bf16[3,128,2560]{2,1,0:T(8,128)(2,1)S(1)}, u32[]{:S(2)}, u32[]{:S(2)}) collective-permute-start(bf16[3,128,2560]{2,1,0:T(8,128)(2,1)} %gather_fusion.7), channel_id=1, source_target_pairs={{8,0},{12,4},{16,8},{20,12},{24,16},{28,20},{32,24},{36,28},{40,32... | collective-permute-start | bytes 5898248 | tf_op jit(solution)/shard_map/ppermute | solution.py:18
  319.5 22.9 %slice-start.2 = ((bf16[256,3840]{1,0:T(8,128)(2,1)}), bf16[256,1280]{1,0:T(8,128)(2,1)S(1)}, s32[]{:S(2)}) async-start(bf16[256,3840]{1,0:T(8,128)(2,1)} %copy-done.4), calls=%async_computation.5 | async-start | bytes 1310720 | tf_op jit(solution)/shard_map/slice | solution.py:118
  319.5 22.9 %copy-start.8 = (bf16[2,128,1280]{2,1,0:T(8,128)(2,1)S(1)}, bf16[2,128,1280]{2,1,0:T(8,128)(2,1)}, u32[]{:S(2)}) copy-start(bf16[2,128,1280]{2,1,0:T(8,128)(2,1)} %custom-call.17) | copy-start | bytes 1966084
  319.5 22.9 %copy-start.9 = (s32[2]{0:T(128)S(1)}, s32[2]{0:T(128)}, u32[]{:S(2)}) copy-start(s32[2]{0:T(128)} %param.16) | copy-start | bytes 28
  337.4 5.0 %copy-start.2 = (bf16[22,128,2560]{2,1,0:T(8,128)(2,1)}, bf16[22,128,2560]{2,1,0:T(8,128)(2,1)S(1)}, u32[]{:S(2)}) copy-start(bf16[22,128,2560]{2,1,0:T(8,128)(2,1)S(1)} %constant_dynamic-update-slice_fusion.1) | copy-start | bytes 43253764
  469.2 3.9 copy-start.1
Sparse Core Ops, SparseCore 0:
  9.0 97.4 all-gather.3
  115.7 58.0 all-gather.5
  191.3 58.1 all-gather.7

commit v3 on v2

--- a/solution.py
+++ b/solution.py
@@ -1,6 +1,8 @@
 import jax
 import jax.numpy as jnp
 from jax import lax
+from jax.experimental import pallas as pl
+from jax.experimental.pallas import tpu as pltpu
 from jax.sharding import PartitionSpec as P
 
 HEADS = 16
@@ -48,21 +50,75 @@
     return picks, rank
 
 
-def attend_tile(query_tile, key_values, key_live, feat_width):
+def attention_kernel(slots_ref, counts_ref, q_ref, kv_ref, o_ref, s_scr, v_scr):
+    tile_at = pl.program_id(0)
+    slot_at = pl.program_id(1)
+    slot_count = KT + GLOBAL
+    feat_width = q_ref.shape[-1]
     head_size = feat_width // HEADS
-    key_rows = key_values.shape[0]
-    queries_h = query_tile.reshape(TILE, HEADS, head_size)
-    keys_h = key_values[:, :feat_width].reshape(key_rows, HEADS, head_size)
-    values_h = key_values[:, feat_width:].reshape(key_rows, HEADS, head_size)
-    scores = jnp.einsum(
-        "qhd,khd->hqk", queries_h, keys_h, preferred_element_type=jnp.float32
-    ) * head_size ** (-0.5)
-    scores = jnp.where(key_live[None, None, :], scores, -jnp.inf)
-    row_max = jnp.max(scores, axis=-1, keepdims=True)
-    weights_raw = jnp.exp(scores - row_max)
-    probs = (weights_raw / jnp.sum(weights_raw, axis=-1, keepdims=True)).astype(jnp.bfloat16)
-    mixed_h = jnp.einsum("hqk,khd->qhd", probs, values_h, preferred_element_type=jnp.float32)
-    return mixed_h.reshape(TILE, feat_width).astype(jnp.bfloat16)
+    live_count = counts_ref[tile_at]
+    live = (slot_at >= KT) | (slot_at < live_count)
+    key_at = pl.multiple_of(slot_at * TILE, TILE)
+
+    @pl.when(live)
+    def _():
+        for head in range(HEADS):
+            cols = slice(head * head_size, (head + 1) * head_size)
+            scores = lax.dot_general(
+                q_ref[0, :, cols], kv_ref[0, :, cols], (((1,), (1,)), ((), ())),
+                preferred_element_type=jnp.float32,
+            )
+            s_scr[head, :, pl.ds(key_at, TILE)] = scores * head_size ** (-0.5)
+        v_scr[pl.ds(key_at, TILE), :] = kv_ref[0, :, feat_width:]
+
+    @pl.when(jnp.logical_not(live))
+    def _():
+        v_scr[pl.ds(key_at, TILE), :] = jnp.zeros((TILE, feat_width), v_scr.dtype)
+
+    @pl.when(slot_at == slot_count - 1)
+    def _():
+        key_slot = lax.broadcasted_iota(jnp.int32, (TILE, slot_count * TILE), 1) // TILE
+        key_live = (key_slot >= KT) | (key_slot < live_count)
+        for head in range(HEADS):
+            cols = slice(head * head_size, (head + 1) * head_size)
+            scores = jnp.where(key_live, s_scr[head], -jnp.inf)
+            row_max = jnp.max(scores, axis=-1, keepdims=True)
+            weights_raw = jnp.exp(scores - row_max)
+            probs = (weights_raw / jnp.sum(weights_raw, axis=-1, keepdims=True)).astype(jnp.bfloat16)
+            mixed = jnp.dot(probs, v_scr[:, cols], preferred_element_type=jnp.float32)
+            o_ref[0, :, cols] = mixed.astype(o_ref.dtype)
+
+
+def attend(query_tiles, window, slots, counts):
+    tile_count, _, feat_width = query_tiles.shape
+    slot_count = KT + GLOBAL
+
+    def kv_map(i, j, slots_ref, counts_ref):
+        live_count = counts_ref[i]
+        fetch = jnp.where((j >= KT) | (j < live_count), j, jnp.maximum(live_count - 1, 0))
+        return (slots_ref[i, fetch], 0, 0)
+
+    grid_spec = pltpu.PrefetchScalarGridSpec(
+        num_scalar_prefetch=2,
+        grid=(tile_count, slot_count),
+        in_specs=[
+            pl.BlockSpec((1, TILE, feat_width), lambda i, j, s, c: (i, 0, 0)),
+            pl.BlockSpec((1, TILE, 2 * feat_width), kv_map),
+        ],
+        out_specs=pl.BlockSpec((1, TILE, feat_width), lambda i, j, s, c: (i, 0, 0)),
+        scratch_shapes=[
+            pltpu.VMEM((HEADS, TILE, slot_count * TILE), jnp.float32),
+            pltpu.VMEM((slot_count * TILE, feat_width), jnp.bfloat16),
+        ],
+    )
+    return pl.pallas_call(
+        attention_kernel,
+        grid_spec=grid_spec,
+        out_shape=jax.ShapeDtypeStruct(query_tiles.shape, jnp.bfloat16),
+        compiler_params=pltpu.CompilerParams(
+            dimension_semantics=("arbitrary", "arbitrary"),
+        ),
+    )(slots, counts, query_tiles, window)
 
 
 def local(
@@ -142,26 +198,15 @@
     reach_slot = jnp.clip(reach_slot, 0, len(REACH) - 1)
     entry_rank = near_rank[reach_slot, entry_local]
     local_lists = jnp.where(
-        reach_of == 0, entry_local, group_tiles + NEAR * reach_slot + entry_rank
+        reach_of == 0, entry_local, group_tiles + NEAR * reach_slot + jnp.clip(entry_rank, 0, NEAR - 1)
     )
     global_slots = group_tiles + NEAR * len(REACH) + jnp.arange(GLOBAL, dtype=jnp.int32)
 
     query_tiles = query.reshape(tile_count, TILE, feat_width)
-
-    def per_tile(tile_args):
-        query_tile, local_ids, live_count = tile_args
-        slot_live_row = jnp.concatenate(
-            [jnp.arange(KT) < live_count, jnp.ones((GLOBAL,), dtype=bool)]
-        )
-        key_live = jnp.repeat(slot_live_row, TILE)
-        key_values = window[jnp.concatenate([local_ids, global_slots])].reshape(
-            (KT + GLOBAL) * TILE, 2 * feat_width
-        )
-        return attend_tile(query_tile, key_values, key_live, feat_width)
-
-    heads_out = lax.map(per_tile, (query_tiles, local_lists, kv_count)).reshape(
-        tok_rows, feat_width
-    )
+    slots = jnp.concatenate(
+        [local_lists, jnp.broadcast_to(global_slots, (tile_count, GLOBAL))], axis=1
+    ).astype(jnp.int32)
+    heads_out = attend(query_tiles, window, slots, kv_count).reshape(tok_rows, feat_width)
     return jnp.dot(
         heads_out,
         lax.all_gather(w_out, "fsdp", axis=0, tiled=True),

time: 481 us -> 404 us (0.84)
  the two profiles are of different devices: /device:TPU:24 before, /device:TPU:2 now
where the time goes in v3:
time: 404 us; the launch traced here: 402 us
  waiting for transfers between devices  217 us (54%)
  Pallas kernels  54.9 us (14%)
  local copies, waits for them, and re-layouts  41.8 us (10%)
  starting transfers between devices  39.3 us (10%)
  between operations  18.6 us (5%)
  matrix products  15.4 us (4%)
  other arithmetic  15 us (4%)
    all_gather x1, waiting for transfers between devices, local(): w_full = lax.all_gather(w_qkv, 'fsdp', axis=0, tiled=True)  95.7 us
    ppermute x7, waiting for transfers between devices, local(): lax.ppermute(global_stream, ('seq', 'fsdp'), [(i, i ^ step) for i in rang...  82.1 us
    pallas_call x1, Pallas kernels, attend(): pl.pallas_call(attention_kernel, grid_spec=grid_spec, out_shape=jax.Shape...  54.9 us
    ppermute x8, waiting for transfers between devices, passed_along(): return lax.ppermute(block, axis, route)  38.4 us
    ppermute x8, starting transfers between devices, passed_along(): return lax.ppermute(block, axis, route)  27.5 us
    gather x4, local copies, waits for them, and re-layouts, local(): near_blocks.append(passed_along(group_block[asked], 'seq', -reach))  18.3 us
    unnamed x29, local copies, waits for them, and re-layouts  15 us
    ppermute x7, starting transfers between devices, local(): lax.ppermute(global_stream, ('seq', 'fsdp'), [(i, i ^ step) for i in rang...  11.7 us
  transfers between devices with their start and end apart: 18, of which 11 were waited for; matrix products, arithmetic and copies ran while one was open for 15% of the time, Pallas kernels for 14%

profile of v3, /device:TPU:2, one launch (start us, length us, event | category | flops | bytes accessed | tf_op | source)
XLA Modules:
  0.0 401.9 jit_solution(9600615068370021710)
XLA Ops:
  7.8 1.2 gather_fusion.1
  9.0 1.2 gather_fusion.2
  11.0 95.7 %all-gather.4.cloned.1.call-done = bf16[1280,3840]{1,0:T(8,128)(2,1)} async-done(((bf16[320,3840]{1,0:T(8,128)(2,1)}), bf16[1280,3840]{1,0:T(8,128)(2,1)}) %all-gather.4.cloned.1.call-update) | async-done | bytes 9830416 | tf_op jit(solution)/shard_map/all_gather | solution.py:171
  106.7 6.6 %convolution_convert_fusion = bf16[256,3840]{1,0:T(8,128)(2,1)S(1)} fusion(bf16[1280,3840]{1,0:T(8,128)(2,1)} %all-gather.4.cloned.1.call-done, bf16[256,1280]{1,0:T(8,128)(2,1)S(1)} %get-tuple-element.26, f32[1280]{0:T(1024)S(1)} %convert_element_type.114, f32[1280]{0:T(1024)S(1)} %convert_element_type.113, f32[256]{0:T(256)S(1)} %add_rsqrt_fusion, ...), kind=kOutput, calls=%fused_computation.9 | convolution fusion | flops 2519531520 | bytes 12464128 | tf_op jit(solution)/shard_map/dot_general | solution.py:173
  113.4 1.3 copy-done.3
  114.6 1.2 slice.35
  120.4 2.2 collective-permute-start.8
  123.8 1.9 pad_add_fusion.2
  125.7 5.5 %collective-permute-start = (s32[3]{0:T(128)S(1)}, s32[3]{0:T(128)S(1)}, u32[]{:S(2)}, u32[]{:S(2)}) collective-permute-start(s32[3]{0:T(128)S(1)} %pad_add_fusion.2), channel_id=1, source_target_pairs={{8,0},{12,4},{16,8},{20,12},{24,16},{28,20},{32,24},{36,28},{40,32... | collective-permute-start | bytes 44 | tf_op jit(solution)/shard_map/ppermute | solution.py:20
  132.8 5.5 %collective-permute-done.8 = bf16[2,128,1280]{2,1,0:T(8,128)(2,1)S(1)} collective-permute-done((bf16[2,128,1280]{2,1,0:T(8,128)(2,1)S(1)}, bf16[2,128,1280]{2,1,0:T(8,128)(2,1)S(1)}, u32[]{:S(2)}, u32[]{:S(2)}) %collective-permute-start.8) | collective-permute-done | bytes 655392 | tf_op jit(solution)/shard_map/ppermute | solution.py:164
  139.8 2.0 pad_add_fusion.3
  141.8 3.8 collective-permute-start.2
  146.5 2.0 pad_add_fusion.4
  148.5 1.9 collective-permute-start.4
  150.6 3.5 collective-permute-done.9
  154.2 3.1 collective-permute-start.10
  158.1 2.0 pad_add_fusion.5
  160.0 2.5 collective-permute-start.6
  162.6 8.0 %collective-permute-done.10 = bf16[2,128,1280]{2,1,0:T(8,128)(2,1)S(1)} collective-permute-done((bf16[2,128,1280]{2,1,0:T(8,128)(2,1)S(1)}, bf16[2,128,1280]{2,1,0:T(8,128)(2,1)S(1)}, u32[]{:S(2)}, u32[]{:S(2)}) %collective-permute-start.10) | collective-permute-done | bytes 655392 | tf_op jit(solution)/shard_map/ppermute | solution.py:164
  170.8 1.6 collective-permute-start.11
  172.4 0.8 gather_fusion
  173.2 11.6 %collective-permute-done.11 = bf16[2,128,1280]{2,1,0:T(8,128)(2,1)S(1)} collective-permute-done((bf16[2,128,1280]{2,1,0:T(8,128)(2,1)S(1)}, bf16[2,128,1280]{2,1,0:T(8,128)(2,1)S(1)}, u32[]{:S(2)}, u32[]{:S(2)}) %collective-permute-start.11) | collective-permute-done | bytes 655392 | tf_op jit(solution)/shard_map/ppermute | solution.py:164
  185.8 1.3 collective-permute-done.12
  187.2 2.7 collective-permute-start.13
  190.0 30.2 %collective-permute-done.13 = bf16[2,128,1280]{2,1,0:T(8,128)(2,1)S(1)} collective-permute-done((bf16[2,128,1280]{2,1,0:T(8,128)(2,1)S(1)}, bf16[2,128,1280]{2,1,0:T(8,128)(2,1)S(1)}, u32[]{:S(2)}, u32[]{:S(2)}) %collective-permute-start.13) | collective-permute-done | bytes 655392 | tf_op jit(solution)/shard_map/ppermute | solution.py:164
  220.3 1.4 collective-permute-start.14
  221.8 22.0 %collective-permute-done.14 = bf16[2,128,1280]{2,1,0:T(8,128)(2,1)S(1)} collective-permute-done((bf16[2,128,1280]{2,1,0:T(8,128)(2,1)S(1)}, bf16[2,128,1280]{2,1,0:T(8,128)(2,1)S(1)}, u32[]{:S(2)}, u32[]{:S(2)}) %collective-permute-start.14) | collective-permute-done | bytes 655392 | tf_op jit(solution)/shard_map/ppermute | solution.py:164
  244.1 4.5 %gather_fusion.3 = bf16[3,128,2560]{2,1,0:T(8,128)(2,1)} fusion(bf16[8,128,2560]{2,1,0:T(8,128)(2,1)} %bitcast.130, s32[1024]{0:T(1024)S(1)} %pad_clamp_fusion.3), kind=kCustom, calls=%fused_computation.3 | custom fusion | bytes 3932172 | tf_op jit(solution)/shard_map/gather | solution.py:189
  248.6 3.4 collective-permute-start.1
  252.3 4.6 %gather_fusion.4 = bf16[3,128,2560]{2,1,0:T(8,128)(2,1)} fusion(bf16[8,128,2560]{2,1,0:T(8,128)(2,1)} %bitcast.131, s32[1024]{0:T(1024)S(1)} %pad_clamp_fusion.2), kind=kCustom, calls=%fused_computation.4 | custom fusion | bytes 3932172 | tf_op jit(solution)/shard_map/gather | solution.py:189
  256.9 1.9 collective-permute-start.3
  258.8 4.6 %gather_fusion.5 = bf16[3,128,2560]{2,1,0:T(8,128)(2,1)} fusion(bf16[8,128,2560]{2,1,0:T(8,128)(2,1)} %bitcast.132, s32[1024]{0:T(1024)S(1)} %pad_clamp_fusion.1), kind=kCustom, calls=%fused_computation.5 | custom fusion | bytes 3932172 | tf_op jit(solution)/shard_map/gather | solution.py:189
  263.4 5.7 %collective-permute-start.5 = (bf16[3,128,2560]{2,1,0:T(8,128)(2,1)}, bf16[3,128,2560]{2,1,0:T(8,128)(2,1)}, u32[]{:S(2)}, u32[]{:S(2)}) collective-permute-start(bf16[3,128,2560]{2,1,0:T(8,128)(2,1)} %gather_fusion.5), channel_id=1, source_target_pairs={{4,0},{8,4},{12,8},{16,12},{20,16},{24,20},{28,24},{32,28},{36,32}... | collective-permute-start | bytes 5898248 | tf_op jit(solution)/shard_map/ppermute | solution.py:20
  269.5 4.6 %gather_fusion.6 = bf16[3,128,2560]{2,1,0:T(8,128)(2,1)} fusion(bf16[8,128,2560]{2,1,0:T(8,128)(2,1)} %bitcast.133, s32[1024]{0:T(1024)S(1)} %pad_clamp_fusion), kind=kCustom, calls=%fused_computation.6 | custom fusion | bytes 3932172 | tf_op jit(solution)/shard_map/gather | solution.py:189
  274.1 2.7 collective-permute-start.7
  276.8 4.7 %fusion.2 = bf16[256,2560]{1,0:T(8,128)(2,1)S(1)} fusion(bf16[256,1280]{1,0:T(8,128)(2,1)S(1)} %fusion.14, bf16[1280,3840]{1,0:T(8,128)(2,1)} %all-gather.4.cloned.1.call-done), kind=kOutput, calls=%fused_computation.10 | convolution fusion | flops 1678376960 | bytes 8519680 | tf_op jit(solution)/shard_map/dot_general | solution.py:177
  281.6 2.0 slice.34
  283.5 2.9 constant_dynamic-update-slice_fusion.5
  286.4 12.2 %collective-permute-done.1 = bf16[3,128,2560]{2,1,0:T(8,128)(2,1)} collective-permute-done((bf16[3,128,2560]{2,1,0:T(8,128)(2,1)}, bf16[3,128,2560]{2,1,0:T(8,128)(2,1)}, u32[]{:S(2)}, u32[]{:S(2)}) %collective-permute-start.1) | collective-permute-done | bytes 1966112 | tf_op jit(solution)/shard_map/ppermute | solution.py:20
  298.6 3.0 constant_dynamic-update-slice_fusion.4
  301.6 16.7 %collective-permute-done.3 = bf16[3,128,2560]{2,1,0:T(8,128)(2,1)} collective-permute-done((bf16[3,128,2560]{2,1,0:T(8,128)(2,1)}, bf16[3,128,2560]{2,1,0:T(8,128)(2,1)}, u32[]{:S(2)}, u32[]{:S(2)}) %collective-permute-start.3) | collective-permute-done | bytes 1966112 | tf_op jit(solution)/shard_map/ppermute | solution.py:20
  318.3 3.0 constant_dynamic-update-slice_fusion.3
  321.3 3.0 constant_dynamic-update-slice_fusion.2
  324.3 9.4 %collective-permute-done.7 = bf16[3,128,2560]{2,1,0:T(8,128)(2,1)S(1)} collective-permute-done((bf16[3,128,2560]{2,1,0:T(8,128)(2,1)}, bf16[3,128,2560]{2,1,0:T(8,128)(2,1)S(1)}, u32[]{:S(2)}, u32[]{:S(2)}) %collective-permute-start.7) | collective-permute-done | bytes 1966112 | tf_op jit(solution)/shard_map/ppermute | solution.py:20
  333.7 1.5 constant_dynamic-update-slice_fusion.1
  335.2 1.1 constant_dynamic-update-slice_fusion.kv_ref
  336.4 54.9 %shard_map.109 = bf16[2,128,1280]{2,1,0:T(8,128)(2,1)} custom-call(s32[2,18]{1,0:T(2,128)} %pad_add_fusion.1.slots_ref, s32[2]{0:T(128)} %counts_ref.1, bf16[2,128,1280]{2,1,0:T(8,128)(2,1)} %bitcast.137, bf16[22,128,2560]{2,1,0:T(8,128)(2,1)} %constant_dynamic-update-slice_fusion.kv_ref), custom_call_target="tpu_custom_call" | custom-call | tf_op jit(solution)/shard_map/pallas_call | solution.py:114
  391.2 4.1 %convolution_convert_fusion.1 = bf16[256,1280]{1,0:T(8,128)(2,1)} fusion(bf16[256,1280]{1,0:T(8,128)(2,1)} %bitcast.139, bf16[1280,1280]{1,0:T(8,128)(2,1)} %all-gather.8.cloned.1.call-done), kind=kOutput, calls=%fused_computation.11 | convolution fusion | flops 839188480 | bytes 4587520 | tf_op jit(solution)/shard_map/dot_general | solution.py:210
  (100 shorter events, 10.2 us)
Async XLA Ops:
  6.5 2.5 copy-start
  6.5 0.8 copy-start.5
  6.5 0.8 copy-start.6
  6.5 0.8 copy-start.9
  6.5 1.2 copy-start.2
  6.5 100.2 %all-gather.4.cloned.1.call-start = ((), (), s32[]{:S(2)}) async-start(), calls=%async_computation | async-start | bytes 12288000 | tf_op jit(solution)/shard_map/all_gather | solution.py:171
  7.3 236.8 %all-gather.6.cloned.1.call-start = ((), (), s32[]{:S(2)}) async-start(), calls=%async_computation.1 | async-start | bytes 6553600 | tf_op jit(solution)/shard_map/all_gather | solution.py:181
  9.0 1.3 copy-start.4
  113.4 1.3 copy-start.3
  114.6 1.2 copy-start.8
  115.8 6.8 %copy-start.7 = (s32[2,16]{1,0:T(2,128)S(1)}, s32[2,16]{1,0:T(2,128)}, u32[]{:S(2)}) copy-start(s32[2,16]{1,0:T(2,128)} %param.13) | copy-start | bytes 388
  115.8 275.4 %all-gather.8.cloned.1.call-start = ((), (), s32[]{:S(2)}) async-start(), calls=%async_computation.2 | async-start | bytes 4096000 | tf_op jit(solution)/shard_map/all_gather | solution.py:212
  120.4 17.9 %collective-permute-start.8 = (bf16[2,128,1280]{2,1,0:T(8,128)(2,1)S(1)}, bf16[2,128,1280]{2,1,0:T(8,128)(2,1)S(1)}, u32[]{:S(2)}, u32[]{:S(2)}) collective-permute-start(bf16[2,128,1280]{2,1,0:T(8,128)(2,1)S(1)} %pad_maximum_fusion), channel_id=1, source_target_pairs={{0,64},{1,65},{2,66},{3,67},{4,68},{5,69},{6,70},{7,71},{8,72},{9,... | collective-permute-start | bytes 1966088 | tf_op jit(solution)/shard_map/ppermute | solution.py:164
  125.7 64.2 %collective-permute-start = (s32[3]{0:T(128)S(1)}, s32[3]{0:T(128)S(1)}, u32[]{:S(2)}, u32[]{:S(2)}) collective-permute-start(s32[3]{0:T(128)S(1)} %pad_add_fusion.2), channel_id=1, source_target_pairs={{8,0},{12,4},{16,8},{20,12},{24,16},{28,20},{32,24},{36,28},{40,32... | collective-permute-start | bytes 44 | tf_op jit(solution)/shard_map/ppermute | solution.py:20
  138.5 15.6 %collective-permute-start.9 = (bf16[2,128,1280]{2,1,0:T(8,128)(2,1)S(1)}, bf16[2,128,1280]{2,1,0:T(8,128)(2,1)S(1)}, u32[]{:S(2)}, u32[]{:S(2)}) collective-permute-start(bf16[2,128,1280]{2,1,0:T(8,128)(2,1)S(1)} %broadcast_select_fusion), channel_id=1, source_target_pairs={{0,32},{1,33},{2,34},{3,35},{4,36},{5,37},{6,38},{7,39},{8,40},{9,... | collective-permute-start | bytes 1966088 | tf_op jit(solution)/shard_map/ppermute | solution.py:164
  141.8 48.1 %collective-permute-start.2 = (s32[3]{0:T(128)S(1)}, s32[3]{0:T(128)S(1)}, u32[]{:S(2)}, u32[]{:S(2)}) collective-permute-start(s32[3]{0:T(128)S(1)} %pad_add_fusion.3), channel_id=1, source_target_pairs={{4,0},{8,4},{12,8},{16,12},{20,16},{24,20},{28,24},{32,28},{36,32}... | collective-permute-start | bytes 44 | tf_op jit(solution)/shard_map/ppermute | solution.py:20
  148.5 41.5 %collective-permute-start.4 = (s32[3]{0:T(128)S(1)}, s32[3]{0:T(128)S(1)}, u32[]{:S(2)}, u32[]{:S(2)}) collective-permute-start(s32[3]{0:T(128)S(1)} %pad_add_fusion.4), channel_id=1, source_target_pairs={{0,4},{4,8},{8,12},{12,16},{16,20},{20,24},{24,28},{28,32},{32,36}... | collective-permute-start | bytes 44 | tf_op jit(solution)/shard_map/ppermute | solution.py:20
  154.2 16.4 %collective-permute-start.10 = (bf16[2,128,1280]{2,1,0:T(8,128)(2,1)S(1)}, bf16[2,128,1280]{2,1,0:T(8,128)(2,1)S(1)}, u32[]{:S(2)}, u32[]{:S(2)}) collective-permute-start(bf16[2,128,1280]{2,1,0:T(8,128)(2,1)S(1)} %broadcast_select_fusion.1), channel_id=1, source_target_pairs={{0,16},{1,17},{2,18},{3,19},{4,20},{5,21},{6,22},{7,23},{8,24},{9,... | collective-permute-start | bytes 1966088 | tf_op jit(solution)/shard_map/ppermute | solution.py:164
  160.0 61.7 %collective-permute-start.6 = (s32[3]{0:T(128)S(1)}, s32[3]{0:T(128)S(1)}, u32[]{:S(2)}, u32[]{:S(2)}) collective-permute-start(s32[3]{0:T(128)S(1)} %pad_add_fusion.5), channel_id=1, source_target_pairs={{0,8},{4,12},{8,16},{12,20},{16,24},{20,28},{24,32},{28,36},{32,40... | collective-permute-start | bytes 44 | tf_op jit(solution)/shard_map/ppermute | solution.py:20
  170.8 14.0 %collective-permute-start.11 = (bf16[2,128,1280]{2,1,0:T(8,128)(2,1)S(1)}, bf16[2,128,1280]{2,1,0:T(8,128)(2,1)S(1)}, u32[]{:S(2)}, u32[]{:S(2)}) collective-permute-start(bf16[2,128,1280]{2,1,0:T(8,128)(2,1)S(1)} %broadcast_select_fusion.2), channel_id=1, source_target_pairs={{0,8},{1,9},{2,10},{3,11},{4,12},{5,13},{6,14},{7,15},{8,0},{9,1},... | collective-permute-start | bytes 1966088 | tf_op jit(solution)/shard_map/ppermute | solution.py:164
  184.9 2.2 collective-permute-start.12
  187.2 32.9 %collective-permute-start.13 = (bf16[2,128,1280]{2,1,0:T(8,128)(2,1)S(1)}, bf16[2,128,1280]{2,1,0:T(8,128)(2,1)S(1)}, u32[]{:S(2)}, u32[]{:S(2)}) collective-permute-start(bf16[2,128,1280]{2,1,0:T(8,128)(2,1)S(1)} %broadcast_select_fusion.4), channel_id=1, source_target_pairs={{0,2},{1,3},{2,0},{3,1},{4,6},{5,7},{6,4},{7,5},{8,10},{9,11},{10,... | collective-permute-start | bytes 1966088 | tf_op jit(solution)/shard_map/ppermute | solution.py:164
  220.3 23.5 %collective-permute-start.14 = (bf16[2,128,1280]{2,1,0:T(8,128)(2,1)S(1)}, bf16[2,128,1280]{2,1,0:T(8,128)(2,1)S(1)}, u32[]{:S(2)}, u32[]{:S(2)}) collective-permute-start(bf16[2,128,1280]{2,1,0:T(8,128)(2,1)S(1)} %broadcast_select_fusion.5), channel_id=1, source_target_pairs={{0,1},{1,0},{2,3},{3,2},{4,5},{5,4},{6,7},{7,6},{8,9},{9,8},{10,11... | collective-permute-start | bytes 1966088 | tf_op jit(solution)/shard_map/ppermute | solution.py:164
  248.6 50.0 %collective-permute-start.1 = (bf16[3,128,2560]{2,1,0:T(8,128)(2,1)}, bf16[3,128,2560]{2,1,0:T(8,128)(2,1)}, u32[]{:S(2)}, u32[]{:S(2)}) collective-permute-start(bf16[3,128,2560]{2,1,0:T(8,128)(2,1)} %gather_fusion.3), channel_id=1, source_target_pairs={{0,8},{4,12},{8,16},{12,20},{16,24},{20,28},{24,32},{28,36},{32,40... | collective-permute-start | bytes 5898248 | tf_op jit(solution)/shard_map/ppermute | solution.py:20
  256.9 61.4 %collective-permute-start.3 = (bf16[3,128,2560]{2,1,0:T(8,128)(2,1)}, bf16[3,128,2560]{2,1,0:T(8,128)(2,1)}, u32[]{:S(2)}, u32[]{:S(2)}) collective-permute-start(bf16[3,128,2560]{2,1,0:T(8,128)(2,1)} %gather_fusion.4), channel_id=1, source_target_pairs={{0,4},{4,8},{8,12},{12,16},{16,20},{20,24},{24,28},{28,32},{32,36}... | collective-permute-start | bytes 5898248 | tf_op jit(solution)/shard_map/ppermute | solution.py:20
  263.4 57.9 %collective-permute-start.5 = (bf16[3,128,2560]{2,1,0:T(8,128)(2,1)}, bf16[3,128,2560]{2,1,0:T(8,128)(2,1)}, u32[]{:S(2)}, u32[]{:S(2)}) collective-permute-start(bf16[3,128,2560]{2,1,0:T(8,128)(2,1)} %gather_fusion.5), channel_id=1, source_target_pairs={{4,0},{8,4},{12,8},{16,12},{20,16},{24,20},{28,24},{32,28},{36,32}... | collective-permute-start | bytes 5898248 | tf_op jit(solution)/shard_map/ppermute | solution.py:20
  269.5 14.0 %slice-start = ((s8[5242880]{0:T(1024)(128)(4,1)}), s8[1048576]{0:T(1024)(128)(4,1)S(1)}, s32[]{:S(2)}) async-start(s8[5242880]{0:T(1024)(128)(4,1)} %bitcast.134), calls=%async_computation.3 | async-start | bytes 2097152
  274.1 9.4 %slice-start.1 = ((s8[5242880]{0:T(1024)(128)(4,1)}), s8[4194304]{0:T(1024)(128)(4,1)S(1)}, s32[]{:S(2)}) async-start(s8[5242880]{0:T(1024)(128)(4,1)} %bitcast.134), calls=%async_computation.4 | async-start | bytes 8388608
  274.1 59.6 %collective-permute-start.7 = (bf16[3,128,2560]{2,1,0:T(8,128)(2,1)}, bf16[3,128,2560]{2,1,0:T(8,128)(2,1)S(1)}, u32[]{:S(2)}, u32[]{:S(2)}) collective-permute-start(bf16[3,128,2560]{2,1,0:T(8,128)(2,1)} %gather_fusion.6), channel_id=1, source_target_pairs={{8,0},{12,4},{16,8},{20,12},{24,16},{28,20},{32,24},{36,28},{40,32... | collective-permute-start | bytes 5898248 | tf_op jit(solution)/shard_map/ppermute | solution.py:20
  391.2 4.1 %copy-start.1 = (bf16[512,1280]{1,0:T(8,128)(2,1)S(1)}, bf16[512,1280]{1,0:T(8,128)(2,1)}, u32[]{:S(2)}) copy-start(bf16[512,1280]{1,0:T(8,128)(2,1)} %param.17) | copy-start | bytes 3932164
Sparse Core Ops, SparseCore 0:
  9.0 97.6 all-gather.3
  115.9 58.1 all-gather.5
  175.8 61.4 all-gather.7

commit v4 on v3

--- a/solution.py
+++ b/solution.py
@@ -168,27 +168,31 @@
         done_bits |= step
     global_stream = global_stream.reshape(GLOBAL * TILE, feat_width)
 
-    w_full = lax.all_gather(w_qkv, "fsdp", axis=0, tiled=True)
     normed = layer_norm(stream, ln_gain, ln_bias)
-    qkv = jnp.dot(normed, w_full, preferred_element_type=jnp.float32).astype(jnp.bfloat16)
-    query = qkv[:, :feat_width]
-    keyval = qkv[:, feat_width:]
     global_normed = layer_norm(global_stream, ln_gain, ln_bias)
-    global_kv = jnp.dot(
-        global_normed, w_full[:, feat_width:], preferred_element_type=jnp.float32
-    ).astype(jnp.bfloat16).reshape(GLOBAL, TILE, 2 * feat_width)
-
-    group_block = lax.all_gather(keyval, "fsdp", axis=0, tiled=True).reshape(
-        group_tiles, TILE, 2 * feat_width
-    )
+    group_rows = lax.all_gather(normed, "fsdp", axis=0, tiled=True).reshape(
+        group_tiles, TILE, feat_width
+    )
+    w_src, group_rows = lax.optimization_barrier((w_qkv, group_rows))
+    w_full = lax.all_gather(w_src, "fsdp", axis=0, tiled=True)
+
     near_blocks = []
     near_rank = []
     for reach in REACH:
         picks, rank = near_tiles(kv_list, seq_at + reach, group_tiles)
         asked = passed_along(picks, "seq", reach)
-        near_blocks.append(passed_along(group_block[asked], "seq", -reach))
+        near_blocks.append(passed_along(group_rows[asked], "seq", -reach))
         near_rank.append(rank)
-    window = jnp.concatenate([group_block] + near_blocks + [global_kv], axis=0)
+    window_rows = jnp.concatenate(
+        [group_rows] + near_blocks + [global_normed.reshape(GLOBAL, TILE, feat_width)], axis=0
+    )
+    window = jnp.dot(
+        window_rows.reshape(-1, feat_width), w_full[:, feat_width:],
+        preferred_element_type=jnp.float32,
+    ).astype(jnp.bfloat16).reshape(-1, TILE, 2 * feat_width)
+    query = jnp.dot(
+        normed, w_full[:, :feat_width], preferred_element_type=jnp.float32
+    ).astype(jnp.bfloat16)
     near_rank = jnp.stack(near_rank)
 
     entry_group = kv_list // group_tiles

time: 404 us -> 321 us (0.79)
  the two profiles are of different devices: /device:TPU:2 before, /device:TPU:24 now
where the time goes in v4:
time: 321 us; the launch traced here: 319 us
  waiting for transfers between devices  131 us (41%)
  Pallas kernels  53.2 us (17%)
  starting transfers between devices  33.4 us (10%)
  matrix products  32.8 us (10%)
  local copies, waits for them, and re-layouts  28.1 us (9%)
  other arithmetic  22.2 us (7%)
  between operations  18.5 us (6%)
    ppermute x7, waiting for transfers between devices, local(): lax.ppermute(global_stream, ('seq', 'fsdp'), [(i, i ^ step) for i in rang...  69.5 us
    pallas_call x1, Pallas kernels, attend(): pl.pallas_call(attention_kernel, grid_spec=grid_spec, out_shape=jax.Shape...  53.2 us
    all_gather x1, waiting for transfers between devices, local(): lax.all_gather(normed, 'fsdp', axis=0, tiled=True)  37.6 us
    dot_general x1, matrix products, local(): jnp.dot(window_rows.reshape(-1, feat_width), w_full[:, feat_width:], pref...  25.1 us
    ppermute x8, waiting for transfers between devices, passed_along(): return lax.ppermute(block, axis, route)  23.8 us
    ppermute x8, starting transfers between devices, passed_along(): return lax.ppermute(block, axis, route)  22.9 us
    gather x4, local copies, waits for them, and re-layouts, local(): near_blocks.append(passed_along(group_rows[asked], 'seq', -reach))  12.6 us
    unnamed x15, local copies, waits for them, and re-layouts  11.3 us
  transfers between devices with their start and end apart: 18, of which 11 were waited for; matrix products, arithmetic and copies ran while one was open for 22% of the time, Pallas kernels for 17%

profile of v4, /device:TPU:24, one launch (start us, length us, event | category | flops | bytes accessed | tf_op | source)
XLA Modules:
  0.0 319.1 jit_solution(8077233699893127475)
XLA Ops:
  8.7 1.2 gather_fusion.2
  10.0 1.3 gather_fusion.1
  11.2 1.4 convert_reduce_fusion.1
  13.1 1.2 fusion.17
  14.3 37.6 %all-gather.4.cloned.1.call-done = bf16[1024,1280]{1,0:T(8,128)(2,1)} async-done(((bf16[256,1280]{1,0:T(8,128)(2,1)}), bf16[1024,1280]{1,0:T(8,128)(2,1)}) %all-gather.4.cloned.1.call-update) | async-done | bytes 2621456 | tf_op jit(solution)/shard_map/all_gather | solution.py:173
  53.2 1.9 pad_add_fusion.2
  55.0 2.7 collective-permute-start
  62.4 3.1 collective-permute-start.8
  66.4 2.0 pad_add_fusion.3
  68.3 1.9 collective-permute-start.2
  71.8 8.2 %collective-permute-done.8 = bf16[2,128,1280]{2,1,0:T(8,128)(2,1)S(1)} collective-permute-done((bf16[2,128,1280]{2,1,0:T(8,128)(2,1)S(1)}, bf16[2,128,1280]{2,1,0:T(8,128)(2,1)S(1)}, u32[]{:S(2)}, u32[]{:S(2)}) %collective-permute-start.8) | collective-permute-done | bytes 655392 | tf_op jit(solution)/shard_map/ppermute | solution.py:164
  80.1 1.5 collective-permute-start.9
  82.4 1.9 pad_add_fusion.4
  84.3 1.9 collective-permute-start.4
  87.1 1.9 pad_add_fusion.5
  88.9 4.0 %collective-permute-start.6 = (s32[3]{0:T(128)S(1)}, s32[3]{0:T(128)S(1)}, u32[]{:S(2)}, u32[]{:S(2)}) collective-permute-start(s32[3]{0:T(128)S(1)} %pad_add_fusion.5), channel_id=1, source_target_pairs={{0,8},{4,12},{8,16},{12,20},{16,24},{20,28},{24,32},{28,36},{32,40... | collective-permute-start | bytes 44 | tf_op jit(solution)/shard_map/ppermute | solution.py:20
  93.0 2.5 collective-permute-done.9
  95.5 1.2 broadcast_select_fusion.1
  96.7 1.2 collective-permute-start.10
  97.9 14.7 %collective-permute-done.10 = bf16[2,128,1280]{2,1,0:T(8,128)(2,1)S(1)} collective-permute-done((bf16[2,128,1280]{2,1,0:T(8,128)(2,1)S(1)}, bf16[2,128,1280]{2,1,0:T(8,128)(2,1)S(1)}, u32[]{:S(2)}, u32[]{:S(2)}) %collective-permute-start.10) | collective-permute-done | bytes 655392 | tf_op jit(solution)/shard_map/ppermute | solution.py:164
  112.8 1.8 collective-permute-start.11
  115.5 12.1 %collective-permute-done.11 = bf16[2,128,1280]{2,1,0:T(8,128)(2,1)S(1)} collective-permute-done((bf16[2,128,1280]{2,1,0:T(8,128)(2,1)S(1)}, bf16[2,128,1280]{2,1,0:T(8,128)(2,1)S(1)}, u32[]{:S(2)}, u32[]{:S(2)}) %collective-permute-start.11) | collective-permute-done | bytes 655392 | tf_op jit(solution)/shard_map/ppermute | solution.py:164
  128.5 1.4 collective-permute-done.12
  130.1 1.8 collective-permute-start.13
  131.9 30.7 %collective-permute-done.13 = bf16[2,128,1280]{2,1,0:T(8,128)(2,1)S(1)} collective-permute-done((bf16[2,128,1280]{2,1,0:T(8,128)(2,1)S(1)}, bf16[2,128,1280]{2,1,0:T(8,128)(2,1)S(1)}, u32[]{:S(2)}, u32[]{:S(2)}) %collective-permute-start.13) | collective-permute-done | bytes 655392 | tf_op jit(solution)/shard_map/ppermute | solution.py:164
  162.8 0.9 collective-permute-start.14
  163.7 3.4 %gather_fusion.3 = bf16[3,128,1280]{2,1,0:T(8,128)(2,1)} fusion(bf16[8,128,1280]{2,1,0:T(8,128)(2,1)} %bitcast.117, s32[1024]{0:T(1024)S(1)} %pad_clamp_fusion.3), kind=kCustom, calls=%fused_computation.3 | custom fusion | bytes 1966092 | tf_op jit(solution)/shard_map/gather | solution.py:184
  167.0 4.6 %collective-permute-start.1 = (bf16[3,128,1280]{2,1,0:T(8,128)(2,1)}, bf16[3,128,1280]{2,1,0:T(8,128)(2,1)}, u32[]{:S(2)}, u32[]{:S(2)}) collective-permute-start(bf16[3,128,1280]{2,1,0:T(8,128)(2,1)} %gather_fusion.3), channel_id=1, source_target_pairs={{0,8},{4,12},{8,16},{12,20},{16,24},{20,28},{24,32},{28,36},{32,40... | collective-permute-start | bytes 2949128 | tf_op jit(solution)/shard_map/ppermute | solution.py:20
  171.7 3.5 %constant_dynamic-update-slice_fusion.4 = bf16[22,128,1280]{2,1,0:T(8,128)(2,1)} fusion(bf16[8,128,1280]{2,1,0:T(8,128)(2,1)} %bitcast.118), kind=kLoop, calls=%fused_computation.45 | loop fusion | bytes 5242880
  175.1 3.5 %gather_fusion.4 = bf16[3,128,1280]{2,1,0:T(8,128)(2,1)} fusion(bf16[8,128,1280]{2,1,0:T(8,128)(2,1)} %bitcast.119, s32[1024]{0:T(1024)S(1)} %pad_clamp_fusion.2), kind=kCustom, calls=%fused_computation.4 | custom fusion | bytes 1966092 | tf_op jit(solution)/shard_map/gather | solution.py:184
  178.6 1.9 collective-permute-start.3
  180.5 3.3 %gather_fusion.5 = bf16[3,128,1280]{2,1,0:T(8,128)(2,1)} fusion(bf16[8,128,1280]{2,1,0:T(8,128)(2,1)} %bitcast.120, s32[1024]{0:T(1024)S(1)} %pad_clamp_fusion.1), kind=kCustom, calls=%fused_computation.5 | custom fusion | bytes 1966092 | tf_op jit(solution)/shard_map/gather | solution.py:184
  183.9 3.7 %collective-permute-start.5 = (bf16[3,128,1280]{2,1,0:T(8,128)(2,1)}, bf16[3,128,1280]{2,1,0:T(8,128)(2,1)}, u32[]{:S(2)}, u32[]{:S(2)}) collective-permute-start(bf16[3,128,1280]{2,1,0:T(8,128)(2,1)} %gather_fusion.5), channel_id=1, source_target_pairs={{4,0},{8,4},{12,8},{16,12},{20,16},{24,20},{28,24},{32,28},{36,32}... | collective-permute-start | bytes 2949128 | tf_op jit(solution)/shard_map/ppermute | solution.py:20
  187.6 2.4 gather_fusion.6
  190.0 2.1 collective-permute-start.7
  192.1 1.4 convert_reduce_fusion
  194.1 2.2 constant_dynamic-update-slice_fusion.3
  196.3 6.2 %collective-permute-done.3 = bf16[3,128,1280]{2,1,0:T(8,128)(2,1)} collective-permute-done((bf16[3,128,1280]{2,1,0:T(8,128)(2,1)}, bf16[3,128,1280]{2,1,0:T(8,128)(2,1)}, u32[]{:S(2)}, u32[]{:S(2)}) %collective-permute-start.3) | collective-permute-done | bytes 983072 | tf_op jit(solution)/shard_map/ppermute | solution.py:20
  202.6 2.2 constant_dynamic-update-slice_fusion.2
  204.8 1.7 collective-permute-done.5
  206.5 2.2 constant_dynamic-update-slice_fusion.1
  208.7 15.6 %collective-permute-done.7 = bf16[3,128,1280]{2,1,0:T(8,128)(2,1)S(1)} collective-permute-done((bf16[3,128,1280]{2,1,0:T(8,128)(2,1)S(1)}, bf16[3,128,1280]{2,1,0:T(8,128)(2,1)S(1)}, u32[]{:S(2)}, u32[]{:S(2)}) %collective-permute-start.7) | collective-permute-done | bytes 983072 | tf_op jit(solution)/shard_map/ppermute | solution.py:20
  224.3 1.1 constant_dynamic-update-slice_fusion
  225.4 1.2 fusion.18
  226.6 3.8 %fusion.3 = bf16[256,1280]{1,0:T(8,128)(2,1)} fusion(bf16[256,1280]{1,0:T(8,128)(2,1)S(1)} %copy-done.2, bf16[1280,3840]{1,0:T(8,128)(2,1)} %all-gather.6.cloned.1.call-done), kind=kOutput, calls=%fused_computation.11 | convolution fusion | flops 839188480 | bytes 4587520 | tf_op jit(solution)/shard_map/dot_general | solution.py:193
  230.4 25.1 %convolution_convert_fusion = bf16[2816,2560]{1,0:T(8,128)(2,1)} fusion(bf16[2816,1280]{1,0:T(8,128)(2,1)} %bitcast.123, bf16[1280,3840]{1,0:T(8,128)(2,1)} %all-gather.6.cloned.1.call-done), kind=kOutput, calls=%fused_computation.7 | convolution fusion | flops 18462146560 | bytes 28180480 | tf_op jit(solution)/shard_map/dot_general | solution.py:189
  255.4 53.2 %shard_map.109 = bf16[2,128,1280]{2,1,0:T(8,128)(2,1)} custom-call(s32[2,18]{1,0:T(2,128)} %pad_add_fusion.1.slots_ref, s32[2]{0:T(128)} %counts_ref.1, bf16[2,128,1280]{2,1,0:T(8,128)(2,1)} %bitcast.125, bf16[22,128,2560]{2,1,0:T(8,128)(2,1)} %bitcast.122), custom_call_target="tpu_custom_call" | custom-call | tf_op jit(solution)/shard_map/pallas_call | solution.py:114
  308.6 4.0 %convolution_convert_fusion.1 = bf16[256,1280]{1,0:T(8,128)(2,1)} fusion(bf16[256,1280]{1,0:T(8,128)(2,1)} %bitcast.124, bf16[1280,1280]{1,0:T(8,128)(2,1)} %all-gather.8.cloned.1.call-done), kind=kOutput, calls=%fused_computation.12 | convolution fusion | flops 839188480 | bytes 4587520 | tf_op jit(solution)/shard_map/dot_general | solution.py:214
  (83 shorter events, 10.4 us)
Async XLA Ops:
  6.5 2.2 copy-start
  6.5 45.3 %all-gather.4.cloned.1.call-start = ((), (), s32[]{:S(2)}) async-start(), calls=%async_computation | async-start | bytes 3276800 | tf_op jit(solution)/shard_map/all_gather | solution.py:173
  8.7 1.3 copy-start.1
  12.7 39.2 %copy-start.3 = (s32[2,16]{1,0:T(2,128)S(1)}, s32[2,16]{1,0:T(2,128)}, u32[]{:S(2)}) copy-start(s32[2,16]{1,0:T(2,128)} %param.13) | copy-start | bytes 388
  12.7 45.1 %copy-start.4 = (s32[2]{0:T(128)S(1)}, s32[2]{0:T(128)}, u32[]{:S(2)}) copy-start(s32[2]{0:T(128)} %param.15) | copy-start | bytes 28
  14.2 212.3 %all-gather.6.cloned.1.call-start = ((), (), s32[]{:S(2)}) async-start(), calls=%async_computation.1 | async-start | bytes 12288000 | tf_op jit(solution)/shard_map/all_gather | solution.py:177
  51.9 256.8 %all-gather.8.cloned.1.call-start = ((), (), s32[]{:S(2)}) async-start(), calls=%async_computation.2 | async-start | bytes 4096000 | tf_op jit(solution)/shard_map/all_gather | solution.py:216
  55.0 73.4 %collective-permute-start = (s32[3]{0:T(128)S(1)}, s32[3]{0:T(128)S(1)}, u32[]{:S(2)}, u32[]{:S(2)}) collective-permute-start(s32[3]{0:T(128)S(1)} %pad_add_fusion.2), channel_id=1, source_target_pairs={{8,0},{12,4},{16,8},{20,12},{24,16},{28,20},{32,24},{36,28},{40,32... | collective-permute-start | bytes 44 | tf_op jit(solution)/shard_map/ppermute | solution.py:20
  62.4 17.6 %collective-permute-start.8 = (bf16[2,128,1280]{2,1,0:T(8,128)(2,1)S(1)}, bf16[2,128,1280]{2,1,0:T(8,128)(2,1)S(1)}, u32[]{:S(2)}, u32[]{:S(2)}) collective-permute-start(bf16[2,128,1280]{2,1,0:T(8,128)(2,1)S(1)} %pad_maximum_fusion), channel_id=1, source_target_pairs={{0,64},{1,65},{2,66},{3,67},{4,68},{5,69},{6,70},{7,71},{8,72},{9,... | collective-permute-start | bytes 1966088 | tf_op jit(solution)/shard_map/ppermute | solution.py:164
  68.3 63.5 %collective-permute-start.2 = (s32[3]{0:T(128)S(1)}, s32[3]{0:T(128)S(1)}, u32[]{:S(2)}, u32[]{:S(2)}) collective-permute-start(s32[3]{0:T(128)S(1)} %pad_add_fusion.3), channel_id=1, source_target_pairs={{4,0},{8,4},{12,8},{16,12},{20,16},{24,20},{28,24},{32,28},{36,32}... | collective-permute-start | bytes 44 | tf_op jit(solution)/shard_map/ppermute | solution.py:20
  80.1 15.4 %collective-permute-start.9 = (bf16[2,128,1280]{2,1,0:T(8,128)(2,1)S(1)}, bf16[2,128,1280]{2,1,0:T(8,128)(2,1)}, u32[]{:S(2)}, u32[]{:S(2)}) collective-permute-start(bf16[2,128,1280]{2,1,0:T(8,128)(2,1)S(1)} %broadcast_select_fusion), channel_id=1, source_target_pairs={{0,32},{1,33},{2,34},{3,35},{4,36},{5,37},{6,38},{7,39},{8,40},{9,... | collective-permute-start | bytes 1966088 | tf_op jit(solution)/shard_map/ppermute | solution.py:164
  84.3 47.6 %collective-permute-start.4 = (s32[3]{0:T(128)S(1)}, s32[3]{0:T(128)S(1)}, u32[]{:S(2)}, u32[]{:S(2)}) collective-permute-start(s32[3]{0:T(128)S(1)} %pad_add_fusion.4), channel_id=1, source_target_pairs={{0,4},{4,8},{8,12},{12,16},{16,20},{20,24},{24,28},{28,32},{32,36}... | collective-permute-start | bytes 44 | tf_op jit(solution)/shard_map/ppermute | solution.py:20
  88.9 74.7 %collective-permute-start.6 = (s32[3]{0:T(128)S(1)}, s32[3]{0:T(128)S(1)}, u32[]{:S(2)}, u32[]{:S(2)}) collective-permute-start(s32[3]{0:T(128)S(1)} %pad_add_fusion.5), channel_id=1, source_target_pairs={{0,8},{4,12},{8,16},{12,20},{16,24},{20,28},{24,32},{28,36},{32,40... | collective-permute-start | bytes 44 | tf_op jit(solution)/shard_map/ppermute | solution.py:20
  96.7 15.9 %collective-permute-start.10 = (bf16[2,128,1280]{2,1,0:T(8,128)(2,1)S(1)}, bf16[2,128,1280]{2,1,0:T(8,128)(2,1)S(1)}, u32[]{:S(2)}, u32[]{:S(2)}) collective-permute-start(bf16[2,128,1280]{2,1,0:T(8,128)(2,1)S(1)} %broadcast_select_fusion.1), channel_id=1, source_target_pairs={{0,16},{1,17},{2,18},{3,19},{4,20},{5,21},{6,22},{7,23},{8,24},{9,... | collective-permute-start | bytes 1966088 | tf_op jit(solution)/shard_map/ppermute | solution.py:164
  112.8 14.8 %collective-permute-start.11 = (bf16[2,128,1280]{2,1,0:T(8,128)(2,1)S(1)}, bf16[2,128,1280]{2,1,0:T(8,128)(2,1)S(1)}, u32[]{:S(2)}, u32[]{:S(2)}) collective-permute-start(bf16[2,128,1280]{2,1,0:T(8,128)(2,1)S(1)} %broadcast_select_fusion.2), channel_id=1, source_target_pairs={{0,8},{1,9},{2,10},{3,11},{4,12},{5,13},{6,14},{7,15},{8,0},{9,1},... | collective-permute-start | bytes 1966088 | tf_op jit(solution)/shard_map/ppermute | solution.py:164
  127.7 2.2 collective-permute-start.12
  130.1 32.6 %collective-permute-start.13 = (bf16[2,128,1280]{2,1,0:T(8,128)(2,1)S(1)}, bf16[2,128,1280]{2,1,0:T(8,128)(2,1)S(1)}, u32[]{:S(2)}, u32[]{:S(2)}) collective-permute-start(bf16[2,128,1280]{2,1,0:T(8,128)(2,1)S(1)} %broadcast_select_fusion.4), channel_id=1, source_target_pairs={{0,2},{1,3},{2,0},{3,1},{4,6},{5,7},{6,4},{7,5},{8,10},{9,11},{10,... | collective-permute-start | bytes 1966088 | tf_op jit(solution)/shard_map/ppermute | solution.py:164
  162.8 29.3 %collective-permute-start.14 = (bf16[2,128,1280]{2,1,0:T(8,128)(2,1)S(1)}, bf16[2,128,1280]{2,1,0:T(8,128)(2,1)}, u32[]{:S(2)}, u32[]{:S(2)}) collective-permute-start(bf16[2,128,1280]{2,1,0:T(8,128)(2,1)S(1)} %broadcast_select_fusion.5), channel_id=1, source_target_pairs={{0,1},{1,0},{2,3},{3,2},{4,5},{5,4},{6,7},{7,6},{8,9},{9,8},{10,11... | collective-permute-start | bytes 1966088 | tf_op jit(solution)/shard_map/ppermute | solution.py:164
  167.0 27.0 %collective-permute-start.1 = (bf16[3,128,1280]{2,1,0:T(8,128)(2,1)}, bf16[3,128,1280]{2,1,0:T(8,128)(2,1)}, u32[]{:S(2)}, u32[]{:S(2)}) collective-permute-start(bf16[3,128,1280]{2,1,0:T(8,128)(2,1)} %gather_fusion.3), channel_id=1, source_target_pairs={{0,8},{4,12},{8,16},{12,20},{16,24},{20,28},{24,32},{28,36},{32,40... | collective-permute-start | bytes 2949128 | tf_op jit(solution)/shard_map/ppermute | solution.py:20
  178.6 23.9 %collective-permute-start.3 = (bf16[3,128,1280]{2,1,0:T(8,128)(2,1)}, bf16[3,128,1280]{2,1,0:T(8,128)(2,1)}, u32[]{:S(2)}, u32[]{:S(2)}) collective-permute-start(bf16[3,128,1280]{2,1,0:T(8,128)(2,1)} %gather_fusion.4), channel_id=1, source_target_pairs={{0,4},{4,8},{8,12},{12,16},{16,20},{20,24},{24,28},{28,32},{32,36}... | collective-permute-start | bytes 2949128 | tf_op jit(solution)/shard_map/ppermute | solution.py:20
  183.9 22.6 %collective-permute-start.5 = (bf16[3,128,1280]{2,1,0:T(8,128)(2,1)}, bf16[3,128,1280]{2,1,0:T(8,128)(2,1)}, u32[]{:S(2)}, u32[]{:S(2)}) collective-permute-start(bf16[3,128,1280]{2,1,0:T(8,128)(2,1)} %gather_fusion.5), channel_id=1, source_target_pairs={{4,0},{8,4},{12,8},{16,12},{20,16},{24,20},{28,24},{32,28},{36,32}... | collective-permute-start | bytes 2949128 | tf_op jit(solution)/shard_map/ppermute | solution.py:20
  190.0 34.4 %collective-permute-start.7 = (bf16[3,128,1280]{2,1,0:T(8,128)(2,1)S(1)}, bf16[3,128,1280]{2,1,0:T(8,128)(2,1)S(1)}, u32[]{:S(2)}, u32[]{:S(2)}) collective-permute-start(bf16[3,128,1280]{2,1,0:T(8,128)(2,1)S(1)} %gather_fusion.6), channel_id=1, source_target_pairs={{8,0},{12,4},{16,8},{20,12},{24,16},{28,20},{32,24},{36,28},{40,32... | collective-permute-start | bytes 2949128 | tf_op jit(solution)/shard_map/ppermute | solution.py:20
  204.8 21.8 %copy-start.2 = (bf16[256,1280]{1,0:T(8,128)(2,1)S(1)}, bf16[256,1280]{1,0:T(8,128)(2,1)}, u32[]{:S(2)}) copy-start(bf16[256,1280]{1,0:T(8,128)(2,1)} %fusion.17) | copy-start | bytes 1966084
Sparse Core Ops, SparseCore 0:
  14.4 37.4 all-gather.3
  53.5 109.2 all-gather.5
  164.5 41.7 all-gather.7

commit v5 on v4

--- a/solution.py
+++ b/solution.py
@@ -18,6 +18,19 @@
     devices = range(lax.axis_size(axis))
     route = [(i - distance, i) for i in devices if i - distance in devices]
     return lax.ppermute(block, axis, route)
+
+
+def gathered_weight(shard):
+    core = lax.axis_index("seq") % 2
+    half = shard.shape[1] // 2
+    mine = lax.all_gather(
+        lax.dynamic_slice_in_dim(shard, core * half, half, 1), "fsdp", axis=0, tiled=True
+    )
+    seq_size = lax.axis_size("seq")
+    other = lax.ppermute(mine, "seq", [(i, i ^ 1) for i in range(seq_size)])
+    low = jnp.where(core == 0, mine, other)
+    high = jnp.where(core == 0, other, mine)
+    return jnp.concatenate([low, high], axis=1)
 
 
 def layer_norm(stream, ln_gain, ln_bias):
@@ -140,42 +153,25 @@
     fsdp_size = lax.axis_size("fsdp")
     seq_size = lax.axis_size("seq")
     seq_at = lax.axis_index("seq")
-    dev_at = seq_at * fsdp_size + lax.axis_index("fsdp")
     group_tiles = tile_count * fsdp_size
 
     stream = embed(patches, vis_index, frame_table, space_table)
 
-    dev_count = seq_size * fsdp_size
-    global_rows = []
-    owners = []
-    for slot_no in range(GLOBAL):
-        tile_id = global_tiles[slot_no]
-        owners.append(tile_id // tile_count)
-        global_rows.append(
-            lax.dynamic_slice_in_dim(stream, tile_id % tile_count * TILE, TILE, 0)
-        )
-    global_stream = jnp.stack(global_rows)
-    owners = jnp.stack(owners)
-    bit_order = sorted(range(dev_count.bit_length() - 1), key=lambda b: -b)
-    done_bits = 0
-    for bit in bit_order:
-        step = 1 << bit
-        held = ((dev_at ^ owners) & ~done_bits) == 0
-        got = lax.ppermute(
-            global_stream, ("seq", "fsdp"), [(i, i ^ step) for i in range(dev_count)]
-        )
-        global_stream = jnp.where(held[:, None, None], global_stream, got)
-        done_bits |= step
-    global_stream = global_stream.reshape(GLOBAL * TILE, feat_width)
-
     normed = layer_norm(stream, ln_gain, ln_bias)
-    global_normed = layer_norm(global_stream, ln_gain, ln_bias)
     group_rows = lax.all_gather(normed, "fsdp", axis=0, tiled=True).reshape(
         group_tiles, TILE, feat_width
     )
     w_src, group_rows = lax.optimization_barrier((w_qkv, group_rows))
-    w_full = lax.all_gather(w_src, "fsdp", axis=0, tiled=True)
-
+    w_full = gathered_weight(w_src)
+
+    global_ids = global_tiles.astype(jnp.int32)
+    global_rows = group_rows[global_ids % group_tiles]
+    owners = global_ids // group_tiles
+    for bit in sorted(range(seq_size.bit_length() - 1), key=lambda b: -b):
+        step = 1 << bit
+        held = ((seq_at ^ owners) & (2 * step - 1)) == 0
+        got = lax.ppermute(global_rows, "seq", [(i, i ^ step) for i in range(seq_size)])
+        global_rows = jnp.where(held[:, None, None], global_rows, got)
     near_blocks = []
     near_rank = []
     for reach in REACH:
@@ -184,7 +180,7 @@
         near_blocks.append(passed_along(group_rows[asked], "seq", -reach))
         near_rank.append(rank)
     window_rows = jnp.concatenate(
-        [group_rows] + near_blocks + [global_normed.reshape(GLOBAL, TILE, feat_width)], axis=0
+        [group_rows] + near_blocks + [global_rows], axis=0
     )
     window = jnp.dot(
         window_rows.reshape(-1, feat_width), w_full[:, feat_width:],
@@ -213,7 +209,7 @@
     heads_out = attend(query_tiles, window, slots, kv_count).reshape(tok_rows, feat_width)
     return jnp.dot(
         heads_out,
-        lax.all_gather(w_out, "fsdp", axis=0, tiled=True),
+        gathered_weight(w_out),
         preferred_element_type=jnp.float32,
     ).astype(jnp.bfloat16)
 

time: 321 us -> 321 us (level)
  the two profiles are of different devices: /device:TPU:24 before, /device:TPU:50 now
where the time goes in v5:
time: 321 us; the launch traced here: 315 us
  waiting for transfers between devices  129 us (40%)
  Pallas kernels  51.4 us (16%)
  matrix products  31.7 us (10%)
  local copies, waits for them, and re-layouts  31.4 us (10%)
  starting transfers between devices  29.7 us (9%)
  other arithmetic  28.8 us (9%)
  between operations  13.5 us (4%)
    pallas_call x1, Pallas kernels, attend(): pl.pallas_call(attention_kernel, grid_spec=grid_spec, out_shape=jax.Shape...  51.4 us
    all_gather x2, waiting for transfers between devices, gathered_weight(): lax.all_gather(lax.dynamic_slice_in_dim(shard, core * half, half, 1), 'fs...  39.8 us
    all_gather x1, waiting for transfers between devices, local(): lax.all_gather(normed, 'fsdp', axis=0, tiled=True)  36.2 us
    ppermute x5, waiting for transfers between devices, local(): lax.ppermute(global_rows, 'seq', [(i, i ^ step) for i in range(seq_size)])  35.5 us
    dot_general x1, matrix products, local(): jnp.dot(window_rows.reshape(-1, feat_width), w_full[:, feat_width:], pref...  23.6 us
    ppermute x8, starting transfers between devices, passed_along(): return lax.ppermute(block, axis, route)  21.8 us
    ppermute x8, waiting for transfers between devices, passed_along(): return lax.ppermute(block, axis, route)  17.3 us
    gather x4, local copies, waits for them, and re-layouts, local(): near_blocks.append(passed_along(group_rows[asked], 'seq', -reach))  13.4 us
  transfers between devices with their start and end apart: 18, of which 7 were waited for; matrix products, arithmetic and copies ran while one was open for 12% of the time, Pallas kernels for 0%

profile of v5, /device:TPU:50, one launch (start us, length us, event | category | flops | bytes accessed | tf_op | source)
XLA Modules:
  0.0 315.5 jit_solution(9496025937560381401)
XLA Ops:
  6.5 0.8 compare_select_fusion.1
  7.4 0.8 convert_element_type.99
  8.2 0.7 convert_element_type.98
  8.9 4.1 %gather_fusion.2 = bf16[256,1280]{1,0:T(8,128)(2,1)} fusion(bf16[512,1280]{1,0:T(8,128)(2,1)} %param.17, s32[1024]{0:T(1024)S(1)} %get-tuple-element.45), kind=kCustom, calls=%fused_computation.2 | custom fusion | bytes 1311744 | tf_op jit(solution)/shard_map/gather | solution.py:51
  13.0 2.1 gather_fusion.1
  15.0 1.8 convert_reduce_fusion
  17.2 1.2 fusion.18
  18.5 36.2 %all-gather.4.cloned.1.call-done = bf16[1024,1280]{1,0:T(8,128)(2,1)} async-done(((bf16[256,1280]{1,0:T(8,128)(2,1)}), bf16[1024,1280]{1,0:T(8,128)(2,1)}) %all-gather.4.cloned.1.call-update) | async-done | bytes 2621456 | tf_op jit(solution)/shard_map/all_gather | solution.py:161
  54.7 1.2 constant_dynamic-slice_fusion.1
  56.5 0.7 fusion.38
  57.2 1.8 pad_add_fusion.2
  59.0 2.4 collective-permute-start.1
  61.6 0.7 fusion.41
  62.3 1.8 pad_add_fusion.3
  64.1 1.9 collective-permute-start.3
  66.9 1.8 pad_add_fusion.4
  68.8 2.4 collective-permute-start.5
  72.0 1.8 pad_add_fusion.5
  73.8 3.4 %collective-permute-start.7 = (s32[3]{0:T(128)S(1)}, s32[3]{0:T(128)S(1)}, u32[]{:S(2)}, u32[]{:S(2)}) collective-permute-start(s32[3]{0:T(128)S(1)} %pad_add_fusion.5), channel_id=1, source_target_pairs={{0,8},{4,12},{8,16},{12,20},{16,24},{20,28},{24,32},{28,36},{32,40... | collective-permute-start | bytes 44 | tf_op jit(solution)/shard_map/ppermute | solution.py:20
  77.3 0.8 constant_dynamic-slice_fusion
  78.3 0.8 gather_fusion
  79.2 2.4 gather_fusion.7
  81.6 2.2 collective-permute-start.9
  84.4 14.7 %collective-permute-done.9 = bf16[2,128,1280]{2,1,0:T(8,128)(2,1)S(1)} collective-permute-done((bf16[2,128,1280]{2,1,0:T(8,128)(2,1)S(1)}, bf16[2,128,1280]{2,1,0:T(8,128)(2,1)S(1)}, u32[]{:S(2)}, u32[]{:S(2)}) %collective-permute-start.9) | collective-permute-done | bytes 655392 | tf_op jit(solution)/shard_map/ppermute | solution.py:173
  99.9 11.2 %all-gather.6.cloned.1.call-done = bf16[1280,1920]{1,0:T(8,128)(2,1)} async-done(((bf16[320,1920]{1,0:T(8,128)(2,1)}), bf16[1280,1920]{1,0:T(8,128)(2,1)}) %all-gather.6.cloned.1.call-update) | async-done | bytes 4915216 | tf_op jit(solution)/shard_map/all_gather | solution.py:26
  111.2 28.6 %all-gather.8.cloned.1.call-done = bf16[1280,640]{1,0:T(8,128)(2,1)} async-done(((bf16[320,640]{1,0:T(8,128)(2,1)}), bf16[1280,640]{1,0:T(8,128)(2,1)}) %all-gather.8.cloned.1.call-update) | async-done | bytes 1638416 | tf_op jit(solution)/shard_map/all_gather | solution.py:26
  140.6 3.4 %gather_fusion.3 = bf16[3,128,1280]{2,1,0:T(8,128)(2,1)} fusion(bf16[8,128,1280]{2,1,0:T(8,128)(2,1)} %bitcast.109, s32[1024]{0:T(1024)S(1)} %pad_clamp_fusion.4), kind=kCustom, calls=%fused_computation.3 | custom fusion | bytes 1966092 | tf_op jit(solution)/shard_map/gather | solution.py:180
  143.9 4.0 %collective-permute-start.2 = (bf16[3,128,1280]{2,1,0:T(8,128)(2,1)}, bf16[3,128,1280]{2,1,0:T(8,128)(2,1)S(1)}, u32[]{:S(2)}, u32[]{:S(2)}) collective-permute-start(bf16[3,128,1280]{2,1,0:T(8,128)(2,1)} %gather_fusion.3), channel_id=1, source_target_pairs={{0,8},{4,12},{8,16},{12,20},{16,24},{20,28},{24,32},{28,36},{32,40... | collective-permute-start | bytes 2949128 | tf_op jit(solution)/shard_map/ppermute | solution.py:20
  147.9 3.3 %gather_fusion.4 = bf16[3,128,1280]{2,1,0:T(8,128)(2,1)} fusion(bf16[8,128,1280]{2,1,0:T(8,128)(2,1)} %bitcast.110, s32[1024]{0:T(1024)S(1)} %pad_clamp_fusion.3), kind=kCustom, calls=%fused_computation.4 | custom fusion | bytes 1966092 | tf_op jit(solution)/shard_map/gather | solution.py:180
  151.3 1.9 collective-permute-start.4
  153.2 3.4 %gather_fusion.5 = bf16[3,128,1280]{2,1,0:T(8,128)(2,1)} fusion(bf16[8,128,1280]{2,1,0:T(8,128)(2,1)} %bitcast.111, s32[1024]{0:T(1024)S(1)} %pad_clamp_fusion.2), kind=kCustom, calls=%fused_computation.5 | custom fusion | bytes 1966092 | tf_op jit(solution)/shard_map/gather | solution.py:180
  156.5 3.3 %gather_fusion.6 = bf16[3,128,1280]{2,1,0:T(8,128)(2,1)} fusion(bf16[8,128,1280]{2,1,0:T(8,128)(2,1)} %bitcast.112, s32[1024]{0:T(1024)S(1)} %pad_clamp_fusion.1), kind=kCustom, calls=%fused_computation.6 | custom fusion | bytes 1966092 | tf_op jit(solution)/shard_map/gather | solution.py:180
  159.9 2.0 constant_dynamic-update-slice_fusion.4
  161.9 3.6 %collective-permute-start.6 = (bf16[3,128,1280]{2,1,0:T(8,128)(2,1)}, bf16[3,128,1280]{2,1,0:T(8,128)(2,1)S(1)}, u32[]{:S(2)}, u32[]{:S(2)}) collective-permute-start(bf16[3,128,1280]{2,1,0:T(8,128)(2,1)} %gather_fusion.5), channel_id=1, source_target_pairs={{4,0},{8,4},{12,8},{16,12},{20,16},{24,20},{28,24},{32,28},{36,32}... | collective-permute-start | bytes 2949128 | tf_op jit(solution)/shard_map/ppermute | solution.py:20
  165.7 3.1 collective-permute-start.12
  168.8 3.4 %broadcast_select_fusion.3 = (bf16[1280,640]{1,0:T(8,128)(2,1)}, bf16[1280,640]{1,0:T(8,128)(2,1)}) fusion(bf16[1280,640]{1,0:T(8,128)(2,1)S(1)} %copy-done.5, bf16[1280,640]{1,0:T(8,128)(2,1)} %collective-permute-done.14, pred[]{:T(512)S(6)} %eq.164), kind=kLoop, calls=%fused_computation.22 | loop fusion | flops 1638400 | bytes 6553601 | tf_op jit(solution)/shard_map/jit(_where)/select_n | solution.py:31
  172.2 8.4 %collective-permute-done.2 = bf16[3,128,1280]{2,1,0:T(8,128)(2,1)S(1)} collective-permute-done((bf16[3,128,1280]{2,1,0:T(8,128)(2,1)}, bf16[3,128,1280]{2,1,0:T(8,128)(2,1)S(1)}, u32[]{:S(2)}, u32[]{:S(2)}) %collective-permute-start.2) | collective-permute-done | bytes 983072 | tf_op jit(solution)/shard_map/ppermute | solution.py:20
  180.6 2.1 collective-permute-start.8
  182.8 20.8 %collective-permute-done.12 = bf16[2,128,1280]{2,1,0:T(8,128)(2,1)S(1)} collective-permute-done((bf16[2,128,1280]{2,1,0:T(8,128)(2,1)S(1)}, bf16[2,128,1280]{2,1,0:T(8,128)(2,1)S(1)}, u32[]{:S(2)}, u32[]{:S(2)}) %collective-permute-start.12) | collective-permute-done | bytes 655392 | tf_op jit(solution)/shard_map/ppermute | solution.py:173
  203.7 1.4 collective-permute-start.13
  205.1 1.3 constant_dynamic-update-slice_fusion.2
  206.5 8.9 %collective-permute-done.8 = bf16[3,128,1280]{2,1,0:T(8,128)(2,1)S(1)} collective-permute-done((bf16[3,128,1280]{2,1,0:T(8,128)(2,1)}, bf16[3,128,1280]{2,1,0:T(8,128)(2,1)S(1)}, u32[]{:S(2)}, u32[]{:S(2)}) %collective-permute-start.8) | collective-permute-done | bytes 983072 | tf_op jit(solution)/shard_map/ppermute | solution.py:20
  215.8 2.9 copy-done.6
  218.7 7.1 %broadcast_select_fusion = (bf16[1280,1920]{1,0:T(8,128)(2,1)}, bf16[1280,1920]{1,0:T(8,128)(2,1)}) fusion(bf16[1280,1920]{1,0:T(8,128)(2,1)} %collective-permute-done, bf16[1280,1920]{1,0:T(8,128)(2,1)S(1)} %bitcast.116, pred[]{:T(512)S(6)} %eq.164), kind=kLoop, calls=%fused_computation.11 | loop fusion | flops 4915200 | bytes 19660800 | tf_op jit(solution)/shard_map/jit(_where)/select_n | solution.py:32
  225.8 3.9 %fusion.7 = bf16[256,1280]{1,0:T(8,128)(2,1)} fusion(bf16[256,1280]{1,0:T(8,128)(2,1)S(1)} %copy-done.4, bf16[1280,1920]{1,0:T(8,128)(2,1)} %get-tuple-element.32), kind=kOutput, calls=%fused_computation.19 | convolution fusion | flops 839188480 | bytes 4587520 | tf_op jit(solution)/shard_map/dot_general | solution.py:189
  229.8 23.6 %convolution_convert_fusion = bf16[2816,2560]{1,0:T(8,128)(2,1)} fusion(bf16[2816,1280]{1,0:T(8,128)(2,1)} %bitcast.117, bf16[1280,1920]{1,0:T(8,128)(2,1)S(1)} %copy-done.3, bf16[1280,1920]{1,0:T(8,128)(2,1)} %get-tuple-element.32), kind=kOutput, calls=%fused_computation.8 | convolution fusion | flops 18475253760 | bytes 31457280 | tf_op jit(solution)/shard_map/dot_general | solution.py:185
  253.4 51.4 %shard_map.109 = bf16[2,128,1280]{2,1,0:T(8,128)(2,1)} custom-call(s32[2,18]{1,0:T(2,128)} %pad_add_fusion.1.slots_ref, s32[2]{0:T(128)} %counts_ref.1, bf16[2,128,1280]{2,1,0:T(8,128)(2,1)} %bitcast.118, bf16[22,128,2560]{2,1,0:T(8,128)(2,1)} %bitcast.114), custom_call_target="tpu_custom_call" | custom-call | tf_op jit(solution)/shard_map/pallas_call | solution.py:127
  304.8 4.1 %fusion.10 = bf16[256,1280]{1,0:T(8,128)(2,1)} fusion(bf16[256,1280]{1,0:T(8,128)(2,1)} %bitcast.119, bf16[1280,640]{1,0:T(8,128)(2,1)} %get-tuple-element.34, bf16[1280,640]{1,0:T(8,128)(2,1)} %get-tuple-element.33), kind=kOutput, calls=%fused_computation.20 | convolution fusion | flops 845742080 | bytes 4587520 | tf_op jit(solution)/shard_map/dot_general | solution.py:210
  (96 shorter events, 6.2 us)
Async XLA Ops:
  6.5 48.2 %copy-start = (bf16[320,3840]{1,0:T(8,128)(2,1)S(1)}, bf16[320,3840]{1,0:T(8,128)(2,1)}, u32[]{:S(2)}) copy-start(bf16[320,3840]{1,0:T(8,128)(2,1)} %param.20) | copy-start | bytes 7372804
  6.5 6.4 %copy-start.2 = (bf16[256,1280]{1,0:T(8,128)(2,1)S(1)}, bf16[256,1280]{1,0:T(8,128)(2,1)}, u32[]{:S(2)}) copy-start(bf16[256,1280]{1,0:T(8,128)(2,1)} %param.16) | copy-start | bytes 1966084
  6.5 48.2 %all-gather.4.cloned.1.call-start = ((), (), s32[]{:S(2)}) async-start(), calls=%async_computation | async-start | bytes 3276800 | tf_op jit(solution)/shard_map/all_gather | solution.py:161
  16.9 39.1 %copy-start.8 = (s32[2,16]{1,0:T(2,128)S(1)}, s32[2,16]{1,0:T(2,128)}, u32[]{:S(2)}) copy-start(s32[2,16]{1,0:T(2,128)} %param.13) | copy-start | bytes 388
  16.9 60.4 %copy-start.7 = (bf16[320,1280]{1,0:T(8,128)(2,1)S(1)}, bf16[320,1280]{1,0:T(8,128)(2,1)}, u32[]{:S(2)}) copy-start(bf16[320,1280]{1,0:T(8,128)(2,1)} %param.21) | copy-start | bytes 2457604
  18.4 60.6 %copy-start.9 = (s32[2]{0:T(128)S(1)}, s32[2]{0:T(128)}, u32[]{:S(2)}) copy-start(s32[2]{0:T(128)} %param.15) | copy-start | bytes 28
  18.4 92.7 %all-gather.6.cloned.1.call-start = ((), (), s32[]{:S(2)}) async-start(), calls=%async_computation.1 | async-start | bytes 6144000 | tf_op jit(solution)/shard_map/all_gather | solution.py:26
  55.9 83.9 %all-gather.8.cloned.1.call-start = ((), (), s32[]{:S(2)}) async-start(), calls=%async_computation.2 | async-start | bytes 2048000 | tf_op jit(solution)/shard_map/all_gather | solution.py:26
  59.0 25.4 %collective-permute-start.1 = (s32[3]{0:T(128)S(1)}, s32[3]{0:T(128)S(1)}, u32[]{:S(2)}, u32[]{:S(2)}) collective-permute-start(s32[3]{0:T(128)S(1)} %pad_add_fusion.2), channel_id=1, source_target_pairs={{8,0},{12,4},{16,8},{20,12},{24,16},{28,20},{32,24},{36,28},{40,32... | collective-permute-start | bytes 44 | tf_op jit(solution)/shard_map/ppermute | solution.py:20
  64.1 35.8 %collective-permute-start.3 = (s32[3]{0:T(128)S(1)}, s32[3]{0:T(128)S(1)}, u32[]{:S(2)}, u32[]{:S(2)}) collective-permute-start(s32[3]{0:T(128)S(1)} %pad_add_fusion.3), channel_id=1, source_target_pairs={{4,0},{8,4},{12,8},{16,12},{20,16},{24,20},{28,24},{32,28},{36,32}... | collective-permute-start | bytes 44 | tf_op jit(solution)/shard_map/ppermute | solution.py:20
  68.8 42.4 %collective-permute-start.5 = (s32[3]{0:T(128)S(1)}, s32[3]{0:T(128)S(1)}, u32[]{:S(2)}, u32[]{:S(2)}) collective-permute-start(s32[3]{0:T(128)S(1)} %pad_add_fusion.4), channel_id=1, source_target_pairs={{0,4},{4,8},{8,12},{12,16},{16,20},{20,24},{24,28},{28,32},{32,36}... | collective-permute-start | bytes 44 | tf_op jit(solution)/shard_map/ppermute | solution.py:20
  73.8 66.7 %collective-permute-start.7 = (s32[3]{0:T(128)S(1)}, s32[3]{0:T(128)S(1)}, u32[]{:S(2)}, u32[]{:S(2)}) collective-permute-start(s32[3]{0:T(128)S(1)} %pad_add_fusion.5), channel_id=1, source_target_pairs={{0,8},{4,12},{8,16},{12,20},{16,24},{20,28},{24,32},{28,36},{32,40... | collective-permute-start | bytes 44 | tf_op jit(solution)/shard_map/ppermute | solution.py:20
  81.6 17.5 %collective-permute-start.9 = (bf16[2,128,1280]{2,1,0:T(8,128)(2,1)S(1)}, bf16[2,128,1280]{2,1,0:T(8,128)(2,1)S(1)}, u32[]{:S(2)}, u32[]{:S(2)}) collective-permute-start(bf16[2,128,1280]{2,1,0:T(8,128)(2,1)S(1)} %gather_fusion.7), channel_id=1, source_target_pairs={{0,64},{4,68},{8,72},{12,76},{16,80},{20,84},{24,88},{28,92},{32,9... | collective-permute-start | bytes 1966088 | tf_op jit(solution)/shard_map/ppermute | solution.py:173
  99.3 40.5 %collective-permute-start.10 = (bf16[2,128,1280]{2,1,0:T(8,128)(2,1)S(1)}, bf16[2,128,1280]{2,1,0:T(8,128)(2,1)S(1)}, u32[]{:S(2)}, u32[]{:S(2)}) collective-permute-start(bf16[2,128,1280]{2,1,0:T(8,128)(2,1)S(1)} %broadcast_select_fusion.4), channel_id=1, source_target_pairs={{0,32},{4,36},{8,40},{12,44},{16,48},{20,52},{24,56},{28,60},{32,0... | collective-permute-start | bytes 1966088 | tf_op jit(solution)/shard_map/ppermute | solution.py:173
  111.1 107.5 %collective-permute-start = (bf16[1280,1920]{1,0:T(8,128)(2,1)}, bf16[1280,1920]{1,0:T(8,128)(2,1)}, u32[]{:S(2)}, u32[]{:S(2)}) collective-permute-start(bf16[1280,1920]{1,0:T(8,128)(2,1)} %all-gather.6.cloned.1.call-done), channel_id=1, source_target_pairs={{0,4},{4,0},{8,12},{12,8},{16,20},{20,16},{24,28},{28,24},{32,36},... | collective-permute-start | bytes 14745608 | tf_op jit(solution)/shard_map/ppermute | solution.py:30
  139.8 25.9 %collective-permute-start.14 = (bf16[1280,640]{1,0:T(8,128)(2,1)}, bf16[1280,640]{1,0:T(8,128)(2,1)}, u32[]{:S(2)}, u32[]{:S(2)}) collective-permute-start(bf16[1280,640]{1,0:T(8,128)(2,1)} %all-gather.8.cloned.1.call-done), channel_id=1, source_target_pairs={{0,4},{4,0},{8,12},{12,8},{16,20},{20,16},{24,28},{28,24},{32,36},... | collective-permute-start | bytes 4915208 | tf_op jit(solution)/shard_map/ppermute | solution.py:30
  139.9 22.0 %collective-permute-start.11 = (bf16[2,128,1280]{2,1,0:T(8,128)(2,1)S(1)}, bf16[2,128,1280]{2,1,0:T(8,128)(2,1)S(1)}, u32[]{:S(2)}, u32[]{:S(2)}) collective-permute-start(bf16[2,128,1280]{2,1,0:T(8,128)(2,1)S(1)} %broadcast_select_fusion.5), channel_id=1, source_target_pairs={{0,16},{4,20},{8,24},{12,28},{16,0},{20,4},{24,8},{28,12},{32,48},... | collective-permute-start | bytes 1966088 | tf_op jit(solution)/shard_map/ppermute | solution.py:173
  143.9 36.7 %collective-permute-start.2 = (bf16[3,128,1280]{2,1,0:T(8,128)(2,1)}, bf16[3,128,1280]{2,1,0:T(8,128)(2,1)S(1)}, u32[]{:S(2)}, u32[]{:S(2)}) collective-permute-start(bf16[3,128,1280]{2,1,0:T(8,128)(2,1)} %gather_fusion.3), channel_id=1, source_target_pairs={{0,8},{4,12},{8,16},{12,20},{16,24},{20,28},{24,32},{28,36},{32,40... | collective-permute-start | bytes 2949128 | tf_op jit(solution)/shard_map/ppermute | solution.py:20
  151.3 53.9 %collective-permute-start.4 = (bf16[3,128,1280]{2,1,0:T(8,128)(2,1)}, bf16[3,128,1280]{2,1,0:T(8,128)(2,1)}, u32[]{:S(2)}, u32[]{:S(2)}) collective-permute-start(bf16[3,128,1280]{2,1,0:T(8,128)(2,1)} %gather_fusion.4), channel_id=1, source_target_pairs={{0,4},{4,8},{8,12},{12,16},{16,20},{20,24},{24,28},{28,32},{32,36}... | collective-permute-start | bytes 2949128 | tf_op jit(solution)/shard_map/ppermute | solution.py:20
  159.9 8.9 %copy-start.5 = (bf16[1280,640]{1,0:T(8,128)(2,1)S(1)}, bf16[1280,640]{1,0:T(8,128)(2,1)}, u32[]{:S(2)}) copy-start(bf16[1280,640]{1,0:T(8,128)(2,1)} %all-gather.8.cloned.1.call-done) | copy-start | bytes 4915204
  161.9 44.5 %collective-permute-start.6 = (bf16[3,128,1280]{2,1,0:T(8,128)(2,1)}, bf16[3,128,1280]{2,1,0:T(8,128)(2,1)S(1)}, u32[]{:S(2)}, u32[]{:S(2)}) collective-permute-start(bf16[3,128,1280]{2,1,0:T(8,128)(2,1)} %gather_fusion.5), channel_id=1, source_target_pairs={{4,0},{8,4},{12,8},{16,12},{20,16},{24,20},{28,24},{32,28},{36,32}... | collective-permute-start | bytes 2949128 | tf_op jit(solution)/shard_map/ppermute | solution.py:20
  165.7 37.8 %collective-permute-start.12 = (bf16[2,128,1280]{2,1,0:T(8,128)(2,1)S(1)}, bf16[2,128,1280]{2,1,0:T(8,128)(2,1)S(1)}, u32[]{:S(2)}, u32[]{:S(2)}) collective-permute-start(bf16[2,128,1280]{2,1,0:T(8,128)(2,1)S(1)} %broadcast_select_fusion.6), channel_id=1, source_target_pairs={{0,8},{4,12},{8,0},{12,4},{16,24},{20,28},{24,16},{28,20},{32,40},... | collective-permute-start | bytes 1966088 | tf_op jit(solution)/shard_map/ppermute | solution.py:173
  180.6 34.8 %collective-permute-start.8 = (bf16[3,128,1280]{2,1,0:T(8,128)(2,1)}, bf16[3,128,1280]{2,1,0:T(8,128)(2,1)S(1)}, u32[]{:S(2)}, u32[]{:S(2)}) collective-permute-start(bf16[3,128,1280]{2,1,0:T(8,128)(2,1)} %gather_fusion.6), channel_id=1, source_target_pairs={{8,0},{12,4},{16,8},{20,12},{24,16},{28,20},{32,24},{36,28},{40,32... | collective-permute-start | bytes 2949128 | tf_op jit(solution)/shard_map/ppermute | solution.py:20
  182.7 36.0 %slice-start = ((s8[4915200]{0:T(1024)(128)(4,1)}), s8[4194304]{0:T(1024)(128)(4,1)S(1)}, s32[]{:S(2)}) async-start(s8[4915200]{0:T(1024)(128)(4,1)} %bitcast.115), calls=%async_computation.3 | async-start | bytes 8388608
  203.7 15.0 %slice-start.1 = ((s8[4915200]{0:T(1024)(128)(4,1)}), s8[720896]{0:T(1024)(128)(4,1)S(1)}, s32[]{:S(2)}) async-start(s8[4915200]{0:T(1024)(128)(4,1)} %bitcast.115), calls=%async_computation.4 | async-start | bytes 1441792
  203.7 11.8 %collective-permute-start.13 = (bf16[2,128,1280]{2,1,0:T(8,128)(2,1)S(1)}, bf16[2,128,1280]{2,1,0:T(8,128)(2,1)S(1)}, u32[]{:S(2)}, u32[]{:S(2)}) collective-permute-start(bf16[2,128,1280]{2,1,0:T(8,128)(2,1)S(1)} %broadcast_select_fusion.7), channel_id=1, source_target_pairs={{0,4},{4,0},{8,12},{12,8},{16,20},{20,16},{24,28},{28,24},{32,36},... | collective-permute-start | bytes 1966088 | tf_op jit(solution)/shard_map/ppermute | solution.py:173
  215.8 2.9 copy-start.6
  218.7 7.2 %copy-start.4 = (bf16[256,1280]{1,0:T(8,128)(2,1)S(1)}, bf16[256,1280]{1,0:T(8,128)(2,1)}, u32[]{:S(2)}) copy-start(bf16[256,1280]{1,0:T(8,128)(2,1)} %fusion.18) | copy-start | bytes 1966084
  225.8 3.9 %copy-start.3 = (bf16[1280,1920]{1,0:T(8,128)(2,1)S(1)}, bf16[1280,1920]{1,0:T(8,128)(2,1)}, u32[]{:S(2)}) copy-start(bf16[1280,1920]{1,0:T(8,128)(2,1)} %get-tuple-element.31) | copy-start | bytes 14745604
  304.8 4.1 %copy-start.1 = (bf16[320,3840]{1,0:T(8,128)(2,1)S(1)}, bf16[320,3840]{1,0:T(8,128)(2,1)}, u32[]{:S(2)}) copy-start(bf16[320,3840]{1,0:T(8,128)(2,1)} %param.20) | copy-start | bytes 7372804
Sparse Core Ops, SparseCore 0:
  18.5 36.1 all-gather.3
  56.4 54.7 all-gather.5
  112.8 26.9 all-gather.7

commit v6 on v5

--- a/solution.py
+++ b/solution.py
@@ -161,27 +161,35 @@
     group_rows = lax.all_gather(normed, "fsdp", axis=0, tiled=True).reshape(
         group_tiles, TILE, feat_width
     )
-    w_src, group_rows = lax.optimization_barrier((w_qkv, group_rows))
+
+    def tiles_at(ids):
+        return jnp.concatenate(
+            [lax.dynamic_slice_in_dim(group_rows, ids[n], 1, 0) for n in range(ids.shape[0])]
+        )
+
+    global_ids = global_tiles.astype(jnp.int32)
+    global_rows = tiles_at(global_ids % group_tiles)
+    owners = global_ids // group_tiles
+
+    sends = []
+    near_rank = []
+    for reach in REACH:
+        picks, rank = near_tiles(kv_list, seq_at + reach, group_tiles)
+        sends.append(tiles_at(passed_along(picks, "seq", reach)))
+        near_rank.append(rank)
+
+    w_src, global_rows, sends = lax.optimization_barrier((w_qkv, global_rows, sends))
     w_full = gathered_weight(w_src)
-
-    global_ids = global_tiles.astype(jnp.int32)
-    global_rows = group_rows[global_ids % group_tiles]
-    owners = global_ids // group_tiles
+    near_blocks = [passed_along(sent, "seq", -reach) for sent, reach in zip(sends, REACH)]
     for bit in sorted(range(seq_size.bit_length() - 1), key=lambda b: -b):
         step = 1 << bit
         held = ((seq_at ^ owners) & (2 * step - 1)) == 0
         got = lax.ppermute(global_rows, "seq", [(i, i ^ step) for i in range(seq_size)])
         global_rows = jnp.where(held[:, None, None], global_rows, got)
-    near_blocks = []
-    near_rank = []
-    for reach in REACH:
-        picks, rank = near_tiles(kv_list, seq_at + reach, group_tiles)
-        asked = passed_along(picks, "seq", reach)
-        near_blocks.append(passed_along(group_rows[asked], "seq", -reach))
-        near_rank.append(rank)
     window_rows = jnp.concatenate(
         [group_rows] + near_blocks + [global_rows], axis=0
     )
+    w_out_src, window_rows = lax.optimization_barrier((w_out, window_rows))
     window = jnp.dot(
         window_rows.reshape(-1, feat_width), w_full[:, feat_width:],
         preferred_element_type=jnp.float32,
@@ -209,7 +217,7 @@
     heads_out = attend(query_tiles, window, slots, kv_count).reshape(tok_rows, feat_width)
     return jnp.dot(
         heads_out,
-        gathered_weight(w_out),
+        gathered_weight(w_out_src),
         preferred_element_type=jnp.float32,
     ).astype(jnp.bfloat16)
 

time: 321 us -> 327 us (1.019)
  the two profiles are of different devices: /device:TPU:50 before, /device:TPU:24 now
where the time goes in v6:
time: 327 us; the launch traced here: 324 us
  waiting for transfers between devices  104 us (32%)
  Pallas kernels  53.7 us (16%)
  between operations  39.6 us (12%)
  other arithmetic  35.5 us (11%)
  starting transfers between devices  35.3 us (11%)
  matrix products  31.7 us (10%)
  local copies, waits for them, and re-layouts  23.8 us (7%)
    pallas_call x1, Pallas kernels, attend(): pl.pallas_call(attention_kernel, grid_spec=grid_spec, out_shape=jax.Shape...  53.7 us
    ppermute x5, waiting for transfers between devices, local(): lax.ppermute(global_rows, 'seq', [(i, i ^ step) for i in range(seq_size)])  49.5 us
    all_gather x2, waiting for transfers between devices, gathered_weight(): lax.all_gather(lax.dynamic_slice_in_dim(shard, core * half, half, 1), 'fs...  30 us
    ppermute x8, starting transfers between devices, passed_along(): return lax.ppermute(block, axis, route)  25.1 us
    dot_general x1, matrix products, local(): jnp.dot(window_rows.reshape(-1, feat_width), w_full[:, feat_width:], pref...  23.6 us
    ppermute x8, waiting for transfers between devices, passed_along(): return lax.ppermute(block, axis, route)  22.8 us
    ppermute x5, starting transfers between devices, local(): lax.ppermute(global_rows, 'seq', [(i, i ^ step) for i in range(seq_size)])  10.2 us
    unnamed x27, local copies, waits for them, and re-layouts  8.4 us
  transfers between devices with their start and end apart: 18, of which 9 were waited for; matrix products, arithmetic and copies ran while one was open for 10% of the time, Pallas kernels for 0%

profile of v6, /device:TPU:24, one launch (start us, length us, event | category | flops | bytes accessed | tf_op | source)
XLA Modules:
  0.0 324.1 jit_solution(1805875028068634366)
XLA Ops:
  6.5 0.8 compare_select_fusion.1
  8.9 4.1 %gather_fusion.2 = bf16[256,1280]{1,0:T(8,128)(2,1)} fusion(bf16[512,1280]{1,0:T(8,128)(2,1)} %param.17, s32[1024]{0:T(1024)S(1)} %get-tuple-element.89), kind=kCustom, calls=%fused_computation.2 | custom fusion | bytes 1311744 | tf_op jit(solution)/shard_map/gather | solution.py:51
  13.0 2.1 gather_fusion.1
  15.0 1.9 convert_reduce_fusion
  17.2 1.2 fusion.18
  20.6 3.8 %pad_add_fusion.4 = (s32[3]{0:T(128)S(1)}, s32[3]{0:T(128)S(1)}) fusion(s32[1]{0:T(128)} %bitcast.34, s32[1]{0:T(128)} %bitcast.32, s32[1]{0:T(128)} %bitcast.30, s32[1]{0:T(128)} %bitcast.43, s32[1]{0:T(128)} %bitcast.41, s32[1]{0:T(128)} %bitcast.39), kind=kLoop, calls=%fused_computation.121 | loop fusion | flops 12 | bytes 48 | tf_op jit(solution)/shard_map/stack | solution.py:60
  24.4 3.0 collective-permute-start.3
  27.5 1.9 collective-permute-start.2
  31.2 3.8 %pad_add_fusion.2 = (s32[3]{0:T(128)S(1)}, s32[3]{0:T(128)S(1)}) fusion(s32[1]{0:T(128)} %bitcast.16, s32[1]{0:T(128)} %bitcast.14, s32[1]{0:T(128)} %bitcast.12, s32[1]{0:T(128)} %bitcast.25, s32[1]{0:T(128)} %bitcast.23, s32[1]{0:T(128)} %bitcast.21), kind=kLoop, calls=%fused_computation.119 | loop fusion | flops 12 | bytes 48 | tf_op jit(solution)/shard_map/stack | solution.py:60
  35.0 3.6 %collective-permute-start.1 = (s32[3]{0:T(128)S(1)}, s32[3]{0:T(128)S(1)}, u32[]{:S(2)}, u32[]{:S(2)}) collective-permute-start(s32[3]{0:T(128)S(1)} %get-tuple-element.82), channel_id=1, source_target_pairs={{4,0},{8,4},{12,8},{16,12},{20,16},{24,20},{28,24},{32,28},{36,32}... | collective-permute-start | bytes 44 | tf_op jit(solution)/shard_map/ppermute | solution.py:20
  38.6 2.8 collective-permute-start
  70.9 3.0 constant_dynamic-slice_fusion.4
  74.0 1.1 pad_maximum_fusion.2
  75.1 1.1 pad_maximum_fusion.3
  76.2 1.1 pad_maximum_fusion.4
  77.3 1.1 pad_maximum_fusion.5
  78.4 1.2 constant_dynamic-slice_fusion.1
  79.6 3.0 collective-permute-start.9
  82.7 14.2 %collective-permute-done.9 = bf16[2,128,1280]{2,1,0:T(8,128)(2,1)S(1)} collective-permute-done((bf16[2,128,1280]{2,1,0:T(8,128)(2,1)S(1)}, bf16[2,128,1280]{2,1,0:T(8,128)(2,1)S(1)}, u32[]{:S(2)}, u32[]{:S(2)}) %collective-permute-start.9) | collective-permute-done | bytes 655392 | tf_op jit(solution)/shard_map/ppermute | solution.py:187
  97.0 1.8 collective-permute-start.10
  98.8 13.3 %collective-permute-done.10 = bf16[2,128,1280]{2,1,0:T(8,128)(2,1)S(1)} collective-permute-done((bf16[2,128,1280]{2,1,0:T(8,128)(2,1)S(1)}, bf16[2,128,1280]{2,1,0:T(8,128)(2,1)S(1)}, u32[]{:S(2)}, u32[]{:S(2)}) %collective-permute-start.10) | collective-permute-done | bytes 655392 | tf_op jit(solution)/shard_map/ppermute | solution.py:187
  113.0 6.2 %collective-permute-start.5 = (bf16[3,128,1280]{2,1,0:T(8,128)(2,1)}, bf16[3,128,1280]{2,1,0:T(8,128)(2,1)S(1)}, u32[]{:S(2)}, u32[]{:S(2)}) collective-permute-start(bf16[3,128,1280]{2,1,0:T(8,128)(2,1)} %pad_maximum_fusion.2), channel_id=1, source_target_pairs={{0,8},{4,12},{8,16},{12,20},{16,24},{20,28},{24,32},{28,36},{32,40... | collective-permute-start | bytes 2949128 | tf_op jit(solution)/shard_map/ppermute | solution.py:20
  119.2 9.0 %collective-permute-done.11 = bf16[2,128,1280]{2,1,0:T(8,128)(2,1)S(1)} collective-permute-done((bf16[2,128,1280]{2,1,0:T(8,128)(2,1)S(1)}, bf16[2,128,1280]{2,1,0:T(8,128)(2,1)S(1)}, u32[]{:S(2)}, u32[]{:S(2)}) %collective-permute-start.11) | collective-permute-done | bytes 655392 | tf_op jit(solution)/shard_map/ppermute | solution.py:187
  128.3 4.5 %collective-permute-start.12 = (bf16[2,128,1280]{2,1,0:T(8,128)(2,1)S(1)}, bf16[2,128,1280]{2,1,0:T(8,128)(2,1)S(1)}, u32[]{:S(2)}, u32[]{:S(2)}) collective-permute-start(bf16[2,128,1280]{2,1,0:T(8,128)(2,1)S(1)} %broadcast_select_fusion.6), channel_id=1, source_target_pairs={{0,8},{4,12},{8,0},{12,4},{16,24},{20,28},{24,16},{28,20},{32,40},... | collective-permute-start | bytes 1966088 | tf_op jit(solution)/shard_map/ppermute | solution.py:187
  132.9 1.9 collective-permute-start.6
  134.8 3.6 %collective-permute-start.7 = (bf16[3,128,1280]{2,1,0:T(8,128)(2,1)}, bf16[3,128,1280]{2,1,0:T(8,128)(2,1)S(1)}, u32[]{:S(2)}, u32[]{:S(2)}) collective-permute-start(bf16[3,128,1280]{2,1,0:T(8,128)(2,1)} %pad_maximum_fusion.4), channel_id=1, source_target_pairs={{4,0},{8,4},{12,8},{16,12},{20,16},{24,20},{28,24},{32,28},{36,32}... | collective-permute-start | bytes 2949128 | tf_op jit(solution)/shard_map/ppermute | solution.py:20
  138.4 1.9 collective-permute-start.8
  140.4 3.4 %constant_dynamic-update-slice_fusion.4 = bf16[22,128,1280]{2,1,0:T(8,128)(2,1)} fusion(bf16[8,128,1280]{2,1,0:T(8,128)(2,1)} %bitcast.123), kind=kLoop, calls=%fused_computation.41 | loop fusion | bytes 5242880
  143.8 9.9 %collective-permute-done.5 = bf16[3,128,1280]{2,1,0:T(8,128)(2,1)S(1)} collective-permute-done((bf16[3,128,1280]{2,1,0:T(8,128)(2,1)}, bf16[3,128,1280]{2,1,0:T(8,128)(2,1)S(1)}, u32[]{:S(2)}, u32[]{:S(2)}) %collective-permute-start.5) | collective-permute-done | bytes 983072 | tf_op jit(solution)/shard_map/ppermute | solution.py:20
  153.7 1.0 constant_dynamic-update-slice_fusion.3
  154.7 13.0 %collective-permute-done.12 = bf16[2,128,1280]{2,1,0:T(8,128)(2,1)S(1)} collective-permute-done((bf16[2,128,1280]{2,1,0:T(8,128)(2,1)S(1)}, bf16[2,128,1280]{2,1,0:T(8,128)(2,1)S(1)}, u32[]{:S(2)}, u32[]{:S(2)}) %collective-permute-start.12) | collective-permute-done | bytes 655392 | tf_op jit(solution)/shard_map/ppermute | solution.py:187
  167.7 0.8 copy-done.7
  168.5 1.2 broadcast_select_fusion.7
  169.8 5.9 %collective-permute-done.6 = bf16[3,128,1280]{2,1,0:T(8,128)(2,1)S(1)} collective-permute-done((bf16[3,128,1280]{2,1,0:T(8,128)(2,1)}, bf16[3,128,1280]{2,1,0:T(8,128)(2,1)S(1)}, u32[]{:S(2)}, u32[]{:S(2)}) %collective-permute-start.6) | collective-permute-done | bytes 983072 | tf_op jit(solution)/shard_map/ppermute | solution.py:20
  175.8 1.1 constant_dynamic-update-slice_fusion.2
  176.9 1.0 constant_dynamic-update-slice_fusion.1
  177.9 7.0 %collective-permute-done.8 = bf16[3,128,1280]{2,1,0:T(8,128)(2,1)S(1)} collective-permute-done((bf16[3,128,1280]{2,1,0:T(8,128)(2,1)S(1)}, bf16[3,128,1280]{2,1,0:T(8,128)(2,1)S(1)}, u32[]{:S(2)}, u32[]{:S(2)}) %collective-permute-start.8) | collective-permute-done | bytes 983072 | tf_op jit(solution)/shard_map/ppermute | solution.py:20
  184.9 1.0 constant_dynamic-update-slice_fusion
  185.9 1.1 select_dynamic-update-slice_fusion
  187.0 0.8 constant_dynamic-slice_fusion
  187.9 30.0 %all-gather.8.cloned.1.call-done = bf16[1280,640]{1,0:T(8,128)(2,1)} async-done(((bf16[320,640]{1,0:T(8,128)(2,1)}), bf16[1280,640]{1,0:T(8,128)(2,1)}) %all-gather.8.cloned.1.call-update) | async-done | bytes 1638416 | tf_op jit(solution)/shard_map/all_gather | solution.py:26
  219.5 2.1 collective-permute-done.14
  221.5 3.4 %broadcast_select_fusion.3 = (bf16[1280,640]{1,0:T(8,128)(2,1)}, bf16[1280,640]{1,0:T(8,128)(2,1)}) fusion(bf16[1280,640]{1,0:T(8,128)(2,1)} %all-gather.8.cloned.1.call-done, bf16[1280,640]{1,0:T(8,128)(2,1)S(1)} %collective-permute-done.14, pred[]{:T(512)S(6)} %eq.164), kind=kLoop, calls=%fused_computation.17 | loop fusion | flops 1638400 | bytes 6553601 | tf_op jit(solution)/shard_map/jit(_where)/select_n | solution.py:31
  225.0 7.1 %broadcast_select_fusion = (bf16[1280,1920]{1,0:T(8,128)(2,1)}, bf16[1280,1920]{1,0:T(8,128)(2,1)}) fusion(bf16[1280,1920]{1,0:T(8,128)(2,1)} %collective-permute-done.4, bf16[1280,1920]{1,0:T(8,128)(2,1)S(1)} %copy-done.3, pred[]{:T(512)S(6)} %eq.164), kind=kLoop, calls=%fused_computation.6 | loop fusion | flops 4915200 | bytes 19660800 | tf_op jit(solution)/shard_map/jit(_where)/select_n | solution.py:32
  232.1 3.9 %fusion.7 = bf16[256,1280]{1,0:T(8,128)(2,1)} fusion(bf16[256,1280]{1,0:T(8,128)(2,1)S(1)} %copy-done.5, bf16[1280,1920]{1,0:T(8,128)(2,1)} %get-tuple-element.44), kind=kOutput, calls=%fused_computation.14 | convolution fusion | flops 839188480 | bytes 4587520 | tf_op jit(solution)/shard_map/dot_general | solution.py:197
  236.1 23.6 %convolution_convert_fusion = bf16[2816,2560]{1,0:T(8,128)(2,1)} fusion(bf16[2816,1280]{1,0:T(8,128)(2,1)} %bitcast.48, bf16[1280,1920]{1,0:T(8,128)(2,1)S(1)} %copy-done.4, bf16[1280,1920]{1,0:T(8,128)(2,1)} %get-tuple-element.44), kind=kOutput, calls=%fused_computation.3 | convolution fusion | flops 18475253760 | bytes 31457280 | tf_op jit(solution)/shard_map/dot_general | solution.py:193
  259.7 53.7 %shard_map.109 = bf16[2,128,1280]{2,1,0:T(8,128)(2,1)} custom-call(s32[2,18]{1,0:T(2,128)} %pad_add_fusion.1.slots_ref, s32[2]{0:T(128)} %counts_ref.1, bf16[2,128,1280]{2,1,0:T(8,128)(2,1)} %bitcast.125, bf16[22,128,2560]{2,1,0:T(8,128)(2,1)} %bitcast.124), custom_call_target="tpu_custom_call" | custom-call | tf_op jit(solution)/shard_map/pallas_call | solution.py:127
  313.4 4.1 %fusion.10 = bf16[256,1280]{1,0:T(8,128)(2,1)} fusion(bf16[256,1280]{1,0:T(8,128)(2,1)} %bitcast.126, bf16[1280,640]{1,0:T(8,128)(2,1)} %get-tuple-element.46, bf16[1280,640]{1,0:T(8,128)(2,1)} %get-tuple-element.45), kind=kOutput, calls=%fused_computation.15 | convolution fusion | flops 845742080 | bytes 4587520 | tf_op jit(solution)/shard_map/dot_general | solution.py:218
  (88 shorter events, 12.0 us)
Async XLA Ops:
  6.5 71.8 %copy-start = (bf16[320,3840]{1,0:T(8,128)(2,1)S(1)}, bf16[320,3840]{1,0:T(8,128)(2,1)}, u32[]{:S(2)}) copy-start(bf16[320,3840]{1,0:T(8,128)(2,1)} %param.20) | copy-start | bytes 7372804
  6.5 6.4 %copy-start.2 = (bf16[256,1280]{1,0:T(8,128)(2,1)S(1)}, bf16[256,1280]{1,0:T(8,128)(2,1)}, u32[]{:S(2)}) copy-start(bf16[256,1280]{1,0:T(8,128)(2,1)} %param.16) | copy-start | bytes 1966084
  6.5 64.4 %all-gather.4.cloned.1.call-start = ((), (), s32[]{:S(2)}) async-start(), calls=%async_computation | async-start | bytes 3276800 | tf_op jit(solution)/shard_map/all_gather | solution.py:161
  15.0 3.4 %copy-start.9 = (s32[2,16]{1,0:T(2,128)S(1)}, s32[2,16]{1,0:T(2,128)}, u32[]{:S(2)}) copy-start(s32[2,16]{1,0:T(2,128)} %param.13) | copy-start | bytes 388
  15.0 26.4 %copy-start.10 = (s32[2]{0:T(128)S(1)}, s32[2]{0:T(128)}, u32[]{:S(2)}) copy-start(s32[2]{0:T(128)} %param.15) | copy-start | bytes 28
  18.4 168.6 %all-gather.6.cloned.1.call-start = ((), (), s32[]{:S(2)}) async-start(), calls=%async_computation.1 | async-start | bytes 6144000 | tf_op jit(solution)/shard_map/all_gather | solution.py:26
  24.4 21.4 %collective-permute-start.3 = (s32[3]{0:T(128)S(1)}, s32[3]{0:T(128)S(1)}, u32[]{:S(2)}, u32[]{:S(2)}) collective-permute-start(s32[3]{0:T(128)S(1)} %get-tuple-element.84), channel_id=1, source_target_pairs={{0,8},{4,12},{8,16},{12,20},{16,24},{20,28},{24,32},{28,36},{32,40... | collective-permute-start | bytes 44 | tf_op jit(solution)/shard_map/ppermute | solution.py:20
  27.5 22.8 %collective-permute-start.2 = (s32[3]{0:T(128)S(1)}, s32[3]{0:T(128)S(1)}, u32[]{:S(2)}, u32[]{:S(2)}) collective-permute-start(s32[3]{0:T(128)S(1)} %get-tuple-element.83), channel_id=1, source_target_pairs={{0,4},{4,8},{8,12},{12,16},{16,20},{20,24},{24,28},{28,32},{32,36}... | collective-permute-start | bytes 44 | tf_op jit(solution)/shard_map/ppermute | solution.py:20
  35.0 19.6 %collective-permute-start.1 = (s32[3]{0:T(128)S(1)}, s32[3]{0:T(128)S(1)}, u32[]{:S(2)}, u32[]{:S(2)}) collective-permute-start(s32[3]{0:T(128)S(1)} %get-tuple-element.82), channel_id=1, source_target_pairs={{4,0},{8,4},{12,8},{16,12},{20,16},{24,20},{28,24},{32,28},{36,32}... | collective-permute-start | bytes 44 | tf_op jit(solution)/shard_map/ppermute | solution.py:20
  38.6 20.2 %collective-permute-start = (s32[3]{0:T(128)S(1)}, s32[3]{0:T(128)S(1)}, u32[]{:S(2)}, u32[]{:S(2)}) collective-permute-start(s32[3]{0:T(128)S(1)} %get-tuple-element.81), channel_id=1, source_target_pairs={{8,0},{12,4},{16,8},{20,12},{24,16},{28,20},{32,24},{36,28},{40,32... | collective-permute-start | bytes 44 | tf_op jit(solution)/shard_map/ppermute | solution.py:20
  79.6 58.9 %copy-start.6 = (bf16[3,128,1280]{2,1,0:T(8,128)(2,1)S(1)}, bf16[3,128,1280]{2,1,0:T(8,128)(2,1)}, u32[]{:S(2)}) copy-start(bf16[3,128,1280]{2,1,0:T(8,128)(2,1)} %pad_maximum_fusion.5) | copy-start | bytes 2949124
  79.6 138.2 %all-gather.8.cloned.1.call-start = ((), (), s32[]{:S(2)}) async-start(), calls=%async_computation.2 | async-start | bytes 2048000 | tf_op jit(solution)/shard_map/all_gather | solution.py:26
  79.6 17.2 %collective-permute-start.9 = (bf16[2,128,1280]{2,1,0:T(8,128)(2,1)S(1)}, bf16[2,128,1280]{2,1,0:T(8,128)(2,1)S(1)}, u32[]{:S(2)}, u32[]{:S(2)}) collective-permute-start(bf16[2,128,1280]{2,1,0:T(8,128)(2,1)S(1)} %pad_maximum_fusion.6), channel_id=1, source_target_pairs={{0,64},{4,68},{8,72},{12,76},{16,80},{20,84},{24,88},{28,92},{32,9... | collective-permute-start | bytes 1966088 | tf_op jit(solution)/shard_map/ppermute | solution.py:187
  97.0 15.2 %collective-permute-start.10 = (bf16[2,128,1280]{2,1,0:T(8,128)(2,1)S(1)}, bf16[2,128,1280]{2,1,0:T(8,128)(2,1)S(1)}, u32[]{:S(2)}, u32[]{:S(2)}) collective-permute-start(bf16[2,128,1280]{2,1,0:T(8,128)(2,1)S(1)} %broadcast_select_fusion.4), channel_id=1, source_target_pairs={{0,32},{4,36},{8,40},{12,44},{16,48},{20,52},{24,56},{28,60},{32,0... | collective-permute-start | bytes 1966088 | tf_op jit(solution)/shard_map/ppermute | solution.py:187
  112.3 15.9 %collective-permute-start.11 = (bf16[2,128,1280]{2,1,0:T(8,128)(2,1)S(1)}, bf16[2,128,1280]{2,1,0:T(8,128)(2,1)S(1)}, u32[]{:S(2)}, u32[]{:S(2)}) collective-permute-start(bf16[2,128,1280]{2,1,0:T(8,128)(2,1)S(1)} %broadcast_select_fusion.5), channel_id=1, source_target_pairs={{0,16},{4,20},{8,24},{12,28},{16,0},{20,4},{24,8},{28,12},{32,48},... | collective-permute-start | bytes 1966088 | tf_op jit(solution)/shard_map/ppermute | solution.py:187
  113.0 40.6 %collective-permute-start.5 = (bf16[3,128,1280]{2,1,0:T(8,128)(2,1)}, bf16[3,128,1280]{2,1,0:T(8,128)(2,1)S(1)}, u32[]{:S(2)}, u32[]{:S(2)}) collective-permute-start(bf16[3,128,1280]{2,1,0:T(8,128)(2,1)} %pad_maximum_fusion.2), channel_id=1, source_target_pairs={{0,8},{4,12},{8,16},{12,20},{16,24},{20,28},{24,32},{28,36},{32,40... | collective-permute-start | bytes 2949128 | tf_op jit(solution)/shard_map/ppermute | solution.py:20
  128.3 39.4 %collective-permute-start.12 = (bf16[2,128,1280]{2,1,0:T(8,128)(2,1)S(1)}, bf16[2,128,1280]{2,1,0:T(8,128)(2,1)S(1)}, u32[]{:S(2)}, u32[]{:S(2)}) collective-permute-start(bf16[2,128,1280]{2,1,0:T(8,128)(2,1)S(1)} %broadcast_select_fusion.6), channel_id=1, source_target_pairs={{0,8},{4,12},{8,0},{12,4},{16,24},{20,28},{24,16},{28,20},{32,40},... | collective-permute-start | bytes 1966088 | tf_op jit(solution)/shard_map/ppermute | solution.py:187
  132.9 42.9 %collective-permute-start.6 = (bf16[3,128,1280]{2,1,0:T(8,128)(2,1)}, bf16[3,128,1280]{2,1,0:T(8,128)(2,1)S(1)}, u32[]{:S(2)}, u32[]{:S(2)}) collective-permute-start(bf16[3,128,1280]{2,1,0:T(8,128)(2,1)} %pad_maximum_fusion.3), channel_id=1, source_target_pairs={{0,4},{4,8},{8,12},{12,16},{16,20},{20,24},{24,28},{28,32},{32,36}... | collective-permute-start | bytes 2949128 | tf_op jit(solution)/shard_map/ppermute | solution.py:20
  134.8 42.1 %collective-permute-start.7 = (bf16[3,128,1280]{2,1,0:T(8,128)(2,1)}, bf16[3,128,1280]{2,1,0:T(8,128)(2,1)S(1)}, u32[]{:S(2)}, u32[]{:S(2)}) collective-permute-start(bf16[3,128,1280]{2,1,0:T(8,128)(2,1)} %pad_maximum_fusion.4), channel_id=1, source_target_pairs={{4,0},{8,4},{12,8},{16,12},{20,16},{24,20},{28,24},{32,28},{36,32}... | collective-permute-start | bytes 2949128 | tf_op jit(solution)/shard_map/ppermute | solution.py:20
  138.4 46.4 %collective-permute-start.8 = (bf16[3,128,1280]{2,1,0:T(8,128)(2,1)S(1)}, bf16[3,128,1280]{2,1,0:T(8,128)(2,1)S(1)}, u32[]{:S(2)}, u32[]{:S(2)}) collective-permute-start(bf16[3,128,1280]{2,1,0:T(8,128)(2,1)S(1)} %copy-done.6), channel_id=1, source_target_pairs={{8,0},{12,4},{16,8},{20,12},{24,16},{28,20},{32,24},{36,28},{40,32... | collective-permute-start | bytes 2949128 | tf_op jit(solution)/shard_map/ppermute | solution.py:20
  167.7 0.8 copy-start.7
  169.8 16.1 %collective-permute-start.13 = (bf16[2,128,1280]{2,1,0:T(8,128)(2,1)S(1)}, bf16[2,128,1280]{2,1,0:T(8,128)(2,1)S(1)}, u32[]{:S(2)}, u32[]{:S(2)}) collective-permute-start(bf16[2,128,1280]{2,1,0:T(8,128)(2,1)S(1)} %broadcast_select_fusion.7), channel_id=1, source_target_pairs={{0,4},{4,0},{8,12},{12,8},{16,20},{20,16},{24,28},{28,24},{32,36},... | collective-permute-start | bytes 1966088 | tf_op jit(solution)/shard_map/ppermute | solution.py:187
  176.9 10.2 %copy-start.8 = (bf16[320,1280]{1,0:T(8,128)(2,1)S(1)}, bf16[320,1280]{1,0:T(8,128)(2,1)}, u32[]{:S(2)}) copy-start(bf16[320,1280]{1,0:T(8,128)(2,1)} %param.21) | copy-start | bytes 2457604
  187.0 37.9 %collective-permute-start.4 = (bf16[1280,1920]{1,0:T(8,128)(2,1)}, bf16[1280,1920]{1,0:T(8,128)(2,1)}, u32[]{:S(2)}, u32[]{:S(2)}) collective-permute-start(bf16[1280,1920]{1,0:T(8,128)(2,1)} %all-gather.6.cloned.1.call-done), channel_id=1, source_target_pairs={{0,4},{4,0},{8,12},{12,8},{16,20},{20,16},{24,28},{28,24},{32,36},... | collective-permute-start | bytes 14745608 | tf_op jit(solution)/shard_map/ppermute | solution.py:30
  217.8 3.7 %collective-permute-start.14 = (bf16[1280,640]{1,0:T(8,128)(2,1)}, bf16[1280,640]{1,0:T(8,128)(2,1)S(1)}, u32[]{:S(2)}, u32[]{:S(2)}) collective-permute-start(bf16[1280,640]{1,0:T(8,128)(2,1)} %all-gather.8.cloned.1.call-done), channel_id=1, source_target_pairs={{0,4},{4,0},{8,12},{12,8},{16,20},{20,16},{24,28},{28,24},{32,36},... | collective-permute-start | bytes 4915208 | tf_op jit(solution)/shard_map/ppermute | solution.py:30
  219.5 5.5 %copy-start.3 = (bf16[1280,1920]{1,0:T(8,128)(2,1)S(1)}, bf16[1280,1920]{1,0:T(8,128)(2,1)}, u32[]{:S(2)}) copy-start(bf16[1280,1920]{1,0:T(8,128)(2,1)} %all-gather.6.cloned.1.call-done) | copy-start | bytes 14745604
  225.0 7.2 %copy-start.5 = (bf16[256,1280]{1,0:T(8,128)(2,1)S(1)}, bf16[256,1280]{1,0:T(8,128)(2,1)}, u32[]{:S(2)}) copy-start(bf16[256,1280]{1,0:T(8,128)(2,1)} %fusion.18) | copy-start | bytes 1966084
  232.1 3.9 %copy-start.4 = (bf16[1280,1920]{1,0:T(8,128)(2,1)S(1)}, bf16[1280,1920]{1,0:T(8,128)(2,1)}, u32[]{:S(2)}) copy-start(bf16[1280,1920]{1,0:T(8,128)(2,1)} %get-tuple-element.43) | copy-start | bytes 14745604
  313.4 4.1 %copy-start.1 = (bf16[320,3840]{1,0:T(8,128)(2,1)S(1)}, bf16[320,3840]{1,0:T(8,128)(2,1)}, u32[]{:S(2)}) copy-start(bf16[320,3840]{1,0:T(8,128)(2,1)} %param.20) | copy-start | bytes 7372804
Sparse Core Ops, SparseCore 0:
  18.6 37.4 all-gather.3
  79.7 57.1 all-gather.5
  188.0 29.7 all-gather.7

commit v7 on v6

--- a/solution.py
+++ b/solution.py
@@ -181,15 +181,20 @@
     w_src, global_rows, sends = lax.optimization_barrier((w_qkv, global_rows, sends))
     w_full = gathered_weight(w_src)
     near_blocks = [passed_along(sent, "seq", -reach) for sent, reach in zip(sends, REACH)]
-    for bit in sorted(range(seq_size.bit_length() - 1), key=lambda b: -b):
-        step = 1 << bit
-        held = ((seq_at ^ owners) & (2 * step - 1)) == 0
-        got = lax.ppermute(global_rows, "seq", [(i, i ^ step) for i in range(seq_size)])
-        global_rows = jnp.where(held[:, None, None], global_rows, got)
+    seq_bits = seq_size.bit_length() - 1
+    digits = [(max(top - 2, 0), top - max(top - 2, 0)) for top in range(seq_bits, 0, -2)]
+    for low, width in digits:
+        diff = ((seq_at ^ owners) >> low) & ((1 << width) - 1)
+        mixed = global_rows
+        for k in range(1, 1 << width):
+            got = lax.ppermute(
+                global_rows, "seq", [(i, i ^ (k << low)) for i in range(seq_size)]
+            )
+            mixed = jnp.where((diff == k)[:, None, None], got, mixed)
+        global_rows = mixed
     window_rows = jnp.concatenate(
         [group_rows] + near_blocks + [global_rows], axis=0
     )
-    w_out_src, window_rows = lax.optimization_barrier((w_out, window_rows))
     window = jnp.dot(
         window_rows.reshape(-1, feat_width), w_full[:, feat_width:],
         preferred_element_type=jnp.float32,
@@ -217,7 +222,7 @@
     heads_out = attend(query_tiles, window, slots, kv_count).reshape(tok_rows, feat_width)
     return jnp.dot(
         heads_out,
-        gathered_weight(w_out_src),
+        lax.all_gather(w_out, "fsdp", axis=0, tiled=True),
         preferred_element_type=jnp.float32,
     ).astype(jnp.bfloat16)
 

time: 327 us -> 373 us (1.14)
  waiting for transfers between devices: 104 us -> 160 us
  Pallas kernels: 53.7 us -> 49.2 us
  other arithmetic: 35.5 us -> 31.3 us
    ppermute x8, waiting for transfers between devices: 22.8 us -> 77.4 us  [passed_along(): return lax.ppermute(block, axis, route)]
    all_gather x2 -> x1, waiting for transfers between devices: 30 us -> 56.3 us  [gathered_weight(): lax.all_gather(lax.dynamic_slice_in_dim(shard, core * half, half, 1), 'fs...]
    ppermute x5 -> x7, waiting for transfers between devices: 49.5 us -> 25.6 us  [local(): lax.ppermute(global_rows, 'seq', [(i, i ^ k << low) for i in range(seq_si...]
    pallas_call x1, Pallas kernels: 53.7 us -> 49.2 us  [attend(): pl.pallas_call(attention_kernel, grid_spec=grid_spec, out_shape=jax.Shape...]
    unnamed x27 -> x29, local copies, waits for them, and re-layouts: 8.4 us -> 6.44 us
    ppermute x5 -> x7, starting transfers between devices: 10.2 us -> 11.6 us  [local(): lax.ppermute(global_rows, 'seq', [(i, i ^ k << low) for i in range(seq_si...]
  transfers between devices with their start and end apart: 18 -> 19, of which waited for: 9 -> 6; matrix products, arithmetic and copies ran while one was open for 10% -> 15% of each run, Pallas kernels for 0% -> 13%
where the time goes in v7:
time: 373 us; the launch traced here: 366 us
  waiting for transfers between devices  160 us (43%)
  Pallas kernels  49.2 us (13%)
  between operations  39.7 us (11%)
  starting transfers between devices  33.9 us (9%)
  matrix products  31.6 us (8%)
  other arithmetic  31.3 us (8%)
  local copies, waits for them, and re-layouts  20.8 us (6%)
    ppermute x8, waiting for transfers between devices, passed_along(): return lax.ppermute(block, axis, route)  77.4 us
    all_gather x1, waiting for transfers between devices, gathered_weight(): lax.all_gather(lax.dynamic_slice_in_dim(shard, core * half, half, 1), 'fs...  56.3 us
    pallas_call x1, Pallas kernels, attend(): pl.pallas_call(attention_kernel, grid_spec=grid_spec, out_shape=jax.Shape...  49.2 us
    ppermute x7, waiting for transfers between devices, local(): lax.ppermute(global_rows, 'seq', [(i, i ^ k << low) for i in range(seq_si...  25.6 us
    dot_general x1, matrix products, local(): jnp.dot(window_rows.reshape(-1, feat_width), w_full[:, feat_width:], pref...  23.6 us
    ppermute x8, starting transfers between devices, passed_along(): return lax.ppermute(block, axis, route)  22.3 us
    ppermute x7, starting transfers between devices, local(): lax.ppermute(global_rows, 'seq', [(i, i ^ k << low) for i in range(seq_si...  11.6 us
    another operation x2, other arithmetic, near_tiles(): jnp.stack([jnp.sum(jnp.where(named & (rank == j), local_ids, 0)) for j in...  7.62 us
  transfers between devices with their start and end apart: 19, of which 6 were waited for; matrix products, arithmetic and copies ran while one was open for 15% of the time, Pallas kernels for 13%

profile of v7, /device:TPU:24, one launch (start us, length us, event | category | flops | bytes accessed | tf_op | source)
XLA Modules:
  0.0 366.5 jit_solution(12875389887800189582)
XLA Ops:
  6.5 0.8 compare_select_fusion.1
  7.4 0.8 convert_element_type.99
  8.2 0.7 convert_element_type.98
  8.9 4.1 %gather_fusion.2 = bf16[256,1280]{1,0:T(8,128)(2,1)} fusion(bf16[512,1280]{1,0:T(8,128)(2,1)} %param.17, s32[1024]{0:T(1024)S(1)} %get-tuple-element.85), kind=kCustom, calls=%fused_computation.2 | custom fusion | bytes 1311744 | tf_op jit(solution)/shard_map/gather | solution.py:51
  13.0 2.1 gather_fusion.1
  15.0 1.8 convert_reduce_fusion
  17.2 1.2 fusion.11
  19.2 0.7 fusion.37
  19.9 0.7 fusion.40
  20.6 3.8 %pad_add_fusion.4 = (s32[3]{0:T(128)S(1)}, s32[3]{0:T(128)S(1)}) fusion(s32[1]{0:T(128)} %bitcast.34, s32[1]{0:T(128)} %bitcast.32, s32[1]{0:T(128)} %bitcast.30, s32[1]{0:T(128)} %bitcast.43, s32[1]{0:T(128)} %bitcast.41, s32[1]{0:T(128)} %bitcast.39), kind=kLoop, calls=%fused_computation.112 | loop fusion | flops 12 | bytes 48 | tf_op jit(solution)/shard_map/stack | solution.py:60
  24.4 3.0 collective-permute-start.3
  27.4 1.9 collective-permute-start.2
  29.8 0.7 fusion.31
  30.5 0.7 fusion.34
  31.2 3.8 %pad_add_fusion.2 = (s32[3]{0:T(128)S(1)}, s32[3]{0:T(128)S(1)}) fusion(s32[1]{0:T(128)} %bitcast.16, s32[1]{0:T(128)} %bitcast.14, s32[1]{0:T(128)} %bitcast.12, s32[1]{0:T(128)} %bitcast.25, s32[1]{0:T(128)} %bitcast.23, s32[1]{0:T(128)} %bitcast.21), kind=kLoop, calls=%fused_computation.110 | loop fusion | flops 12 | bytes 48 | tf_op jit(solution)/shard_map/stack | solution.py:60
  35.0 3.6 collective-permute-start.1
  38.6 2.8 collective-permute-start
  70.9 2.8 constant_dynamic-slice_fusion.3
  73.8 1.1 pad_maximum_fusion.2
  74.8 1.1 pad_maximum_fusion.3
  76.0 1.1 pad_maximum_fusion.4
  77.0 1.1 pad_maximum_fusion.5
  78.1 1.2 constant_dynamic-slice_fusion
  79.3 0.7 all-gather.8.cloned.1.call-update
  80.0 56.3 %all-gather.6.cloned.1.call-done = bf16[1280,1920]{1,0:T(8,128)(2,1)} async-done(((bf16[320,1920]{1,0:T(8,128)(2,1)}), bf16[1280,1920]{1,0:T(8,128)(2,1)}) %all-gather.6.cloned.1.call-update) | async-done | bytes 4915216 | tf_op jit(solution)/shard_map/all_gather | solution.py:26
  136.4 0.8 gather_fusion
  137.3 2.7 collective-permute-start.9
  140.0 0.8 collective-permute-start.10
  141.4 3.3 collective-permute-start.5
  144.7 24.9 %collective-permute-done.9 = bf16[2,128,1280]{2,1,0:T(8,128)(2,1)S(1)} collective-permute-done((bf16[2,128,1280]{2,1,0:T(8,128)(2,1)S(1)}, bf16[2,128,1280]{2,1,0:T(8,128)(2,1)S(1)}, u32[]{:S(2)}, u32[]{:S(2)}) %collective-permute-start.9) | collective-permute-done | bytes 655392 | tf_op jit(solution)/shard_map/ppermute | solution.py:190
  171.2 2.4 collective-permute-start.13
  173.7 1.2 collective-permute-start.14
  175.4 29.1 %collective-permute-done.5 = bf16[3,128,1280]{2,1,0:T(8,128)(2,1)} collective-permute-done((bf16[3,128,1280]{2,1,0:T(8,128)(2,1)}, bf16[3,128,1280]{2,1,0:T(8,128)(2,1)}, u32[]{:S(2)}, u32[]{:S(2)}) %collective-permute-start.5) | collective-permute-done | bytes 983072 | tf_op jit(solution)/shard_map/ppermute | solution.py:20
  204.5 1.9 collective-permute-start.6
  206.5 1.9 constant_dynamic-update-slice_fusion.4
  208.4 3.6 collective-permute-start.7
  212.0 1.4 constant_dynamic-update-slice_fusion.3
  213.5 2.1 collective-permute-start.8
  215.6 1.5 select_select_fusion
  217.0 3.3 collective-permute-start.15
  220.4 8.4 %collective-permute-done.7 = bf16[3,128,1280]{2,1,0:T(8,128)(2,1)S(1)} collective-permute-done((bf16[3,128,1280]{2,1,0:T(8,128)(2,1)}, bf16[3,128,1280]{2,1,0:T(8,128)(2,1)S(1)}, u32[]{:S(2)}, u32[]{:S(2)}) %collective-permute-start.7) | collective-permute-done | bytes 983072 | tf_op jit(solution)/shard_map/ppermute | solution.py:20
  228.9 39.9 %collective-permute-done.8 = bf16[3,128,1280]{2,1,0:T(8,128)(2,1)S(1)} collective-permute-done((bf16[3,128,1280]{2,1,0:T(8,128)(2,1)S(1)}, bf16[3,128,1280]{2,1,0:T(8,128)(2,1)S(1)}, u32[]{:S(2)}, u32[]{:S(2)}) %collective-permute-start.8) | collective-permute-done | bytes 983072 | tf_op jit(solution)/shard_map/ppermute | solution.py:20
  269.2 2.9 copy-done.6
  272.1 7.1 %broadcast_select_fusion = (bf16[1280,1920]{1,0:T(8,128)(2,1)}, bf16[1280,1920]{1,0:T(8,128)(2,1)}) fusion(bf16[1280,1920]{1,0:T(8,128)(2,1)} %collective-permute-done.4, bf16[1280,1920]{1,0:T(8,128)(2,1)S(1)} %bitcast.127, pred[]{:T(512)S(6)} %eq.167), kind=kLoop, calls=%fused_computation.6 | loop fusion | flops 4915200 | bytes 19660800 | tf_op jit(solution)/shard_map/jit(_where)/select_n | solution.py:32
  279.2 3.9 %fusion.3 = bf16[256,1280]{1,0:T(8,128)(2,1)} fusion(bf16[256,1280]{1,0:T(8,128)(2,1)S(1)} %copy-done.4, bf16[1280,1920]{1,0:T(8,128)(2,1)} %get-tuple-element.40), kind=kOutput, calls=%fused_computation.10 | convolution fusion | flops 839188480 | bytes 4587520 | tf_op jit(solution)/shard_map/dot_general | solution.py:202
  283.2 23.6 %convolution_convert_fusion = bf16[2816,2560]{1,0:T(8,128)(2,1)} fusion(bf16[2816,1280]{1,0:T(8,128)(2,1)} %bitcast.128, bf16[1280,1920]{1,0:T(8,128)(2,1)S(1)} %copy-done.3, bf16[1280,1920]{1,0:T(8,128)(2,1)} %get-tuple-element.40), kind=kOutput, calls=%fused_computation.3 | convolution fusion | flops 18475253760 | bytes 31457280 | tf_op jit(solution)/shard_map/dot_general | solution.py:198
  306.8 49.2 %shard_map.109 = bf16[2,128,1280]{2,1,0:T(8,128)(2,1)} custom-call(s32[2,18]{1,0:T(2,128)} %pad_add_fusion.1.slots_ref, s32[2]{0:T(128)} %counts_ref.1, bf16[2,128,1280]{2,1,0:T(8,128)(2,1)} %bitcast.129, bf16[22,128,2560]{2,1,0:T(8,128)(2,1)} %bitcast.125), custom_call_target="tpu_custom_call" | custom-call | tf_op jit(solution)/shard_map/pallas_call | solution.py:127
  356.0 4.0 %convolution_convert_fusion.1 = bf16[256,1280]{1,0:T(8,128)(2,1)} fusion(bf16[256,1280]{1,0:T(8,128)(2,1)} %bitcast.130, bf16[1280,1280]{1,0:T(8,128)(2,1)} %all-gather.8.cloned.1.call-done), kind=kOutput, calls=%fused_computation.11 | convolution fusion | flops 839188480 | bytes 4587520 | tf_op jit(solution)/shard_map/dot_general | solution.py:223
  (89 shorter events, 8.2 us)
Async XLA Ops:
  6.5 71.6 %copy-start = (bf16[320,3840]{1,0:T(8,128)(2,1)S(1)}, bf16[320,3840]{1,0:T(8,128)(2,1)}, u32[]{:S(2)}) copy-start(bf16[320,3840]{1,0:T(8,128)(2,1)} %param.20) | copy-start | bytes 7372804
  6.5 6.4 %copy-start.2 = (bf16[256,1280]{1,0:T(8,128)(2,1)S(1)}, bf16[256,1280]{1,0:T(8,128)(2,1)}, u32[]{:S(2)}) copy-start(bf16[256,1280]{1,0:T(8,128)(2,1)} %param.16) | copy-start | bytes 1966084
  6.5 64.3 %all-gather.4.cloned.1.call-start = ((), (), s32[]{:S(2)}) async-start(), calls=%async_computation | async-start | bytes 3276800 | tf_op jit(solution)/shard_map/all_gather | solution.py:161
  13.0 5.5 %copy-start.8 = (s32[2,16]{1,0:T(2,128)S(1)}, s32[2,16]{1,0:T(2,128)}, u32[]{:S(2)}) copy-start(s32[2,16]{1,0:T(2,128)} %param.13) | copy-start | bytes 388
  13.0 28.5 %copy-start.9 = (s32[2]{0:T(128)S(1)}, s32[2]{0:T(128)}, u32[]{:S(2)}) copy-start(s32[2]{0:T(128)} %param.15) | copy-start | bytes 28
  18.4 117.9 %all-gather.6.cloned.1.call-start = ((), (), s32[]{:S(2)}) async-start(), calls=%async_computation.1 | async-start | bytes 6144000 | tf_op jit(solution)/shard_map/all_gather | solution.py:26
  24.4 21.4 %collective-permute-start.3 = (s32[3]{0:T(128)S(1)}, s32[3]{0:T(128)S(1)}, u32[]{:S(2)}, u32[]{:S(2)}) collective-permute-start(s32[3]{0:T(128)S(1)} %get-tuple-element.80), channel_id=1, source_target_pairs={{0,8},{4,12},{8,16},{12,20},{16,24},{20,28},{24,32},{28,36},{32,40... | collective-permute-start | bytes 44 | tf_op jit(solution)/shard_map/ppermute | solution.py:20
  27.4 22.8 %collective-permute-start.2 = (s32[3]{0:T(128)S(1)}, s32[3]{0:T(128)S(1)}, u32[]{:S(2)}, u32[]{:S(2)}) collective-permute-start(s32[3]{0:T(128)S(1)} %get-tuple-element.79), channel_id=1, source_target_pairs={{0,4},{4,8},{8,12},{12,16},{16,20},{20,24},{24,28},{28,32},{32,36}... | collective-permute-start | bytes 44 | tf_op jit(solution)/shard_map/ppermute | solution.py:20
  35.0 19.6 %collective-permute-start.1 = (s32[3]{0:T(128)S(1)}, s32[3]{0:T(128)S(1)}, u32[]{:S(2)}, u32[]{:S(2)}) collective-permute-start(s32[3]{0:T(128)S(1)} %get-tuple-element.78), channel_id=1, source_target_pairs={{4,0},{8,4},{12,8},{16,12},{20,16},{24,20},{28,24},{32,28},{36,32}... | collective-permute-start | bytes 44 | tf_op jit(solution)/shard_map/ppermute | solution.py:20
  38.6 20.2 %collective-permute-start = (s32[3]{0:T(128)S(1)}, s32[3]{0:T(128)S(1)}, u32[]{:S(2)}, u32[]{:S(2)}) collective-permute-start(s32[3]{0:T(128)S(1)} %get-tuple-element.77), channel_id=1, source_target_pairs={{8,0},{12,4},{16,8},{20,12},{24,16},{28,20},{32,24},{36,28},{40,32... | collective-permute-start | bytes 44 | tf_op jit(solution)/shard_map/ppermute | solution.py:20
  79.3 276.7 %all-gather.8.cloned.1.call-start = ((), (), s32[]{:S(2)}) async-start(), calls=%async_computation.2 | async-start | bytes 4096000 | tf_op jit(solution)/shard_map/all_gather | solution.py:225
  136.3 135.8 %collective-permute-start.4 = (bf16[1280,1920]{1,0:T(8,128)(2,1)}, bf16[1280,1920]{1,0:T(8,128)(2,1)}, u32[]{:S(2)}, u32[]{:S(2)}) collective-permute-start(bf16[1280,1920]{1,0:T(8,128)(2,1)} %all-gather.6.cloned.1.call-done), channel_id=1, source_target_pairs={{0,4},{4,0},{8,12},{12,8},{16,20},{20,16},{24,28},{28,24},{32,36},... | collective-permute-start | bytes 14745608 | tf_op jit(solution)/shard_map/ppermute | solution.py:30
  137.3 32.4 %collective-permute-start.9 = (bf16[2,128,1280]{2,1,0:T(8,128)(2,1)S(1)}, bf16[2,128,1280]{2,1,0:T(8,128)(2,1)S(1)}, u32[]{:S(2)}, u32[]{:S(2)}) collective-permute-start(bf16[2,128,1280]{2,1,0:T(8,128)(2,1)S(1)} %pad_maximum_fusion.6), channel_id=1, source_target_pairs={{0,96},{4,100},{8,104},{12,108},{16,112},{20,116},{24,120},{28,124... | collective-permute-start | bytes 1966088 | tf_op jit(solution)/shard_map/ppermute | solution.py:190
  140.0 29.7 %collective-permute-start.10 = (bf16[2,128,1280]{2,1,0:T(8,128)(2,1)S(1)}, bf16[2,128,1280]{2,1,0:T(8,128)(2,1)S(1)}, u32[]{:S(2)}, u32[]{:S(2)}) collective-permute-start(bf16[2,128,1280]{2,1,0:T(8,128)(2,1)S(1)} %pad_maximum_fusion.6), channel_id=1, source_target_pairs={{0,64},{4,68},{8,72},{12,76},{16,80},{20,84},{24,88},{28,92},{32,9... | collective-permute-start | bytes 1966088 | tf_op jit(solution)/shard_map/ppermute | solution.py:190
  140.8 29.5 %collective-permute-start.11 = (bf16[2,128,1280]{2,1,0:T(8,128)(2,1)S(1)}, bf16[2,128,1280]{2,1,0:T(8,128)(2,1)S(1)}, u32[]{:S(2)}, u32[]{:S(2)}) collective-permute-start(bf16[2,128,1280]{2,1,0:T(8,128)(2,1)S(1)} %pad_maximum_fusion.6), channel_id=1, source_target_pairs={{0,32},{4,36},{8,40},{12,44},{16,48},{20,52},{24,56},{28,60},{32,0... | collective-permute-start | bytes 1966088 | tf_op jit(solution)/shard_map/ppermute | solution.py:190
  141.4 63.1 %collective-permute-start.5 = (bf16[3,128,1280]{2,1,0:T(8,128)(2,1)}, bf16[3,128,1280]{2,1,0:T(8,128)(2,1)}, u32[]{:S(2)}, u32[]{:S(2)}) collective-permute-start(bf16[3,128,1280]{2,1,0:T(8,128)(2,1)} %pad_maximum_fusion.2), channel_id=1, source_target_pairs={{0,8},{4,12},{8,16},{12,20},{16,24},{20,28},{24,32},{28,36},{32,40... | collective-permute-start | bytes 2949128 | tf_op jit(solution)/shard_map/ppermute | solution.py:20
  170.3 43.2 %copy-start.5 = (bf16[3,128,1280]{2,1,0:T(8,128)(2,1)S(1)}, bf16[3,128,1280]{2,1,0:T(8,128)(2,1)}, u32[]{:S(2)}) copy-start(bf16[3,128,1280]{2,1,0:T(8,128)(2,1)} %pad_maximum_fusion.5) | copy-start | bytes 2949124
  170.6 37.8 %collective-permute-start.12 = (bf16[2,128,1280]{2,1,0:T(8,128)(2,1)S(1)}, bf16[2,128,1280]{2,1,0:T(8,128)(2,1)S(1)}, u32[]{:S(2)}, u32[]{:S(2)}) collective-permute-start(bf16[2,128,1280]{2,1,0:T(8,128)(2,1)S(1)} %select_select_fusion.1), channel_id=1, source_target_pairs={{0,24},{4,28},{8,16},{12,20},{16,8},{20,12},{24,0},{28,4},{32,56},... | collective-permute-start | bytes 1966088 | tf_op jit(solution)/shard_map/ppermute | solution.py:190
  171.2 42.2 %collective-permute-start.13 = (bf16[2,128,1280]{2,1,0:T(8,128)(2,1)S(1)}, bf16[2,128,1280]{2,1,0:T(8,128)(2,1)S(1)}, u32[]{:S(2)}, u32[]{:S(2)}) collective-permute-start(bf16[2,128,1280]{2,1,0:T(8,128)(2,1)S(1)} %select_select_fusion.1), channel_id=1, source_target_pairs={{0,16},{4,20},{8,24},{12,28},{16,0},{20,4},{24,8},{28,12},{32,48},... | collective-permute-start | bytes 1966088 | tf_op jit(solution)/shard_map/ppermute | solution.py:190
  173.7 41.9 %collective-permute-start.14 = (bf16[2,128,1280]{2,1,0:T(8,128)(2,1)S(1)}, bf16[2,128,1280]{2,1,0:T(8,128)(2,1)}, u32[]{:S(2)}, u32[]{:S(2)}) collective-permute-start(bf16[2,128,1280]{2,1,0:T(8,128)(2,1)S(1)} %select_select_fusion.1), channel_id=1, source_target_pairs={{0,8},{4,12},{8,0},{12,4},{16,24},{20,28},{24,16},{28,20},{32,40},... | collective-permute-start | bytes 1966088 | tf_op jit(solution)/shard_map/ppermute | solution.py:190
  204.5 15.8 %collective-permute-start.6 = (bf16[3,128,1280]{2,1,0:T(8,128)(2,1)}, bf16[3,128,1280]{2,1,0:T(8,128)(2,1)S(1)}, u32[]{:S(2)}, u32[]{:S(2)}) collective-permute-start(bf16[3,128,1280]{2,1,0:T(8,128)(2,1)} %pad_maximum_fusion.3), channel_id=1, source_target_pairs={{0,4},{4,8},{8,12},{12,16},{16,20},{20,24},{24,28},{28,32},{32,36}... | collective-permute-start | bytes 2949128 | tf_op jit(solution)/shard_map/ppermute | solution.py:20
  208.4 20.4 %collective-permute-start.7 = (bf16[3,128,1280]{2,1,0:T(8,128)(2,1)}, bf16[3,128,1280]{2,1,0:T(8,128)(2,1)S(1)}, u32[]{:S(2)}, u32[]{:S(2)}) collective-permute-start(bf16[3,128,1280]{2,1,0:T(8,128)(2,1)} %pad_maximum_fusion.4), channel_id=1, source_target_pairs={{4,0},{8,4},{12,8},{16,12},{20,16},{24,20},{28,24},{32,28},{36,32}... | collective-permute-start | bytes 2949128 | tf_op jit(solution)/shard_map/ppermute | solution.py:20
  212.0 60.0 %slice-start = ((s8[4915200]{0:T(1024)(128)(4,1)}), s8[4194304]{0:T(1024)(128)(4,1)S(1)}, s32[]{:S(2)}) async-start(s8[4915200]{0:T(1024)(128)(4,1)} %bitcast.126), calls=%async_computation.3 | async-start | bytes 8388608
  213.5 2.1 copy-start.7
  213.5 55.3 %collective-permute-start.8 = (bf16[3,128,1280]{2,1,0:T(8,128)(2,1)S(1)}, bf16[3,128,1280]{2,1,0:T(8,128)(2,1)S(1)}, u32[]{:S(2)}, u32[]{:S(2)}) collective-permute-start(bf16[3,128,1280]{2,1,0:T(8,128)(2,1)S(1)} %copy-done.5), channel_id=1, source_target_pairs={{8,0},{12,4},{16,8},{20,12},{24,16},{28,20},{32,24},{36,28},{40,32... | collective-permute-start | bytes 2949128 | tf_op jit(solution)/shard_map/ppermute | solution.py:20
  217.0 55.0 %slice-start.1 = ((s8[4915200]{0:T(1024)(128)(4,1)}), s8[720896]{0:T(1024)(128)(4,1)S(1)}, s32[]{:S(2)}) async-start(s8[4915200]{0:T(1024)(128)(4,1)} %bitcast.126), calls=%async_computation.4 | async-start | bytes 1441792
  217.0 51.8 %collective-permute-start.15 = (bf16[2,128,1280]{2,1,0:T(8,128)(2,1)S(1)}, bf16[2,128,1280]{2,1,0:T(8,128)(2,1)S(1)}, u32[]{:S(2)}, u32[]{:S(2)}) collective-permute-start(bf16[2,128,1280]{2,1,0:T(8,128)(2,1)S(1)} %select_select_fusion), channel_id=1, source_target_pairs={{0,4},{4,0},{8,12},{12,8},{16,20},{20,16},{24,28},{28,24},{32,36},... | collective-permute-start | bytes 1966088 | tf_op jit(solution)/shard_map/ppermute | solution.py:190
  269.2 2.9 copy-start.6
  272.1 7.2 %copy-start.4 = (bf16[256,1280]{1,0:T(8,128)(2,1)S(1)}, bf16[256,1280]{1,0:T(8,128)(2,1)}, u32[]{:S(2)}) copy-start(bf16[256,1280]{1,0:T(8,128)(2,1)} %fusion.11) | copy-start | bytes 1966084
  279.2 3.9 %copy-start.3 = (bf16[1280,1920]{1,0:T(8,128)(2,1)S(1)}, bf16[1280,1920]{1,0:T(8,128)(2,1)}, u32[]{:S(2)}) copy-start(bf16[1280,1920]{1,0:T(8,128)(2,1)} %get-tuple-element.39) | copy-start | bytes 14745604
  306.8 53.2 %copy-start.1 = (bf16[320,3840]{1,0:T(8,128)(2,1)S(1)}, bf16[320,3840]{1,0:T(8,128)(2,1)}, u32[]{:S(2)}) copy-start(bf16[320,3840]{1,0:T(8,128)(2,1)} %param.20) | copy-start | bytes 7372804
Sparse Core Ops, SparseCore 0:
  18.5 37.4 all-gather.3
  79.4 56.8 all-gather.5
  138.0 41.0 all-gather.7

commit v8 on v5

--- a/solution.py
+++ b/solution.py
@@ -209,7 +209,7 @@
     heads_out = attend(query_tiles, window, slots, kv_count).reshape(tok_rows, feat_width)
     return jnp.dot(
         heads_out,
-        gathered_weight(w_out),
+        lax.all_gather(w_out, "fsdp", axis=0, tiled=True),
         preferred_element_type=jnp.float32,
     ).astype(jnp.bfloat16)
 

time: 321 us -> 297 us (0.925)
  the two profiles are of different devices: /device:TPU:50 before, /device:TPU:24 now
where the time goes in v8:
time: 297 us; the launch traced here: 295 us
  waiting for transfers between devices  105 us (35%)
  Pallas kernels  53.4 us (18%)
  local copies, waits for them, and re-layouts  32.5 us (11%)
  starting transfers between devices  32 us (11%)
  matrix products  31.5 us (11%)
  other arithmetic  27.6 us (9%)
  between operations  13.5 us (5%)
    pallas_call x1, Pallas kernels, attend(): pl.pallas_call(attention_kernel, grid_spec=grid_spec, out_shape=jax.Shape...  53.4 us
    all_gather x1, waiting for transfers between devices, local(): lax.all_gather(normed, 'fsdp', axis=0, tiled=True)  37.5 us
    ppermute x5, waiting for transfers between devices, local(): lax.ppermute(global_rows, 'seq', [(i, i ^ step) for i in range(seq_size)])  32 us
    ppermute x8, starting transfers between devices, passed_along(): return lax.ppermute(block, axis, route)  24 us
    dot_general x1, matrix products, local(): jnp.dot(window_rows.reshape(-1, feat_width), w_full[:, feat_width:], pref...  23.6 us
    ppermute x8, waiting for transfers between devices, passed_along(): return lax.ppermute(block, axis, route)  19.3 us
    all_gather x1, waiting for transfers between devices, gathered_weight(): lax.all_gather(lax.dynamic_slice_in_dim(shard, core * half, half, 1), 'fs...  16 us
    gather x4, local copies, waits for them, and re-layouts, local(): near_blocks.append(passed_along(group_rows[asked], 'seq', -reach))  12.5 us
  transfers between devices with their start and end apart: 17, of which 8 were waited for; matrix products, arithmetic and copies ran while one was open for 24% of the time, Pallas kernels for 18%

profile of v8, /device:TPU:24, one launch (start us, length us, event | category | flops | bytes accessed | tf_op | source)
XLA Modules:
  0.0 295.4 jit_solution(7140112596936230570)
XLA Ops:
  6.5 0.8 compare_select_fusion.1
  7.4 0.8 convert_element_type.99
  8.9 4.1 %gather_fusion.2 = bf16[256,1280]{1,0:T(8,128)(2,1)} fusion(bf16[512,1280]{1,0:T(8,128)(2,1)} %param.17, s32[1024]{0:T(1024)S(1)} %get-tuple-element.43), kind=kCustom, calls=%fused_computation.2 | custom fusion | bytes 1311744 | tf_op jit(solution)/shard_map/gather | solution.py:51
  13.0 2.1 gather_fusion.1
  15.0 1.9 convert_reduce_fusion
  17.2 1.2 fusion.11
  18.5 37.5 %all-gather.4.cloned.1.call-done = bf16[1024,1280]{1,0:T(8,128)(2,1)} async-done(((bf16[256,1280]{1,0:T(8,128)(2,1)}), bf16[1024,1280]{1,0:T(8,128)(2,1)}) %all-gather.4.cloned.1.call-update) | async-done | bytes 2621456 | tf_op jit(solution)/shard_map/all_gather | solution.py:161
  56.0 1.2 constant_dynamic-slice_fusion
  58.5 1.8 pad_add_fusion.2
  60.3 2.7 collective-permute-start.1
  63.9 1.8 pad_add_fusion.3
  65.7 1.9 collective-permute-start.3
  68.5 1.8 pad_add_fusion.4
  70.4 2.4 collective-permute-start.5
  74.8 2.3 gather_fusion.7
  77.1 3.1 %collective-permute-start.9 = (bf16[2,128,1280]{2,1,0:T(8,128)(2,1)S(1)}, bf16[2,128,1280]{2,1,0:T(8,128)(2,1)S(1)}, u32[]{:S(2)}, u32[]{:S(2)}) collective-permute-start(bf16[2,128,1280]{2,1,0:T(8,128)(2,1)S(1)} %gather_fusion.7), channel_id=1, source_target_pairs={{0,64},{4,68},{8,72},{12,76},{16,80},{20,84},{24,88},{28,92},{32,9... | collective-permute-start | bytes 1966088 | tf_op jit(solution)/shard_map/ppermute | solution.py:173
  80.8 13.6 %collective-permute-done.9 = bf16[2,128,1280]{2,1,0:T(8,128)(2,1)S(1)} collective-permute-done((bf16[2,128,1280]{2,1,0:T(8,128)(2,1)S(1)}, bf16[2,128,1280]{2,1,0:T(8,128)(2,1)S(1)}, u32[]{:S(2)}, u32[]{:S(2)}) %collective-permute-start.9) | collective-permute-done | bytes 655392 | tf_op jit(solution)/shard_map/ppermute | solution.py:173
  94.5 1.5 collective-permute-start.10
  96.1 16.0 %all-gather.6.cloned.1.call-done = bf16[1280,1920]{1,0:T(8,128)(2,1)} async-done(((bf16[320,1920]{1,0:T(8,128)(2,1)}), bf16[1280,1920]{1,0:T(8,128)(2,1)}) %all-gather.6.cloned.1.call-update) | async-done | bytes 4915216 | tf_op jit(solution)/shard_map/all_gather | solution.py:26
  112.1 1.9 pad_add_fusion.5
  114.0 3.3 %collective-permute-start.7 = (s32[3]{0:T(128)S(1)}, s32[3]{0:T(128)S(1)}, u32[]{:S(2)}, u32[]{:S(2)}) collective-permute-start(s32[3]{0:T(128)S(1)} %pad_add_fusion.5), channel_id=1, source_target_pairs={{0,8},{4,12},{8,16},{12,20},{16,24},{20,28},{24,32},{28,36},{32,40... | collective-permute-start | bytes 44 | tf_op jit(solution)/shard_map/ppermute | solution.py:20
  117.5 1.6 collective-permute-start.11
  119.4 2.3 gather_fusion.3
  121.8 5.6 %collective-permute-start.2 = (bf16[3,128,1280]{2,1,0:T(8,128)(2,1)S(1)}, bf16[3,128,1280]{2,1,0:T(8,128)(2,1)S(1)}, u32[]{:S(2)}, u32[]{:S(2)}) collective-permute-start(bf16[3,128,1280]{2,1,0:T(8,128)(2,1)S(1)} %gather_fusion.3), channel_id=1, source_target_pairs={{0,8},{4,12},{8,16},{12,20},{16,24},{20,28},{24,32},{28,36},{32,40... | collective-permute-start | bytes 2949128 | tf_op jit(solution)/shard_map/ppermute | solution.py:20
  127.3 8.6 %collective-permute-done.11 = bf16[2,128,1280]{2,1,0:T(8,128)(2,1)S(1)} collective-permute-done((bf16[2,128,1280]{2,1,0:T(8,128)(2,1)S(1)}, bf16[2,128,1280]{2,1,0:T(8,128)(2,1)S(1)}, u32[]{:S(2)}, u32[]{:S(2)}) %collective-permute-start.11) | collective-permute-done | bytes 655392 | tf_op jit(solution)/shard_map/ppermute | solution.py:173
  135.9 0.9 copy-done.7
  136.8 1.2 broadcast_select_fusion.4
  138.0 1.5 collective-permute-start.12
  139.5 3.4 %gather_fusion.4 = bf16[3,128,1280]{2,1,0:T(8,128)(2,1)} fusion(bf16[8,128,1280]{2,1,0:T(8,128)(2,1)} %bitcast.111, s32[1024]{0:T(1024)S(1)} %pad_clamp_fusion.3), kind=kCustom, calls=%fused_computation.4 | custom fusion | bytes 1966092 | tf_op jit(solution)/shard_map/gather | solution.py:180
  142.9 1.9 collective-permute-start.4
  144.8 3.4 %gather_fusion.5 = bf16[3,128,1280]{2,1,0:T(8,128)(2,1)} fusion(bf16[8,128,1280]{2,1,0:T(8,128)(2,1)} %bitcast.112, s32[1024]{0:T(1024)S(1)} %pad_clamp_fusion.2), kind=kCustom, calls=%fused_computation.5 | custom fusion | bytes 1966092 | tf_op jit(solution)/shard_map/gather | solution.py:180
  148.2 3.6 %collective-permute-start.6 = (bf16[3,128,1280]{2,1,0:T(8,128)(2,1)}, bf16[3,128,1280]{2,1,0:T(8,128)(2,1)}, u32[]{:S(2)}, u32[]{:S(2)}) collective-permute-start(bf16[3,128,1280]{2,1,0:T(8,128)(2,1)} %gather_fusion.5), channel_id=1, source_target_pairs={{4,0},{8,4},{12,8},{16,12},{20,16},{24,20},{28,24},{32,28},{36,32}... | collective-permute-start | bytes 2949128 | tf_op jit(solution)/shard_map/ppermute | solution.py:20
  151.8 3.3 %gather_fusion.6 = bf16[3,128,1280]{2,1,0:T(8,128)(2,1)} fusion(bf16[8,128,1280]{2,1,0:T(8,128)(2,1)} %bitcast.113, s32[1024]{0:T(1024)S(1)} %pad_clamp_fusion.1), kind=kCustom, calls=%fused_computation.6 | custom fusion | bytes 1966092 | tf_op jit(solution)/shard_map/gather | solution.py:180
  155.2 2.1 constant_dynamic-update-slice_fusion.4
  157.2 2.5 collective-permute-start.8
  159.8 9.8 %collective-permute-done.12 = bf16[2,128,1280]{2,1,0:T(8,128)(2,1)S(1)} collective-permute-done((bf16[2,128,1280]{2,1,0:T(8,128)(2,1)S(1)}, bf16[2,128,1280]{2,1,0:T(8,128)(2,1)S(1)}, u32[]{:S(2)}, u32[]{:S(2)}) %collective-permute-start.12) | collective-permute-done | bytes 655392 | tf_op jit(solution)/shard_map/ppermute | solution.py:173
  169.7 0.8 copy-done.6
  170.5 1.3 broadcast_select_fusion.5
  172.1 7.5 %collective-permute-done.4 = bf16[3,128,1280]{2,1,0:T(8,128)(2,1)} collective-permute-done((bf16[3,128,1280]{2,1,0:T(8,128)(2,1)}, bf16[3,128,1280]{2,1,0:T(8,128)(2,1)}, u32[]{:S(2)}, u32[]{:S(2)}) %collective-permute-start.4) | collective-permute-done | bytes 983072 | tf_op jit(solution)/shard_map/ppermute | solution.py:20
  179.6 1.3 constant_dynamic-update-slice_fusion.2
  180.8 1.3 constant_dynamic-update-slice_fusion.1
  182.1 11.4 %collective-permute-done.8 = bf16[3,128,1280]{2,1,0:T(8,128)(2,1)S(1)} collective-permute-done((bf16[3,128,1280]{2,1,0:T(8,128)(2,1)}, bf16[3,128,1280]{2,1,0:T(8,128)(2,1)S(1)}, u32[]{:S(2)}, u32[]{:S(2)}) %collective-permute-start.8) | collective-permute-done | bytes 983072 | tf_op jit(solution)/shard_map/ppermute | solution.py:20
  193.9 2.9 copy-done.5
  196.8 7.1 %broadcast_select_fusion = (bf16[1280,1920]{1,0:T(8,128)(2,1)}, bf16[1280,1920]{1,0:T(8,128)(2,1)}) fusion(bf16[1280,1920]{1,0:T(8,128)(2,1)} %collective-permute-done, bf16[1280,1920]{1,0:T(8,128)(2,1)S(1)} %bitcast.117, pred[]{:T(512)S(6)} %eq.161), kind=kLoop, calls=%fused_computation.11 | loop fusion | flops 4915200 | bytes 19660800 | tf_op jit(solution)/shard_map/jit(_where)/select_n | solution.py:32
  203.9 3.9 %fusion.3 = bf16[256,1280]{1,0:T(8,128)(2,1)} fusion(bf16[256,1280]{1,0:T(8,128)(2,1)S(1)} %copy-done.4, bf16[1280,1920]{1,0:T(8,128)(2,1)} %get-tuple-element.32), kind=kOutput, calls=%fused_computation.15 | convolution fusion | flops 839188480 | bytes 4587520 | tf_op jit(solution)/shard_map/dot_general | solution.py:189
  207.9 23.6 %convolution_convert_fusion = bf16[2816,2560]{1,0:T(8,128)(2,1)} fusion(bf16[2816,1280]{1,0:T(8,128)(2,1)} %bitcast.118, bf16[1280,1920]{1,0:T(8,128)(2,1)S(1)} %copy-done.3, bf16[1280,1920]{1,0:T(8,128)(2,1)} %get-tuple-element.32), kind=kOutput, calls=%fused_computation.8 | convolution fusion | flops 18475253760 | bytes 31457280 | tf_op jit(solution)/shard_map/dot_general | solution.py:185
  231.5 53.4 %shard_map.109 = bf16[2,128,1280]{2,1,0:T(8,128)(2,1)} custom-call(s32[2,18]{1,0:T(2,128)} %pad_add_fusion.1.slots_ref, s32[2]{0:T(128)} %counts_ref.1, bf16[2,128,1280]{2,1,0:T(8,128)(2,1)} %bitcast.119, bf16[22,128,2560]{2,1,0:T(8,128)(2,1)} %bitcast.115), custom_call_target="tpu_custom_call" | custom-call | tf_op jit(solution)/shard_map/pallas_call | solution.py:127
  284.9 4.0 %convolution_convert_fusion.1 = bf16[256,1280]{1,0:T(8,128)(2,1)} fusion(bf16[256,1280]{1,0:T(8,128)(2,1)} %bitcast.120, bf16[1280,1280]{1,0:T(8,128)(2,1)} %all-gather.8.cloned.1.call-done), kind=kOutput, calls=%fused_computation.16 | convolution fusion | flops 839188480 | bytes 4587520 | tf_op jit(solution)/shard_map/dot_general | solution.py:210
  (92 shorter events, 8.0 us)
Async XLA Ops:
  6.5 49.5 %copy-start = (bf16[320,3840]{1,0:T(8,128)(2,1)S(1)}, bf16[320,3840]{1,0:T(8,128)(2,1)}, u32[]{:S(2)}) copy-start(bf16[320,3840]{1,0:T(8,128)(2,1)} %param.20) | copy-start | bytes 7372804
  6.5 6.4 %copy-start.2 = (bf16[256,1280]{1,0:T(8,128)(2,1)S(1)}, bf16[256,1280]{1,0:T(8,128)(2,1)}, u32[]{:S(2)}) copy-start(bf16[256,1280]{1,0:T(8,128)(2,1)} %param.16) | copy-start | bytes 1966084
  6.5 49.5 %all-gather.4.cloned.1.call-start = ((), (), s32[]{:S(2)}) async-start(), calls=%async_computation | async-start | bytes 3276800 | tf_op jit(solution)/shard_map/all_gather | solution.py:161
  15.0 42.2 %copy-start.8 = (s32[2,16]{1,0:T(2,128)S(1)}, s32[2,16]{1,0:T(2,128)}, u32[]{:S(2)}) copy-start(s32[2,16]{1,0:T(2,128)} %param.13) | copy-start | bytes 388
  15.0 59.7 %copy-start.9 = (s32[2]{0:T(128)S(1)}, s32[2]{0:T(128)}, u32[]{:S(2)}) copy-start(s32[2]{0:T(128)} %param.15) | copy-start | bytes 28
  18.4 93.7 %all-gather.6.cloned.1.call-start = ((), (), s32[]{:S(2)}) async-start(), calls=%async_computation.1 | async-start | bytes 6144000 | tf_op jit(solution)/shard_map/all_gather | solution.py:26
  57.2 227.7 %all-gather.8.cloned.1.call-start = ((), (), s32[]{:S(2)}) async-start(), calls=%async_computation.2 | async-start | bytes 4096000 | tf_op jit(solution)/shard_map/all_gather | solution.py:212
  60.3 53.6 %collective-permute-start.1 = (s32[3]{0:T(128)S(1)}, s32[3]{0:T(128)S(1)}, u32[]{:S(2)}, u32[]{:S(2)}) collective-permute-start(s32[3]{0:T(128)S(1)} %pad_add_fusion.2), channel_id=1, source_target_pairs={{8,0},{12,4},{16,8},{20,12},{24,16},{28,20},{32,24},{36,28},{40,32... | collective-permute-start | bytes 44 | tf_op jit(solution)/shard_map/ppermute | solution.py:20
  65.7 51.5 %collective-permute-start.3 = (s32[3]{0:T(128)S(1)}, s32[3]{0:T(128)S(1)}, u32[]{:S(2)}, u32[]{:S(2)}) collective-permute-start(s32[3]{0:T(128)S(1)} %pad_add_fusion.3), channel_id=1, source_target_pairs={{4,0},{8,4},{12,8},{16,12},{20,16},{24,20},{28,24},{32,28},{36,32}... | collective-permute-start | bytes 44 | tf_op jit(solution)/shard_map/ppermute | solution.py:20
  70.4 48.7 %collective-permute-start.5 = (s32[3]{0:T(128)S(1)}, s32[3]{0:T(128)S(1)}, u32[]{:S(2)}, u32[]{:S(2)}) collective-permute-start(s32[3]{0:T(128)S(1)} %pad_add_fusion.4), channel_id=1, source_target_pairs={{0,4},{4,8},{8,12},{12,16},{16,20},{20,24},{24,28},{28,32},{32,36}... | collective-permute-start | bytes 44 | tf_op jit(solution)/shard_map/ppermute | solution.py:20
  77.1 17.2 %collective-permute-start.9 = (bf16[2,128,1280]{2,1,0:T(8,128)(2,1)S(1)}, bf16[2,128,1280]{2,1,0:T(8,128)(2,1)S(1)}, u32[]{:S(2)}, u32[]{:S(2)}) collective-permute-start(bf16[2,128,1280]{2,1,0:T(8,128)(2,1)S(1)} %gather_fusion.7), channel_id=1, source_target_pairs={{0,64},{4,68},{8,72},{12,76},{16,80},{20,84},{24,88},{28,92},{32,9... | collective-permute-start | bytes 1966088 | tf_op jit(solution)/shard_map/ppermute | solution.py:173
  94.5 22.8 %collective-permute-start.10 = (bf16[2,128,1280]{2,1,0:T(8,128)(2,1)S(1)}, bf16[2,128,1280]{2,1,0:T(8,128)(2,1)S(1)}, u32[]{:S(2)}, u32[]{:S(2)}) collective-permute-start(bf16[2,128,1280]{2,1,0:T(8,128)(2,1)S(1)} %broadcast_select_fusion.2), channel_id=1, source_target_pairs={{0,32},{4,36},{8,40},{12,44},{16,48},{20,52},{24,56},{28,60},{32,0... | collective-permute-start | bytes 1966088 | tf_op jit(solution)/shard_map/ppermute | solution.py:173
  112.1 84.7 %collective-permute-start = (bf16[1280,1920]{1,0:T(8,128)(2,1)}, bf16[1280,1920]{1,0:T(8,128)(2,1)}, u32[]{:S(2)}, u32[]{:S(2)}) collective-permute-start(bf16[1280,1920]{1,0:T(8,128)(2,1)} %all-gather.6.cloned.1.call-done), channel_id=1, source_target_pairs={{0,4},{4,0},{8,12},{12,8},{16,20},{20,16},{24,28},{28,24},{32,36},... | collective-permute-start | bytes 14745608 | tf_op jit(solution)/shard_map/ppermute | solution.py:30
  114.0 5.5 %collective-permute-start.7 = (s32[3]{0:T(128)S(1)}, s32[3]{0:T(128)S(1)}, u32[]{:S(2)}, u32[]{:S(2)}) collective-permute-start(s32[3]{0:T(128)S(1)} %pad_add_fusion.5), channel_id=1, source_target_pairs={{0,8},{4,12},{8,16},{12,20},{16,24},{20,28},{24,32},{28,36},{32,40... | collective-permute-start | bytes 44 | tf_op jit(solution)/shard_map/ppermute | solution.py:20
  117.5 18.4 %collective-permute-start.11 = (bf16[2,128,1280]{2,1,0:T(8,128)(2,1)S(1)}, bf16[2,128,1280]{2,1,0:T(8,128)(2,1)S(1)}, u32[]{:S(2)}, u32[]{:S(2)}) collective-permute-start(bf16[2,128,1280]{2,1,0:T(8,128)(2,1)S(1)} %broadcast_select_fusion.3), channel_id=1, source_target_pairs={{0,16},{4,20},{8,24},{12,28},{16,0},{20,4},{24,8},{28,12},{32,48},... | collective-permute-start | bytes 1966088 | tf_op jit(solution)/shard_map/ppermute | solution.py:173
  121.8 35.5 %collective-permute-start.2 = (bf16[3,128,1280]{2,1,0:T(8,128)(2,1)S(1)}, bf16[3,128,1280]{2,1,0:T(8,128)(2,1)S(1)}, u32[]{:S(2)}, u32[]{:S(2)}) collective-permute-start(bf16[3,128,1280]{2,1,0:T(8,128)(2,1)S(1)} %gather_fusion.3), channel_id=1, source_target_pairs={{0,8},{4,12},{8,16},{12,20},{16,24},{20,28},{24,32},{28,36},{32,40... | collective-permute-start | bytes 2949128 | tf_op jit(solution)/shard_map/ppermute | solution.py:20
  135.9 0.9 copy-start.7
  138.0 31.7 %collective-permute-start.12 = (bf16[2,128,1280]{2,1,0:T(8,128)(2,1)S(1)}, bf16[2,128,1280]{2,1,0:T(8,128)(2,1)S(1)}, u32[]{:S(2)}, u32[]{:S(2)}) collective-permute-start(bf16[2,128,1280]{2,1,0:T(8,128)(2,1)S(1)} %broadcast_select_fusion.4), channel_id=1, source_target_pairs={{0,8},{4,12},{8,0},{12,4},{16,24},{20,28},{24,16},{28,20},{32,40},... | collective-permute-start | bytes 1966088 | tf_op jit(solution)/shard_map/ppermute | solution.py:173
  142.9 36.7 %collective-permute-start.4 = (bf16[3,128,1280]{2,1,0:T(8,128)(2,1)}, bf16[3,128,1280]{2,1,0:T(8,128)(2,1)}, u32[]{:S(2)}, u32[]{:S(2)}) collective-permute-start(bf16[3,128,1280]{2,1,0:T(8,128)(2,1)} %gather_fusion.4), channel_id=1, source_target_pairs={{0,4},{4,8},{8,12},{12,16},{16,20},{20,24},{24,28},{28,32},{32,36}... | collective-permute-start | bytes 2949128 | tf_op jit(solution)/shard_map/ppermute | solution.py:20
  148.2 32.6 %collective-permute-start.6 = (bf16[3,128,1280]{2,1,0:T(8,128)(2,1)}, bf16[3,128,1280]{2,1,0:T(8,128)(2,1)}, u32[]{:S(2)}, u32[]{:S(2)}) collective-permute-start(bf16[3,128,1280]{2,1,0:T(8,128)(2,1)} %gather_fusion.5), channel_id=1, source_target_pairs={{4,0},{8,4},{12,8},{16,12},{20,16},{24,20},{28,24},{32,28},{36,32}... | collective-permute-start | bytes 2949128 | tf_op jit(solution)/shard_map/ppermute | solution.py:20
  155.2 41.6 %slice-start = ((s8[4915200]{0:T(1024)(128)(4,1)}), s8[4194304]{0:T(1024)(128)(4,1)S(1)}, s32[]{:S(2)}) async-start(s8[4915200]{0:T(1024)(128)(4,1)} %bitcast.116), calls=%async_computation.3 | async-start | bytes 8388608
  157.2 36.3 %collective-permute-start.8 = (bf16[3,128,1280]{2,1,0:T(8,128)(2,1)}, bf16[3,128,1280]{2,1,0:T(8,128)(2,1)S(1)}, u32[]{:S(2)}, u32[]{:S(2)}) collective-permute-start(bf16[3,128,1280]{2,1,0:T(8,128)(2,1)} %gather_fusion.6), channel_id=1, source_target_pairs={{8,0},{12,4},{16,8},{20,12},{24,16},{28,20},{32,24},{36,28},{40,32... | collective-permute-start | bytes 2949128 | tf_op jit(solution)/shard_map/ppermute | solution.py:20
  169.7 0.8 copy-start.6
  170.5 26.3 %slice-start.1 = ((s8[4915200]{0:T(1024)(128)(4,1)}), s8[720896]{0:T(1024)(128)(4,1)S(1)}, s32[]{:S(2)}) async-start(s8[4915200]{0:T(1024)(128)(4,1)} %bitcast.116), calls=%async_computation.4 | async-start | bytes 1441792
  171.8 21.8 %collective-permute-start.13 = (bf16[2,128,1280]{2,1,0:T(8,128)(2,1)S(1)}, bf16[2,128,1280]{2,1,0:T(8,128)(2,1)S(1)}, u32[]{:S(2)}, u32[]{:S(2)}) collective-permute-start(bf16[2,128,1280]{2,1,0:T(8,128)(2,1)S(1)} %broadcast_select_fusion.5), channel_id=1, source_target_pairs={{0,4},{4,0},{8,12},{12,8},{16,20},{20,16},{24,28},{28,24},{32,36},... | collective-permute-start | bytes 1966088 | tf_op jit(solution)/shard_map/ppermute | solution.py:173
  193.9 2.9 copy-start.5
  196.8 7.2 %copy-start.4 = (bf16[256,1280]{1,0:T(8,128)(2,1)S(1)}, bf16[256,1280]{1,0:T(8,128)(2,1)}, u32[]{:S(2)}) copy-start(bf16[256,1280]{1,0:T(8,128)(2,1)} %fusion.11) | copy-start | bytes 1966084
  203.9 3.9 %copy-start.3 = (bf16[1280,1920]{1,0:T(8,128)(2,1)S(1)}, bf16[1280,1920]{1,0:T(8,128)(2,1)}, u32[]{:S(2)}) copy-start(bf16[1280,1920]{1,0:T(8,128)(2,1)} %get-tuple-element.31) | copy-start | bytes 14745604
  231.5 57.4 %copy-start.1 = (bf16[320,3840]{1,0:T(8,128)(2,1)S(1)}, bf16[320,3840]{1,0:T(8,128)(2,1)}, u32[]{:S(2)}) copy-start(bf16[320,3840]{1,0:T(8,128)(2,1)} %param.20) | copy-start | bytes 7372804
Sparse Core Ops, SparseCore 0:
  18.6 37.4 all-gather.3
  57.7 54.3 all-gather.5
  113.8 41.0 all-gather.7

commit v9 on v8

--- a/solution.py
+++ b/solution.py
@@ -164,14 +164,25 @@
     w_src, group_rows = lax.optimization_barrier((w_qkv, group_rows))
     w_full = gathered_weight(w_src)
 
+    dev_count = seq_size * fsdp_size
+    dev_at = seq_at * fsdp_size + lax.axis_index("fsdp")
     global_ids = global_tiles.astype(jnp.int32)
-    global_rows = group_rows[global_ids % group_tiles]
-    owners = global_ids // group_tiles
-    for bit in sorted(range(seq_size.bit_length() - 1), key=lambda b: -b):
+    global_rows = jnp.stack(
+        [
+            lax.dynamic_slice_in_dim(normed, global_ids[n] % tile_count * TILE, TILE, 0)
+            for n in range(GLOBAL)
+        ]
+    )
+    owners = global_ids // tile_count
+    done_bits = 0
+    for bit in sorted(range(dev_count.bit_length() - 1), key=lambda b: -b):
         step = 1 << bit
-        held = ((seq_at ^ owners) & (2 * step - 1)) == 0
-        got = lax.ppermute(global_rows, "seq", [(i, i ^ step) for i in range(seq_size)])
+        held = ((dev_at ^ owners) & ~done_bits) == 0
+        got = lax.ppermute(
+            global_rows, ("seq", "fsdp"), [(i, i ^ step) for i in range(dev_count)]
+        )
         global_rows = jnp.where(held[:, None, None], global_rows, got)
+        done_bits |= step
     near_blocks = []
     near_rank = []
     for reach in REACH:

time: 297 us -> 306 us (1.030)
  between operations: 13.5 us -> 16.9 us
    ppermute x5 -> x7, waiting for transfers between devices: 32 us -> 49.3 us  [local(): lax.ppermute(global_rows, ('seq', 'fsdp'), [(i, i ^ step) for i in range(...]
    all_gather x1, waiting for transfers between devices: 16 us -> 0.01 us  [gathered_weight(): lax.all_gather(lax.dynamic_slice_in_dim(shard, core * half, half, 1), 'fs...]
    ppermute x5 -> x7, starting transfers between devices: 7.94 us -> 10.8 us  [local(): lax.ppermute(global_rows, ('seq', 'fsdp'), [(i, i ^ step) for i in range(...]
  transfers between devices with their start and end apart: 17 -> 19, of which waited for: 8 -> 9; matrix products, arithmetic and copies ran while one was open for 24% -> 23% of each run, Pallas kernels for 18% -> 17%
where the time goes in v9:
time: 306 us; the launch traced here: 303 us
  waiting for transfers between devices  106 us (35%)
  Pallas kernels  52.3 us (17%)
  starting transfers between devices  34.7 us (11%)
  local copies, waits for them, and re-layouts  31.8 us (10%)
  matrix products  31.5 us (10%)
  other arithmetic  29.2 us (10%)
  between operations  16.9 us (6%)
    pallas_call x1, Pallas kernels, attend(): pl.pallas_call(attention_kernel, grid_spec=grid_spec, out_shape=jax.Shape...  52.3 us
    ppermute x7, waiting for transfers between devices, local(): lax.ppermute(global_rows, ('seq', 'fsdp'), [(i, i ^ step) for i in range(...  49.3 us
    all_gather x1, waiting for transfers between devices, local(): lax.all_gather(normed, 'fsdp', axis=0, tiled=True)  37.5 us
    ppermute x8, starting transfers between devices, passed_along(): return lax.ppermute(block, axis, route)  23.9 us
    dot_general x1, matrix products, local(): jnp.dot(window_rows.reshape(-1, feat_width), w_full[:, feat_width:], pref...  23.6 us
    ppermute x8, waiting for transfers between devices, passed_along(): return lax.ppermute(block, axis, route)  19.3 us
    gather x4, local copies, waits for them, and re-layouts, local(): near_blocks.append(passed_along(group_rows[asked], 'seq', -reach))  13.5 us
    ppermute x7, starting transfers between devices, local(): lax.ppermute(global_rows, ('seq', 'fsdp'), [(i, i ^ step) for i in range(...  10.8 us
  transfers between devices with their start and end apart: 19, of which 9 were waited for; matrix products, arithmetic and copies ran while one was open for 23% of the time, Pallas kernels for 17%

profile of v9, /device:TPU:24, one launch (start us, length us, event | category | flops | bytes accessed | tf_op | source)
XLA Modules:
  0.0 302.8 jit_solution(8334333474110254584)
XLA Ops:
  6.5 0.8 compare_select_fusion.1
  8.9 4.1 %gather_fusion.2 = bf16[256,1280]{1,0:T(8,128)(2,1)} fusion(bf16[512,1280]{1,0:T(8,128)(2,1)} %param.17, s32[1024]{0:T(1024)S(1)} %get-tuple-element.53), kind=kCustom, calls=%fused_computation.2 | custom fusion | bytes 1311744 | tf_op jit(solution)/shard_map/gather | solution.py:51
  13.0 2.1 gather_fusion.1
  15.0 1.9 convert_reduce_fusion
  17.2 1.2 fusion.11
  18.5 37.5 %all-gather.4.cloned.1.call-done = bf16[1024,1280]{1,0:T(8,128)(2,1)} async-done(((bf16[256,1280]{1,0:T(8,128)(2,1)}), bf16[1024,1280]{1,0:T(8,128)(2,1)}) %all-gather.4.cloned.1.call-update) | async-done | bytes 2621456 | tf_op jit(solution)/shard_map/all_gather | solution.py:161
  56.0 1.2 constant_dynamic-slice_fusion
  58.5 1.8 pad_add_fusion.3
  60.3 2.0 collective-permute-start.3
  66.5 3.1 %collective-permute-start.9 = (bf16[2,128,1280]{2,1,0:T(8,128)(2,1)S(1)}, bf16[2,128,1280]{2,1,0:T(8,128)(2,1)S(1)}, u32[]{:S(2)}, u32[]{:S(2)}) collective-permute-start(bf16[2,128,1280]{2,1,0:T(8,128)(2,1)S(1)} %pad_maximum_fusion.2), channel_id=1, source_target_pairs={{0,64},{1,65},{2,66},{3,67},{4,68},{5,69},{6,70},{7,71},{8,72},{9,... | collective-permute-start | bytes 1966088 | tf_op jit(solution)/shard_map/ppermute | solution.py:181
  70.4 1.8 pad_add_fusion.2
  72.2 2.6 collective-permute-start.1
  74.9 10.2 %collective-permute-done.9 = bf16[2,128,1280]{2,1,0:T(8,128)(2,1)S(1)} collective-permute-done((bf16[2,128,1280]{2,1,0:T(8,128)(2,1)S(1)}, bf16[2,128,1280]{2,1,0:T(8,128)(2,1)S(1)}, u32[]{:S(2)}, u32[]{:S(2)}) %collective-permute-start.9) | collective-permute-done | bytes 655392 | tf_op jit(solution)/shard_map/ppermute | solution.py:181
  85.2 1.5 collective-permute-start.10
  87.7 2.0 pad_add_fusion.5
  89.8 2.4 collective-permute-start.7
  92.4 9.2 %collective-permute-done.10 = bf16[2,128,1280]{2,1,0:T(8,128)(2,1)} collective-permute-done((bf16[2,128,1280]{2,1,0:T(8,128)(2,1)S(1)}, bf16[2,128,1280]{2,1,0:T(8,128)(2,1)}, u32[]{:S(2)}, u32[]{:S(2)}) %collective-permute-start.10) | collective-permute-done | bytes 655392 | tf_op jit(solution)/shard_map/ppermute | solution.py:181
  101.6 1.2 broadcast_select_fusion.3
  102.8 1.6 collective-permute-start.11
  104.5 15.2 %collective-permute-done.11 = bf16[2,128,1280]{2,1,0:T(8,128)(2,1)S(1)} collective-permute-done((bf16[2,128,1280]{2,1,0:T(8,128)(2,1)S(1)}, bf16[2,128,1280]{2,1,0:T(8,128)(2,1)S(1)}, u32[]{:S(2)}, u32[]{:S(2)}) %collective-permute-start.11) | collective-permute-done | bytes 655392 | tf_op jit(solution)/shard_map/ppermute | solution.py:181
  120.6 1.2 broadcast_select_fusion.4
  121.8 1.1 collective-permute-start.12
  124.5 1.9 pad_add_fusion.4
  126.4 10.0 %collective-permute-done.12 = bf16[2,128,1280]{2,1,0:T(8,128)(2,1)S(1)} collective-permute-done((bf16[2,128,1280]{2,1,0:T(8,128)(2,1)S(1)}, bf16[2,128,1280]{2,1,0:T(8,128)(2,1)S(1)}, u32[]{:S(2)}, u32[]{:S(2)}) %collective-permute-start.12) | collective-permute-done | bytes 655392 | tf_op jit(solution)/shard_map/ppermute | solution.py:181
  137.2 2.4 collective-permute-start.5
  139.8 1.9 collective-permute-start.14
  142.1 3.4 %gather_fusion.3 = bf16[3,128,1280]{2,1,0:T(8,128)(2,1)} fusion(bf16[8,128,1280]{2,1,0:T(8,128)(2,1)} %bitcast.115, s32[1024]{0:T(1024)S(1)} %pad_clamp_fusion.3), kind=kCustom, calls=%fused_computation.3 | custom fusion | bytes 1966092 | tf_op jit(solution)/shard_map/gather | solution.py:191
  145.5 6.0 %collective-permute-start.2 = (bf16[3,128,1280]{2,1,0:T(8,128)(2,1)}, bf16[3,128,1280]{2,1,0:T(8,128)(2,1)S(1)}, u32[]{:S(2)}, u32[]{:S(2)}) collective-permute-start(bf16[3,128,1280]{2,1,0:T(8,128)(2,1)} %gather_fusion.3), channel_id=1, source_target_pairs={{0,8},{4,12},{8,16},{12,20},{16,24},{20,28},{24,32},{28,36},{32,40... | collective-permute-start | bytes 2949128 | tf_op jit(solution)/shard_map/ppermute | solution.py:20
  151.6 3.3 %gather_fusion.4 = bf16[3,128,1280]{2,1,0:T(8,128)(2,1)} fusion(bf16[8,128,1280]{2,1,0:T(8,128)(2,1)} %bitcast.116, s32[1024]{0:T(1024)S(1)} %pad_clamp_fusion.2), kind=kCustom, calls=%fused_computation.4 | custom fusion | bytes 1966092 | tf_op jit(solution)/shard_map/gather | solution.py:191
  154.9 1.9 collective-permute-start.4
  156.8 3.3 %gather_fusion.5 = bf16[3,128,1280]{2,1,0:T(8,128)(2,1)} fusion(bf16[8,128,1280]{2,1,0:T(8,128)(2,1)} %bitcast.117, s32[1024]{0:T(1024)S(1)} %pad_clamp_fusion.1), kind=kCustom, calls=%fused_computation.5 | custom fusion | bytes 1966092 | tf_op jit(solution)/shard_map/gather | solution.py:191
  160.2 3.6 %collective-permute-start.6 = (bf16[3,128,1280]{2,1,0:T(8,128)(2,1)}, bf16[3,128,1280]{2,1,0:T(8,128)(2,1)}, u32[]{:S(2)}, u32[]{:S(2)}) collective-permute-start(bf16[3,128,1280]{2,1,0:T(8,128)(2,1)} %gather_fusion.5), channel_id=1, source_target_pairs={{4,0},{8,4},{12,8},{16,12},{20,16},{24,20},{28,24},{32,28},{36,32}... | collective-permute-start | bytes 2949128 | tf_op jit(solution)/shard_map/ppermute | solution.py:20
  163.8 4.8 %collective-permute-done.14 = bf16[2,128,1280]{2,1,0:T(8,128)(2,1)S(1)} collective-permute-done((bf16[2,128,1280]{2,1,0:T(8,128)(2,1)S(1)}, bf16[2,128,1280]{2,1,0:T(8,128)(2,1)S(1)}, u32[]{:S(2)}, u32[]{:S(2)}) %collective-permute-start.14) | collective-permute-done | bytes 655392 | tf_op jit(solution)/shard_map/ppermute | solution.py:181
  169.4 1.2 broadcast_select_fusion.7
  170.7 3.3 %gather_fusion.6 = bf16[3,128,1280]{2,1,0:T(8,128)(2,1)} fusion(bf16[8,128,1280]{2,1,0:T(8,128)(2,1)} %bitcast.118, s32[1024]{0:T(1024)S(1)} %pad_clamp_fusion), kind=kCustom, calls=%fused_computation.6 | custom fusion | bytes 1966092 | tf_op jit(solution)/shard_map/gather | solution.py:191
  174.0 2.9 collective-permute-start.8
  176.9 2.1 constant_dynamic-update-slice_fusion.4
  179.0 1.4 collective-permute-start.15
  180.5 2.1 collective-permute-done.4
  182.6 1.3 constant_dynamic-update-slice_fusion.2
  183.9 1.3 constant_dynamic-update-slice_fusion.1
  185.2 16.8 %collective-permute-done.8 = bf16[3,128,1280]{2,1,0:T(8,128)(2,1)S(1)} collective-permute-done((bf16[3,128,1280]{2,1,0:T(8,128)(2,1)}, bf16[3,128,1280]{2,1,0:T(8,128)(2,1)S(1)}, u32[]{:S(2)}, u32[]{:S(2)}) %collective-permute-start.8) | collective-permute-done | bytes 983072 | tf_op jit(solution)/shard_map/ppermute | solution.py:20
  202.4 2.9 copy-done.5
  205.3 7.1 %broadcast_select_fusion = (bf16[1280,1920]{1,0:T(8,128)(2,1)}, bf16[1280,1920]{1,0:T(8,128)(2,1)}) fusion(bf16[1280,1920]{1,0:T(8,128)(2,1)} %collective-permute-done, bf16[1280,1920]{1,0:T(8,128)(2,1)S(1)} %bitcast.122, pred[]{:T(512)S(6)} %eq.167), kind=kLoop, calls=%fused_computation.10 | loop fusion | flops 4915200 | bytes 19660800 | tf_op jit(solution)/shard_map/jit(_where)/select_n | solution.py:32
  212.3 3.9 %fusion.3 = bf16[256,1280]{1,0:T(8,128)(2,1)} fusion(bf16[256,1280]{1,0:T(8,128)(2,1)S(1)} %copy-done.3, bf16[1280,1920]{1,0:T(8,128)(2,1)} %get-tuple-element.32), kind=kOutput, calls=%fused_computation.14 | convolution fusion | flops 839188480 | bytes 4587520 | tf_op jit(solution)/shard_map/dot_general | solution.py:200
  216.3 23.6 %convolution_convert_fusion = bf16[2816,2560]{1,0:T(8,128)(2,1)} fusion(bf16[2816,1280]{1,0:T(8,128)(2,1)} %bitcast.123, bf16[1280,1920]{1,0:T(8,128)(2,1)S(1)} %copy-done.4, bf16[1280,1920]{1,0:T(8,128)(2,1)} %get-tuple-element.32), kind=kOutput, calls=%fused_computation.7 | convolution fusion | flops 18475253760 | bytes 31457280 | tf_op jit(solution)/shard_map/dot_general | solution.py:196
  239.9 52.3 %shard_map.109 = bf16[2,128,1280]{2,1,0:T(8,128)(2,1)} custom-call(s32[2,18]{1,0:T(2,128)} %pad_add_fusion.1.slots_ref, s32[2]{0:T(128)} %counts_ref.1, bf16[2,128,1280]{2,1,0:T(8,128)(2,1)} %bitcast.124, bf16[22,128,2560]{2,1,0:T(8,128)(2,1)} %bitcast.120), custom_call_target="tpu_custom_call" | custom-call | tf_op jit(solution)/shard_map/pallas_call | solution.py:127
  292.2 4.0 %convolution_convert_fusion.1 = bf16[256,1280]{1,0:T(8,128)(2,1)} fusion(bf16[256,1280]{1,0:T(8,128)(2,1)} %bitcast.125, bf16[1280,1280]{1,0:T(8,128)(2,1)} %all-gather.8.cloned.1.call-done), kind=kOutput, calls=%fused_computation.15 | convolution fusion | flops 839188480 | bytes 4587520 | tf_op jit(solution)/shard_map/dot_general | solution.py:221
  (96 shorter events, 11.1 us)
Async XLA Ops:
  6.5 49.5 %copy-start = (bf16[320,3840]{1,0:T(8,128)(2,1)S(1)}, bf16[320,3840]{1,0:T(8,128)(2,1)}, u32[]{:S(2)}) copy-start(bf16[320,3840]{1,0:T(8,128)(2,1)} %param.20) | copy-start | bytes 7372804
  6.5 6.4 %copy-start.2 = (bf16[256,1280]{1,0:T(8,128)(2,1)S(1)}, bf16[256,1280]{1,0:T(8,128)(2,1)}, u32[]{:S(2)}) copy-start(bf16[256,1280]{1,0:T(8,128)(2,1)} %param.16) | copy-start | bytes 1966084
  6.5 49.5 %all-gather.4.cloned.1.call-start = ((), (), s32[]{:S(2)}) async-start(), calls=%async_computation | async-start | bytes 3276800 | tf_op jit(solution)/shard_map/all_gather | solution.py:161
  15.0 42.2 %copy-start.9 = (s32[2,16]{1,0:T(2,128)S(1)}, s32[2,16]{1,0:T(2,128)}, u32[]{:S(2)}) copy-start(s32[2,16]{1,0:T(2,128)} %param.13) | copy-start | bytes 388
  15.0 47.3 %copy-start.8 = (s32[2]{0:T(128)S(1)}, s32[2]{0:T(128)}, u32[]{:S(2)}) copy-start(s32[2]{0:T(128)} %param.15) | copy-start | bytes 28
  18.4 47.9 %copy-start.3 = (bf16[256,1280]{1,0:T(8,128)(2,1)S(1)}, bf16[256,1280]{1,0:T(8,128)(2,1)}, u32[]{:S(2)}) copy-start(bf16[256,1280]{1,0:T(8,128)(2,1)} %fusion.11) | copy-start | bytes 1966084
  18.4 106.1 %all-gather.6.cloned.1.call-start = ((), (), s32[]{:S(2)}) async-start(), calls=%async_computation.1 | async-start | bytes 6144000 | tf_op jit(solution)/shard_map/all_gather | solution.py:26
  57.2 235.0 %all-gather.8.cloned.1.call-start = ((), (), s32[]{:S(2)}) async-start(), calls=%async_computation.2 | async-start | bytes 4096000 | tf_op jit(solution)/shard_map/all_gather | solution.py:223
  60.3 76.9 %collective-permute-start.3 = (s32[3]{0:T(128)S(1)}, s32[3]{0:T(128)S(1)}, u32[]{:S(2)}, u32[]{:S(2)}) collective-permute-start(s32[3]{0:T(128)S(1)} %pad_add_fusion.3), channel_id=1, source_target_pairs={{4,0},{8,4},{12,8},{16,12},{20,16},{24,20},{28,24},{32,28},{36,32}... | collective-permute-start | bytes 44 | tf_op jit(solution)/shard_map/ppermute | solution.py:20
  66.5 18.6 %collective-permute-start.9 = (bf16[2,128,1280]{2,1,0:T(8,128)(2,1)S(1)}, bf16[2,128,1280]{2,1,0:T(8,128)(2,1)S(1)}, u32[]{:S(2)}, u32[]{:S(2)}) collective-permute-start(bf16[2,128,1280]{2,1,0:T(8,128)(2,1)S(1)} %pad_maximum_fusion.2), channel_id=1, source_target_pairs={{0,64},{1,65},{2,66},{3,67},{4,68},{5,69},{6,70},{7,71},{8,72},{9,... | collective-permute-start | bytes 1966088 | tf_op jit(solution)/shard_map/ppermute | solution.py:181
  72.2 67.4 %collective-permute-start.1 = (s32[3]{0:T(128)S(1)}, s32[3]{0:T(128)S(1)}, u32[]{:S(2)}, u32[]{:S(2)}) collective-permute-start(s32[3]{0:T(128)S(1)} %pad_add_fusion.2), channel_id=1, source_target_pairs={{8,0},{12,4},{16,8},{20,12},{24,16},{28,20},{32,24},{36,28},{40,32... | collective-permute-start | bytes 44 | tf_op jit(solution)/shard_map/ppermute | solution.py:20
  85.2 16.4 %collective-permute-start.10 = (bf16[2,128,1280]{2,1,0:T(8,128)(2,1)S(1)}, bf16[2,128,1280]{2,1,0:T(8,128)(2,1)}, u32[]{:S(2)}, u32[]{:S(2)}) collective-permute-start(bf16[2,128,1280]{2,1,0:T(8,128)(2,1)S(1)} %broadcast_select_fusion.2), channel_id=1, source_target_pairs={{0,32},{1,33},{2,34},{3,35},{4,36},{5,37},{6,38},{7,39},{8,40},{9,... | collective-permute-start | bytes 1966088 | tf_op jit(solution)/shard_map/ppermute | solution.py:181
  89.8 52.0 %collective-permute-start.7 = (s32[3]{0:T(128)S(1)}, s32[3]{0:T(128)S(1)}, u32[]{:S(2)}, u32[]{:S(2)}) collective-permute-start(s32[3]{0:T(128)S(1)} %pad_add_fusion.5), channel_id=1, source_target_pairs={{0,8},{4,12},{8,16},{12,20},{16,24},{20,28},{24,32},{28,36},{32,40... | collective-permute-start | bytes 44 | tf_op jit(solution)/shard_map/ppermute | solution.py:20
  102.8 16.9 %collective-permute-start.11 = (bf16[2,128,1280]{2,1,0:T(8,128)(2,1)S(1)}, bf16[2,128,1280]{2,1,0:T(8,128)(2,1)S(1)}, u32[]{:S(2)}, u32[]{:S(2)}) collective-permute-start(bf16[2,128,1280]{2,1,0:T(8,128)(2,1)S(1)} %broadcast_select_fusion.3), channel_id=1, source_target_pairs={{0,16},{1,17},{2,18},{3,19},{4,20},{5,21},{6,22},{7,23},{8,24},{9,... | collective-permute-start | bytes 1966088 | tf_op jit(solution)/shard_map/ppermute | solution.py:181
  119.7 0.8 copy-start.7
  121.8 14.5 %collective-permute-start.12 = (bf16[2,128,1280]{2,1,0:T(8,128)(2,1)S(1)}, bf16[2,128,1280]{2,1,0:T(8,128)(2,1)S(1)}, u32[]{:S(2)}, u32[]{:S(2)}) collective-permute-start(bf16[2,128,1280]{2,1,0:T(8,128)(2,1)S(1)} %broadcast_select_fusion.4), channel_id=1, source_target_pairs={{0,8},{1,9},{2,10},{3,11},{4,12},{5,13},{6,14},{7,15},{8,0},{9,1},... | collective-permute-start | bytes 1966088 | tf_op jit(solution)/shard_map/ppermute | solution.py:181
  124.5 80.7 %collective-permute-start = (bf16[1280,1920]{1,0:T(8,128)(2,1)}, bf16[1280,1920]{1,0:T(8,128)(2,1)}, u32[]{:S(2)}, u32[]{:S(2)}) collective-permute-start(bf16[1280,1920]{1,0:T(8,128)(2,1)} %all-gather.6.cloned.1.call-done), channel_id=1, source_target_pairs={{0,4},{4,0},{8,12},{12,8},{16,20},{20,16},{24,28},{28,24},{32,36},... | collective-permute-start | bytes 14745608 | tf_op jit(solution)/shard_map/ppermute | solution.py:30
  136.5 3.1 %collective-permute-start.13 = (bf16[2,128,1280]{2,1,0:T(8,128)(2,1)S(1)}, bf16[2,128,1280]{2,1,0:T(8,128)(2,1)S(1)}, u32[]{:S(2)}, u32[]{:S(2)}) collective-permute-start(bf16[2,128,1280]{2,1,0:T(8,128)(2,1)S(1)} %broadcast_select_fusion.5), channel_id=1, source_target_pairs={{0,4},{1,5},{2,6},{3,7},{4,0},{5,1},{6,2},{7,3},{8,12},{9,13},{10,... | collective-permute-start | bytes 1966088 | tf_op jit(solution)/shard_map/ppermute | solution.py:181
  137.2 4.9 %collective-permute-start.5 = (s32[3]{0:T(128)S(1)}, s32[3]{0:T(128)S(1)}, u32[]{:S(2)}, u32[]{:S(2)}) collective-permute-start(s32[3]{0:T(128)S(1)} %pad_add_fusion.4), channel_id=1, source_target_pairs={{0,4},{4,8},{8,12},{12,16},{16,20},{20,24},{24,28},{28,32},{32,36}... | collective-permute-start | bytes 44 | tf_op jit(solution)/shard_map/ppermute | solution.py:20
  139.8 28.8 %collective-permute-start.14 = (bf16[2,128,1280]{2,1,0:T(8,128)(2,1)S(1)}, bf16[2,128,1280]{2,1,0:T(8,128)(2,1)S(1)}, u32[]{:S(2)}, u32[]{:S(2)}) collective-permute-start(bf16[2,128,1280]{2,1,0:T(8,128)(2,1)S(1)} %broadcast_select_fusion.6), channel_id=1, source_target_pairs={{0,2},{1,3},{2,0},{3,1},{4,6},{5,7},{6,4},{7,5},{8,10},{9,11},{10,... | collective-permute-start | bytes 1966088 | tf_op jit(solution)/shard_map/ppermute | solution.py:181
  145.5 33.5 %collective-permute-start.2 = (bf16[3,128,1280]{2,1,0:T(8,128)(2,1)}, bf16[3,128,1280]{2,1,0:T(8,128)(2,1)S(1)}, u32[]{:S(2)}, u32[]{:S(2)}) collective-permute-start(bf16[3,128,1280]{2,1,0:T(8,128)(2,1)} %gather_fusion.3), channel_id=1, source_target_pairs={{0,8},{4,12},{8,16},{12,20},{16,24},{20,28},{24,32},{28,36},{32,40... | collective-permute-start | bytes 2949128 | tf_op jit(solution)/shard_map/ppermute | solution.py:20
  154.9 27.7 %collective-permute-start.4 = (bf16[3,128,1280]{2,1,0:T(8,128)(2,1)}, bf16[3,128,1280]{2,1,0:T(8,128)(2,1)}, u32[]{:S(2)}, u32[]{:S(2)}) collective-permute-start(bf16[3,128,1280]{2,1,0:T(8,128)(2,1)} %gather_fusion.4), channel_id=1, source_target_pairs={{0,4},{4,8},{8,12},{12,16},{16,20},{20,24},{24,28},{28,32},{32,36}... | collective-permute-start | bytes 2949128 | tf_op jit(solution)/shard_map/ppermute | solution.py:20
  160.2 23.7 %collective-permute-start.6 = (bf16[3,128,1280]{2,1,0:T(8,128)(2,1)}, bf16[3,128,1280]{2,1,0:T(8,128)(2,1)}, u32[]{:S(2)}, u32[]{:S(2)}) collective-permute-start(bf16[3,128,1280]{2,1,0:T(8,128)(2,1)} %gather_fusion.5), channel_id=1, source_target_pairs={{4,0},{8,4},{12,8},{16,12},{20,16},{24,20},{28,24},{32,28},{36,32}... | collective-permute-start | bytes 2949128 | tf_op jit(solution)/shard_map/ppermute | solution.py:20
  168.6 0.8 copy-start.6
  174.0 28.0 %collective-permute-start.8 = (bf16[3,128,1280]{2,1,0:T(8,128)(2,1)}, bf16[3,128,1280]{2,1,0:T(8,128)(2,1)S(1)}, u32[]{:S(2)}, u32[]{:S(2)}) collective-permute-start(bf16[3,128,1280]{2,1,0:T(8,128)(2,1)} %gather_fusion.6), channel_id=1, source_target_pairs={{8,0},{12,4},{16,8},{20,12},{24,16},{28,20},{32,24},{36,28},{40,32... | collective-permute-start | bytes 2949128 | tf_op jit(solution)/shard_map/ppermute | solution.py:20
  176.9 28.3 %slice-start = ((s8[4915200]{0:T(1024)(128)(4,1)}), s8[4194304]{0:T(1024)(128)(4,1)S(1)}, s32[]{:S(2)}) async-start(s8[4915200]{0:T(1024)(128)(4,1)} %bitcast.121), calls=%async_computation.3 | async-start | bytes 8388608
  179.0 23.1 %collective-permute-start.15 = (bf16[2,128,1280]{2,1,0:T(8,128)(2,1)S(1)}, bf16[2,128,1280]{2,1,0:T(8,128)(2,1)S(1)}, u32[]{:S(2)}, u32[]{:S(2)}) collective-permute-start(bf16[2,128,1280]{2,1,0:T(8,128)(2,1)S(1)} %broadcast_select_fusion.7), channel_id=1, source_target_pairs={{0,1},{1,0},{2,3},{3,2},{4,5},{5,4},{6,7},{7,6},{8,9},{9,8},{10,11... | collective-permute-start | bytes 1966088 | tf_op jit(solution)/shard_map/ppermute | solution.py:181
  180.5 24.8 %slice-start.1 = ((s8[4915200]{0:T(1024)(128)(4,1)}), s8[720896]{0:T(1024)(128)(4,1)S(1)}, s32[]{:S(2)}) async-start(s8[4915200]{0:T(1024)(128)(4,1)} %bitcast.121), calls=%async_computation.4 | async-start | bytes 1441792
  202.4 2.9 copy-start.5
  212.3 3.9 %copy-start.4 = (bf16[1280,1920]{1,0:T(8,128)(2,1)S(1)}, bf16[1280,1920]{1,0:T(8,128)(2,1)}, u32[]{:S(2)}) copy-start(bf16[1280,1920]{1,0:T(8,128)(2,1)} %get-tuple-element.31) | copy-start | bytes 14745604
  239.9 56.3 %copy-start.1 = (bf16[320,3840]{1,0:T(8,128)(2,1)S(1)}, bf16[320,3840]{1,0:T(8,128)(2,1)}, u32[]{:S(2)}) copy-start(bf16[320,3840]{1,0:T(8,128)(2,1)} %param.20) | copy-start | bytes 7372804
Sparse Core Ops, SparseCore 0:
  18.6 37.4 all-gather.3
  57.7 54.3 all-gather.5
  113.8 50.7 all-gather.7

commit v10 on v8

--- a/solution.py
+++ b/solution.py
@@ -167,9 +167,14 @@
     global_ids = global_tiles.astype(jnp.int32)
     global_rows = group_rows[global_ids % group_tiles]
     owners = global_ids // group_tiles
-    for bit in sorted(range(seq_size.bit_length() - 1), key=lambda b: -b):
+    seq_bits = seq_size.bit_length() - 1
+    bit_order = [b for b in (1, 2) if b < seq_bits]
+    bit_order += [b for b in range(seq_bits - 1, -1, -1) if b not in bit_order]
+    done_bits = 0
+    for bit in bit_order:
         step = 1 << bit
-        held = ((seq_at ^ owners) & (2 * step - 1)) == 0
+        held = ((seq_at ^ owners) & ~done_bits & (seq_size - 1)) == 0
+        done_bits |= step
         got = lax.ppermute(global_rows, "seq", [(i, i ^ step) for i in range(seq_size)])
         global_rows = jnp.where(held[:, None, None], global_rows, got)
     near_blocks = []

time: 297 us -> 292 us (0.983)
  waiting for transfers between devices: 105 us -> 101 us
    ppermute x8, waiting for transfers between devices: 19.3 us -> 12.4 us  [passed_along(): return lax.ppermute(block, axis, route)]
  transfers between devices with their start and end apart: 17 -> 17, of which waited for: 8 -> 6; matrix products, arithmetic and copies ran while one was open for 24% -> 24% of each run, Pallas kernels for 18% -> 19%
where the time goes in v10:
time: 292 us; the launch traced here: 291 us
  waiting for transfers between devices  101 us (35%)
  Pallas kernels  55.1 us (19%)
  local copies, waits for them, and re-layouts  32.5 us (11%)
  matrix products  31.5 us (11%)
  starting transfers between devices  30.6 us (10%)
  other arithmetic  27.6 us (9%)
  between operations  13.5 us (5%)
    pallas_call x1, Pallas kernels, attend(): pl.pallas_call(attention_kernel, grid_spec=grid_spec, out_shape=jax.Shape...  55.1 us
    all_gather x1, waiting for transfers between devices, local(): lax.all_gather(normed, 'fsdp', axis=0, tiled=True)  37.5 us
    ppermute x5, waiting for transfers between devices, local(): lax.ppermute(global_rows, 'seq', [(i, i ^ step) for i in range(seq_size)])  34.4 us
    dot_general x1, matrix products, local(): jnp.dot(window_rows.reshape(-1, feat_width), w_full[:, feat_width:], pref...  23.6 us
    ppermute x8, starting transfers between devices, passed_along(): return lax.ppermute(block, axis, route)  23.1 us
    all_gather x1, waiting for transfers between devices, gathered_weight(): lax.all_gather(lax.dynamic_slice_in_dim(shard, core * half, half, 1), 'fs...  16.1 us
    gather x4, local copies, waits for them, and re-layouts, local(): near_blocks.append(passed_along(group_rows[asked], 'seq', -reach))  12.5 us
    ppermute x8, waiting for transfers between devices, passed_along(): return lax.ppermute(block, axis, route)  12.4 us
  transfers between devices with their start and end apart: 17, of which 6 were waited for; matrix products, arithmetic and copies ran while one was open for 24% of the time, Pallas kernels for 19%

profile of v10, /device:TPU:24, one launch (start us, length us, event | category | flops | bytes accessed | tf_op | source)
XLA Modules:
  0.0 291.4 jit_solution(12992404977864924610)
XLA Ops:
  6.5 0.8 compare_select_fusion.1
  7.4 0.8 convert_element_type.99
  8.2 0.7 convert_element_type.98
  8.9 4.1 %gather_fusion.2 = bf16[256,1280]{1,0:T(8,128)(2,1)} fusion(bf16[512,1280]{1,0:T(8,128)(2,1)} %param.17, s32[1024]{0:T(1024)S(1)} %get-tuple-element.43), kind=kCustom, calls=%fused_computation.2 | custom fusion | bytes 1311744 | tf_op jit(solution)/shard_map/gather | solution.py:51
  13.0 2.1 gather_fusion.1
  15.0 1.9 convert_reduce_fusion
  17.2 1.2 fusion.11
  18.5 37.5 %all-gather.4.cloned.1.call-done = bf16[1024,1280]{1,0:T(8,128)(2,1)} async-done(((bf16[256,1280]{1,0:T(8,128)(2,1)}), bf16[1024,1280]{1,0:T(8,128)(2,1)}) %all-gather.4.cloned.1.call-update) | async-done | bytes 2621456 | tf_op jit(solution)/shard_map/all_gather | solution.py:161
  56.0 1.2 constant_dynamic-slice_fusion
  58.5 1.8 pad_add_fusion.2
  60.3 2.7 collective-permute-start.1
  63.9 1.8 pad_add_fusion.3
  65.7 1.9 collective-permute-start.3
  68.5 1.8 pad_add_fusion.4
  70.4 2.4 collective-permute-start.5
  73.8 0.8 gather_fusion
  74.8 2.3 gather_fusion.7
  78.4 14.5 %collective-permute-done.9 = bf16[2,128,1280]{2,1,0:T(8,128)(2,1)S(1)} collective-permute-done((bf16[2,128,1280]{2,1,0:T(8,128)(2,1)S(1)}, bf16[2,128,1280]{2,1,0:T(8,128)(2,1)S(1)}, u32[]{:S(2)}, u32[]{:S(2)}) %collective-permute-start.9) | collective-permute-done | bytes 655392 | tf_op jit(solution)/shard_map/ppermute | solution.py:178
  93.0 3.0 %collective-permute-start.10 = (bf16[2,128,1280]{2,1,0:T(8,128)(2,1)S(1)}, bf16[2,128,1280]{2,1,0:T(8,128)(2,1)S(1)}, u32[]{:S(2)}, u32[]{:S(2)}) collective-permute-start(bf16[2,128,1280]{2,1,0:T(8,128)(2,1)S(1)} %broadcast_select_fusion.2), channel_id=1, source_target_pairs={{0,16},{4,20},{8,24},{12,28},{16,0},{20,4},{24,8},{28,12},{32,48},... | collective-permute-start | bytes 1966088 | tf_op jit(solution)/shard_map/ppermute | solution.py:178
  96.0 16.1 %all-gather.6.cloned.1.call-done = bf16[1280,1920]{1,0:T(8,128)(2,1)} async-done(((bf16[320,1920]{1,0:T(8,128)(2,1)}), bf16[1280,1920]{1,0:T(8,128)(2,1)}) %all-gather.6.cloned.1.call-update) | async-done | bytes 4915216 | tf_op jit(solution)/shard_map/all_gather | solution.py:26
  112.1 1.9 pad_add_fusion.5
  114.0 3.3 %collective-permute-start.7 = (s32[3]{0:T(128)S(1)}, s32[3]{0:T(128)S(1)}, u32[]{:S(2)}, u32[]{:S(2)}) collective-permute-start(s32[3]{0:T(128)S(1)} %pad_add_fusion.5), channel_id=1, source_target_pairs={{0,8},{4,12},{8,16},{12,20},{16,24},{20,28},{24,32},{28,36},{32,40... | collective-permute-start | bytes 44 | tf_op jit(solution)/shard_map/ppermute | solution.py:20
  117.5 2.8 collective-permute-start.11
  120.3 2.4 gather_fusion.3
  122.6 4.7 %collective-permute-start.2 = (bf16[3,128,1280]{2,1,0:T(8,128)(2,1)S(1)}, bf16[3,128,1280]{2,1,0:T(8,128)(2,1)S(1)}, u32[]{:S(2)}, u32[]{:S(2)}) collective-permute-start(bf16[3,128,1280]{2,1,0:T(8,128)(2,1)S(1)} %gather_fusion.3), channel_id=1, source_target_pairs={{0,8},{4,12},{8,16},{12,20},{16,24},{20,28},{24,32},{28,36},{32,40... | collective-permute-start | bytes 2949128 | tf_op jit(solution)/shard_map/ppermute | solution.py:20
  127.3 9.3 %collective-permute-done.11 = bf16[2,128,1280]{2,1,0:T(8,128)(2,1)S(1)} collective-permute-done((bf16[2,128,1280]{2,1,0:T(8,128)(2,1)S(1)}, bf16[2,128,1280]{2,1,0:T(8,128)(2,1)S(1)}, u32[]{:S(2)}, u32[]{:S(2)}) %collective-permute-start.11) | collective-permute-done | bytes 655392 | tf_op jit(solution)/shard_map/ppermute | solution.py:178
  136.6 0.9 copy-done.7
  137.5 1.2 broadcast_select_fusion.4
  138.7 0.8 collective-permute-start.12
  139.5 3.4 %gather_fusion.4 = bf16[3,128,1280]{2,1,0:T(8,128)(2,1)} fusion(bf16[8,128,1280]{2,1,0:T(8,128)(2,1)} %bitcast.111, s32[1024]{0:T(1024)S(1)} %pad_clamp_fusion.3), kind=kCustom, calls=%fused_computation.4 | custom fusion | bytes 1966092 | tf_op jit(solution)/shard_map/gather | solution.py:185
  143.0 1.9 collective-permute-start.4
  144.9 3.4 %gather_fusion.5 = bf16[3,128,1280]{2,1,0:T(8,128)(2,1)} fusion(bf16[8,128,1280]{2,1,0:T(8,128)(2,1)} %bitcast.112, s32[1024]{0:T(1024)S(1)} %pad_clamp_fusion.2), kind=kCustom, calls=%fused_computation.5 | custom fusion | bytes 1966092 | tf_op jit(solution)/shard_map/gather | solution.py:185
  148.2 3.6 %collective-permute-start.6 = (bf16[3,128,1280]{2,1,0:T(8,128)(2,1)}, bf16[3,128,1280]{2,1,0:T(8,128)(2,1)}, u32[]{:S(2)}, u32[]{:S(2)}) collective-permute-start(bf16[3,128,1280]{2,1,0:T(8,128)(2,1)} %gather_fusion.5), channel_id=1, source_target_pairs={{4,0},{8,4},{12,8},{16,12},{20,16},{24,20},{28,24},{32,28},{36,32}... | collective-permute-start | bytes 2949128 | tf_op jit(solution)/shard_map/ppermute | solution.py:20
  151.9 3.3 %gather_fusion.6 = bf16[3,128,1280]{2,1,0:T(8,128)(2,1)} fusion(bf16[8,128,1280]{2,1,0:T(8,128)(2,1)} %bitcast.113, s32[1024]{0:T(1024)S(1)} %pad_clamp_fusion.1), kind=kCustom, calls=%fused_computation.6 | custom fusion | bytes 1966092 | tf_op jit(solution)/shard_map/gather | solution.py:185
  155.2 2.1 constant_dynamic-update-slice_fusion.4
  157.3 2.5 collective-permute-start.8
  159.9 10.6 %collective-permute-done.12 = bf16[2,128,1280]{2,1,0:T(8,128)(2,1)S(1)} collective-permute-done((bf16[2,128,1280]{2,1,0:T(8,128)(2,1)S(1)}, bf16[2,128,1280]{2,1,0:T(8,128)(2,1)S(1)}, u32[]{:S(2)}, u32[]{:S(2)}) %collective-permute-start.12) | collective-permute-done | bytes 655392 | tf_op jit(solution)/shard_map/ppermute | solution.py:178
  170.5 0.8 copy-done.6
  171.3 1.3 broadcast_select_fusion.5
  172.9 1.3 constant_dynamic-update-slice_fusion.2
  174.2 1.3 constant_dynamic-update-slice_fusion.1
  175.5 12.4 %collective-permute-done.8 = bf16[3,128,1280]{2,1,0:T(8,128)(2,1)S(1)} collective-permute-done((bf16[3,128,1280]{2,1,0:T(8,128)(2,1)}, bf16[3,128,1280]{2,1,0:T(8,128)(2,1)S(1)}, u32[]{:S(2)}, u32[]{:S(2)}) %collective-permute-start.8) | collective-permute-done | bytes 983072 | tf_op jit(solution)/shard_map/ppermute | solution.py:20
  188.3 2.9 copy-done.5
  191.1 7.1 %broadcast_select_fusion = (bf16[1280,1920]{1,0:T(8,128)(2,1)}, bf16[1280,1920]{1,0:T(8,128)(2,1)}) fusion(bf16[1280,1920]{1,0:T(8,128)(2,1)} %collective-permute-done, bf16[1280,1920]{1,0:T(8,128)(2,1)S(1)} %bitcast.117, pred[]{:T(512)S(6)} %eq.161), kind=kLoop, calls=%fused_computation.11 | loop fusion | flops 4915200 | bytes 19660800 | tf_op jit(solution)/shard_map/jit(_where)/select_n | solution.py:32
  198.3 3.9 %fusion.3 = bf16[256,1280]{1,0:T(8,128)(2,1)} fusion(bf16[256,1280]{1,0:T(8,128)(2,1)S(1)} %copy-done.4, bf16[1280,1920]{1,0:T(8,128)(2,1)} %get-tuple-element.32), kind=kOutput, calls=%fused_computation.15 | convolution fusion | flops 839188480 | bytes 4587520 | tf_op jit(solution)/shard_map/dot_general | solution.py:194
  202.2 23.6 %convolution_convert_fusion = bf16[2816,2560]{1,0:T(8,128)(2,1)} fusion(bf16[2816,1280]{1,0:T(8,128)(2,1)} %bitcast.118, bf16[1280,1920]{1,0:T(8,128)(2,1)S(1)} %copy-done.3, bf16[1280,1920]{1,0:T(8,128)(2,1)} %get-tuple-element.32), kind=kOutput, calls=%fused_computation.8 | convolution fusion | flops 18475253760 | bytes 31457280 | tf_op jit(solution)/shard_map/dot_general | solution.py:190
  225.8 55.1 %shard_map.109 = bf16[2,128,1280]{2,1,0:T(8,128)(2,1)} custom-call(s32[2,18]{1,0:T(2,128)} %pad_add_fusion.1.slots_ref, s32[2]{0:T(128)} %counts_ref.1, bf16[2,128,1280]{2,1,0:T(8,128)(2,1)} %bitcast.119, bf16[22,128,2560]{2,1,0:T(8,128)(2,1)} %bitcast.115), custom_call_target="tpu_custom_call" | custom-call | tf_op jit(solution)/shard_map/pallas_call | solution.py:127
  280.9 4.0 %convolution_convert_fusion.1 = bf16[256,1280]{1,0:T(8,128)(2,1)} fusion(bf16[256,1280]{1,0:T(8,128)(2,1)} %bitcast.120, bf16[1280,1280]{1,0:T(8,128)(2,1)} %all-gather.8.cloned.1.call-done), kind=kOutput, calls=%fused_computation.16 | convolution fusion | flops 839188480 | bytes 4587520 | tf_op jit(solution)/shard_map/dot_general | solution.py:215
  (92 shorter events, 6.9 us)
Async XLA Ops:
  6.5 49.5 %copy-start = (bf16[320,3840]{1,0:T(8,128)(2,1)S(1)}, bf16[320,3840]{1,0:T(8,128)(2,1)}, u32[]{:S(2)}) copy-start(bf16[320,3840]{1,0:T(8,128)(2,1)} %param.20) | copy-start | bytes 7372804
  6.5 6.4 %copy-start.2 = (bf16[256,1280]{1,0:T(8,128)(2,1)S(1)}, bf16[256,1280]{1,0:T(8,128)(2,1)}, u32[]{:S(2)}) copy-start(bf16[256,1280]{1,0:T(8,128)(2,1)} %param.16) | copy-start | bytes 1966084
  6.5 49.5 %all-gather.4.cloned.1.call-start = ((), (), s32[]{:S(2)}) async-start(), calls=%async_computation | async-start | bytes 3276800 | tf_op jit(solution)/shard_map/all_gather | solution.py:161
  15.0 42.2 %copy-start.8 = (s32[2,16]{1,0:T(2,128)S(1)}, s32[2,16]{1,0:T(2,128)}, u32[]{:S(2)}) copy-start(s32[2,16]{1,0:T(2,128)} %param.13) | copy-start | bytes 388
  15.0 59.7 %copy-start.9 = (s32[2]{0:T(128)S(1)}, s32[2]{0:T(128)}, u32[]{:S(2)}) copy-start(s32[2]{0:T(128)} %param.15) | copy-start | bytes 28
  18.4 93.7 %all-gather.6.cloned.1.call-start = ((), (), s32[]{:S(2)}) async-start(), calls=%async_computation.1 | async-start | bytes 6144000 | tf_op jit(solution)/shard_map/all_gather | solution.py:26
  57.2 223.7 %all-gather.8.cloned.1.call-start = ((), (), s32[]{:S(2)}) async-start(), calls=%async_computation.2 | async-start | bytes 4096000 | tf_op jit(solution)/shard_map/all_gather | solution.py:217
  60.3 53.6 %collective-permute-start.1 = (s32[3]{0:T(128)S(1)}, s32[3]{0:T(128)S(1)}, u32[]{:S(2)}, u32[]{:S(2)}) collective-permute-start(s32[3]{0:T(128)S(1)} %pad_add_fusion.2), channel_id=1, source_target_pairs={{8,0},{12,4},{16,8},{20,12},{24,16},{28,20},{32,24},{36,28},{40,32... | collective-permute-start | bytes 44 | tf_op jit(solution)/shard_map/ppermute | solution.py:20
  65.7 51.5 %collective-permute-start.3 = (s32[3]{0:T(128)S(1)}, s32[3]{0:T(128)S(1)}, u32[]{:S(2)}, u32[]{:S(2)}) collective-permute-start(s32[3]{0:T(128)S(1)} %pad_add_fusion.3), channel_id=1, source_target_pairs={{4,0},{8,4},{12,8},{16,12},{20,16},{24,20},{28,24},{32,28},{36,32}... | collective-permute-start | bytes 44 | tf_op jit(solution)/shard_map/ppermute | solution.py:20
  70.4 49.9 %collective-permute-start.5 = (s32[3]{0:T(128)S(1)}, s32[3]{0:T(128)S(1)}, u32[]{:S(2)}, u32[]{:S(2)}) collective-permute-start(s32[3]{0:T(128)S(1)} %pad_add_fusion.4), channel_id=1, source_target_pairs={{0,4},{4,8},{8,12},{12,16},{16,20},{20,24},{24,28},{28,32},{32,36}... | collective-permute-start | bytes 44 | tf_op jit(solution)/shard_map/ppermute | solution.py:20
  77.1 15.7 %collective-permute-start.9 = (bf16[2,128,1280]{2,1,0:T(8,128)(2,1)S(1)}, bf16[2,128,1280]{2,1,0:T(8,128)(2,1)S(1)}, u32[]{:S(2)}, u32[]{:S(2)}) collective-permute-start(bf16[2,128,1280]{2,1,0:T(8,128)(2,1)S(1)} %gather_fusion.7), channel_id=1, source_target_pairs={{0,8},{4,12},{8,0},{12,4},{16,24},{20,28},{24,16},{28,20},{32,40},... | collective-permute-start | bytes 1966088 | tf_op jit(solution)/shard_map/ppermute | solution.py:178
  93.0 24.3 %collective-permute-start.10 = (bf16[2,128,1280]{2,1,0:T(8,128)(2,1)S(1)}, bf16[2,128,1280]{2,1,0:T(8,128)(2,1)S(1)}, u32[]{:S(2)}, u32[]{:S(2)}) collective-permute-start(bf16[2,128,1280]{2,1,0:T(8,128)(2,1)S(1)} %broadcast_select_fusion.2), channel_id=1, source_target_pairs={{0,16},{4,20},{8,24},{12,28},{16,0},{20,4},{24,8},{28,12},{32,48},... | collective-permute-start | bytes 1966088 | tf_op jit(solution)/shard_map/ppermute | solution.py:178
  112.1 79.0 %collective-permute-start = (bf16[1280,1920]{1,0:T(8,128)(2,1)}, bf16[1280,1920]{1,0:T(8,128)(2,1)}, u32[]{:S(2)}, u32[]{:S(2)}) collective-permute-start(bf16[1280,1920]{1,0:T(8,128)(2,1)} %all-gather.6.cloned.1.call-done), channel_id=1, source_target_pairs={{0,4},{4,0},{8,12},{12,8},{16,20},{20,16},{24,28},{28,24},{32,36},... | collective-permute-start | bytes 14745608 | tf_op jit(solution)/shard_map/ppermute | solution.py:30
  114.0 6.3 %collective-permute-start.7 = (s32[3]{0:T(128)S(1)}, s32[3]{0:T(128)S(1)}, u32[]{:S(2)}, u32[]{:S(2)}) collective-permute-start(s32[3]{0:T(128)S(1)} %pad_add_fusion.5), channel_id=1, source_target_pairs={{0,8},{4,12},{8,16},{12,20},{16,24},{20,28},{24,32},{28,36},{32,40... | collective-permute-start | bytes 44 | tf_op jit(solution)/shard_map/ppermute | solution.py:20
  117.5 19.2 %collective-permute-start.11 = (bf16[2,128,1280]{2,1,0:T(8,128)(2,1)S(1)}, bf16[2,128,1280]{2,1,0:T(8,128)(2,1)S(1)}, u32[]{:S(2)}, u32[]{:S(2)}) collective-permute-start(bf16[2,128,1280]{2,1,0:T(8,128)(2,1)S(1)} %broadcast_select_fusion.3), channel_id=1, source_target_pairs={{0,64},{4,68},{8,72},{12,76},{16,80},{20,84},{24,88},{28,92},{32,9... | collective-permute-start | bytes 1966088 | tf_op jit(solution)/shard_map/ppermute | solution.py:178
  122.6 34.7 %collective-permute-start.2 = (bf16[3,128,1280]{2,1,0:T(8,128)(2,1)S(1)}, bf16[3,128,1280]{2,1,0:T(8,128)(2,1)S(1)}, u32[]{:S(2)}, u32[]{:S(2)}) collective-permute-start(bf16[3,128,1280]{2,1,0:T(8,128)(2,1)S(1)} %gather_fusion.3), channel_id=1, source_target_pairs={{0,8},{4,12},{8,16},{12,20},{16,24},{20,28},{24,32},{28,36},{32,40... | collective-permute-start | bytes 2949128 | tf_op jit(solution)/shard_map/ppermute | solution.py:20
  136.6 0.9 copy-start.7
  138.7 31.8 %collective-permute-start.12 = (bf16[2,128,1280]{2,1,0:T(8,128)(2,1)S(1)}, bf16[2,128,1280]{2,1,0:T(8,128)(2,1)S(1)}, u32[]{:S(2)}, u32[]{:S(2)}) collective-permute-start(bf16[2,128,1280]{2,1,0:T(8,128)(2,1)S(1)} %broadcast_select_fusion.4), channel_id=1, source_target_pairs={{0,32},{4,36},{8,40},{12,44},{16,48},{20,52},{24,56},{28,60},{32,0... | collective-permute-start | bytes 1966088 | tf_op jit(solution)/shard_map/ppermute | solution.py:178
  143.0 29.9 %collective-permute-start.4 = (bf16[3,128,1280]{2,1,0:T(8,128)(2,1)}, bf16[3,128,1280]{2,1,0:T(8,128)(2,1)}, u32[]{:S(2)}, u32[]{:S(2)}) collective-permute-start(bf16[3,128,1280]{2,1,0:T(8,128)(2,1)} %gather_fusion.4), channel_id=1, source_target_pairs={{0,4},{4,8},{8,12},{12,16},{16,20},{20,24},{24,28},{28,32},{32,36}... | collective-permute-start | bytes 2949128 | tf_op jit(solution)/shard_map/ppermute | solution.py:20
  148.2 25.9 %collective-permute-start.6 = (bf16[3,128,1280]{2,1,0:T(8,128)(2,1)}, bf16[3,128,1280]{2,1,0:T(8,128)(2,1)}, u32[]{:S(2)}, u32[]{:S(2)}) collective-permute-start(bf16[3,128,1280]{2,1,0:T(8,128)(2,1)} %gather_fusion.5), channel_id=1, source_target_pairs={{4,0},{8,4},{12,8},{16,12},{20,16},{24,20},{28,24},{32,28},{36,32}... | collective-permute-start | bytes 2949128 | tf_op jit(solution)/shard_map/ppermute | solution.py:20
  155.2 35.9 %slice-start = ((s8[4915200]{0:T(1024)(128)(4,1)}), s8[4194304]{0:T(1024)(128)(4,1)S(1)}, s32[]{:S(2)}) async-start(s8[4915200]{0:T(1024)(128)(4,1)} %bitcast.116), calls=%async_computation.3 | async-start | bytes 8388608
  157.3 30.6 %collective-permute-start.8 = (bf16[3,128,1280]{2,1,0:T(8,128)(2,1)}, bf16[3,128,1280]{2,1,0:T(8,128)(2,1)S(1)}, u32[]{:S(2)}, u32[]{:S(2)}) collective-permute-start(bf16[3,128,1280]{2,1,0:T(8,128)(2,1)} %gather_fusion.6), channel_id=1, source_target_pairs={{8,0},{12,4},{16,8},{20,12},{24,16},{28,20},{32,24},{36,28},{40,32... | collective-permute-start | bytes 2949128 | tf_op jit(solution)/shard_map/ppermute | solution.py:20
  170.5 0.8 copy-start.6
  171.3 19.8 %slice-start.1 = ((s8[4915200]{0:T(1024)(128)(4,1)}), s8[720896]{0:T(1024)(128)(4,1)S(1)}, s32[]{:S(2)}) async-start(s8[4915200]{0:T(1024)(128)(4,1)} %bitcast.116), calls=%async_computation.4 | async-start | bytes 1441792
  172.6 15.3 %collective-permute-start.13 = (bf16[2,128,1280]{2,1,0:T(8,128)(2,1)S(1)}, bf16[2,128,1280]{2,1,0:T(8,128)(2,1)S(1)}, u32[]{:S(2)}, u32[]{:S(2)}) collective-permute-start(bf16[2,128,1280]{2,1,0:T(8,128)(2,1)S(1)} %broadcast_select_fusion.5), channel_id=1, source_target_pairs={{0,4},{4,0},{8,12},{12,8},{16,20},{20,16},{24,28},{28,24},{32,36},... | collective-permute-start | bytes 1966088 | tf_op jit(solution)/shard_map/ppermute | solution.py:178
  188.2 2.9 copy-start.5
  191.1 7.2 %copy-start.4 = (bf16[256,1280]{1,0:T(8,128)(2,1)S(1)}, bf16[256,1280]{1,0:T(8,128)(2,1)}, u32[]{:S(2)}) copy-start(bf16[256,1280]{1,0:T(8,128)(2,1)} %fusion.11) | copy-start | bytes 1966084
  198.3 3.9 %copy-start.3 = (bf16[1280,1920]{1,0:T(8,128)(2,1)S(1)}, bf16[1280,1920]{1,0:T(8,128)(2,1)}, u32[]{:S(2)}) copy-start(bf16[1280,1920]{1,0:T(8,128)(2,1)} %get-tuple-element.31) | copy-start | bytes 14745604
  225.8 59.1 %copy-start.1 = (bf16[320,3840]{1,0:T(8,128)(2,1)S(1)}, bf16[320,3840]{1,0:T(8,128)(2,1)}, u32[]{:S(2)}) copy-start(bf16[320,3840]{1,0:T(8,128)(2,1)} %param.20) | copy-start | bytes 7372804
Sparse Core Ops, SparseCore 0:
  18.6 37.4 all-gather.3
  57.7 54.3 all-gather.5
  113.8 41.0 all-gather.7

commit v11 on v10

--- a/solution.py
+++ b/solution.py
@@ -179,11 +179,14 @@
         global_rows = jnp.where(held[:, None, None], global_rows, got)
     near_blocks = []
     near_rank = []
+    asked = []
     for reach in REACH:
         picks, rank = near_tiles(kv_list, seq_at + reach, group_tiles)
-        asked = passed_along(picks, "seq", reach)
-        near_blocks.append(passed_along(group_rows[asked], "seq", -reach))
+        asked.append(passed_along(picks, "seq", reach))
         near_rank.append(rank)
+    asked, group_rows = lax.optimization_barrier((asked, group_rows))
+    for reach, ids in zip(REACH, asked):
+        near_blocks.append(passed_along(group_rows[ids], "seq", -reach))
     window_rows = jnp.concatenate(
         [group_rows] + near_blocks + [global_rows], axis=0
     )

time: 292 us -> 301 us (1.031); the launches traced: 291 us -> 297 us
  waiting for transfers between devices: 101 us -> 110 us
  Pallas kernels: 55.1 us -> 50.6 us
  starting transfers between devices: 30.6 us -> 34.7 us
    ppermute x5, waiting for transfers between devices: 34.4 us -> 46.4 us  [local(): lax.ppermute(global_rows, 'seq', [(i, i ^ step) for i in range(seq_size)])]
    pallas_call x1, Pallas kernels: 55.1 us -> 50.6 us  [attend(): pl.pallas_call(attention_kernel, grid_spec=grid_spec, out_shape=jax.Shape...]
    ppermute x5, starting transfers between devices: 7.43 us -> 11.2 us  [local(): lax.ppermute(global_rows, 'seq', [(i, i ^ step) for i in range(seq_size)])]
    unnamed x29 -> x25, local copies, waits for them, and re-layouts: 9.33 us -> 7.63 us
  transfers between devices with their start and end apart: 17 -> 17, of which waited for: 6 -> 7; matrix products, arithmetic and copies ran while one was open for 24% -> 23% of each run, Pallas kernels for 19% -> 17%
where the time goes in v11:
time: 301 us; the launch traced here: 297 us
  waiting for transfers between devices  110 us (37%)
  Pallas kernels  50.6 us (17%)
  starting transfers between devices  34.7 us (12%)
  local copies, waits for them, and re-layouts  31.8 us (11%)
  matrix products  31.6 us (10%)
  other arithmetic  25.4 us (8%)
  between operations  13.5 us (4%)
    pallas_call x1, Pallas kernels, attend(): pl.pallas_call(attention_kernel, grid_spec=grid_spec, out_shape=jax.Shape...  50.6 us
    ppermute x5, waiting for transfers between devices, local(): lax.ppermute(global_rows, 'seq', [(i, i ^ step) for i in range(seq_size)])  46.4 us
    all_gather x1, waiting for transfers between devices, local(): lax.all_gather(normed, 'fsdp', axis=0, tiled=True)  37.5 us
    dot_general x1, matrix products, local(): jnp.dot(window_rows.reshape(-1, feat_width), w_full[:, feat_width:], pref...  23.6 us
    ppermute x8, starting transfers between devices, passed_along(): return lax.ppermute(block, axis, route)  23.4 us
    all_gather x1, waiting for transfers between devices, gathered_weight(): lax.all_gather(lax.dynamic_slice_in_dim(shard, core * half, half, 1), 'fs...  16.1 us
    gather x4, local copies, waits for them, and re-layouts, local(): near_blocks.append(passed_along(group_rows[ids], 'seq', -reach))  13.5 us
    ppermute x5, starting transfers between devices, local(): lax.ppermute(global_rows, 'seq', [(i, i ^ step) for i in range(seq_size)])  11.2 us
  transfers between devices with their start and end apart: 17, of which 7 were waited for; matrix products, arithmetic and copies ran while one was open for 23% of the time, Pallas kernels for 17%

profile of v11, /device:TPU:24, one launch (start us, length us, event | category | flops | bytes accessed | tf_op | source)
XLA Modules:
  0.0 297.2 jit_solution(15409652585609649569)
XLA Ops:
  6.5 0.8 compare_select_fusion.1
  7.4 0.8 convert_element_type.99
  8.2 0.7 convert_element_type.98
  8.9 4.1 %gather_fusion.2 = bf16[256,1280]{1,0:T(8,128)(2,1)} fusion(bf16[512,1280]{1,0:T(8,128)(2,1)} %param.17, s32[1024]{0:T(1024)S(1)} %get-tuple-element.53), kind=kCustom, calls=%fused_computation.2 | custom fusion | bytes 1311744 | tf_op jit(solution)/shard_map/gather | solution.py:51
  13.0 2.1 gather_fusion.1
  15.0 1.9 convert_reduce_fusion
  17.2 1.2 fusion.11
  18.5 37.5 %all-gather.4.cloned.1.call-done = bf16[1024,1280]{1,0:T(8,128)(2,1)} async-done(((bf16[256,1280]{1,0:T(8,128)(2,1)}), bf16[1024,1280]{1,0:T(8,128)(2,1)}) %all-gather.4.cloned.1.call-update) | async-done | bytes 2621456 | tf_op jit(solution)/shard_map/all_gather | solution.py:161
  56.0 1.2 constant_dynamic-slice_fusion
  57.8 0.7 fusion.31
  58.5 1.8 pad_add_fusion.2
  60.3 2.7 collective-permute-start.1
  63.2 0.7 fusion.34
  63.9 1.8 pad_add_fusion.3
  65.7 1.9 collective-permute-start.2
  67.9 0.7 fusion.37
  68.5 1.8 pad_add_fusion.4
  70.4 2.4 collective-permute-start.3
  73.8 0.8 gather_fusion
  74.8 2.3 gather_fusion.7
  78.4 14.5 %collective-permute-done.9 = bf16[2,128,1280]{2,1,0:T(8,128)(2,1)S(1)} collective-permute-done((bf16[2,128,1280]{2,1,0:T(8,128)(2,1)S(1)}, bf16[2,128,1280]{2,1,0:T(8,128)(2,1)S(1)}, u32[]{:S(2)}, u32[]{:S(2)}) %collective-permute-start.9) | collective-permute-done | bytes 655392 | tf_op jit(solution)/shard_map/ppermute | solution.py:178
  93.0 3.0 collective-permute-start.10
  96.0 16.1 %all-gather.6.cloned.1.call-done = bf16[1280,1920]{1,0:T(8,128)(2,1)} async-done(((bf16[320,1920]{1,0:T(8,128)(2,1)}), bf16[1280,1920]{1,0:T(8,128)(2,1)}) %all-gather.6.cloned.1.call-update) | async-done | bytes 4915216 | tf_op jit(solution)/shard_map/all_gather | solution.py:26
  112.1 1.9 pad_add_fusion.5
  114.0 3.3 %collective-permute-start.4 = (s32[3]{0:T(128)S(1)}, s32[3]{0:T(128)S(1)}, u32[]{:S(2)}, u32[]{:S(2)}) collective-permute-start(s32[3]{0:T(128)S(1)} %pad_add_fusion.5), channel_id=1, source_target_pairs={{0,8},{4,12},{8,16},{12,20},{16,24},{20,28},{24,32},{28,36},{32,40... | collective-permute-start | bytes 44 | tf_op jit(solution)/shard_map/ppermute | solution.py:20
  117.3 2.1 collective-permute-done.4
  119.4 3.4 %gather_fusion.3 = bf16[3,128,1280]{2,1,0:T(8,128)(2,1)} fusion(bf16[8,128,1280]{2,1,0:T(8,128)(2,1)} %bitcast.110, s32[1024]{0:T(1024)S(1)} %pad_clamp_fusion.4), kind=kCustom, calls=%fused_computation.3 | custom fusion | bytes 1966092 | tf_op jit(solution)/shard_map/gather | solution.py:189
  122.8 5.5 %collective-permute-start.5 = (bf16[3,128,1280]{2,1,0:T(8,128)(2,1)}, bf16[3,128,1280]{2,1,0:T(8,128)(2,1)S(1)}, u32[]{:S(2)}, u32[]{:S(2)}) collective-permute-start(bf16[3,128,1280]{2,1,0:T(8,128)(2,1)} %gather_fusion.3), channel_id=1, source_target_pairs={{0,8},{4,12},{8,16},{12,20},{16,24},{20,28},{24,32},{28,36},{32,40... | collective-permute-start | bytes 2949128 | tf_op jit(solution)/shard_map/ppermute | solution.py:20
  128.5 2.8 collective-permute-start.11
  131.3 3.4 %gather_fusion.4 = bf16[3,128,1280]{2,1,0:T(8,128)(2,1)} fusion(bf16[8,128,1280]{2,1,0:T(8,128)(2,1)} %bitcast.111, s32[1024]{0:T(1024)S(1)} %pad_clamp_fusion.3), kind=kCustom, calls=%fused_computation.4 | custom fusion | bytes 1966092 | tf_op jit(solution)/shard_map/gather | solution.py:189
  134.7 1.9 collective-permute-start.6
  136.6 3.3 %gather_fusion.5 = bf16[3,128,1280]{2,1,0:T(8,128)(2,1)} fusion(bf16[8,128,1280]{2,1,0:T(8,128)(2,1)} %bitcast.112, s32[1024]{0:T(1024)S(1)} %pad_clamp_fusion.2), kind=kCustom, calls=%fused_computation.5 | custom fusion | bytes 1966092 | tf_op jit(solution)/shard_map/gather | solution.py:189
  140.0 3.6 %collective-permute-start.7 = (bf16[3,128,1280]{2,1,0:T(8,128)(2,1)}, bf16[3,128,1280]{2,1,0:T(8,128)(2,1)}, u32[]{:S(2)}, u32[]{:S(2)}) collective-permute-start(bf16[3,128,1280]{2,1,0:T(8,128)(2,1)} %gather_fusion.5), channel_id=1, source_target_pairs={{4,0},{8,4},{12,8},{16,12},{20,16},{24,20},{28,24},{32,28},{36,32}... | collective-permute-start | bytes 2949128 | tf_op jit(solution)/shard_map/ppermute | solution.py:20
  143.6 24.3 %collective-permute-done.11 = bf16[2,128,1280]{2,1,0:T(8,128)(2,1)S(1)} collective-permute-done((bf16[2,128,1280]{2,1,0:T(8,128)(2,1)S(1)}, bf16[2,128,1280]{2,1,0:T(8,128)(2,1)S(1)}, u32[]{:S(2)}, u32[]{:S(2)}) %collective-permute-start.11) | collective-permute-done | bytes 655392 | tf_op jit(solution)/shard_map/ppermute | solution.py:178
  168.1 3.3 %gather_fusion.6 = bf16[3,128,1280]{2,1,0:T(8,128)(2,1)} fusion(bf16[8,128,1280]{2,1,0:T(8,128)(2,1)} %bitcast.113, s32[1024]{0:T(1024)S(1)} %pad_clamp_fusion.1), kind=kCustom, calls=%fused_computation.6 | custom fusion | bytes 1966092 | tf_op jit(solution)/shard_map/gather | solution.py:189
  171.5 2.1 constant_dynamic-update-slice_fusion.4
  173.5 1.9 collective-permute-start.8
  175.5 7.7 %collective-permute-done.12 = bf16[2,128,1280]{2,1,0:T(8,128)(2,1)S(1)} collective-permute-done((bf16[2,128,1280]{2,1,0:T(8,128)(2,1)S(1)}, bf16[2,128,1280]{2,1,0:T(8,128)(2,1)S(1)}, u32[]{:S(2)}, u32[]{:S(2)}) %collective-permute-start.12) | collective-permute-done | bytes 655392 | tf_op jit(solution)/shard_map/ppermute | solution.py:178
  183.4 4.8 %collective-permute-start.13 = (bf16[2,128,1280]{2,1,0:T(8,128)(2,1)S(1)}, bf16[2,128,1280]{2,1,0:T(8,128)(2,1)S(1)}, u32[]{:S(2)}, u32[]{:S(2)}) collective-permute-start(bf16[2,128,1280]{2,1,0:T(8,128)(2,1)S(1)} %broadcast_select_fusion.5), channel_id=1, source_target_pairs={{0,4},{4,0},{8,12},{12,8},{16,20},{20,16},{24,28},{28,24},{32,36},... | collective-permute-start | bytes 1966088 | tf_op jit(solution)/shard_map/ppermute | solution.py:178
  188.1 1.3 constant_dynamic-update-slice_fusion.2
  189.4 1.3 constant_dynamic-update-slice_fusion.1
  190.7 7.3 %collective-permute-done.8 = bf16[3,128,1280]{2,1,0:T(8,128)(2,1)S(1)} collective-permute-done((bf16[3,128,1280]{2,1,0:T(8,128)(2,1)}, bf16[3,128,1280]{2,1,0:T(8,128)(2,1)S(1)}, u32[]{:S(2)}, u32[]{:S(2)}) %collective-permute-start.8) | collective-permute-done | bytes 983072 | tf_op jit(solution)/shard_map/ppermute | solution.py:20
  198.4 2.9 copy-done.5
  201.3 7.1 %broadcast_select_fusion = (bf16[1280,1920]{1,0:T(8,128)(2,1)}, bf16[1280,1920]{1,0:T(8,128)(2,1)}) fusion(bf16[1280,1920]{1,0:T(8,128)(2,1)} %collective-permute-done, bf16[1280,1920]{1,0:T(8,128)(2,1)S(1)} %bitcast.117, pred[]{:T(512)S(6)} %eq.161), kind=kLoop, calls=%fused_computation.11 | loop fusion | flops 4915200 | bytes 19660800 | tf_op jit(solution)/shard_map/jit(_where)/select_n | solution.py:32
  208.5 3.9 %fusion.3 = bf16[256,1280]{1,0:T(8,128)(2,1)} fusion(bf16[256,1280]{1,0:T(8,128)(2,1)S(1)} %copy-done.4, bf16[1280,1920]{1,0:T(8,128)(2,1)} %get-tuple-element.42), kind=kOutput, calls=%fused_computation.15 | convolution fusion | flops 839188480 | bytes 4587520 | tf_op jit(solution)/shard_map/dot_general | solution.py:197
  212.4 23.6 %convolution_convert_fusion = bf16[2816,2560]{1,0:T(8,128)(2,1)} fusion(bf16[2816,1280]{1,0:T(8,128)(2,1)} %bitcast.118, bf16[1280,1920]{1,0:T(8,128)(2,1)S(1)} %copy-done.3, bf16[1280,1920]{1,0:T(8,128)(2,1)} %get-tuple-element.42), kind=kOutput, calls=%fused_computation.8 | convolution fusion | flops 18475253760 | bytes 31457280 | tf_op jit(solution)/shard_map/dot_general | solution.py:193
  236.0 50.6 %shard_map.109 = bf16[2,128,1280]{2,1,0:T(8,128)(2,1)} custom-call(s32[2,18]{1,0:T(2,128)} %pad_add_fusion.1.slots_ref, s32[2]{0:T(128)} %counts_ref.1, bf16[2,128,1280]{2,1,0:T(8,128)(2,1)} %bitcast.119, bf16[22,128,2560]{2,1,0:T(8,128)(2,1)} %bitcast.115), custom_call_target="tpu_custom_call" | custom-call | tf_op jit(solution)/shard_map/pallas_call | solution.py:127
  286.6 4.0 %convolution_convert_fusion.1 = bf16[256,1280]{1,0:T(8,128)(2,1)} fusion(bf16[256,1280]{1,0:T(8,128)(2,1)} %bitcast.120, bf16[1280,1280]{1,0:T(8,128)(2,1)} %all-gather.8.cloned.1.call-done), kind=kOutput, calls=%fused_computation.16 | convolution fusion | flops 839188480 | bytes 4587520 | tf_op jit(solution)/shard_map/dot_general | solution.py:218
  (88 shorter events, 4.9 us)
Async XLA Ops:
  6.5 49.5 %copy-start = (bf16[320,3840]{1,0:T(8,128)(2,1)S(1)}, bf16[320,3840]{1,0:T(8,128)(2,1)}, u32[]{:S(2)}) copy-start(bf16[320,3840]{1,0:T(8,128)(2,1)} %param.20) | copy-start | bytes 7372804
  6.5 6.4 %copy-start.2 = (bf16[256,1280]{1,0:T(8,128)(2,1)S(1)}, bf16[256,1280]{1,0:T(8,128)(2,1)}, u32[]{:S(2)}) copy-start(bf16[256,1280]{1,0:T(8,128)(2,1)} %param.16) | copy-start | bytes 1966084
  6.5 49.5 %all-gather.4.cloned.1.call-start = ((), (), s32[]{:S(2)}) async-start(), calls=%async_computation | async-start | bytes 3276800 | tf_op jit(solution)/shard_map/all_gather | solution.py:161
  15.0 42.2 %copy-start.6 = (s32[2,16]{1,0:T(2,128)S(1)}, s32[2,16]{1,0:T(2,128)}, u32[]{:S(2)}) copy-start(s32[2,16]{1,0:T(2,128)} %param.13) | copy-start | bytes 388
  15.0 59.7 %copy-start.7 = (s32[2]{0:T(128)S(1)}, s32[2]{0:T(128)}, u32[]{:S(2)}) copy-start(s32[2]{0:T(128)} %param.15) | copy-start | bytes 28
  18.4 93.7 %all-gather.6.cloned.1.call-start = ((), (), s32[]{:S(2)}) async-start(), calls=%async_computation.1 | async-start | bytes 6144000 | tf_op jit(solution)/shard_map/all_gather | solution.py:26
  57.2 229.4 %all-gather.8.cloned.1.call-start = ((), (), s32[]{:S(2)}) async-start(), calls=%async_computation.2 | async-start | bytes 4096000 | tf_op jit(solution)/shard_map/all_gather | solution.py:220
  60.3 53.6 %collective-permute-start.1 = (s32[3]{0:T(128)S(1)}, s32[3]{0:T(128)S(1)}, u32[]{:S(2)}, u32[]{:S(2)}) collective-permute-start(s32[3]{0:T(128)S(1)} %pad_add_fusion.2), channel_id=1, source_target_pairs={{8,0},{12,4},{16,8},{20,12},{24,16},{28,20},{32,24},{36,28},{40,32... | collective-permute-start | bytes 44 | tf_op jit(solution)/shard_map/ppermute | solution.py:20
  65.7 51.5 %collective-permute-start.2 = (s32[3]{0:T(128)S(1)}, s32[3]{0:T(128)S(1)}, u32[]{:S(2)}, u32[]{:S(2)}) collective-permute-start(s32[3]{0:T(128)S(1)} %pad_add_fusion.3), channel_id=1, source_target_pairs={{4,0},{8,4},{12,8},{16,12},{20,16},{24,20},{28,24},{32,28},{36,32}... | collective-permute-start | bytes 44 | tf_op jit(solution)/shard_map/ppermute | solution.py:20
  70.4 46.9 %collective-permute-start.3 = (s32[3]{0:T(128)S(1)}, s32[3]{0:T(128)S(1)}, u32[]{:S(2)}, u32[]{:S(2)}) collective-permute-start(s32[3]{0:T(128)S(1)} %pad_add_fusion.4), channel_id=1, source_target_pairs={{0,4},{4,8},{8,12},{12,16},{16,20},{20,24},{24,28},{28,32},{32,36}... | collective-permute-start | bytes 44 | tf_op jit(solution)/shard_map/ppermute | solution.py:20
  77.1 15.7 %collective-permute-start.9 = (bf16[2,128,1280]{2,1,0:T(8,128)(2,1)S(1)}, bf16[2,128,1280]{2,1,0:T(8,128)(2,1)S(1)}, u32[]{:S(2)}, u32[]{:S(2)}) collective-permute-start(bf16[2,128,1280]{2,1,0:T(8,128)(2,1)S(1)} %gather_fusion.7), channel_id=1, source_target_pairs={{0,8},{4,12},{8,0},{12,4},{16,24},{20,28},{24,16},{28,20},{32,40},... | collective-permute-start | bytes 1966088 | tf_op jit(solution)/shard_map/ppermute | solution.py:178
  93.0 35.4 %collective-permute-start.10 = (bf16[2,128,1280]{2,1,0:T(8,128)(2,1)S(1)}, bf16[2,128,1280]{2,1,0:T(8,128)(2,1)S(1)}, u32[]{:S(2)}, u32[]{:S(2)}) collective-permute-start(bf16[2,128,1280]{2,1,0:T(8,128)(2,1)S(1)} %broadcast_select_fusion.2), channel_id=1, source_target_pairs={{0,16},{4,20},{8,24},{12,28},{16,0},{20,4},{24,8},{28,12},{32,48},... | collective-permute-start | bytes 1966088 | tf_op jit(solution)/shard_map/ppermute | solution.py:178
  112.1 89.2 %collective-permute-start = (bf16[1280,1920]{1,0:T(8,128)(2,1)}, bf16[1280,1920]{1,0:T(8,128)(2,1)}, u32[]{:S(2)}, u32[]{:S(2)}) collective-permute-start(bf16[1280,1920]{1,0:T(8,128)(2,1)} %all-gather.6.cloned.1.call-done), channel_id=1, source_target_pairs={{0,4},{4,0},{8,12},{12,8},{16,20},{20,16},{24,28},{28,24},{32,36},... | collective-permute-start | bytes 14745608 | tf_op jit(solution)/shard_map/ppermute | solution.py:30
  114.0 5.5 %collective-permute-start.4 = (s32[3]{0:T(128)S(1)}, s32[3]{0:T(128)S(1)}, u32[]{:S(2)}, u32[]{:S(2)}) collective-permute-start(s32[3]{0:T(128)S(1)} %pad_add_fusion.5), channel_id=1, source_target_pairs={{0,8},{4,12},{8,16},{12,20},{16,24},{20,28},{24,32},{28,36},{32,40... | collective-permute-start | bytes 44 | tf_op jit(solution)/shard_map/ppermute | solution.py:20
  122.8 50.7 %collective-permute-start.5 = (bf16[3,128,1280]{2,1,0:T(8,128)(2,1)}, bf16[3,128,1280]{2,1,0:T(8,128)(2,1)S(1)}, u32[]{:S(2)}, u32[]{:S(2)}) collective-permute-start(bf16[3,128,1280]{2,1,0:T(8,128)(2,1)} %gather_fusion.3), channel_id=1, source_target_pairs={{0,8},{4,12},{8,16},{12,20},{16,24},{20,28},{24,32},{28,36},{32,40... | collective-permute-start | bytes 2949128 | tf_op jit(solution)/shard_map/ppermute | solution.py:20
  128.5 39.4 %collective-permute-start.11 = (bf16[2,128,1280]{2,1,0:T(8,128)(2,1)S(1)}, bf16[2,128,1280]{2,1,0:T(8,128)(2,1)S(1)}, u32[]{:S(2)}, u32[]{:S(2)}) collective-permute-start(bf16[2,128,1280]{2,1,0:T(8,128)(2,1)S(1)} %broadcast_select_fusion.3), channel_id=1, source_target_pairs={{0,64},{4,68},{8,72},{12,76},{16,80},{20,84},{24,88},{28,92},{32,9... | collective-permute-start | bytes 1966088 | tf_op jit(solution)/shard_map/ppermute | solution.py:178
  134.7 53.4 %collective-permute-start.6 = (bf16[3,128,1280]{2,1,0:T(8,128)(2,1)}, bf16[3,128,1280]{2,1,0:T(8,128)(2,1)}, u32[]{:S(2)}, u32[]{:S(2)}) collective-permute-start(bf16[3,128,1280]{2,1,0:T(8,128)(2,1)} %gather_fusion.4), channel_id=1, source_target_pairs={{0,4},{4,8},{8,12},{12,16},{16,20},{20,24},{24,28},{28,32},{32,36}... | collective-permute-start | bytes 2949128 | tf_op jit(solution)/shard_map/ppermute | solution.py:20
  140.0 49.4 %collective-permute-start.7 = (bf16[3,128,1280]{2,1,0:T(8,128)(2,1)}, bf16[3,128,1280]{2,1,0:T(8,128)(2,1)}, u32[]{:S(2)}, u32[]{:S(2)}) collective-permute-start(bf16[3,128,1280]{2,1,0:T(8,128)(2,1)} %gather_fusion.5), channel_id=1, source_target_pairs={{4,0},{8,4},{12,8},{16,12},{20,16},{24,20},{28,24},{32,28},{36,32}... | collective-permute-start | bytes 2949128 | tf_op jit(solution)/shard_map/ppermute | solution.py:20
  168.0 15.2 %collective-permute-start.12 = (bf16[2,128,1280]{2,1,0:T(8,128)(2,1)S(1)}, bf16[2,128,1280]{2,1,0:T(8,128)(2,1)S(1)}, u32[]{:S(2)}, u32[]{:S(2)}) collective-permute-start(bf16[2,128,1280]{2,1,0:T(8,128)(2,1)S(1)} %broadcast_select_fusion.4), channel_id=1, source_target_pairs={{0,32},{4,36},{8,40},{12,44},{16,48},{20,52},{24,56},{28,60},{32,0... | collective-permute-start | bytes 1966088 | tf_op jit(solution)/shard_map/ppermute | solution.py:178
  171.5 29.8 %slice-start = ((s8[4915200]{0:T(1024)(128)(4,1)}), s8[4194304]{0:T(1024)(128)(4,1)S(1)}, s32[]{:S(2)}) async-start(s8[4915200]{0:T(1024)(128)(4,1)} %bitcast.116), calls=%async_computation.3 | async-start | bytes 8388608
  173.5 24.5 %collective-permute-start.8 = (bf16[3,128,1280]{2,1,0:T(8,128)(2,1)}, bf16[3,128,1280]{2,1,0:T(8,128)(2,1)S(1)}, u32[]{:S(2)}, u32[]{:S(2)}) collective-permute-start(bf16[3,128,1280]{2,1,0:T(8,128)(2,1)} %gather_fusion.6), channel_id=1, source_target_pairs={{8,0},{12,4},{16,8},{20,12},{24,16},{28,20},{32,24},{36,28},{40,32... | collective-permute-start | bytes 2949128 | tf_op jit(solution)/shard_map/ppermute | solution.py:20
  183.2 18.1 %slice-start.1 = ((s8[4915200]{0:T(1024)(128)(4,1)}), s8[720896]{0:T(1024)(128)(4,1)S(1)}, s32[]{:S(2)}) async-start(s8[4915200]{0:T(1024)(128)(4,1)} %bitcast.116), calls=%async_computation.4 | async-start | bytes 1441792
  183.4 14.7 %collective-permute-start.13 = (bf16[2,128,1280]{2,1,0:T(8,128)(2,1)S(1)}, bf16[2,128,1280]{2,1,0:T(8,128)(2,1)S(1)}, u32[]{:S(2)}, u32[]{:S(2)}) collective-permute-start(bf16[2,128,1280]{2,1,0:T(8,128)(2,1)S(1)} %broadcast_select_fusion.5), channel_id=1, source_target_pairs={{0,4},{4,0},{8,12},{12,8},{16,20},{20,16},{24,28},{28,24},{32,36},... | collective-permute-start | bytes 1966088 | tf_op jit(solution)/shard_map/ppermute | solution.py:178
  198.4 2.9 copy-start.5
  201.3 7.2 %copy-start.4 = (bf16[256,1280]{1,0:T(8,128)(2,1)S(1)}, bf16[256,1280]{1,0:T(8,128)(2,1)}, u32[]{:S(2)}) copy-start(bf16[256,1280]{1,0:T(8,128)(2,1)} %fusion.11) | copy-start | bytes 1966084
  208.4 3.9 %copy-start.3 = (bf16[1280,1920]{1,0:T(8,128)(2,1)S(1)}, bf16[1280,1920]{1,0:T(8,128)(2,1)}, u32[]{:S(2)}) copy-start(bf16[1280,1920]{1,0:T(8,128)(2,1)} %get-tuple-element.41) | copy-start | bytes 14745604
  236.0 54.6 %copy-start.1 = (bf16[320,3840]{1,0:T(8,128)(2,1)S(1)}, bf16[320,3840]{1,0:T(8,128)(2,1)}, u32[]{:S(2)}) copy-start(bf16[320,3840]{1,0:T(8,128)(2,1)} %param.20) | copy-start | bytes 7372804
Sparse Core Ops, SparseCore 0:
  18.6 37.4 all-gather.3
  57.7 54.3 all-gather.5
  113.8 41.0 all-gather.7

commit v12 on v10

--- a/solution.py
+++ b/solution.py
@@ -171,7 +171,9 @@
     bit_order = [b for b in (1, 2) if b < seq_bits]
     bit_order += [b for b in range(seq_bits - 1, -1, -1) if b not in bit_order]
     done_bits = 0
-    for bit in bit_order:
+    for stage, bit in enumerate(bit_order):
+        if stage == 3:
+            w_full, global_rows = lax.optimization_barrier((w_full, global_rows))
         step = 1 << bit
         held = ((seq_at ^ owners) & ~done_bits & (seq_size - 1)) == 0
         done_bits |= step

time: 292 us -> 328 us (1.12)
  waiting for transfers between devices: 101 us -> 130 us
  other arithmetic: 27.6 us -> 34.3 us
    all_gather x1, waiting for transfers between devices: 16.1 us -> 39.1 us  [gathered_weight(): lax.all_gather(lax.dynamic_slice_in_dim(shard, core * half, half, 1), 'fs...]
    concatenate x0 -> x1, other arithmetic: none -> 7.06 us  [gathered_weight(): return jnp.concatenate([low, high], axis=1)]
    ppermute x5, starting transfers between devices: 7.43 us -> 13.8 us  [local(): lax.ppermute(global_rows, 'seq', [(i, i ^ step) for i in range(seq_size)])]
    ppermute x5, waiting for transfers between devices: 34.4 us -> 40.7 us  [local(): lax.ppermute(global_rows, 'seq', [(i, i ^ step) for i in range(seq_size)])]
    ppermute x8, starting transfers between devices: 23.1 us -> 19.3 us  [passed_along(): return lax.ppermute(block, axis, route)]
    unnamed x29 -> x21, local copies, waits for them, and re-layouts: 9.33 us -> 9.87 us
  transfers between devices with their start and end apart: 17 -> 17, of which waited for: 6 -> 7; matrix products, arithmetic and copies ran while one was open for 24% -> 24% of each run, Pallas kernels for 19% -> 17%
where the time goes in v12:
time: 328 us; the launch traced here: 327 us
  waiting for transfers between devices  130 us (40%)
  Pallas kernels  54.2 us (17%)
  other arithmetic  34.3 us (10%)
  starting transfers between devices  33.2 us (10%)
  local copies, waits for them, and re-layouts  32.1 us (10%)
  matrix products  29 us (9%)
  between operations  13.4 us (4%)
    pallas_call x1, Pallas kernels, attend(): pl.pallas_call(attention_kernel, grid_spec=grid_spec, out_shape=jax.Shape...  54.2 us
    ppermute x5, waiting for transfers between devices, local(): lax.ppermute(global_rows, 'seq', [(i, i ^ step) for i in range(seq_size)])  40.7 us
    all_gather x1, waiting for transfers between devices, gathered_weight(): lax.all_gather(lax.dynamic_slice_in_dim(shard, core * half, half, 1), 'fs...  39.1 us
    all_gather x1, waiting for transfers between devices, local(): lax.all_gather(normed, 'fsdp', axis=0, tiled=True)  37.5 us
    dot_general x1, matrix products, local(): jnp.dot(window_rows.reshape(-1, feat_width), w_full[:, feat_width:], pref...  23.2 us
    ppermute x8, starting transfers between devices, passed_along(): return lax.ppermute(block, axis, route)  19.3 us
    ppermute x5, starting transfers between devices, local(): lax.ppermute(global_rows, 'seq', [(i, i ^ step) for i in range(seq_size)])  13.8 us
    ppermute x8, waiting for transfers between devices, passed_along(): return lax.ppermute(block, axis, route)  12.9 us
  transfers between devices with their start and end apart: 17, of which 7 were waited for; matrix products, arithmetic and copies ran while one was open for 24% of the time, Pallas kernels for 17%

profile of v12, /device:TPU:24, one launch (start us, length us, event | category | flops | bytes accessed | tf_op | source)
XLA Modules:
  0.0 326.6 jit_solution(14682872978033626267)
XLA Ops:
  6.5 0.8 compare_select_fusion.1
  7.4 0.8 convert_element_type.99
  8.9 4.1 %gather_fusion.2 = bf16[256,1280]{1,0:T(8,128)(2,1)} fusion(bf16[512,1280]{1,0:T(8,128)(2,1)} %param.17, s32[1024]{0:T(1024)S(1)} %get-tuple-element.47), kind=kCustom, calls=%fused_computation.2 | custom fusion | bytes 1311744 | tf_op jit(solution)/shard_map/gather | solution.py:51
  13.0 2.1 gather_fusion.1
  15.0 1.9 convert_reduce_fusion
  17.2 1.2 fusion.11
  18.5 37.5 %all-gather.4.cloned.1.call-done = bf16[1024,1280]{1,0:T(8,128)(2,1)} async-done(((bf16[256,1280]{1,0:T(8,128)(2,1)}), bf16[1024,1280]{1,0:T(8,128)(2,1)}) %all-gather.4.cloned.1.call-update) | async-done | bytes 2621456 | tf_op jit(solution)/shard_map/all_gather | solution.py:161
  56.0 1.2 constant_dynamic-slice_fusion
  58.5 1.8 pad_add_fusion.2
  60.3 2.7 collective-permute-start.4
  63.9 1.8 pad_add_fusion.3
  65.7 1.9 collective-permute-start.6
  68.5 1.8 pad_add_fusion.4
  70.4 2.4 collective-permute-start.8
  73.0 39.1 %all-gather.6.cloned.1.call-done = bf16[1280,1920]{1,0:T(8,128)(2,1)} async-done(((bf16[320,1920]{1,0:T(8,128)(2,1)}), bf16[1280,1920]{1,0:T(8,128)(2,1)}) %all-gather.6.cloned.1.call-update) | async-done | bytes 4915216 | tf_op jit(solution)/shard_map/all_gather | solution.py:26
  113.8 1.9 pad_add_fusion.5
  115.8 2.3 gather_fusion.3
  118.1 0.9 collective-permute-start.1
  119.6 15.7 %collective-permute-done.1 = bf16[2,128,1280]{2,1,0:T(8,128)(2,1)S(1)} collective-permute-done((bf16[2,128,1280]{2,1,0:T(8,128)(2,1)S(1)}, bf16[2,128,1280]{2,1,0:T(8,128)(2,1)S(1)}, u32[]{:S(2)}, u32[]{:S(2)}) %collective-permute-start.1) | collective-permute-done | bytes 655392 | tf_op jit(solution)/shard_map/ppermute | solution.py:180
  135.3 3.3 %collective-permute-start.10 = (s32[3]{0:T(128)S(1)}, s32[3]{0:T(128)S(1)}, u32[]{:S(2)}, u32[]{:S(2)}) collective-permute-start(s32[3]{0:T(128)S(1)} %pad_add_fusion.5), channel_id=1, source_target_pairs={{0,8},{4,12},{8,16},{12,20},{16,24},{20,28},{24,32},{28,36},{32,40... | collective-permute-start | bytes 44 | tf_op jit(solution)/shard_map/ppermute | solution.py:20
  138.8 1.6 collective-permute-start.2
  140.4 16.1 %collective-permute-done.2 = bf16[2,128,1280]{2,1,0:T(8,128)(2,1)S(1)} collective-permute-done((bf16[2,128,1280]{2,1,0:T(8,128)(2,1)S(1)}, bf16[2,128,1280]{2,1,0:T(8,128)(2,1)S(1)}, u32[]{:S(2)}, u32[]{:S(2)}) %collective-permute-start.2) | collective-permute-done | bytes 655392 | tf_op jit(solution)/shard_map/ppermute | solution.py:180
  156.6 2.8 collective-permute-start.3
  159.4 3.4 %gather_fusion.4 = bf16[3,128,1280]{2,1,0:T(8,128)(2,1)} fusion(bf16[8,128,1280]{2,1,0:T(8,128)(2,1)} %bitcast.110, s32[1024]{0:T(1024)S(1)} %pad_clamp_fusion.3), kind=kCustom, calls=%fused_computation.4 | custom fusion | bytes 1966092 | tf_op jit(solution)/shard_map/gather | solution.py:187
  162.8 2.8 collective-permute-start.5
  165.6 2.4 gather_fusion.5
  168.0 1.9 collective-permute-start.7
  169.9 5.9 %collective-permute-done.3 = bf16[2,128,1280]{2,1,0:T(8,128)(2,1)S(1)} collective-permute-done((bf16[2,128,1280]{2,1,0:T(8,128)(2,1)S(1)}, bf16[2,128,1280]{2,1,0:T(8,128)(2,1)S(1)}, u32[]{:S(2)}, u32[]{:S(2)}) %collective-permute-start.3) | collective-permute-done | bytes 655392 | tf_op jit(solution)/shard_map/ppermute | solution.py:180
  176.0 7.0 %broadcast_select_fusion.1 = (bf16[1280,1920]{1,0:T(8,128)(2,1)S(1)}, bf16[1280,1920]{1,0:T(8,128)(2,1)}) fusion(bf16[1280,1920]{1,0:T(8,128)(2,1)} %all-gather.6.cloned.1.call-done, bf16[1280,1920]{1,0:T(8,128)(2,1)} %collective-permute-done, pred[]{:T(512)S(6)} %eq.161), kind=kLoop, calls=%fused_computation.12 | loop fusion | flops 4915200 | bytes 19660800 | tf_op jit(solution)/shard_map/jit(_where)/select_n | solution.py:31
  183.0 7.1 %pad_maximum_fusion = bf16[1280,3840]{1,0:T(8,128)(2,1)} fusion(bf16[1280,1920]{1,0:T(8,128)(2,1)} %get-tuple-element.36, bf16[1280,1920]{1,0:T(8,128)(2,1)S(1)} %get-tuple-element.35), kind=kLoop, calls=%fused_computation.9 | loop fusion | flops 19660800 | bytes 19660800 | tf_op jit(solution)/shard_map/concatenate | solution.py:33
  190.1 1.6 constant_dynamic-update-slice_fusion.4
  191.7 3.3 %gather_fusion.6 = bf16[3,128,1280]{2,1,0:T(8,128)(2,1)} fusion(bf16[8,128,1280]{2,1,0:T(8,128)(2,1)} %bitcast.112, s32[1024]{0:T(1024)S(1)} %pad_clamp_fusion.1), kind=kCustom, calls=%fused_computation.6 | custom fusion | bytes 1966092 | tf_op jit(solution)/shard_map/gather | solution.py:187
  195.0 1.9 collective-permute-start.9
  197.0 2.4 gather_fusion.7
  199.4 2.3 collective-permute-start.11
  201.7 2.7 constant_dynamic-update-slice_fusion.3
  204.4 2.3 constant_dynamic-update-slice_fusion.2
  206.7 3.0 collective-permute-done.12
  209.7 1.2 broadcast_select_fusion.2
  210.9 8.6 %collective-permute-start.13 = (bf16[2,128,1280]{2,1,0:T(8,128)(2,1)S(1)}, bf16[2,128,1280]{2,1,0:T(8,128)(2,1)S(1)}, u32[]{:S(2)}, u32[]{:S(2)}) collective-permute-start(bf16[2,128,1280]{2,1,0:T(8,128)(2,1)S(1)} %broadcast_select_fusion.2), channel_id=1, source_target_pairs={{0,4},{4,0},{8,12},{12,8},{16,20},{20,16},{24,28},{28,24},{32,36},... | collective-permute-start | bytes 1966088 | tf_op jit(solution)/shard_map/ppermute | solution.py:180
  219.5 2.2 constant_dynamic-update-slice_fusion.1
  221.7 12.9 %collective-permute-done.11 = bf16[3,128,1280]{2,1,0:T(8,128)(2,1)S(1)} collective-permute-done((bf16[3,128,1280]{2,1,0:T(8,128)(2,1)S(1)}, bf16[3,128,1280]{2,1,0:T(8,128)(2,1)S(1)}, u32[]{:S(2)}, u32[]{:S(2)}) %collective-permute-start.11) | collective-permute-done | bytes 983072 | tf_op jit(solution)/shard_map/ppermute | solution.py:20
  234.6 1.0 constant_dynamic-update-slice_fusion
  235.7 1.9 fusion.3
  237.5 1.1 select_dynamic-update-slice_fusion
  238.7 23.2 %convolution_convert_fusion = bf16[2816,2560]{1,0:T(8,128)(2,1)} fusion(bf16[2816,1280]{1,0:T(8,128)(2,1)} %bitcast.116, bf16[1280,3840]{1,0:T(8,128)(2,1)S(1)} %copy-done.4), kind=kOutput, calls=%fused_computation.8 | convolution fusion | flops 18462146560 | bytes 28180480 | tf_op jit(solution)/shard_map/dot_general | solution.py:192
  261.8 54.2 %shard_map.109 = bf16[2,128,1280]{2,1,0:T(8,128)(2,1)} custom-call(s32[2,18]{1,0:T(2,128)} %pad_add_fusion.1.slots_ref, s32[2]{0:T(128)} %counts_ref.1, bf16[2,128,1280]{2,1,0:T(8,128)(2,1)} %bitcast.117, bf16[22,128,2560]{2,1,0:T(8,128)(2,1)} %bitcast.115), custom_call_target="tpu_custom_call" | custom-call | tf_op jit(solution)/shard_map/pallas_call | solution.py:127
  316.1 4.0 %convolution_convert_fusion.1 = bf16[256,1280]{1,0:T(8,128)(2,1)} fusion(bf16[256,1280]{1,0:T(8,128)(2,1)} %bitcast.118, bf16[1280,1280]{1,0:T(8,128)(2,1)} %all-gather.8.cloned.1.call-done), kind=kOutput, calls=%fused_computation.16 | convolution fusion | flops 839188480 | bytes 4587520 | tf_op jit(solution)/shard_map/dot_general | solution.py:217
  (84 shorter events, 7.2 us)
Async XLA Ops:
  6.5 49.5 %copy-start = (bf16[320,3840]{1,0:T(8,128)(2,1)S(1)}, bf16[320,3840]{1,0:T(8,128)(2,1)}, u32[]{:S(2)}) copy-start(bf16[320,3840]{1,0:T(8,128)(2,1)} %param.20) | copy-start | bytes 7372804
  6.5 6.4 %copy-start.2 = (bf16[256,1280]{1,0:T(8,128)(2,1)S(1)}, bf16[256,1280]{1,0:T(8,128)(2,1)}, u32[]{:S(2)}) copy-start(bf16[256,1280]{1,0:T(8,128)(2,1)} %param.16) | copy-start | bytes 1966084
  6.5 49.5 %all-gather.4.cloned.1.call-start = ((), (), s32[]{:S(2)}) async-start(), calls=%async_computation | async-start | bytes 3276800 | tf_op jit(solution)/shard_map/all_gather | solution.py:161
  15.0 42.2 %copy-start.6 = (s32[2,16]{1,0:T(2,128)S(1)}, s32[2,16]{1,0:T(2,128)}, u32[]{:S(2)}) copy-start(s32[2,16]{1,0:T(2,128)} %param.13) | copy-start | bytes 388
  15.0 100.7 %copy-start.7 = (s32[2]{0:T(128)S(1)}, s32[2]{0:T(128)}, u32[]{:S(2)}) copy-start(s32[2]{0:T(128)} %param.15) | copy-start | bytes 28
  18.4 93.7 %all-gather.6.cloned.1.call-start = ((), (), s32[]{:S(2)}) async-start(), calls=%async_computation.1 | async-start | bytes 6144000 | tf_op jit(solution)/shard_map/all_gather | solution.py:26
  57.2 258.8 %all-gather.8.cloned.1.call-start = ((), (), s32[]{:S(2)}) async-start(), calls=%async_computation.2 | async-start | bytes 4096000 | tf_op jit(solution)/shard_map/all_gather | solution.py:219
  60.3 78.5 %collective-permute-start.4 = (s32[3]{0:T(128)S(1)}, s32[3]{0:T(128)S(1)}, u32[]{:S(2)}, u32[]{:S(2)}) collective-permute-start(s32[3]{0:T(128)S(1)} %pad_add_fusion.2), channel_id=1, source_target_pairs={{8,0},{12,4},{16,8},{20,12},{24,16},{28,20},{32,24},{36,28},{40,32... | collective-permute-start | bytes 44 | tf_op jit(solution)/shard_map/ppermute | solution.py:20
  65.7 74.6 %collective-permute-start.6 = (s32[3]{0:T(128)S(1)}, s32[3]{0:T(128)S(1)}, u32[]{:S(2)}, u32[]{:S(2)}) collective-permute-start(s32[3]{0:T(128)S(1)} %pad_add_fusion.3), channel_id=1, source_target_pairs={{4,0},{8,4},{12,8},{16,12},{20,16},{24,20},{28,24},{32,28},{36,32}... | collective-permute-start | bytes 44 | tf_op jit(solution)/shard_map/ppermute | solution.py:20
  70.4 89.0 %collective-permute-start.8 = (s32[3]{0:T(128)S(1)}, s32[3]{0:T(128)S(1)}, u32[]{:S(2)}, u32[]{:S(2)}) collective-permute-start(s32[3]{0:T(128)S(1)} %pad_add_fusion.4), channel_id=1, source_target_pairs={{0,4},{4,8},{8,12},{12,16},{16,20},{20,24},{24,28},{28,32},{32,36}... | collective-permute-start | bytes 44 | tf_op jit(solution)/shard_map/ppermute | solution.py:20
  112.1 63.9 %collective-permute-start = (bf16[1280,1920]{1,0:T(8,128)(2,1)}, bf16[1280,1920]{1,0:T(8,128)(2,1)}, u32[]{:S(2)}, u32[]{:S(2)}) collective-permute-start(bf16[1280,1920]{1,0:T(8,128)(2,1)} %all-gather.6.cloned.1.call-done), channel_id=1, source_target_pairs={{0,4},{4,0},{8,12},{12,8},{16,20},{20,16},{24,28},{28,24},{32,36},... | collective-permute-start | bytes 14745608 | tf_op jit(solution)/shard_map/ppermute | solution.py:30
  118.1 17.2 %collective-permute-start.1 = (bf16[2,128,1280]{2,1,0:T(8,128)(2,1)S(1)}, bf16[2,128,1280]{2,1,0:T(8,128)(2,1)S(1)}, u32[]{:S(2)}, u32[]{:S(2)}) collective-permute-start(bf16[2,128,1280]{2,1,0:T(8,128)(2,1)S(1)} %gather_fusion.3), channel_id=1, source_target_pairs={{0,8},{4,12},{8,0},{12,4},{16,24},{20,28},{24,16},{28,20},{32,40},... | collective-permute-start | bytes 1966088 | tf_op jit(solution)/shard_map/ppermute | solution.py:180
  135.3 24.1 %collective-permute-start.10 = (s32[3]{0:T(128)S(1)}, s32[3]{0:T(128)S(1)}, u32[]{:S(2)}, u32[]{:S(2)}) collective-permute-start(s32[3]{0:T(128)S(1)} %pad_add_fusion.5), channel_id=1, source_target_pairs={{0,8},{4,12},{8,16},{12,20},{16,24},{20,28},{24,32},{28,36},{32,40... | collective-permute-start | bytes 44 | tf_op jit(solution)/shard_map/ppermute | solution.py:20
  138.8 17.7 %collective-permute-start.2 = (bf16[2,128,1280]{2,1,0:T(8,128)(2,1)S(1)}, bf16[2,128,1280]{2,1,0:T(8,128)(2,1)S(1)}, u32[]{:S(2)}, u32[]{:S(2)}) collective-permute-start(bf16[2,128,1280]{2,1,0:T(8,128)(2,1)S(1)} %broadcast_select_fusion.3), channel_id=1, source_target_pairs={{0,16},{4,20},{8,24},{12,28},{16,0},{20,4},{24,8},{28,12},{32,48},... | collective-permute-start | bytes 1966088 | tf_op jit(solution)/shard_map/ppermute | solution.py:180
  156.6 19.2 %collective-permute-start.3 = (bf16[2,128,1280]{2,1,0:T(8,128)(2,1)S(1)}, bf16[2,128,1280]{2,1,0:T(8,128)(2,1)S(1)}, u32[]{:S(2)}, u32[]{:S(2)}) collective-permute-start(bf16[2,128,1280]{2,1,0:T(8,128)(2,1)S(1)} %broadcast_select_fusion.4), channel_id=1, source_target_pairs={{0,64},{4,68},{8,72},{12,76},{16,80},{20,84},{24,88},{28,92},{32,9... | collective-permute-start | bytes 1966088 | tf_op jit(solution)/shard_map/ppermute | solution.py:180
  162.8 38.9 %collective-permute-start.5 = (bf16[3,128,1280]{2,1,0:T(8,128)(2,1)}, bf16[3,128,1280]{2,1,0:T(8,128)(2,1)}, u32[]{:S(2)}, u32[]{:S(2)}) collective-permute-start(bf16[3,128,1280]{2,1,0:T(8,128)(2,1)} %gather_fusion.4), channel_id=1, source_target_pairs={{0,8},{4,12},{8,16},{12,20},{16,24},{20,28},{24,32},{28,36},{32,40... | collective-permute-start | bytes 2949128 | tf_op jit(solution)/shard_map/ppermute | solution.py:20
  168.0 36.4 %collective-permute-start.7 = (bf16[3,128,1280]{2,1,0:T(8,128)(2,1)S(1)}, bf16[3,128,1280]{2,1,0:T(8,128)(2,1)}, u32[]{:S(2)}, u32[]{:S(2)}) collective-permute-start(bf16[3,128,1280]{2,1,0:T(8,128)(2,1)S(1)} %gather_fusion.5), channel_id=1, source_target_pairs={{0,4},{4,8},{8,12},{12,16},{16,20},{20,24},{24,28},{28,32},{32,36}... | collective-permute-start | bytes 2949128 | tf_op jit(solution)/shard_map/ppermute | solution.py:20
  183.0 7.1 %copy-start.3 = (bf16[1024,1280]{1,0:T(8,128)(2,1)S(1)}, bf16[1024,1280]{1,0:T(8,128)(2,1)}, u32[]{:S(2)}) copy-start(bf16[1024,1280]{1,0:T(8,128)(2,1)} %all-gather.4.cloned.1.call-done) | copy-start | bytes 7864324
  190.1 19.6 %collective-permute-start.12 = (bf16[2,128,1280]{2,1,0:T(8,128)(2,1)S(1)}, bf16[2,128,1280]{2,1,0:T(8,128)(2,1)}, u32[]{:S(2)}, u32[]{:S(2)}) collective-permute-start(bf16[2,128,1280]{2,1,0:T(8,128)(2,1)S(1)} %broadcast_select_fusion.5), channel_id=1, source_target_pairs={{0,32},{4,36},{8,40},{12,44},{16,48},{20,52},{24,56},{28,60},{32,0... | collective-permute-start | bytes 1966088 | tf_op jit(solution)/shard_map/ppermute | solution.py:180
  195.0 24.4 %collective-permute-start.9 = (bf16[3,128,1280]{2,1,0:T(8,128)(2,1)}, bf16[3,128,1280]{2,1,0:T(8,128)(2,1)}, u32[]{:S(2)}, u32[]{:S(2)}) collective-permute-start(bf16[3,128,1280]{2,1,0:T(8,128)(2,1)} %gather_fusion.6), channel_id=1, source_target_pairs={{4,0},{8,4},{12,8},{16,12},{20,16},{24,20},{28,24},{32,28},{36,32}... | collective-permute-start | bytes 2949128 | tf_op jit(solution)/shard_map/ppermute | solution.py:20
  197.0 38.7 %copy-start.5 = (bf16[256,1280]{1,0:T(8,128)(2,1)S(1)}, bf16[256,1280]{1,0:T(8,128)(2,1)}, u32[]{:S(2)}) copy-start(bf16[256,1280]{1,0:T(8,128)(2,1)} %fusion.11) | copy-start | bytes 1966084
  199.4 36.3 %copy-start.4 = (bf16[1280,3840]{1,0:T(8,128)(2,1)S(1)}, bf16[1280,3840]{1,0:T(8,128)(2,1)}, u32[]{:S(2)}) copy-start(bf16[1280,3840]{1,0:T(8,128)(2,1)} %pad_maximum_fusion) | copy-start | bytes 29491204
  199.4 35.2 %collective-permute-start.11 = (bf16[3,128,1280]{2,1,0:T(8,128)(2,1)S(1)}, bf16[3,128,1280]{2,1,0:T(8,128)(2,1)S(1)}, u32[]{:S(2)}, u32[]{:S(2)}) collective-permute-start(bf16[3,128,1280]{2,1,0:T(8,128)(2,1)S(1)} %gather_fusion.7), channel_id=1, source_target_pairs={{8,0},{12,4},{16,8},{20,12},{24,16},{28,20},{32,24},{36,28},{40,32... | collective-permute-start | bytes 2949128 | tf_op jit(solution)/shard_map/ppermute | solution.py:20
  210.9 26.6 %collective-permute-start.13 = (bf16[2,128,1280]{2,1,0:T(8,128)(2,1)S(1)}, bf16[2,128,1280]{2,1,0:T(8,128)(2,1)S(1)}, u32[]{:S(2)}, u32[]{:S(2)}) collective-permute-start(bf16[2,128,1280]{2,1,0:T(8,128)(2,1)S(1)} %broadcast_select_fusion.2), channel_id=1, source_target_pairs={{0,4},{4,0},{8,12},{12,8},{16,20},{20,16},{24,28},{28,24},{32,36},... | collective-permute-start | bytes 1966088 | tf_op jit(solution)/shard_map/ppermute | solution.py:180
  261.8 58.2 %copy-start.1 = (bf16[320,3840]{1,0:T(8,128)(2,1)S(1)}, bf16[320,3840]{1,0:T(8,128)(2,1)}, u32[]{:S(2)}) copy-start(bf16[320,3840]{1,0:T(8,128)(2,1)} %param.20) | copy-start | bytes 7372804
Sparse Core Ops, SparseCore 0:
  18.6 37.4 all-gather.3
  57.7 54.3 all-gather.5
  113.8 41.0 all-gather.7

commit v13 on v10

--- a/solution.py
+++ b/solution.py
@@ -67,8 +67,8 @@
     tile_at = pl.program_id(0)
     slot_at = pl.program_id(1)
     slot_count = KT + GLOBAL
-    feat_width = q_ref.shape[-1]
-    head_size = feat_width // HEADS
+    head_size = q_ref.shape[-1]
+    feat_width = head_size * HEADS
     live_count = counts_ref[tile_at]
     live = (slot_at >= KT) | (slot_at < live_count)
     key_at = pl.multiple_of(slot_at * TILE, TILE)
@@ -78,7 +78,7 @@
         for head in range(HEADS):
             cols = slice(head * head_size, (head + 1) * head_size)
             scores = lax.dot_general(
-                q_ref[0, :, cols], kv_ref[0, :, cols], (((1,), (1,)), ((), ())),
+                q_ref[0, head], kv_ref[0, :, cols], (((1,), (1,)), ((), ())),
                 preferred_element_type=jnp.float32,
             )
             s_scr[head, :, pl.ds(key_at, TILE)] = scores * head_size ** (-0.5)
@@ -105,6 +105,8 @@
 def attend(query_tiles, window, slots, counts):
     tile_count, _, feat_width = query_tiles.shape
     slot_count = KT + GLOBAL
+    head_size = feat_width // HEADS
+    query_heads = query_tiles.reshape(tile_count, TILE, HEADS, head_size).transpose(0, 2, 1, 3)
 
     def kv_map(i, j, slots_ref, counts_ref):
         live_count = counts_ref[i]
@@ -115,7 +117,7 @@
         num_scalar_prefetch=2,
         grid=(tile_count, slot_count),
         in_specs=[
-            pl.BlockSpec((1, TILE, feat_width), lambda i, j, s, c: (i, 0, 0)),
+            pl.BlockSpec((1, HEADS, TILE, head_size), lambda i, j, s, c: (i, 0, 0, 0)),
             pl.BlockSpec((1, TILE, 2 * feat_width), kv_map),
         ],
         out_specs=pl.BlockSpec((1, TILE, feat_width), lambda i, j, s, c: (i, 0, 0)),
@@ -131,7 +133,7 @@
         compiler_params=pltpu.CompilerParams(
             dimension_semantics=("arbitrary", "arbitrary"),
         ),
-    )(slots, counts, query_tiles, window)
+    )(slots, counts, query_heads, window)
 
 
 def local(

time: 292 us -> 293 us (level)
  local copies, waits for them, and re-layouts: 32.5 us -> 36.3 us
  Pallas kernels: 55.1 us -> 51.7 us
    pallas_call x1, Pallas kernels: 55.1 us -> 51.7 us  [attend(): pl.pallas_call(attention_kernel, grid_spec=grid_spec, out_shape=jax.Shape...]
  transfers between devices with their start and end apart: 17 -> 17, of which waited for: 6 -> 6; matrix products, arithmetic and copies ran while one was open for 24% -> 25% of each run, Pallas kernels for 19% -> 18%
where the time goes in v13:
time: 293 us; the launch traced here: 291 us
  waiting for transfers between devices  101 us (34%)
  Pallas kernels  51.7 us (18%)
  local copies, waits for them, and re-layouts  36.3 us (12%)
  matrix products  32 us (11%)
  starting transfers between devices  30.6 us (10%)
  other arithmetic  26 us (9%)
  between operations  13.6 us (5%)
    pallas_call x1, Pallas kernels, attend(): pl.pallas_call(attention_kernel, grid_spec=grid_spec, out_shape=jax.Shape...  51.7 us
    all_gather x1, waiting for transfers between devices, local(): lax.all_gather(normed, 'fsdp', axis=0, tiled=True)  37.5 us
    ppermute x5, waiting for transfers between devices, local(): lax.ppermute(global_rows, 'seq', [(i, i ^ step) for i in range(seq_size)])  34.4 us
    dot_general x1, matrix products, local(): jnp.dot(window_rows.reshape(-1, feat_width), w_full[:, feat_width:], pref...  25 us
    ppermute x8, starting transfers between devices, passed_along(): return lax.ppermute(block, axis, route)  23.1 us
    all_gather x1, waiting for transfers between devices, gathered_weight(): lax.all_gather(lax.dynamic_slice_in_dim(shard, core * half, half, 1), 'fs...  16.1 us
    gather x4, local copies, waits for them, and re-layouts, local(): near_blocks.append(passed_along(group_rows[asked], 'seq', -reach))  12.5 us
    ppermute x8, waiting for transfers between devices, passed_along(): return lax.ppermute(block, axis, route)  12.4 us
  transfers between devices with their start and end apart: 17, of which 6 were waited for; matrix products, arithmetic and copies ran while one was open for 25% of the time, Pallas kernels for 18%

profile of v13, /device:TPU:24, one launch (start us, length us, event | category | flops | bytes accessed | tf_op | source)
XLA Modules:
  0.0 290.6 jit_solution(9958461641816396689)
XLA Ops:
  6.5 0.8 compare_select_fusion.1
  7.4 2.9 %gather_fusion.1 = bf16[256,1280]{1,0:T(8,128)(2,1)S(1)} fusion(bf16[256,1280]{1,0:T(8,128)(2,1)} %param.16, s32[1024]{0:T(1024)S(1)} %get-tuple-element.44), kind=kCustom, calls=%fused_computation.1 | custom fusion | bytes 1311744 | tf_op jit(solution)/shard_map/gather | solution.py:50
  10.4 4.1 %gather_fusion.2 = bf16[256,1280]{1,0:T(8,128)(2,1)} fusion(bf16[512,1280]{1,0:T(8,128)(2,1)} %param.17, s32[1024]{0:T(1024)S(1)} %get-tuple-element.43), kind=kCustom, calls=%fused_computation.2 | custom fusion | bytes 1311744 | tf_op jit(solution)/shard_map/gather | solution.py:51
  14.5 1.7 convert_reduce_fusion
  16.5 1.2 fusion.11
  17.8 37.5 %all-gather.4.cloned.1.call-done = bf16[1024,1280]{1,0:T(8,128)(2,1)} async-done(((bf16[256,1280]{1,0:T(8,128)(2,1)}), bf16[1024,1280]{1,0:T(8,128)(2,1)}) %all-gather.4.cloned.1.call-update) | async-done | bytes 2621456 | tf_op jit(solution)/shard_map/all_gather | solution.py:163
  55.3 1.2 constant_dynamic-slice_fusion
  57.8 1.8 pad_add_fusion.2
  59.6 2.7 collective-permute-start.1
  63.2 1.8 pad_add_fusion.3
  65.0 1.9 collective-permute-start.3
  67.8 1.8 pad_add_fusion.4
  69.7 2.4 collective-permute-start.5
  73.2 0.8 gather_fusion
  74.1 2.3 gather_fusion.7
  77.7 14.5 %collective-permute-done.9 = bf16[2,128,1280]{2,1,0:T(8,128)(2,1)S(1)} collective-permute-done((bf16[2,128,1280]{2,1,0:T(8,128)(2,1)S(1)}, bf16[2,128,1280]{2,1,0:T(8,128)(2,1)S(1)}, u32[]{:S(2)}, u32[]{:S(2)}) %collective-permute-start.9) | collective-permute-done | bytes 655392 | tf_op jit(solution)/shard_map/ppermute | solution.py:180
  92.3 3.0 %collective-permute-start.10 = (bf16[2,128,1280]{2,1,0:T(8,128)(2,1)S(1)}, bf16[2,128,1280]{2,1,0:T(8,128)(2,1)S(1)}, u32[]{:S(2)}, u32[]{:S(2)}) collective-permute-start(bf16[2,128,1280]{2,1,0:T(8,128)(2,1)S(1)} %broadcast_select_fusion.2), channel_id=1, source_target_pairs={{0,16},{4,20},{8,24},{12,28},{16,0},{20,4},{24,8},{28,12},{32,48},... | collective-permute-start | bytes 1966088 | tf_op jit(solution)/shard_map/ppermute | solution.py:180
  95.3 16.1 %all-gather.6.cloned.1.call-done = bf16[1280,1920]{1,0:T(8,128)(2,1)} async-done(((bf16[320,1920]{1,0:T(8,128)(2,1)}), bf16[1280,1920]{1,0:T(8,128)(2,1)}) %all-gather.6.cloned.1.call-update) | async-done | bytes 4915216 | tf_op jit(solution)/shard_map/all_gather | solution.py:26
  111.4 1.9 pad_add_fusion.5
  113.3 3.3 %collective-permute-start.7 = (s32[3]{0:T(128)S(1)}, s32[3]{0:T(128)S(1)}, u32[]{:S(2)}, u32[]{:S(2)}) collective-permute-start(s32[3]{0:T(128)S(1)} %pad_add_fusion.5), channel_id=1, source_target_pairs={{0,8},{4,12},{8,16},{12,20},{16,24},{20,28},{24,32},{28,36},{32,40... | collective-permute-start | bytes 44 | tf_op jit(solution)/shard_map/ppermute | solution.py:20
  116.8 2.8 collective-permute-start.11
  119.6 2.4 gather_fusion.3
  121.9 4.7 %collective-permute-start.2 = (bf16[3,128,1280]{2,1,0:T(8,128)(2,1)S(1)}, bf16[3,128,1280]{2,1,0:T(8,128)(2,1)S(1)}, u32[]{:S(2)}, u32[]{:S(2)}) collective-permute-start(bf16[3,128,1280]{2,1,0:T(8,128)(2,1)S(1)} %gather_fusion.3), channel_id=1, source_target_pairs={{0,8},{4,12},{8,16},{12,20},{16,24},{20,28},{24,32},{28,36},{32,40... | collective-permute-start | bytes 2949128 | tf_op jit(solution)/shard_map/ppermute | solution.py:20
  126.7 9.3 %collective-permute-done.11 = bf16[2,128,1280]{2,1,0:T(8,128)(2,1)S(1)} collective-permute-done((bf16[2,128,1280]{2,1,0:T(8,128)(2,1)S(1)}, bf16[2,128,1280]{2,1,0:T(8,128)(2,1)S(1)}, u32[]{:S(2)}, u32[]{:S(2)}) %collective-permute-start.11) | collective-permute-done | bytes 655392 | tf_op jit(solution)/shard_map/ppermute | solution.py:180
  136.0 0.9 copy-done.5
  136.8 1.2 broadcast_select_fusion.4
  138.0 0.8 collective-permute-start.12
  138.9 3.4 %gather_fusion.4 = bf16[3,128,1280]{2,1,0:T(8,128)(2,1)} fusion(bf16[8,128,1280]{2,1,0:T(8,128)(2,1)} %bitcast.113, s32[1024]{0:T(1024)S(1)} %pad_clamp_fusion.3), kind=kCustom, calls=%fused_computation.4 | custom fusion | bytes 1966092 | tf_op jit(solution)/shard_map/gather | solution.py:187
  142.3 1.9 collective-permute-start.4
  144.2 3.4 %gather_fusion.5 = bf16[3,128,1280]{2,1,0:T(8,128)(2,1)} fusion(bf16[8,128,1280]{2,1,0:T(8,128)(2,1)} %bitcast.114, s32[1024]{0:T(1024)S(1)} %pad_clamp_fusion.2), kind=kCustom, calls=%fused_computation.5 | custom fusion | bytes 1966092 | tf_op jit(solution)/shard_map/gather | solution.py:187
  147.6 3.6 %collective-permute-start.6 = (bf16[3,128,1280]{2,1,0:T(8,128)(2,1)}, bf16[3,128,1280]{2,1,0:T(8,128)(2,1)}, u32[]{:S(2)}, u32[]{:S(2)}) collective-permute-start(bf16[3,128,1280]{2,1,0:T(8,128)(2,1)} %gather_fusion.5), channel_id=1, source_target_pairs={{4,0},{8,4},{12,8},{16,12},{20,16},{24,20},{28,24},{32,28},{36,32}... | collective-permute-start | bytes 2949128 | tf_op jit(solution)/shard_map/ppermute | solution.py:20
  151.2 3.3 %gather_fusion.6 = bf16[3,128,1280]{2,1,0:T(8,128)(2,1)} fusion(bf16[8,128,1280]{2,1,0:T(8,128)(2,1)} %bitcast.115, s32[1024]{0:T(1024)S(1)} %pad_clamp_fusion.1), kind=kCustom, calls=%fused_computation.6 | custom fusion | bytes 1966092 | tf_op jit(solution)/shard_map/gather | solution.py:187
  154.5 2.1 constant_dynamic-update-slice_fusion.4
  156.6 2.5 collective-permute-start.8
  159.2 10.6 %collective-permute-done.12 = bf16[2,128,1280]{2,1,0:T(8,128)(2,1)S(1)} collective-permute-done((bf16[2,128,1280]{2,1,0:T(8,128)(2,1)S(1)}, bf16[2,128,1280]{2,1,0:T(8,128)(2,1)S(1)}, u32[]{:S(2)}, u32[]{:S(2)}) %collective-permute-start.12) | collective-permute-done | bytes 655392 | tf_op jit(solution)/shard_map/ppermute | solution.py:180
  169.8 0.8 copy-done.4
  170.7 1.3 broadcast_select_fusion.5
  172.2 1.3 constant_dynamic-update-slice_fusion.2
  173.5 1.3 constant_dynamic-update-slice_fusion.1
  174.8 12.4 %collective-permute-done.8 = bf16[3,128,1280]{2,1,0:T(8,128)(2,1)S(1)} collective-permute-done((bf16[3,128,1280]{2,1,0:T(8,128)(2,1)}, bf16[3,128,1280]{2,1,0:T(8,128)(2,1)S(1)}, u32[]{:S(2)}, u32[]{:S(2)}) %collective-permute-start.8) | collective-permute-done | bytes 983072 | tf_op jit(solution)/shard_map/ppermute | solution.py:20
  187.6 2.9 copy-done.3
  190.5 7.1 %broadcast_select_fusion = (bf16[1280,1920]{1,0:T(8,128)(2,1)}, bf16[1280,1920]{1,0:T(8,128)(2,1)}) fusion(bf16[1280,1920]{1,0:T(8,128)(2,1)} %collective-permute-done, bf16[1280,1920]{1,0:T(8,128)(2,1)S(1)} %bitcast.119, pred[]{:T(512)S(6)} %eq.161), kind=kLoop, calls=%fused_computation.11 | loop fusion | flops 4915200 | bytes 19660800 | tf_op jit(solution)/shard_map/jit(_where)/select_n | solution.py:32
  197.6 2.9 %fusion.3 = bf16[256,1280]{1,0:T(8,128)(2,1)S(1)} fusion(bf16[256,1280]{1,0:T(8,128)(2,1)S(1)} %copy-done.2, bf16[1280,1920]{1,0:T(8,128)(2,1)} %get-tuple-element.32), kind=kOutput, calls=%fused_computation.15 | convolution fusion | flops 839188480 | bytes 4587520 | tf_op jit(solution)/shard_map/dot_general | solution.py:196
  200.6 1.6 reshape.268
  202.1 1.3 copy.19
  203.4 25.0 %convolution_convert_fusion = bf16[2816,2560]{1,0:T(8,128)(2,1)} fusion(bf16[2816,1280]{1,0:T(8,128)(2,1)} %bitcast.121, bf16[1280,1920]{1,0:T(8,128)(2,1)} %get-tuple-element.31, bf16[1280,1920]{1,0:T(8,128)(2,1)} %get-tuple-element.32), kind=kOutput, calls=%fused_computation.8 | convolution fusion | flops 18475253760 | bytes 31457280 | tf_op jit(solution)/shard_map/dot_general | solution.py:192
  228.4 51.7 %shard_map.109 = bf16[2,128,1280]{2,1,0:T(8,128)(2,1)} custom-call(s32[2,18]{1,0:T(2,128)} %pad_add_fusion.1.slots_ref, s32[2]{0:T(128)} %counts_ref.1, bf16[2,16,128,80]{3,2,1,0:T(8,128)(2,1)} %bitcast.120, bf16[22,128,2560]{2,1,0:T(8,128)(2,1)} %bitcast.117), custom_call_target="tpu_custom_call" | custom-call | tf_op jit(solution)/shard_map/pallas_call | solution.py:129
  280.1 4.0 %convolution_convert_fusion.1 = bf16[256,1280]{1,0:T(8,128)(2,1)} fusion(bf16[256,1280]{1,0:T(8,128)(2,1)} %bitcast.122, bf16[1280,1280]{1,0:T(8,128)(2,1)} %all-gather.8.cloned.1.call-done), kind=kOutput, calls=%fused_computation.16 | convolution fusion | flops 839188480 | bytes 4587520 | tf_op jit(solution)/shard_map/dot_general | solution.py:217
  (94 shorter events, 6.9 us)
Async XLA Ops:
  6.5 48.8 %copy-start = (bf16[320,3840]{1,0:T(8,128)(2,1)S(1)}, bf16[320,3840]{1,0:T(8,128)(2,1)}, u32[]{:S(2)}) copy-start(bf16[320,3840]{1,0:T(8,128)(2,1)} %param.20) | copy-start | bytes 7372804
  6.5 48.8 %all-gather.4.cloned.1.call-start = ((), (), s32[]{:S(2)}) async-start(), calls=%async_computation | async-start | bytes 3276800 | tf_op jit(solution)/shard_map/all_gather | solution.py:163
  10.3 6.1 %copy-start.6 = (bf16[1280]{0:T(1024)(128)(2,1)S(1)}, bf16[1280]{0:T(1024)(128)(2,1)}, u32[]{:S(2)}) copy-start(bf16[1280]{0:T(1024)(128)(2,1)} %param.18) | copy-start | bytes 7684
  10.4 6.2 %copy-start.7 = (bf16[1280]{0:T(1024)(128)(2,1)S(1)}, bf16[1280]{0:T(1024)(128)(2,1)}, u32[]{:S(2)}) copy-start(bf16[1280]{0:T(1024)(128)(2,1)} %param.19) | copy-start | bytes 7684
  14.5 42.1 %copy-start.8 = (s32[2,16]{1,0:T(2,128)S(1)}, s32[2,16]{1,0:T(2,128)}, u32[]{:S(2)}) copy-start(s32[2,16]{1,0:T(2,128)} %param.13) | copy-start | bytes 388
  14.5 58.6 %copy-start.9 = (s32[2]{0:T(128)S(1)}, s32[2]{0:T(128)}, u32[]{:S(2)}) copy-start(s32[2]{0:T(128)} %param.15) | copy-start | bytes 28
  17.7 93.7 %all-gather.6.cloned.1.call-start = ((), (), s32[]{:S(2)}) async-start(), calls=%async_computation.1 | async-start | bytes 6144000 | tf_op jit(solution)/shard_map/all_gather | solution.py:26
  56.5 223.6 %all-gather.8.cloned.1.call-start = ((), (), s32[]{:S(2)}) async-start(), calls=%async_computation.2 | async-start | bytes 4096000 | tf_op jit(solution)/shard_map/all_gather | solution.py:219
  59.6 53.7 %collective-permute-start.1 = (s32[3]{0:T(128)S(1)}, s32[3]{0:T(128)S(1)}, u32[]{:S(2)}, u32[]{:S(2)}) collective-permute-start(s32[3]{0:T(128)S(1)} %pad_add_fusion.2), channel_id=1, source_target_pairs={{8,0},{12,4},{16,8},{20,12},{24,16},{28,20},{32,24},{36,28},{40,32... | collective-permute-start | bytes 44 | tf_op jit(solution)/shard_map/ppermute | solution.py:20
  65.0 51.6 %collective-permute-start.3 = (s32[3]{0:T(128)S(1)}, s32[3]{0:T(128)S(1)}, u32[]{:S(2)}, u32[]{:S(2)}) collective-permute-start(s32[3]{0:T(128)S(1)} %pad_add_fusion.3), channel_id=1, source_target_pairs={{4,0},{8,4},{12,8},{16,12},{20,16},{24,20},{28,24},{32,28},{36,32}... | collective-permute-start | bytes 44 | tf_op jit(solution)/shard_map/ppermute | solution.py:20
  69.7 49.9 %collective-permute-start.5 = (s32[3]{0:T(128)S(1)}, s32[3]{0:T(128)S(1)}, u32[]{:S(2)}, u32[]{:S(2)}) collective-permute-start(s32[3]{0:T(128)S(1)} %pad_add_fusion.4), channel_id=1, source_target_pairs={{0,4},{4,8},{8,12},{12,16},{16,20},{20,24},{24,28},{28,32},{32,36}... | collective-permute-start | bytes 44 | tf_op jit(solution)/shard_map/ppermute | solution.py:20
  76.5 15.7 %collective-permute-start.9 = (bf16[2,128,1280]{2,1,0:T(8,128)(2,1)S(1)}, bf16[2,128,1280]{2,1,0:T(8,128)(2,1)S(1)}, u32[]{:S(2)}, u32[]{:S(2)}) collective-permute-start(bf16[2,128,1280]{2,1,0:T(8,128)(2,1)S(1)} %gather_fusion.7), channel_id=1, source_target_pairs={{0,8},{4,12},{8,0},{12,4},{16,24},{20,28},{24,16},{28,20},{32,40},... | collective-permute-start | bytes 1966088 | tf_op jit(solution)/shard_map/ppermute | solution.py:180
  92.3 24.3 %collective-permute-start.10 = (bf16[2,128,1280]{2,1,0:T(8,128)(2,1)S(1)}, bf16[2,128,1280]{2,1,0:T(8,128)(2,1)S(1)}, u32[]{:S(2)}, u32[]{:S(2)}) collective-permute-start(bf16[2,128,1280]{2,1,0:T(8,128)(2,1)S(1)} %broadcast_select_fusion.2), channel_id=1, source_target_pairs={{0,16},{4,20},{8,24},{12,28},{16,0},{20,4},{24,8},{28,12},{32,48},... | collective-permute-start | bytes 1966088 | tf_op jit(solution)/shard_map/ppermute | solution.py:180
  111.4 79.1 %collective-permute-start = (bf16[1280,1920]{1,0:T(8,128)(2,1)}, bf16[1280,1920]{1,0:T(8,128)(2,1)}, u32[]{:S(2)}, u32[]{:S(2)}) collective-permute-start(bf16[1280,1920]{1,0:T(8,128)(2,1)} %all-gather.6.cloned.1.call-done), channel_id=1, source_target_pairs={{0,4},{4,0},{8,12},{12,8},{16,20},{20,16},{24,28},{28,24},{32,36},... | collective-permute-start | bytes 14745608 | tf_op jit(solution)/shard_map/ppermute | solution.py:30
  113.3 6.3 %collective-permute-start.7 = (s32[3]{0:T(128)S(1)}, s32[3]{0:T(128)S(1)}, u32[]{:S(2)}, u32[]{:S(2)}) collective-permute-start(s32[3]{0:T(128)S(1)} %pad_add_fusion.5), channel_id=1, source_target_pairs={{0,8},{4,12},{8,16},{12,20},{16,24},{20,28},{24,32},{28,36},{32,40... | collective-permute-start | bytes 44 | tf_op jit(solution)/shard_map/ppermute | solution.py:20
  116.8 19.2 %collective-permute-start.11 = (bf16[2,128,1280]{2,1,0:T(8,128)(2,1)S(1)}, bf16[2,128,1280]{2,1,0:T(8,128)(2,1)S(1)}, u32[]{:S(2)}, u32[]{:S(2)}) collective-permute-start(bf16[2,128,1280]{2,1,0:T(8,128)(2,1)S(1)} %broadcast_select_fusion.3), channel_id=1, source_target_pairs={{0,64},{4,68},{8,72},{12,76},{16,80},{20,84},{24,88},{28,92},{32,9... | collective-permute-start | bytes 1966088 | tf_op jit(solution)/shard_map/ppermute | solution.py:180
  121.9 34.7 %collective-permute-start.2 = (bf16[3,128,1280]{2,1,0:T(8,128)(2,1)S(1)}, bf16[3,128,1280]{2,1,0:T(8,128)(2,1)S(1)}, u32[]{:S(2)}, u32[]{:S(2)}) collective-permute-start(bf16[3,128,1280]{2,1,0:T(8,128)(2,1)S(1)} %gather_fusion.3), channel_id=1, source_target_pairs={{0,8},{4,12},{8,16},{12,20},{16,24},{20,28},{24,32},{28,36},{32,40... | collective-permute-start | bytes 2949128 | tf_op jit(solution)/shard_map/ppermute | solution.py:20
  136.0 0.9 copy-start.5
  138.0 31.8 %collective-permute-start.12 = (bf16[2,128,1280]{2,1,0:T(8,128)(2,1)S(1)}, bf16[2,128,1280]{2,1,0:T(8,128)(2,1)S(1)}, u32[]{:S(2)}, u32[]{:S(2)}) collective-permute-start(bf16[2,128,1280]{2,1,0:T(8,128)(2,1)S(1)} %broadcast_select_fusion.4), channel_id=1, source_target_pairs={{0,32},{4,36},{8,40},{12,44},{16,48},{20,52},{24,56},{28,60},{32,0... | collective-permute-start | bytes 1966088 | tf_op jit(solution)/shard_map/ppermute | solution.py:180
  142.3 29.9 %collective-permute-start.4 = (bf16[3,128,1280]{2,1,0:T(8,128)(2,1)}, bf16[3,128,1280]{2,1,0:T(8,128)(2,1)}, u32[]{:S(2)}, u32[]{:S(2)}) collective-permute-start(bf16[3,128,1280]{2,1,0:T(8,128)(2,1)} %gather_fusion.4), channel_id=1, source_target_pairs={{0,4},{4,8},{8,12},{12,16},{16,20},{20,24},{24,28},{28,32},{32,36}... | collective-permute-start | bytes 2949128 | tf_op jit(solution)/shard_map/ppermute | solution.py:20
  147.6 25.9 %collective-permute-start.6 = (bf16[3,128,1280]{2,1,0:T(8,128)(2,1)}, bf16[3,128,1280]{2,1,0:T(8,128)(2,1)}, u32[]{:S(2)}, u32[]{:S(2)}) collective-permute-start(bf16[3,128,1280]{2,1,0:T(8,128)(2,1)} %gather_fusion.5), channel_id=1, source_target_pairs={{4,0},{8,4},{12,8},{16,12},{20,16},{24,20},{28,24},{32,28},{36,32}... | collective-permute-start | bytes 2949128 | tf_op jit(solution)/shard_map/ppermute | solution.py:20
  154.5 35.9 %slice-start = ((s8[4915200]{0:T(1024)(128)(4,1)}), s8[4194304]{0:T(1024)(128)(4,1)S(1)}, s32[]{:S(2)}) async-start(s8[4915200]{0:T(1024)(128)(4,1)} %bitcast.118), calls=%async_computation.3 | async-start | bytes 8388608
  156.6 30.6 %collective-permute-start.8 = (bf16[3,128,1280]{2,1,0:T(8,128)(2,1)}, bf16[3,128,1280]{2,1,0:T(8,128)(2,1)S(1)}, u32[]{:S(2)}, u32[]{:S(2)}) collective-permute-start(bf16[3,128,1280]{2,1,0:T(8,128)(2,1)} %gather_fusion.6), channel_id=1, source_target_pairs={{8,0},{12,4},{16,8},{20,12},{24,16},{28,20},{32,24},{36,28},{40,32... | collective-permute-start | bytes 2949128 | tf_op jit(solution)/shard_map/ppermute | solution.py:20
  169.8 0.8 copy-start.4
  170.7 19.8 %slice-start.1 = ((s8[4915200]{0:T(1024)(128)(4,1)}), s8[720896]{0:T(1024)(128)(4,1)S(1)}, s32[]{:S(2)}) async-start(s8[4915200]{0:T(1024)(128)(4,1)} %bitcast.118), calls=%async_computation.4 | async-start | bytes 1441792
  171.9 15.3 %collective-permute-start.13 = (bf16[2,128,1280]{2,1,0:T(8,128)(2,1)S(1)}, bf16[2,128,1280]{2,1,0:T(8,128)(2,1)S(1)}, u32[]{:S(2)}, u32[]{:S(2)}) collective-permute-start(bf16[2,128,1280]{2,1,0:T(8,128)(2,1)S(1)} %broadcast_select_fusion.5), channel_id=1, source_target_pairs={{0,4},{4,0},{8,12},{12,8},{16,20},{20,16},{24,28},{28,24},{32,36},... | collective-permute-start | bytes 1966088 | tf_op jit(solution)/shard_map/ppermute | solution.py:180
  187.6 2.9 copy-start.3
  190.4 7.2 %copy-start.2 = (bf16[256,1280]{1,0:T(8,128)(2,1)S(1)}, bf16[256,1280]{1,0:T(8,128)(2,1)}, u32[]{:S(2)}) copy-start(bf16[256,1280]{1,0:T(8,128)(2,1)} %fusion.11) | copy-start | bytes 1966084
  228.4 55.7 %copy-start.1 = (bf16[320,3840]{1,0:T(8,128)(2,1)S(1)}, bf16[320,3840]{1,0:T(8,128)(2,1)}, u32[]{:S(2)}) copy-start(bf16[320,3840]{1,0:T(8,128)(2,1)} %param.20) | copy-start | bytes 7372804
Sparse Core Ops, SparseCore 0:
  17.8 37.4 all-gather.3
  57.0 54.3 all-gather.5
  113.0 41.0 all-gather.7

commit v14 on v13

--- a/solution.py
+++ b/solution.py
@@ -170,15 +170,21 @@
     global_rows = group_rows[global_ids % group_tiles]
     owners = global_ids // group_tiles
     seq_bits = seq_size.bit_length() - 1
-    bit_order = [b for b in (1, 2) if b < seq_bits]
-    bit_order += [b for b in range(seq_bits - 1, -1, -1) if b not in bit_order]
-    done_bits = 0
-    for bit in bit_order:
-        step = 1 << bit
-        held = ((seq_at ^ owners) & ~done_bits & (seq_size - 1)) == 0
-        done_bits |= step
-        got = lax.ppermute(global_rows, "seq", [(i, i ^ step) for i in range(seq_size)])
-        global_rows = jnp.where(held[:, None, None], global_rows, got)
+    y_first = [b for b in (1, 2) if b < seq_bits]
+    y_first += [b for b in range(seq_bits - 1, -1, -1) if b not in y_first]
+    x_first = [b for b in range(seq_bits - 1, -1, -1) if b not in (1, 2)]
+    x_first += [b for b in (1, 2) if b < seq_bits]
+    halves = []
+    for bit_order, part in zip((y_first, x_first), jnp.split(global_rows, 2, axis=2)):
+        done_bits = 0
+        for bit in bit_order:
+            step = 1 << bit
+            held = ((seq_at ^ owners) & ~done_bits & (seq_size - 1)) == 0
+            done_bits |= step
+            got = lax.ppermute(part, "seq", [(i, i ^ step) for i in range(seq_size)])
+            part = jnp.where(held[:, None, None], part, got)
+        halves.append(part)
+    global_rows = jnp.concatenate(halves, axis=2)
     near_blocks = []
     near_rank = []
     for reach in REACH:

time: 293 us -> 325 us (1.11); the launches traced: 291 us -> 318 us
  starting transfers between devices: 30.6 us -> 57.9 us
    ppermute x8, starting transfers between devices: 23.1 us -> 43.9 us  [passed_along(): return lax.ppermute(block, axis, route)]
    all_gather x1, waiting for transfers between devices: 16.1 us -> 30.5 us  [gathered_weight(): lax.all_gather(lax.dynamic_slice_in_dim(shard, core * half, half, 1), 'fs...]
    ppermute x8, waiting for transfers between devices: 12.4 us -> 3.18 us  [passed_along(): return lax.ppermute(block, axis, route)]
    ppermute x5 -> x10, starting transfers between devices: 7.42 us -> 13.9 us  [local(): got = lax.ppermute(part, 'seq', [(i, i ^ step) for i in range(seq_size)])]
    ppermute x5 -> x10, waiting for transfers between devices: 34.4 us -> 30.7 us  [local(): got = lax.ppermute(part, 'seq', [(i, i ^ step) for i in range(seq_size)])]
    unnamed x29 -> x27, local copies, waits for them, and re-layouts: 9.33 us -> 8.97 us
  transfers between devices with their start and end apart: 17 -> 22, of which waited for: 6 -> 7; matrix products, arithmetic and copies ran while one was open for 25% -> 25% of each run, Pallas kernels for 18% -> 16%
where the time goes in v14:
time: 325 us; the launch traced here: 318 us
  waiting for transfers between devices  102 us (31%)
  starting transfers between devices  57.9 us (18%)
  Pallas kernels  49.9 us (15%)
  local copies, waits for them, and re-layouts  36.2 us (11%)
  matrix products  32 us (10%)
  other arithmetic  26.7 us (8%)
  between operations  13.6 us (4%)
    pallas_call x1, Pallas kernels, attend(): pl.pallas_call(attention_kernel, grid_spec=grid_spec, out_shape=jax.Shape...  49.9 us
    ppermute x8, starting transfers between devices, passed_along(): return lax.ppermute(block, axis, route)  43.9 us
    all_gather x1, waiting for transfers between devices, local(): lax.all_gather(normed, 'fsdp', axis=0, tiled=True)  37.5 us
    ppermute x10, waiting for transfers between devices, local(): got = lax.ppermute(part, 'seq', [(i, i ^ step) for i in range(seq_size)])  30.7 us
    all_gather x1, waiting for transfers between devices, gathered_weight(): lax.all_gather(lax.dynamic_slice_in_dim(shard, core * half, half, 1), 'fs...  30.5 us
    dot_general x1, matrix products, local(): jnp.dot(window_rows.reshape(-1, feat_width), w_full[:, feat_width:], pref...  25 us
    ppermute x10, starting transfers between devices, local(): got = lax.ppermute(part, 'seq', [(i, i ^ step) for i in range(seq_size)])  13.9 us
    gather x4, local copies, waits for them, and re-layouts, local(): near_blocks.append(passed_along(group_rows[asked], 'seq', -reach))  12.7 us
  transfers between devices with their start and end apart: 22, of which 7 were waited for; matrix products, arithmetic and copies ran while one was open for 25% of the time, Pallas kernels for 16%

profile of v14, /device:TPU:24, one launch (start us, length us, event | category | flops | bytes accessed | tf_op | source)
XLA Modules:
  0.0 318.3 jit_solution(14283971651443924175)
XLA Ops:
  6.5 0.8 compare_select_fusion.1
  7.4 2.9 gather_fusion.1
  10.4 4.1 %gather_fusion.2 = bf16[256,1280]{1,0:T(8,128)(2,1)} fusion(bf16[512,1280]{1,0:T(8,128)(2,1)} %param.17, s32[1024]{0:T(1024)S(1)} %get-tuple-element.47), kind=kCustom, calls=%fused_computation.2 | custom fusion | bytes 1311744 | tf_op jit(solution)/shard_map/gather | solution.py:51
  14.5 1.7 convert_reduce_fusion
  16.5 1.2 fusion.11
  17.8 37.5 %all-gather.4.cloned.1.call-done = bf16[1024,1280]{1,0:T(8,128)(2,1)} async-done(((bf16[256,1280]{1,0:T(8,128)(2,1)}), bf16[1024,1280]{1,0:T(8,128)(2,1)}) %all-gather.4.cloned.1.call-update) | async-done | bytes 2621456 | tf_op jit(solution)/shard_map/all_gather | solution.py:163
  55.3 1.2 constant_dynamic-slice_fusion
  57.8 1.8 pad_add_fusion.5
  59.6 3.3 %collective-permute-start.7 = (s32[3]{0:T(128)S(1)}, s32[3]{0:T(128)S(1)}, u32[]{:S(2)}, u32[]{:S(2)}) collective-permute-start(s32[3]{0:T(128)S(1)} %pad_add_fusion.5), channel_id=1, source_target_pairs={{0,8},{4,12},{8,16},{12,20},{16,24},{20,28},{24,32},{28,36},{32,40... | collective-permute-start | bytes 44 | tf_op jit(solution)/shard_map/ppermute | solution.py:20
  63.8 1.8 pad_add_fusion.2
  65.6 2.5 collective-permute-start.1
  69.0 1.8 pad_add_fusion.4
  70.8 1.9 collective-permute-start.5
  73.6 1.8 pad_add_fusion.3
  75.5 3.6 %collective-permute-start.3 = (s32[3]{0:T(128)S(1)}, s32[3]{0:T(128)S(1)}, u32[]{:S(2)}, u32[]{:S(2)}) collective-permute-start(s32[3]{0:T(128)S(1)} %pad_add_fusion.3), channel_id=1, source_target_pairs={{4,0},{8,4},{12,8},{16,12},{20,16},{24,20},{28,24},{32,28},{36,32}... | collective-permute-start | bytes 44 | tf_op jit(solution)/shard_map/ppermute | solution.py:20
  80.9 30.5 %all-gather.6.cloned.1.call-done = bf16[1280,1920]{1,0:T(8,128)(2,1)} async-done(((bf16[320,1920]{1,0:T(8,128)(2,1)}), bf16[1280,1920]{1,0:T(8,128)(2,1)}) %all-gather.6.cloned.1.call-update) | async-done | bytes 4915216 | tf_op jit(solution)/shard_map/all_gather | solution.py:26
  111.5 2.3 gather_fusion.7
  113.9 3.1 collective-permute-start.14
  117.8 3.4 %gather_fusion.3 = bf16[3,128,1280]{2,1,0:T(8,128)(2,1)} fusion(bf16[8,128,1280]{2,1,0:T(8,128)(2,1)} %bitcast.112, s32[1024]{0:T(1024)S(1)} %pad_clamp_fusion.4), kind=kCustom, calls=%fused_computation.3 | custom fusion | bytes 1966092 | tf_op jit(solution)/shard_map/gather | solution.py:193
  121.1 3.0 collective-permute-start.2
  124.2 3.6 %gather_fusion.4 = bf16[3,128,1280]{2,1,0:T(8,128)(2,1)} fusion(bf16[8,128,1280]{2,1,0:T(8,128)(2,1)} %bitcast.113, s32[1024]{0:T(1024)S(1)} %get-tuple-element.52), kind=kCustom, calls=%fused_computation.4 | custom fusion | bytes 1966092 | tf_op jit(solution)/shard_map/gather | solution.py:193
  127.8 1.9 collective-permute-start.4
  129.8 2.0 collective-permute-start.10
  132.6 3.4 %constant_dynamic-update-slice_fusion.4 = bf16[22,128,1280]{2,1,0:T(8,128)(2,1)} fusion(bf16[8,128,1280]{2,1,0:T(8,128)(2,1)} %bitcast.114), kind=kLoop, calls=%fused_computation.42 | loop fusion | bytes 5242880
  136.0 3.4 %gather_fusion.5 = bf16[3,128,1280]{2,1,0:T(8,128)(2,1)} fusion(bf16[8,128,1280]{2,1,0:T(8,128)(2,1)} %bitcast.115, s32[1024]{0:T(1024)S(1)} %get-tuple-element.51), kind=kCustom, calls=%fused_computation.5 | custom fusion | bytes 1966092 | tf_op jit(solution)/shard_map/gather | solution.py:193
  139.4 2.4 gather_fusion.6
  141.8 25.7 %collective-permute-start.6 = (bf16[3,128,1280]{2,1,0:T(8,128)(2,1)}, bf16[3,128,1280]{2,1,0:T(8,128)(2,1)S(1)}, u32[]{:S(2)}, u32[]{:S(2)}) collective-permute-start(bf16[3,128,1280]{2,1,0:T(8,128)(2,1)} %gather_fusion.5), channel_id=1, source_target_pairs={{4,0},{8,4},{12,8},{16,12},{20,16},{24,20},{28,24},{32,28},{36,32}... | collective-permute-start | bytes 2949128 | tf_op jit(solution)/shard_map/ppermute | solution.py:20
  167.5 1.1 broadcast_select_fusion.8
  168.6 1.9 collective-permute-start.8
  170.6 1.1 broadcast_select_fusion.2
  172.5 2.4 constant_dynamic-update-slice_fusion.3
  174.9 1.1 constant_dynamic-update-slice_fusion.2
  176.0 7.0 %collective-permute-done.11 = bf16[2,128,640]{2,1,0:T(8,128)(2,1)S(1)} collective-permute-done((bf16[2,128,640]{2,1,0:T(8,128)(2,1)S(1)}, bf16[2,128,640]{2,1,0:T(8,128)(2,1)S(1)}, u32[]{:S(2)}, u32[]{:S(2)}) %collective-permute-start.11) | collective-permute-done | bytes 327712 | tf_op jit(solution)/shard_map/ppermute | solution.py:184
  184.6 3.2 collective-permute-done.6
  187.7 1.0 constant_dynamic-update-slice_fusion.1
  188.8 3.3 %collective-permute-done.12 = bf16[2,128,640]{2,1,0:T(8,128)(2,1)S(1)} collective-permute-done((bf16[2,128,640]{2,1,0:T(8,128)(2,1)S(1)}, bf16[2,128,640]{2,1,0:T(8,128)(2,1)S(1)}, u32[]{:S(2)}, u32[]{:S(2)}) %collective-permute-start.12) | collective-permute-done | bytes 327712 | tf_op jit(solution)/shard_map/ppermute | solution.py:184
  192.3 15.2 %collective-permute-done.17 = bf16[2,128,640]{2,1,0:T(8,128)(2,1)S(1)} collective-permute-done((bf16[2,128,640]{2,1,0:T(8,128)(2,1)S(1)}, bf16[2,128,640]{2,1,0:T(8,128)(2,1)S(1)}, u32[]{:S(2)}, u32[]{:S(2)}) %collective-permute-start.17) | collective-permute-done | bytes 327712 | tf_op jit(solution)/shard_map/ppermute | solution.py:184
  207.5 4.9 %collective-permute-start.18 = (bf16[2,128,640]{2,1,0:T(8,128)(2,1)S(1)}, bf16[2,128,640]{2,1,0:T(8,128)(2,1)S(1)}, u32[]{:S(2)}, u32[]{:S(2)}) collective-permute-start(bf16[2,128,640]{2,1,0:T(8,128)(2,1)S(1)} %broadcast_select_fusion.4), channel_id=1, source_target_pairs={{0,16},{4,20},{8,24},{12,28},{16,0},{20,4},{24,8},{28,12},{32,48},... | collective-permute-start | bytes 983048 | tf_op jit(solution)/shard_map/ppermute | solution.py:184
  212.5 1.0 constant_dynamic-update-slice_fusion
  213.6 5.2 %collective-permute-done.18 = bf16[2,128,640]{2,1,0:T(8,128)(2,1)S(1)} collective-permute-done((bf16[2,128,640]{2,1,0:T(8,128)(2,1)S(1)}, bf16[2,128,640]{2,1,0:T(8,128)(2,1)S(1)}, u32[]{:S(2)}, u32[]{:S(2)}) %collective-permute-start.18) | collective-permute-done | bytes 327712 | tf_op jit(solution)/shard_map/ppermute | solution.py:184
  219.0 0.9 maximum_dynamic-update-slice_fusion
  219.9 7.1 %broadcast_select_fusion = (bf16[1280,1920]{1,0:T(8,128)(2,1)}, bf16[1280,1920]{1,0:T(8,128)(2,1)}) fusion(bf16[1280,1920]{1,0:T(8,128)(2,1)} %collective-permute-done, bf16[1280,1920]{1,0:T(8,128)(2,1)S(1)} %bitcast.119, pred[]{:T(512)S(6)} %eq.174), kind=kLoop, calls=%fused_computation.11 | loop fusion | flops 4915200 | bytes 19660800 | tf_op jit(solution)/shard_map/jit(_where)/select_n | solution.py:32
  227.0 2.9 fusion.3
  230.0 1.6 reshape.272
  231.5 1.3 copy.19
  232.8 25.0 %convolution_convert_fusion = bf16[2816,2560]{1,0:T(8,128)(2,1)} fusion(bf16[2816,1280]{1,0:T(8,128)(2,1)} %bitcast.121, bf16[1280,1920]{1,0:T(8,128)(2,1)} %get-tuple-element.31, bf16[1280,1920]{1,0:T(8,128)(2,1)} %get-tuple-element.32), kind=kOutput, calls=%fused_computation.8 | convolution fusion | flops 18475253760 | bytes 31457280 | tf_op jit(solution)/shard_map/dot_general | solution.py:198
  257.9 49.9 %shard_map.109 = bf16[2,128,1280]{2,1,0:T(8,128)(2,1)} custom-call(s32[2,18]{1,0:T(2,128)} %pad_add_fusion.1.slots_ref, s32[2]{0:T(128)} %counts_ref.1, bf16[2,16,128,80]{3,2,1,0:T(8,128)(2,1)} %bitcast.120, bf16[22,128,2560]{2,1,0:T(8,128)(2,1)} %bitcast.117), custom_call_target="tpu_custom_call" | custom-call | tf_op jit(solution)/shard_map/pallas_call | solution.py:129
  307.8 4.0 %convolution_convert_fusion.1 = bf16[256,1280]{1,0:T(8,128)(2,1)} fusion(bf16[256,1280]{1,0:T(8,128)(2,1)} %bitcast.122, bf16[1280,1280]{1,0:T(8,128)(2,1)} %all-gather.8.cloned.1.call-done), kind=kOutput, calls=%fused_computation.16 | convolution fusion | flops 839188480 | bytes 4587520 | tf_op jit(solution)/shard_map/dot_general | solution.py:223
  (106 shorter events, 10.8 us)
Async XLA Ops:
  6.5 48.8 %copy-start = (bf16[320,3840]{1,0:T(8,128)(2,1)S(1)}, bf16[320,3840]{1,0:T(8,128)(2,1)}, u32[]{:S(2)}) copy-start(bf16[320,3840]{1,0:T(8,128)(2,1)} %param.20) | copy-start | bytes 7372804
  6.5 48.8 %all-gather.4.cloned.1.call-start = ((), (), s32[]{:S(2)}) async-start(), calls=%async_computation | async-start | bytes 3276800 | tf_op jit(solution)/shard_map/all_gather | solution.py:163
  10.3 6.1 %copy-start.5 = (bf16[1280]{0:T(1024)(128)(2,1)S(1)}, bf16[1280]{0:T(1024)(128)(2,1)}, u32[]{:S(2)}) copy-start(bf16[1280]{0:T(1024)(128)(2,1)} %param.18) | copy-start | bytes 7684
  10.4 6.2 %copy-start.6 = (bf16[1280]{0:T(1024)(128)(2,1)S(1)}, bf16[1280]{0:T(1024)(128)(2,1)}, u32[]{:S(2)}) copy-start(bf16[1280]{0:T(1024)(128)(2,1)} %param.19) | copy-start | bytes 7684
  14.5 42.1 %copy-start.7 = (s32[2,16]{1,0:T(2,128)S(1)}, s32[2,16]{1,0:T(2,128)}, u32[]{:S(2)}) copy-start(s32[2,16]{1,0:T(2,128)} %param.13) | copy-start | bytes 388
  14.5 64.7 %copy-start.8 = (s32[2]{0:T(128)S(1)}, s32[2]{0:T(128)}, u32[]{:S(2)}) copy-start(s32[2]{0:T(128)} %param.15) | copy-start | bytes 28
  17.7 93.7 %all-gather.6.cloned.1.call-start = ((), (), s32[]{:S(2)}) async-start(), calls=%async_computation.1 | async-start | bytes 6144000 | tf_op jit(solution)/shard_map/all_gather | solution.py:26
  56.5 251.3 %all-gather.8.cloned.1.call-start = ((), (), s32[]{:S(2)}) async-start(), calls=%async_computation.2 | async-start | bytes 4096000 | tf_op jit(solution)/shard_map/all_gather | solution.py:225
  59.6 21.3 %collective-permute-start.7 = (s32[3]{0:T(128)S(1)}, s32[3]{0:T(128)S(1)}, u32[]{:S(2)}, u32[]{:S(2)}) collective-permute-start(s32[3]{0:T(128)S(1)} %pad_add_fusion.5), channel_id=1, source_target_pairs={{0,8},{4,12},{8,16},{12,20},{16,24},{20,28},{24,32},{28,36},{32,40... | collective-permute-start | bytes 44 | tf_op jit(solution)/shard_map/ppermute | solution.py:20
  65.6 15.3 %collective-permute-start.1 = (s32[3]{0:T(128)S(1)}, s32[3]{0:T(128)S(1)}, u32[]{:S(2)}, u32[]{:S(2)}) collective-permute-start(s32[3]{0:T(128)S(1)} %pad_add_fusion.2), channel_id=1, source_target_pairs={{8,0},{12,4},{16,8},{20,12},{24,16},{28,20},{32,24},{36,28},{40,32... | collective-permute-start | bytes 44 | tf_op jit(solution)/shard_map/ppermute | solution.py:20
  70.8 40.6 %collective-permute-start.5 = (s32[3]{0:T(128)S(1)}, s32[3]{0:T(128)S(1)}, u32[]{:S(2)}, u32[]{:S(2)}) collective-permute-start(s32[3]{0:T(128)S(1)} %pad_add_fusion.4), channel_id=1, source_target_pairs={{0,4},{4,8},{8,12},{12,16},{16,20},{20,24},{24,28},{28,32},{32,36}... | collective-permute-start | bytes 44 | tf_op jit(solution)/shard_map/ppermute | solution.py:20
  75.5 42.3 %collective-permute-start.3 = (s32[3]{0:T(128)S(1)}, s32[3]{0:T(128)S(1)}, u32[]{:S(2)}, u32[]{:S(2)}) collective-permute-start(s32[3]{0:T(128)S(1)} %pad_add_fusion.3), channel_id=1, source_target_pairs={{4,0},{8,4},{12,8},{16,12},{20,16},{24,20},{28,24},{32,28},{36,32}... | collective-permute-start | bytes 44 | tf_op jit(solution)/shard_map/ppermute | solution.py:20
  111.4 108.4 %collective-permute-start = (bf16[1280,1920]{1,0:T(8,128)(2,1)}, bf16[1280,1920]{1,0:T(8,128)(2,1)}, u32[]{:S(2)}, u32[]{:S(2)}) collective-permute-start(bf16[1280,1920]{1,0:T(8,128)(2,1)} %all-gather.6.cloned.1.call-done), channel_id=1, source_target_pairs={{0,4},{4,0},{8,12},{12,8},{16,20},{20,16},{24,28},{28,24},{32,36},... | collective-permute-start | bytes 14745608 | tf_op jit(solution)/shard_map/ppermute | solution.py:30
  113.9 15.8 %collective-permute-start.14 = (bf16[2,128,640]{2,1,0:T(8,128)(2,1)S(1)}, bf16[2,128,640]{2,1,0:T(8,128)(2,1)S(1)}, u32[]{:S(2)}, u32[]{:S(2)}) collective-permute-start(bf16[2,128,640]{2,1,0:T(8,128)(2,1)S(1)} %get-tuple-element.36), channel_id=1, source_target_pairs={{0,64},{4,68},{8,72},{12,76},{16,80},{20,84},{24,88},{28,92},{32,9... | collective-permute-start | bytes 983048 | tf_op jit(solution)/shard_map/ppermute | solution.py:184
  116.9 12.7 %collective-permute-start.9 = (bf16[2,128,640]{2,1,0:T(8,128)(2,1)S(1)}, bf16[2,128,640]{2,1,0:T(8,128)(2,1)S(1)}, u32[]{:S(2)}, u32[]{:S(2)}) collective-permute-start(bf16[2,128,640]{2,1,0:T(8,128)(2,1)S(1)} %get-tuple-element.35), channel_id=1, source_target_pairs={{0,8},{4,12},{8,0},{12,4},{16,24},{20,28},{24,16},{28,20},{32,40},... | collective-permute-start | bytes 983048 | tf_op jit(solution)/shard_map/ppermute | solution.py:184
  121.1 50.5 %collective-permute-start.2 = (bf16[3,128,1280]{2,1,0:T(8,128)(2,1)}, bf16[3,128,1280]{2,1,0:T(8,128)(2,1)}, u32[]{:S(2)}, u32[]{:S(2)}) collective-permute-start(bf16[3,128,1280]{2,1,0:T(8,128)(2,1)} %gather_fusion.3), channel_id=1, source_target_pairs={{0,8},{4,12},{8,16},{12,20},{16,24},{20,28},{24,32},{28,36},{32,40... | collective-permute-start | bytes 2949128 | tf_op jit(solution)/shard_map/ppermute | solution.py:20
  127.8 47.1 %collective-permute-start.4 = (bf16[3,128,1280]{2,1,0:T(8,128)(2,1)}, bf16[3,128,1280]{2,1,0:T(8,128)(2,1)S(1)}, u32[]{:S(2)}, u32[]{:S(2)}) collective-permute-start(bf16[3,128,1280]{2,1,0:T(8,128)(2,1)} %gather_fusion.4), channel_id=1, source_target_pairs={{0,4},{4,8},{8,12},{12,16},{16,20},{20,24},{24,28},{28,32},{32,36}... | collective-permute-start | bytes 2949128 | tf_op jit(solution)/shard_map/ppermute | solution.py:20
  129.8 12.0 %collective-permute-start.10 = (bf16[2,128,640]{2,1,0:T(8,128)(2,1)S(1)}, bf16[2,128,640]{2,1,0:T(8,128)(2,1)S(1)}, u32[]{:S(2)}, u32[]{:S(2)}) collective-permute-start(bf16[2,128,640]{2,1,0:T(8,128)(2,1)S(1)} %get-tuple-element.33), channel_id=1, source_target_pairs={{0,16},{4,20},{8,24},{12,28},{16,0},{20,4},{24,8},{28,12},{32,48},... | collective-permute-start | bytes 983048 | tf_op jit(solution)/shard_map/ppermute | solution.py:184
  131.9 36.8 %collective-permute-start.15 = (bf16[2,128,640]{2,1,0:T(8,128)(2,1)S(1)}, bf16[2,128,640]{2,1,0:T(8,128)(2,1)S(1)}, u32[]{:S(2)}, u32[]{:S(2)}) collective-permute-start(bf16[2,128,640]{2,1,0:T(8,128)(2,1)S(1)} %get-tuple-element.34), channel_id=1, source_target_pairs={{0,32},{4,36},{8,40},{12,44},{16,48},{20,52},{24,56},{28,60},{32,0... | collective-permute-start | bytes 983048 | tf_op jit(solution)/shard_map/ppermute | solution.py:184
  141.8 25.7 %copy-start.4 = (bf16[2,128,640]{2,1,0:T(8,128)(2,1)}, bf16[2,128,640]{2,1,0:T(8,128)(2,1)S(1)}, u32[]{:S(2)}) copy-start(bf16[2,128,640]{2,1,0:T(8,128)(2,1)S(1)} %collective-permute-done.10) | copy-start | bytes 983044
  141.8 45.9 %collective-permute-start.6 = (bf16[3,128,1280]{2,1,0:T(8,128)(2,1)}, bf16[3,128,1280]{2,1,0:T(8,128)(2,1)S(1)}, u32[]{:S(2)}, u32[]{:S(2)}) collective-permute-start(bf16[3,128,1280]{2,1,0:T(8,128)(2,1)} %gather_fusion.5), channel_id=1, source_target_pairs={{4,0},{8,4},{12,8},{16,12},{20,16},{24,20},{28,24},{32,28},{36,32}... | collective-permute-start | bytes 2949128 | tf_op jit(solution)/shard_map/ppermute | solution.py:20
  168.6 1.9 copy-start.3
  168.6 43.8 %collective-permute-start.8 = (bf16[3,128,1280]{2,1,0:T(8,128)(2,1)S(1)}, bf16[3,128,1280]{2,1,0:T(8,128)(2,1)S(1)}, u32[]{:S(2)}, u32[]{:S(2)}) collective-permute-start(bf16[3,128,1280]{2,1,0:T(8,128)(2,1)S(1)} %gather_fusion.6), channel_id=1, source_target_pairs={{8,0},{12,4},{16,8},{20,12},{24,16},{28,20},{32,24},{36,28},{40,32... | collective-permute-start | bytes 2949128 | tf_op jit(solution)/shard_map/ppermute | solution.py:20
  171.7 11.3 %collective-permute-start.11 = (bf16[2,128,640]{2,1,0:T(8,128)(2,1)S(1)}, bf16[2,128,640]{2,1,0:T(8,128)(2,1)S(1)}, u32[]{:S(2)}, u32[]{:S(2)}) collective-permute-start(bf16[2,128,640]{2,1,0:T(8,128)(2,1)S(1)} %broadcast_select_fusion.8), channel_id=1, source_target_pairs={{0,64},{4,68},{8,72},{12,76},{16,80},{20,84},{24,88},{28,92},{32,9... | collective-permute-start | bytes 983048 | tf_op jit(solution)/shard_map/ppermute | solution.py:184
  172.5 47.3 %slice-start = ((s8[4915200]{0:T(1024)(128)(4,1)}), s8[4194304]{0:T(1024)(128)(4,1)S(1)}, s32[]{:S(2)}) async-start(s8[4915200]{0:T(1024)(128)(4,1)} %bitcast.118), calls=%async_computation.3 | async-start | bytes 8388608
  174.9 8.9 %collective-permute-start.16 = (bf16[2,128,640]{2,1,0:T(8,128)(2,1)S(1)}, bf16[2,128,640]{2,1,0:T(8,128)(2,1)S(1)}, u32[]{:S(2)}, u32[]{:S(2)}) collective-permute-start(bf16[2,128,640]{2,1,0:T(8,128)(2,1)S(1)} %broadcast_select_fusion.2), channel_id=1, source_target_pairs={{0,4},{4,0},{8,12},{12,8},{16,20},{20,16},{24,28},{28,24},{32,36},... | collective-permute-start | bytes 983048 | tf_op jit(solution)/shard_map/ppermute | solution.py:184
  183.1 9.0 %collective-permute-start.12 = (bf16[2,128,640]{2,1,0:T(8,128)(2,1)S(1)}, bf16[2,128,640]{2,1,0:T(8,128)(2,1)S(1)}, u32[]{:S(2)}, u32[]{:S(2)}) collective-permute-start(bf16[2,128,640]{2,1,0:T(8,128)(2,1)S(1)} %broadcast_select_fusion.9), channel_id=1, source_target_pairs={{0,32},{4,36},{8,40},{12,44},{16,48},{20,52},{24,56},{28,60},{32,0... | collective-permute-start | bytes 983048 | tf_op jit(solution)/shard_map/ppermute | solution.py:184
  183.9 36.0 %slice-start.1 = ((s8[4915200]{0:T(1024)(128)(4,1)}), s8[720896]{0:T(1024)(128)(4,1)S(1)}, s32[]{:S(2)}) async-start(s8[4915200]{0:T(1024)(128)(4,1)} %bitcast.118), calls=%async_computation.4 | async-start | bytes 1441792
  183.9 23.6 %collective-permute-start.17 = (bf16[2,128,640]{2,1,0:T(8,128)(2,1)S(1)}, bf16[2,128,640]{2,1,0:T(8,128)(2,1)S(1)}, u32[]{:S(2)}, u32[]{:S(2)}) collective-permute-start(bf16[2,128,640]{2,1,0:T(8,128)(2,1)S(1)} %broadcast_select_fusion.3), channel_id=1, source_target_pairs={{0,8},{4,12},{8,0},{12,4},{16,24},{20,28},{24,16},{28,20},{32,40},... | collective-permute-start | bytes 983048 | tf_op jit(solution)/shard_map/ppermute | solution.py:184
  192.2 21.3 %collective-permute-start.13 = (bf16[2,128,640]{2,1,0:T(8,128)(2,1)S(1)}, bf16[2,128,640]{2,1,0:T(8,128)(2,1)S(1)}, u32[]{:S(2)}, u32[]{:S(2)}) collective-permute-start(bf16[2,128,640]{2,1,0:T(8,128)(2,1)S(1)} %broadcast_select_fusion.10), channel_id=1, source_target_pairs={{0,4},{4,0},{8,12},{12,8},{16,20},{20,16},{24,28},{28,24},{32,36},... | collective-permute-start | bytes 983048 | tf_op jit(solution)/shard_map/ppermute | solution.py:184
  207.5 11.3 %collective-permute-start.18 = (bf16[2,128,640]{2,1,0:T(8,128)(2,1)S(1)}, bf16[2,128,640]{2,1,0:T(8,128)(2,1)S(1)}, u32[]{:S(2)}, u32[]{:S(2)}) collective-permute-start(bf16[2,128,640]{2,1,0:T(8,128)(2,1)S(1)} %broadcast_select_fusion.4), channel_id=1, source_target_pairs={{0,16},{4,20},{8,24},{12,28},{16,0},{20,4},{24,8},{28,12},{32,48},... | collective-permute-start | bytes 983048 | tf_op jit(solution)/shard_map/ppermute | solution.py:184
  219.8 7.2 %copy-start.2 = (bf16[256,1280]{1,0:T(8,128)(2,1)S(1)}, bf16[256,1280]{1,0:T(8,128)(2,1)}, u32[]{:S(2)}) copy-start(bf16[256,1280]{1,0:T(8,128)(2,1)} %fusion.11) | copy-start | bytes 1966084
  257.9 53.9 %copy-start.1 = (bf16[320,3840]{1,0:T(8,128)(2,1)S(1)}, bf16[320,3840]{1,0:T(8,128)(2,1)}, u32[]{:S(2)}) copy-start(bf16[320,3840]{1,0:T(8,128)(2,1)} %param.20) | copy-start | bytes 7372804
Sparse Core Ops, SparseCore 0:
  17.8 37.4 all-gather.3
  57.0 54.4 all-gather.5
  113.1 41.0 all-gather.7

commit v15 on v13

--- a/solution.py
+++ b/solution.py
@@ -63,7 +63,7 @@
     return picks, rank
 
 
-def attention_kernel(slots_ref, counts_ref, q_ref, kv_ref, o_ref, s_scr, v_scr):
+def attention_kernel(own_ref, rest_ref, src_ref, counts_ref, q_ref, kv_own, kv_rest, o_ref, s_scr, v_scr):
     tile_at = pl.program_id(0)
     slot_at = pl.program_id(1)
     slot_count = KT + GLOBAL
@@ -73,8 +73,9 @@
     live = (slot_at >= KT) | (slot_at < live_count)
     key_at = pl.multiple_of(slot_at * TILE, TILE)
 
-    @pl.when(live)
-    def _():
+    from_rest = src_ref[tile_at, slot_at] == 1
+
+    def take(kv_ref):
         for head in range(HEADS):
             cols = slice(head * head_size, (head + 1) * head_size)
             scores = lax.dot_general(
@@ -83,6 +84,14 @@
             )
             s_scr[head, :, pl.ds(key_at, TILE)] = scores * head_size ** (-0.5)
         v_scr[pl.ds(key_at, TILE), :] = kv_ref[0, :, feat_width:]
+
+    @pl.when(live & jnp.logical_not(from_rest))
+    def _():
+        take(kv_own)
+
+    @pl.when(live & from_rest)
+    def _():
+        take(kv_rest)
 
     @pl.when(jnp.logical_not(live))
     def _():
@@ -102,25 +111,36 @@
             o_ref[0, :, cols] = mixed.astype(o_ref.dtype)
 
 
-def attend(query_tiles, window, slots, counts):
+def attend(query_tiles, window_own, window_rest, slots, counts):
     tile_count, _, feat_width = query_tiles.shape
     slot_count = KT + GLOBAL
     head_size = feat_width // HEADS
+    own_tiles = window_own.shape[0]
     query_heads = query_tiles.reshape(tile_count, TILE, HEADS, head_size).transpose(0, 2, 1, 3)
-
-    def kv_map(i, j, slots_ref, counts_ref):
-        live_count = counts_ref[i]
-        fetch = jnp.where((j >= KT) | (j < live_count), j, jnp.maximum(live_count - 1, 0))
-        return (slots_ref[i, fetch], 0, 0)
+    own_at = jnp.zeros((tile_count,), jnp.int32)
+    rest_at = jnp.zeros((tile_count,), jnp.int32)
+    own_cols, rest_cols, src_cols = [], [], []
+    for j in range(slot_count):
+        live = (j >= KT) | (j < counts)
+        use_rest = slots[:, j] >= own_tiles
+        own_at = jnp.where(live & ~use_rest, slots[:, j], own_at)
+        rest_at = jnp.where(live & use_rest, slots[:, j] - own_tiles, rest_at)
+        own_cols.append(own_at)
+        rest_cols.append(rest_at)
+        src_cols.append(use_rest.astype(jnp.int32))
+    own_table = jnp.clip(jnp.stack(own_cols, axis=1), 0, own_tiles - 1)
+    rest_table = jnp.clip(jnp.stack(rest_cols, axis=1), 0, window_rest.shape[0] - 1)
+    src_table = jnp.stack(src_cols, axis=1)
 
     grid_spec = pltpu.PrefetchScalarGridSpec(
-        num_scalar_prefetch=2,
+        num_scalar_prefetch=4,
         grid=(tile_count, slot_count),
         in_specs=[
-            pl.BlockSpec((1, HEADS, TILE, head_size), lambda i, j, s, c: (i, 0, 0, 0)),
-            pl.BlockSpec((1, TILE, 2 * feat_width), kv_map),
+            pl.BlockSpec((1, HEADS, TILE, head_size), lambda i, j, o, r, s, c: (i, 0, 0, 0)),
+            pl.BlockSpec((1, TILE, 2 * feat_width), lambda i, j, o, r, s, c: (o[i, j], 0, 0)),
+            pl.BlockSpec((1, TILE, 2 * feat_width), lambda i, j, o, r, s, c: (r[i, j], 0, 0)),
         ],
-        out_specs=pl.BlockSpec((1, TILE, feat_width), lambda i, j, s, c: (i, 0, 0)),
+        out_specs=pl.BlockSpec((1, TILE, feat_width), lambda i, j, o, r, s, c: (i, 0, 0)),
         scratch_shapes=[
             pltpu.VMEM((HEADS, TILE, slot_count * TILE), jnp.float32),
             pltpu.VMEM((slot_count * TILE, feat_width), jnp.bfloat16),
@@ -133,7 +153,7 @@
         compiler_params=pltpu.CompilerParams(
             dimension_semantics=("arbitrary", "arbitrary"),
         ),
-    )(slots, counts, query_heads, window)
+    )(own_table, rest_table, src_table, counts, query_heads, window_own, window_rest)
 
 
 def local(
@@ -186,13 +206,14 @@
         asked = passed_along(picks, "seq", reach)
         near_blocks.append(passed_along(group_rows[asked], "seq", -reach))
         near_rank.append(rank)
-    window_rows = jnp.concatenate(
-        [group_rows] + near_blocks + [global_rows], axis=0
-    )
-    window = jnp.dot(
-        window_rows.reshape(-1, feat_width), w_full[:, feat_width:],
-        preferred_element_type=jnp.float32,
-    ).astype(jnp.bfloat16).reshape(-1, TILE, 2 * feat_width)
+    def project(rows):
+        return jnp.dot(
+            rows.reshape(-1, feat_width), w_full[:, feat_width:],
+            preferred_element_type=jnp.float32,
+        ).astype(jnp.bfloat16).reshape(-1, TILE, 2 * feat_width)
+
+    window_own = project(group_rows)
+    window_rest = project(jnp.concatenate(near_blocks + [global_rows], axis=0))
     query = jnp.dot(
         normed, w_full[:, :feat_width], preferred_element_type=jnp.float32
     ).astype(jnp.bfloat16)
@@ -213,7 +234,7 @@
     slots = jnp.concatenate(
         [local_lists, jnp.broadcast_to(global_slots, (tile_count, GLOBAL))], axis=1
     ).astype(jnp.int32)
-    heads_out = attend(query_tiles, window, slots, kv_count).reshape(tok_rows, feat_width)
+    heads_out = attend(query_tiles, window_own, window_rest, slots, kv_count).reshape(tok_rows, feat_width)
     return jnp.dot(
         heads_out,
         lax.all_gather(w_out, "fsdp", axis=0, tiled=True),

time: 293 us -> 301 us (1.027)
  the two profiles are of different devices: /device:TPU:24 before, /device:TPU:34 now
where the time goes in v15:
time: 301 us; the launch traced here: 296 us
  waiting for transfers between devices  100 us (33%)
  Pallas kernels  49.2 us (16%)
  local copies, waits for them, and re-layouts  39 us (13%)
  matrix products  34.1 us (11%)
  other arithmetic  28.2 us (9%)
  starting transfers between devices  27.7 us (9%)
  between operations  17.5 us (6%)
    pallas_call x1, Pallas kernels, attend(): pl.pallas_call(attention_kernel, grid_spec=grid_spec, out_shape=jax.Shape...  49.2 us
    all_gather x1, waiting for transfers between devices, local(): lax.all_gather(normed, 'fsdp', axis=0, tiled=True)  36.4 us
    ppermute x5, waiting for transfers between devices, local(): lax.ppermute(global_rows, 'seq', [(i, i ^ step) for i in range(seq_size)])  35.1 us
    dot_general x2, matrix products, project(): jnp.dot(rows.reshape(-1, feat_width), w_full[:, feat_width:], preferred_e...  27.1 us
    ppermute x8, waiting for transfers between devices, passed_along(): return lax.ppermute(block, axis, route)  25.7 us
    ppermute x8, starting transfers between devices, passed_along(): return lax.ppermute(block, axis, route)  23.5 us
    gather x4, local copies, waits for them, and re-layouts, local(): near_blocks.append(passed_along(group_rows[asked], 'seq', -reach))  12.5 us
    another operation x4, other arithmetic, near_tiles(): jnp.stack([jnp.sum(jnp.where(named & (rank == j), local_ids, 0)) for j in...  7.99 us
  transfers between devices with their start and end apart: 17, of which 7 were waited for; matrix products, arithmetic and copies ran while one was open for 28% of the time, Pallas kernels for 17%

profile of v15, /device:TPU:34, one launch (start us, length us, event | category | flops | bytes accessed | tf_op | source)
XLA Modules:
  0.0 295.9 jit_solution(12484623622708654934)
XLA Ops:
  6.5 0.8 compare_select_fusion.1
  7.4 2.9 gather_fusion.1
  10.4 4.1 %gather_fusion.2 = bf16[256,1280]{1,0:T(8,128)(2,1)} fusion(bf16[512,1280]{1,0:T(8,128)(2,1)} %param.17, s32[1024]{0:T(1024)S(1)} %get-tuple-element.111), kind=kCustom, calls=%fused_computation.2 | custom fusion | bytes 1311744 | tf_op jit(solution)/shard_map/gather | solution.py:51
  14.5 1.7 convert_reduce_fusion
  16.5 1.2 fusion.10
  17.8 36.4 %all-gather.4.cloned.1.call-done = bf16[1024,1280]{1,0:T(8,128)(2,1)} async-done(((bf16[256,1280]{1,0:T(8,128)(2,1)}), bf16[1024,1280]{1,0:T(8,128)(2,1)}) %all-gather.4.cloned.1.call-update) | async-done | bytes 2621456 | tf_op jit(solution)/shard_map/all_gather | solution.py:183
  54.2 1.1 constant_dynamic-slice_fusion
  56.7 2.0 pad_add_fusion.1
  58.6 4.6 %collective-permute-start.1 = (s32[3]{0:T(128)S(1)}, s32[3]{0:T(128)S(1)}, u32[]{:S(2)}, u32[]{:S(2)}) collective-permute-start(s32[3]{0:T(128)S(1)} %pad_add_fusion.1), channel_id=1, source_target_pairs={{8,0},{12,4},{16,8},{20,12},{24,16},{28,20},{32,24},{36,28},{40,32... | collective-permute-start | bytes 44 | tf_op jit(solution)/shard_map/ppermute | solution.py:20
  64.2 2.0 pad_add_fusion.2
  66.2 1.9 collective-permute-start.3
  69.1 2.0 pad_add_fusion.3
  71.0 2.4 collective-permute-start.5
  79.5 1.3 fusion.30
  84.8 2.4 gather_fusion.7
  88.8 15.7 %collective-permute-done.9 = bf16[2,128,1280]{2,1,0:T(8,128)(2,1)S(1)} collective-permute-done((bf16[2,128,1280]{2,1,0:T(8,128)(2,1)S(1)}, bf16[2,128,1280]{2,1,0:T(8,128)(2,1)S(1)}, u32[]{:S(2)}, u32[]{:S(2)}) %collective-permute-start.9) | collective-permute-done | bytes 655392 | tf_op jit(solution)/shard_map/ppermute | solution.py:200
  104.7 0.8 fusion.41
  105.5 2.1 pad_add_fusion.4
  107.6 3.0 %all-gather.6.cloned.1.call-done = bf16[1280,1920]{1,0:T(8,128)(2,1)} async-done(((bf16[320,1920]{1,0:T(8,128)(2,1)}), bf16[1280,1920]{1,0:T(8,128)(2,1)}) %all-gather.6.cloned.1.call-update) | async-done | bytes 4915216 | tf_op jit(solution)/shard_map/all_gather | solution.py:26
  111.7 11.0 %collective-permute-done.10 = bf16[2,128,1280]{2,1,0:T(8,128)(2,1)S(1)} collective-permute-done((bf16[2,128,1280]{2,1,0:T(8,128)(2,1)S(1)}, bf16[2,128,1280]{2,1,0:T(8,128)(2,1)S(1)}, u32[]{:S(2)}, u32[]{:S(2)}) %collective-permute-start.10) | collective-permute-done | bytes 655392 | tf_op jit(solution)/shard_map/ppermute | solution.py:200
  122.7 1.9 collective-permute-start.7
  124.8 2.4 collective-permute-start.11
  127.3 3.3 %gather_fusion.3 = bf16[3,128,1280]{2,1,0:T(8,128)(2,1)} fusion(bf16[8,128,1280]{2,1,0:T(8,128)(2,1)} %bitcast.162, s32[1024]{0:T(1024)S(1)} %pad_clamp_fusion.4), kind=kCustom, calls=%fused_computation.3 | custom fusion | bytes 1966092 | tf_op jit(solution)/shard_map/gather | solution.py:207
  130.7 3.0 %collective-permute-start.2 = (bf16[3,128,1280]{2,1,0:T(8,128)(2,1)}, bf16[3,128,1280]{2,1,0:T(8,128)(2,1)}, u32[]{:S(2)}, u32[]{:S(2)}) collective-permute-start(bf16[3,128,1280]{2,1,0:T(8,128)(2,1)} %gather_fusion.3), channel_id=1, source_target_pairs={{0,8},{4,12},{8,16},{12,20},{16,24},{20,28},{24,32},{28,36},{32,40... | collective-permute-start | bytes 2949128 | tf_op jit(solution)/shard_map/ppermute | solution.py:20
  133.7 8.4 %collective-permute-done.11 = bf16[2,128,1280]{2,1,0:T(8,128)(2,1)S(1)} collective-permute-done((bf16[2,128,1280]{2,1,0:T(8,128)(2,1)S(1)}, bf16[2,128,1280]{2,1,0:T(8,128)(2,1)S(1)}, u32[]{:S(2)}, u32[]{:S(2)}) %collective-permute-start.11) | collective-permute-done | bytes 655392 | tf_op jit(solution)/shard_map/ppermute | solution.py:200
  142.2 0.8 collective-permute-start.12
  143.0 2.4 gather_fusion.4
  145.4 1.9 collective-permute-start.4
  147.3 3.3 %gather_fusion.5 = bf16[3,128,1280]{2,1,0:T(8,128)(2,1)} fusion(bf16[8,128,1280]{2,1,0:T(8,128)(2,1)} %bitcast.164, s32[1024]{0:T(1024)S(1)} %pad_clamp_fusion.2), kind=kCustom, calls=%fused_computation.5 | custom fusion | bytes 1966092 | tf_op jit(solution)/shard_map/gather | solution.py:207
  150.7 5.7 %collective-permute-start.6 = (bf16[3,128,1280]{2,1,0:T(8,128)(2,1)}, bf16[3,128,1280]{2,1,0:T(8,128)(2,1)}, u32[]{:S(2)}, u32[]{:S(2)}) collective-permute-start(bf16[3,128,1280]{2,1,0:T(8,128)(2,1)} %gather_fusion.5), channel_id=1, source_target_pairs={{4,0},{8,4},{12,8},{16,12},{20,16},{24,20},{28,24},{32,28},{36,32}... | collective-permute-start | bytes 2949128 | tf_op jit(solution)/shard_map/ppermute | solution.py:20
  156.4 3.4 %gather_fusion.6 = bf16[3,128,1280]{2,1,0:T(8,128)(2,1)} fusion(bf16[8,128,1280]{2,1,0:T(8,128)(2,1)} %bitcast.165, s32[1024]{0:T(1024)S(1)} %pad_clamp_fusion.1), kind=kCustom, calls=%fused_computation.6 | custom fusion | bytes 1966092 | tf_op jit(solution)/shard_map/gather | solution.py:207
  159.9 8.9 %collective-permute-done.2 = bf16[3,128,1280]{2,1,0:T(8,128)(2,1)} collective-permute-done((bf16[3,128,1280]{2,1,0:T(8,128)(2,1)}, bf16[3,128,1280]{2,1,0:T(8,128)(2,1)}, u32[]{:S(2)}, u32[]{:S(2)}) %collective-permute-start.2) | collective-permute-done | bytes 983072 | tf_op jit(solution)/shard_map/ppermute | solution.py:20
  168.8 1.9 collective-permute-start.8
  170.7 1.3 constant_dynamic-update-slice_fusion.3
  172.0 0.8 copy-done.3
  172.8 1.2 broadcast_select_fusion.5
  174.3 16.8 %collective-permute-done.4 = bf16[3,128,1280]{2,1,0:T(8,128)(2,1)} collective-permute-done((bf16[3,128,1280]{2,1,0:T(8,128)(2,1)S(1)}, bf16[3,128,1280]{2,1,0:T(8,128)(2,1)}, u32[]{:S(2)}, u32[]{:S(2)}) %collective-permute-start.4) | collective-permute-done | bytes 983072 | tf_op jit(solution)/shard_map/ppermute | solution.py:20
  191.1 1.3 constant_dynamic-update-slice_fusion.2
  192.4 1.3 constant_dynamic-update-slice_fusion.1
  194.1 2.1 copy-done.4
  196.2 7.1 %broadcast_select_fusion = (bf16[1280,1920]{1,0:T(8,128)(2,1)}, bf16[1280,1920]{1,0:T(8,128)(2,1)}) fusion(bf16[1280,1920]{1,0:T(8,128)(2,1)} %collective-permute-done, bf16[1280,1920]{1,0:T(8,128)(2,1)S(1)} %bitcast.168, pred[]{:T(512)S(6)} %eq.161), kind=kLoop, calls=%fused_computation.11 | loop fusion | flops 4915200 | bytes 19660800 | tf_op jit(solution)/shard_map/jit(_where)/select_n | solution.py:32
  203.2 2.9 fusion.2
  206.2 1.6 reshape.290
  207.8 1.3 copy.127
  209.1 12.6 %convolution_convert_fusion.1 = bf16[1024,2560]{1,0:T(8,128)(2,1)} fusion(bf16[1024,1280]{1,0:T(8,128)(2,1)} %all-gather.4.cloned.1.call-done, bf16[1280,1920]{1,0:T(8,128)(2,1)} %get-tuple-element.79, bf16[1280,1920]{1,0:T(8,128)(2,1)} %get-tuple-element.80), kind=kOutput, calls=%fused_computation.10 | convolution fusion | flops 6726615040 | bytes 17694720 | tf_op jit(solution)/shard_map/dot_general | solution.py:210
  221.7 14.5 %convolution_convert_fusion = bf16[1792,2560]{1,0:T(8,128)(2,1)} fusion(bf16[1792,1280]{1,0:T(8,128)(2,1)S(1)} %bitcast.177, bf16[1280,1920]{1,0:T(8,128)(2,1)S(1)} %bitcast.170, bf16[1280,1920]{1,0:T(8,128)(2,1)S(1)} %bitcast.172), kind=kOutput, calls=%fused_computation.8 | convolution fusion | flops 11761745920 | bytes 23592960 | tf_op jit(solution)/shard_map/dot_general | solution.py:210
  236.2 49.2 %shard_map.109 = bf16[2,128,1280]{2,1,0:T(8,128)(2,1)} custom-call(s32[2,18]{1,0:T(2,128)} %broadcast_clamp_fusion.1.own_ref, s32[2,18]{1,0:T(2,128)} %broadcast_clamp_fusion.rest_ref, s32[2,18]{1,0:T(2,128)} %stack.229.src_ref, s32[2]{0:T(128)} %counts_ref.1, bf16[2,16,128,80]{3,2,1,0:T(8,128)(2,1)} %bitcast.173, bf16[8,128,2560]{2,1,0:T(8,128)(2,1)} %bitcast.166, ...), custom_call_target="tpu_custom_call" | custom-call | tf_op jit(solution)/shard_map/pallas_call | solution.py:149
  285.4 4.0 %convolution_convert_fusion.2 = bf16[256,1280]{1,0:T(8,128)(2,1)} fusion(bf16[256,1280]{1,0:T(8,128)(2,1)} %bitcast.174, bf16[1280,1280]{1,0:T(8,128)(2,1)} %all-gather.8.cloned.1.call-done), kind=kOutput, calls=%fused_computation.16 | convolution fusion | flops 839188480 | bytes 4587520 | tf_op jit(solution)/shard_map/dot_general | solution.py:238
  (158 shorter events, 13.8 us)
Async XLA Ops:
  6.5 47.7 %copy-start = (bf16[320,3840]{1,0:T(8,128)(2,1)S(1)}, bf16[320,3840]{1,0:T(8,128)(2,1)}, u32[]{:S(2)}) copy-start(bf16[320,3840]{1,0:T(8,128)(2,1)} %param.20) | copy-start | bytes 7372804
  6.5 47.6 %all-gather.4.cloned.1.call-start = ((), (), s32[]{:S(2)}) async-start(), calls=%async_computation | async-start | bytes 3276800 | tf_op jit(solution)/shard_map/all_gather | solution.py:183
  10.3 6.2 %copy-start.6 = (bf16[1280]{0:T(1024)(128)(2,1)S(1)}, bf16[1280]{0:T(1024)(128)(2,1)}, u32[]{:S(2)}) copy-start(bf16[1280]{0:T(1024)(128)(2,1)} %param.18) | copy-start | bytes 7684
  10.4 6.2 %copy-start.7 = (bf16[1280]{0:T(1024)(128)(2,1)S(1)}, bf16[1280]{0:T(1024)(128)(2,1)}, u32[]{:S(2)}) copy-start(bf16[1280]{0:T(1024)(128)(2,1)} %param.19) | copy-start | bytes 7684
  14.5 40.9 %copy-start.8 = (s32[2,16]{1,0:T(2,128)S(1)}, s32[2,16]{1,0:T(2,128)}, u32[]{:S(2)}) copy-start(s32[2,16]{1,0:T(2,128)} %param.13) | copy-start | bytes 388
  14.5 63.4 %copy-start.9 = (s32[2]{0:T(128)S(1)}, s32[2]{0:T(128)}, u32[]{:S(2)}) copy-start(s32[2]{0:T(128)} %param.15) | copy-start | bytes 28
  16.1 63.4 %copy-start.5 = (s32[2]{0:T(128)S(1)}, s32[2]{0:T(128)}, u32[]{:S(2)}) copy-start(s32[2]{0:T(128)} %counts_ref.1) | copy-start | bytes 28
  17.7 92.9 %all-gather.6.cloned.1.call-start = ((), (), s32[]{:S(2)}) async-start(), calls=%async_computation.1 | async-start | bytes 6144000 | tf_op jit(solution)/shard_map/all_gather | solution.py:26
  55.3 230.1 %all-gather.8.cloned.1.call-start = ((), (), s32[]{:S(2)}) async-start(), calls=%async_computation.2 | async-start | bytes 4096000 | tf_op jit(solution)/shard_map/all_gather | solution.py:240
  58.6 66.2 %collective-permute-start.1 = (s32[3]{0:T(128)S(1)}, s32[3]{0:T(128)S(1)}, u32[]{:S(2)}, u32[]{:S(2)}) collective-permute-start(s32[3]{0:T(128)S(1)} %pad_add_fusion.1), channel_id=1, source_target_pairs={{8,0},{12,4},{16,8},{20,12},{24,16},{28,20},{32,24},{36,28},{40,32... | collective-permute-start | bytes 44 | tf_op jit(solution)/shard_map/ppermute | solution.py:20
  66.2 61.1 %collective-permute-start.3 = (s32[3]{0:T(128)S(1)}, s32[3]{0:T(128)S(1)}, u32[]{:S(2)}, u32[]{:S(2)}) collective-permute-start(s32[3]{0:T(128)S(1)} %pad_add_fusion.2), channel_id=1, source_target_pairs={{4,0},{8,4},{12,8},{16,12},{20,16},{24,20},{28,24},{32,28},{36,32}... | collective-permute-start | bytes 44 | tf_op jit(solution)/shard_map/ppermute | solution.py:20
  71.0 56.3 %collective-permute-start.5 = (s32[3]{0:T(128)S(1)}, s32[3]{0:T(128)S(1)}, u32[]{:S(2)}, u32[]{:S(2)}) collective-permute-start(s32[3]{0:T(128)S(1)} %pad_add_fusion.3), channel_id=1, source_target_pairs={{0,4},{4,8},{8,12},{12,16},{16,20},{20,24},{24,28},{28,32},{32,36}... | collective-permute-start | bytes 44 | tf_op jit(solution)/shard_map/ppermute | solution.py:20
  87.1 17.4 %collective-permute-start.9 = (bf16[2,128,1280]{2,1,0:T(8,128)(2,1)S(1)}, bf16[2,128,1280]{2,1,0:T(8,128)(2,1)S(1)}, u32[]{:S(2)}, u32[]{:S(2)}) collective-permute-start(bf16[2,128,1280]{2,1,0:T(8,128)(2,1)S(1)} %gather_fusion.7), channel_id=1, source_target_pairs={{0,8},{4,12},{8,0},{12,4},{16,24},{20,28},{24,16},{28,20},{32,40},... | collective-permute-start | bytes 1966088 | tf_op jit(solution)/shard_map/ppermute | solution.py:200
  104.6 18.1 %collective-permute-start.10 = (bf16[2,128,1280]{2,1,0:T(8,128)(2,1)S(1)}, bf16[2,128,1280]{2,1,0:T(8,128)(2,1)S(1)}, u32[]{:S(2)}, u32[]{:S(2)}) collective-permute-start(bf16[2,128,1280]{2,1,0:T(8,128)(2,1)S(1)} %broadcast_select_fusion.2), channel_id=1, source_target_pairs={{0,16},{4,20},{8,24},{12,28},{16,0},{20,4},{24,8},{28,12},{32,48},... | collective-permute-start | bytes 1966088 | tf_op jit(solution)/shard_map/ppermute | solution.py:200
  110.6 85.5 %collective-permute-start = (bf16[1280,1920]{1,0:T(8,128)(2,1)}, bf16[1280,1920]{1,0:T(8,128)(2,1)}, u32[]{:S(2)}, u32[]{:S(2)}) collective-permute-start(bf16[1280,1920]{1,0:T(8,128)(2,1)} %all-gather.6.cloned.1.call-done), channel_id=1, source_target_pairs={{0,4},{4,0},{8,12},{12,8},{16,20},{20,16},{24,28},{28,24},{32,36},... | collective-permute-start | bytes 14745608 | tf_op jit(solution)/shard_map/ppermute | solution.py:30
  122.7 20.2 %collective-permute-start.7 = (s32[3]{0:T(128)S(1)}, s32[3]{0:T(128)S(1)}, u32[]{:S(2)}, u32[]{:S(2)}) collective-permute-start(s32[3]{0:T(128)S(1)} %pad_add_fusion.4), channel_id=1, source_target_pairs={{0,8},{4,12},{8,16},{12,20},{16,24},{20,28},{24,32},{28,36},{32,40... | collective-permute-start | bytes 44 | tf_op jit(solution)/shard_map/ppermute | solution.py:20
  124.8 17.2 %collective-permute-start.11 = (bf16[2,128,1280]{2,1,0:T(8,128)(2,1)S(1)}, bf16[2,128,1280]{2,1,0:T(8,128)(2,1)S(1)}, u32[]{:S(2)}, u32[]{:S(2)}) collective-permute-start(bf16[2,128,1280]{2,1,0:T(8,128)(2,1)S(1)} %broadcast_select_fusion.3), channel_id=1, source_target_pairs={{0,64},{4,68},{8,72},{12,76},{16,80},{20,84},{24,88},{28,92},{32,9... | collective-permute-start | bytes 1966088 | tf_op jit(solution)/shard_map/ppermute | solution.py:200
  130.7 38.1 %collective-permute-start.2 = (bf16[3,128,1280]{2,1,0:T(8,128)(2,1)}, bf16[3,128,1280]{2,1,0:T(8,128)(2,1)}, u32[]{:S(2)}, u32[]{:S(2)}) collective-permute-start(bf16[3,128,1280]{2,1,0:T(8,128)(2,1)} %gather_fusion.3), channel_id=1, source_target_pairs={{0,8},{4,12},{8,16},{12,20},{16,24},{20,28},{24,32},{28,36},{32,40... | collective-permute-start | bytes 2949128 | tf_op jit(solution)/shard_map/ppermute | solution.py:20
  142.2 29.8 %collective-permute-start.12 = (bf16[2,128,1280]{2,1,0:T(8,128)(2,1)S(1)}, bf16[2,128,1280]{2,1,0:T(8,128)(2,1)S(1)}, u32[]{:S(2)}, u32[]{:S(2)}) collective-permute-start(bf16[2,128,1280]{2,1,0:T(8,128)(2,1)S(1)} %broadcast_select_fusion.4), channel_id=1, source_target_pairs={{0,32},{4,36},{8,40},{12,44},{16,48},{20,52},{24,56},{28,60},{32,0... | collective-permute-start | bytes 1966088 | tf_op jit(solution)/shard_map/ppermute | solution.py:200
  145.4 45.7 %collective-permute-start.4 = (bf16[3,128,1280]{2,1,0:T(8,128)(2,1)S(1)}, bf16[3,128,1280]{2,1,0:T(8,128)(2,1)}, u32[]{:S(2)}, u32[]{:S(2)}) collective-permute-start(bf16[3,128,1280]{2,1,0:T(8,128)(2,1)S(1)} %gather_fusion.4), channel_id=1, source_target_pairs={{0,4},{4,8},{8,12},{12,16},{16,20},{20,24},{24,28},{28,32},{32,36}... | collective-permute-start | bytes 2949128 | tf_op jit(solution)/shard_map/ppermute | solution.py:20
  150.7 41.7 %collective-permute-start.6 = (bf16[3,128,1280]{2,1,0:T(8,128)(2,1)}, bf16[3,128,1280]{2,1,0:T(8,128)(2,1)}, u32[]{:S(2)}, u32[]{:S(2)}) collective-permute-start(bf16[3,128,1280]{2,1,0:T(8,128)(2,1)} %gather_fusion.5), channel_id=1, source_target_pairs={{4,0},{8,4},{12,8},{16,12},{20,16},{24,20},{28,24},{32,28},{36,32}... | collective-permute-start | bytes 2949128 | tf_op jit(solution)/shard_map/ppermute | solution.py:20
  156.4 39.7 %slice-start = ((s8[4915200]{0:T(1024)(128)(4,1)}), s8[720896]{0:T(1024)(128)(4,1)S(1)}, s32[]{:S(2)}) async-start(s8[4915200]{0:T(1024)(128)(4,1)} %bitcast.167), calls=%async_computation.3 | async-start | bytes 1441792
  168.8 24.9 %collective-permute-start.8 = (bf16[3,128,1280]{2,1,0:T(8,128)(2,1)}, bf16[3,128,1280]{2,1,0:T(8,128)(2,1)S(1)}, u32[]{:S(2)}, u32[]{:S(2)}) collective-permute-start(bf16[3,128,1280]{2,1,0:T(8,128)(2,1)} %gather_fusion.6), channel_id=1, source_target_pairs={{8,0},{12,4},{16,8},{20,12},{24,16},{28,20},{32,24},{36,28},{40,32... | collective-permute-start | bytes 2949128 | tf_op jit(solution)/shard_map/ppermute | solution.py:20
  172.0 0.9 copy-start.3
  174.0 22.1 %slice-start.1 = ((s8[4915200]{0:T(1024)(128)(4,1)}), s8[4194304]{0:T(1024)(128)(4,1)S(1)}, s32[]{:S(2)}) async-start(s8[4915200]{0:T(1024)(128)(4,1)} %bitcast.167), calls=%async_computation.4 | async-start | bytes 8388608
  174.0 19.7 %collective-permute-start.13 = (bf16[2,128,1280]{2,1,0:T(8,128)(2,1)S(1)}, bf16[2,128,1280]{2,1,0:T(8,128)(2,1)S(1)}, u32[]{:S(2)}, u32[]{:S(2)}) collective-permute-start(bf16[2,128,1280]{2,1,0:T(8,128)(2,1)S(1)} %broadcast_select_fusion.5), channel_id=1, source_target_pairs={{0,4},{4,0},{8,12},{12,8},{16,20},{20,16},{24,28},{28,24},{32,36},... | collective-permute-start | bytes 1966088 | tf_op jit(solution)/shard_map/ppermute | solution.py:200
  194.0 2.1 copy-start.4
  196.1 7.1 %copy-start.2 = (bf16[256,1280]{1,0:T(8,128)(2,1)S(1)}, bf16[256,1280]{1,0:T(8,128)(2,1)}, u32[]{:S(2)}) copy-start(bf16[256,1280]{1,0:T(8,128)(2,1)} %fusion.10) | copy-start | bytes 1966084
  207.7 13.9 %slice-start.2 = ((s8[4915200]{0:T(1024)(128)(4,1)}), s8[4194304]{0:T(1024)(128)(4,1)S(1)}, s32[]{:S(2)}) async-start(s8[4915200]{0:T(1024)(128)(4,1)} %bitcast.169), calls=%async_computation.5 | async-start | bytes 8388608
  207.8 13.9 %slice-start.4 = ((s8[4915200]{0:T(1024)(128)(4,1)}), s8[4194304]{0:T(1024)(128)(4,1)S(1)}, s32[]{:S(2)}) async-start(s8[4915200]{0:T(1024)(128)(4,1)} %bitcast.171), calls=%async_computation.7 | async-start | bytes 8388608
  207.8 13.9 %slice-start.6 = ((s8[4587520]{0:T(1024)(128)(4,1)}), s8[4194304]{0:T(1024)(128)(4,1)S(1)}, s32[]{:S(2)}) async-start(s8[4587520]{0:T(1024)(128)(4,1)} %bitcast.175), calls=%async_computation.9 | async-start | bytes 8388608
  209.0 12.6 %slice-start.3 = ((s8[4915200]{0:T(1024)(128)(4,1)}), s8[720896]{0:T(1024)(128)(4,1)S(1)}, s32[]{:S(2)}) async-start(s8[4915200]{0:T(1024)(128)(4,1)} %bitcast.169), calls=%async_computation.6 | async-start | bytes 1441792
  209.0 12.6 %slice-start.5 = ((s8[4915200]{0:T(1024)(128)(4,1)}), s8[720896]{0:T(1024)(128)(4,1)S(1)}, s32[]{:S(2)}) async-start(s8[4915200]{0:T(1024)(128)(4,1)} %bitcast.171), calls=%async_computation.8 | async-start | bytes 1441792
  209.0 12.7 %slice-start.7 = ((s8[4587520]{0:T(1024)(128)(4,1)}), s8[393216]{0:T(1024)(128)(4,1)S(1)}, s32[]{:S(2)}) async-start(s8[4587520]{0:T(1024)(128)(4,1)} %bitcast.175), calls=%async_computation.10 | async-start | bytes 786432
  236.2 53.2 %copy-start.1 = (bf16[320,3840]{1,0:T(8,128)(2,1)S(1)}, bf16[320,3840]{1,0:T(8,128)(2,1)}, u32[]{:S(2)}) copy-start(bf16[320,3840]{1,0:T(8,128)(2,1)} %param.20) | copy-start | bytes 7372804
Sparse Core Ops, SparseCore 0:
  17.8 36.3 all-gather.3
  55.8 54.7 all-gather.5
  112.3 40.8 all-gather.7

commit v16 on v10

--- a/solution.py
+++ b/solution.py
@@ -168,7 +168,7 @@
     global_rows = group_rows[global_ids % group_tiles]
     owners = global_ids // group_tiles
     seq_bits = seq_size.bit_length() - 1
-    bit_order = [b for b in (1, 2) if b < seq_bits]
+    bit_order = [b for b in (0, 1, 2) if b < seq_bits]
     bit_order += [b for b in range(seq_bits - 1, -1, -1) if b not in bit_order]
     done_bits = 0
     for bit in bit_order:

time: 292 us -> 313 us (1.072)
  the two profiles are of different devices: /device:TPU:24 before, /device:TPU:4 now
where the time goes in v16:
time: 313 us; the launch traced here: 307 us
  waiting for transfers between devices  124 us (40%)
  Pallas kernels  49.4 us (16%)
  local copies, waits for them, and re-layouts  32.7 us (10%)
  matrix products  31.6 us (10%)
  starting transfers between devices  28.1 us (9%)
  other arithmetic  27.7 us (9%)
  between operations  13.5 us (4%)
    pallas_call x1, Pallas kernels, attend(): pl.pallas_call(attention_kernel, grid_spec=grid_spec, out_shape=jax.Shape...  49.4 us
    all_gather x1, waiting for transfers between devices, local(): lax.all_gather(normed, 'fsdp', axis=0, tiled=True)  37.8 us
    ppermute x5, waiting for transfers between devices, local(): lax.ppermute(global_rows, 'seq', [(i, i ^ step) for i in range(seq_size)])  34.2 us
    all_gather x1, waiting for transfers between devices, gathered_weight(): lax.all_gather(lax.dynamic_slice_in_dim(shard, core * half, half, 1), 'fs...  30.1 us
    ppermute x8, starting transfers between devices, passed_along(): return lax.ppermute(block, axis, route)  23.8 us
    dot_general x1, matrix products, local(): jnp.dot(window_rows.reshape(-1, feat_width), w_full[:, feat_width:], pref...  23.6 us
    ppermute x8, waiting for transfers between devices, passed_along(): return lax.ppermute(block, axis, route)  21.8 us
    gather x4, local copies, waits for them, and re-layouts, local(): near_blocks.append(passed_along(group_rows[asked], 'seq', -reach))  12.6 us
  transfers between devices with their start and end apart: 17, of which 9 were waited for; matrix products, arithmetic and copies ran while one was open for 23% of the time, Pallas kernels for 16%

profile of v16, /device:TPU:4, one launch (start us, length us, event | category | flops | bytes accessed | tf_op | source)
XLA Modules:
  0.0 306.8 jit_solution(1041635042281516482)
XLA Ops:
  6.5 0.8 compare_select_fusion.1
  7.4 0.8 convert_element_type.99
  8.9 4.1 %gather_fusion.2 = bf16[256,1280]{1,0:T(8,128)(2,1)} fusion(bf16[512,1280]{1,0:T(8,128)(2,1)} %param.17, s32[1024]{0:T(1024)S(1)} %get-tuple-element.43), kind=kCustom, calls=%fused_computation.2 | custom fusion | bytes 1311744 | tf_op jit(solution)/shard_map/gather | solution.py:51
  13.0 2.1 gather_fusion.1
  15.0 1.9 convert_reduce_fusion
  17.2 1.2 fusion.11
  18.5 37.8 %all-gather.4.cloned.1.call-done = bf16[1024,1280]{1,0:T(8,128)(2,1)} async-done(((bf16[256,1280]{1,0:T(8,128)(2,1)}), bf16[1024,1280]{1,0:T(8,128)(2,1)}) %all-gather.4.cloned.1.call-update) | async-done | bytes 2621456 | tf_op jit(solution)/shard_map/all_gather | solution.py:161
  56.3 1.2 constant_dynamic-slice_fusion
  58.7 1.8 pad_add_fusion.2
  60.5 4.6 %collective-permute-start.1 = (s32[3]{0:T(128)S(1)}, s32[3]{0:T(128)S(1)}, u32[]{:S(2)}, u32[]{:S(2)}) collective-permute-start(s32[3]{0:T(128)S(1)} %pad_add_fusion.2), channel_id=1, source_target_pairs={{8,0},{12,4},{16,8},{20,12},{24,16},{28,20},{32,24},{36,28},{40,32... | collective-permute-start | bytes 44 | tf_op jit(solution)/shard_map/ppermute | solution.py:20
  66.0 1.8 pad_add_fusion.3
  67.9 1.9 collective-permute-start.3
  70.7 1.8 pad_add_fusion.4
  72.5 2.4 collective-permute-start.5
  76.0 0.8 gather_fusion
  76.9 2.4 gather_fusion.7
  80.6 1.1 collective-permute-done.9
  82.2 30.1 %all-gather.6.cloned.1.call-done = bf16[1280,1920]{1,0:T(8,128)(2,1)} async-done(((bf16[320,1920]{1,0:T(8,128)(2,1)}), bf16[1280,1920]{1,0:T(8,128)(2,1)}) %all-gather.6.cloned.1.call-update) | async-done | bytes 4915216 | tf_op jit(solution)/shard_map/all_gather | solution.py:26
  112.3 1.9 pad_add_fusion.5
  114.2 3.4 %collective-permute-start.7 = (s32[3]{0:T(128)S(1)}, s32[3]{0:T(128)S(1)}, u32[]{:S(2)}, u32[]{:S(2)}) collective-permute-start(s32[3]{0:T(128)S(1)} %pad_add_fusion.5), channel_id=1, source_target_pairs={{0,8},{4,12},{8,16},{12,20},{16,24},{20,28},{24,32},{28,36},{32,40... | collective-permute-start | bytes 44 | tf_op jit(solution)/shard_map/ppermute | solution.py:20
  117.8 2.8 collective-permute-start.11
  120.6 1.2 collective-permute-done.7
  121.7 2.5 gather_fusion.3
  124.2 1.9 collective-permute-start.2
  126.2 16.2 %collective-permute-done.11 = bf16[2,128,1280]{2,1,0:T(8,128)(2,1)S(1)} collective-permute-done((bf16[2,128,1280]{2,1,0:T(8,128)(2,1)S(1)}, bf16[2,128,1280]{2,1,0:T(8,128)(2,1)S(1)}, u32[]{:S(2)}, u32[]{:S(2)}) %collective-permute-start.11) | collective-permute-done | bytes 655392 | tf_op jit(solution)/shard_map/ppermute | solution.py:178
  142.4 0.9 copy-done.7
  143.2 1.2 broadcast_select_fusion.4
  144.6 3.4 %gather_fusion.4 = bf16[3,128,1280]{2,1,0:T(8,128)(2,1)} fusion(bf16[8,128,1280]{2,1,0:T(8,128)(2,1)} %bitcast.111, s32[1024]{0:T(1024)S(1)} %pad_clamp_fusion.3), kind=kCustom, calls=%fused_computation.4 | custom fusion | bytes 1966092 | tf_op jit(solution)/shard_map/gather | solution.py:185
  148.0 1.9 collective-permute-start.4
  149.9 3.3 %gather_fusion.5 = bf16[3,128,1280]{2,1,0:T(8,128)(2,1)} fusion(bf16[8,128,1280]{2,1,0:T(8,128)(2,1)} %bitcast.112, s32[1024]{0:T(1024)S(1)} %pad_clamp_fusion.2), kind=kCustom, calls=%fused_computation.5 | custom fusion | bytes 1966092 | tf_op jit(solution)/shard_map/gather | solution.py:185
  153.3 5.7 %collective-permute-start.6 = (bf16[3,128,1280]{2,1,0:T(8,128)(2,1)}, bf16[3,128,1280]{2,1,0:T(8,128)(2,1)}, u32[]{:S(2)}, u32[]{:S(2)}) collective-permute-start(bf16[3,128,1280]{2,1,0:T(8,128)(2,1)} %gather_fusion.5), channel_id=1, source_target_pairs={{4,0},{8,4},{12,8},{16,12},{20,16},{24,20},{28,24},{32,28},{36,32}... | collective-permute-start | bytes 2949128 | tf_op jit(solution)/shard_map/ppermute | solution.py:20
  159.0 3.3 %gather_fusion.6 = bf16[3,128,1280]{2,1,0:T(8,128)(2,1)} fusion(bf16[8,128,1280]{2,1,0:T(8,128)(2,1)} %bitcast.113, s32[1024]{0:T(1024)S(1)} %pad_clamp_fusion.1), kind=kCustom, calls=%fused_computation.6 | custom fusion | bytes 1966092 | tf_op jit(solution)/shard_map/gather | solution.py:185
  162.3 2.1 constant_dynamic-update-slice_fusion.4
  164.4 8.2 %collective-permute-done.2 = bf16[3,128,1280]{2,1,0:T(8,128)(2,1)S(1)} collective-permute-done((bf16[3,128,1280]{2,1,0:T(8,128)(2,1)S(1)}, bf16[3,128,1280]{2,1,0:T(8,128)(2,1)S(1)}, u32[]{:S(2)}, u32[]{:S(2)}) %collective-permute-start.2) | collective-permute-done | bytes 983072 | tf_op jit(solution)/shard_map/ppermute | solution.py:20
  172.6 1.9 collective-permute-start.8
  174.6 0.8 copy-done.6
  175.4 1.3 broadcast_select_fusion.5
  177.0 4.9 %collective-permute-done.4 = bf16[3,128,1280]{2,1,0:T(8,128)(2,1)} collective-permute-done((bf16[3,128,1280]{2,1,0:T(8,128)(2,1)}, bf16[3,128,1280]{2,1,0:T(8,128)(2,1)}, u32[]{:S(2)}, u32[]{:S(2)}) %collective-permute-start.4) | collective-permute-done | bytes 983072 | tf_op jit(solution)/shard_map/ppermute | solution.py:20
  181.9 1.3 constant_dynamic-update-slice_fusion.2
  183.2 1.3 constant_dynamic-update-slice_fusion.1
  184.5 7.5 %collective-permute-done.8 = bf16[3,128,1280]{2,1,0:T(8,128)(2,1)S(1)} collective-permute-done((bf16[3,128,1280]{2,1,0:T(8,128)(2,1)}, bf16[3,128,1280]{2,1,0:T(8,128)(2,1)S(1)}, u32[]{:S(2)}, u32[]{:S(2)}) %collective-permute-start.8) | collective-permute-done | bytes 983072 | tf_op jit(solution)/shard_map/ppermute | solution.py:20
  192.1 16.9 %collective-permute-done.13 = bf16[2,128,1280]{2,1,0:T(8,128)(2,1)S(1)} collective-permute-done((bf16[2,128,1280]{2,1,0:T(8,128)(2,1)S(1)}, bf16[2,128,1280]{2,1,0:T(8,128)(2,1)S(1)}, u32[]{:S(2)}, u32[]{:S(2)}) %collective-permute-start.13) | collective-permute-done | bytes 655392 | tf_op jit(solution)/shard_map/ppermute | solution.py:178
  209.2 2.9 copy-done.5
  212.1 7.1 %broadcast_select_fusion = (bf16[1280,1920]{1,0:T(8,128)(2,1)}, bf16[1280,1920]{1,0:T(8,128)(2,1)}) fusion(bf16[1280,1920]{1,0:T(8,128)(2,1)} %collective-permute-done, bf16[1280,1920]{1,0:T(8,128)(2,1)S(1)} %bitcast.117, pred[]{:T(512)S(6)} %eq.161), kind=kLoop, calls=%fused_computation.11 | loop fusion | flops 4915200 | bytes 19660800 | tf_op jit(solution)/shard_map/jit(_where)/select_n | solution.py:32
  219.3 3.9 %fusion.3 = bf16[256,1280]{1,0:T(8,128)(2,1)} fusion(bf16[256,1280]{1,0:T(8,128)(2,1)S(1)} %copy-done.4, bf16[1280,1920]{1,0:T(8,128)(2,1)} %get-tuple-element.32), kind=kOutput, calls=%fused_computation.15 | convolution fusion | flops 839188480 | bytes 4587520 | tf_op jit(solution)/shard_map/dot_general | solution.py:194
  223.2 23.6 %convolution_convert_fusion = bf16[2816,2560]{1,0:T(8,128)(2,1)} fusion(bf16[2816,1280]{1,0:T(8,128)(2,1)} %bitcast.118, bf16[1280,1920]{1,0:T(8,128)(2,1)S(1)} %copy-done.3, bf16[1280,1920]{1,0:T(8,128)(2,1)} %get-tuple-element.32), kind=kOutput, calls=%fused_computation.8 | convolution fusion | flops 18475253760 | bytes 31457280 | tf_op jit(solution)/shard_map/dot_general | solution.py:190
  246.9 49.4 %shard_map.109 = bf16[2,128,1280]{2,1,0:T(8,128)(2,1)} custom-call(s32[2,18]{1,0:T(2,128)} %pad_add_fusion.1.slots_ref, s32[2]{0:T(128)} %counts_ref.1, bf16[2,128,1280]{2,1,0:T(8,128)(2,1)} %bitcast.119, bf16[22,128,2560]{2,1,0:T(8,128)(2,1)} %bitcast.115), custom_call_target="tpu_custom_call" | custom-call | tf_op jit(solution)/shard_map/pallas_call | solution.py:127
  296.3 4.0 %convolution_convert_fusion.1 = bf16[256,1280]{1,0:T(8,128)(2,1)} fusion(bf16[256,1280]{1,0:T(8,128)(2,1)} %bitcast.120, bf16[1280,1280]{1,0:T(8,128)(2,1)} %all-gather.8.cloned.1.call-done), kind=kOutput, calls=%fused_computation.16 | convolution fusion | flops 839188480 | bytes 4587520 | tf_op jit(solution)/shard_map/dot_general | solution.py:215
  (92 shorter events, 8.1 us)
Async XLA Ops:
  6.5 49.7 %copy-start = (bf16[320,3840]{1,0:T(8,128)(2,1)S(1)}, bf16[320,3840]{1,0:T(8,128)(2,1)}, u32[]{:S(2)}) copy-start(bf16[320,3840]{1,0:T(8,128)(2,1)} %param.20) | copy-start | bytes 7372804
  6.5 6.4 %copy-start.2 = (bf16[256,1280]{1,0:T(8,128)(2,1)S(1)}, bf16[256,1280]{1,0:T(8,128)(2,1)}, u32[]{:S(2)}) copy-start(bf16[256,1280]{1,0:T(8,128)(2,1)} %param.16) | copy-start | bytes 1966084
  6.5 49.7 %all-gather.4.cloned.1.call-start = ((), (), s32[]{:S(2)}) async-start(), calls=%async_computation | async-start | bytes 3276800 | tf_op jit(solution)/shard_map/all_gather | solution.py:161
  15.0 42.5 %copy-start.8 = (s32[2,16]{1,0:T(2,128)S(1)}, s32[2,16]{1,0:T(2,128)}, u32[]{:S(2)}) copy-start(s32[2,16]{1,0:T(2,128)} %param.13) | copy-start | bytes 388
  15.0 61.9 %copy-start.9 = (s32[2]{0:T(128)S(1)}, s32[2]{0:T(128)}, u32[]{:S(2)}) copy-start(s32[2]{0:T(128)} %param.15) | copy-start | bytes 28
  18.4 93.9 %all-gather.6.cloned.1.call-start = ((), (), s32[]{:S(2)}) async-start(), calls=%async_computation.1 | async-start | bytes 6144000 | tf_op jit(solution)/shard_map/all_gather | solution.py:26
  57.4 238.8 %all-gather.8.cloned.1.call-start = ((), (), s32[]{:S(2)}) async-start(), calls=%async_computation.2 | async-start | bytes 4096000 | tf_op jit(solution)/shard_map/all_gather | solution.py:217
  60.5 53.6 %collective-permute-start.1 = (s32[3]{0:T(128)S(1)}, s32[3]{0:T(128)S(1)}, u32[]{:S(2)}, u32[]{:S(2)}) collective-permute-start(s32[3]{0:T(128)S(1)} %pad_add_fusion.2), channel_id=1, source_target_pairs={{8,0},{12,4},{16,8},{20,12},{24,16},{28,20},{32,24},{36,28},{40,32... | collective-permute-start | bytes 44 | tf_op jit(solution)/shard_map/ppermute | solution.py:20
  67.9 49.7 %collective-permute-start.3 = (s32[3]{0:T(128)S(1)}, s32[3]{0:T(128)S(1)}, u32[]{:S(2)}, u32[]{:S(2)}) collective-permute-start(s32[3]{0:T(128)S(1)} %pad_add_fusion.3), channel_id=1, source_target_pairs={{4,0},{8,4},{12,8},{16,12},{20,16},{24,20},{28,24},{32,28},{36,32}... | collective-permute-start | bytes 44 | tf_op jit(solution)/shard_map/ppermute | solution.py:20
  72.5 48.1 %collective-permute-start.5 = (s32[3]{0:T(128)S(1)}, s32[3]{0:T(128)S(1)}, u32[]{:S(2)}, u32[]{:S(2)}) collective-permute-start(s32[3]{0:T(128)S(1)} %pad_add_fusion.4), channel_id=1, source_target_pairs={{0,4},{4,8},{8,12},{12,16},{16,20},{20,24},{24,28},{28,32},{32,36}... | collective-permute-start | bytes 44 | tf_op jit(solution)/shard_map/ppermute | solution.py:20
  79.3 2.4 collective-permute-start.9
  81.8 35.8 %collective-permute-start.10 = (bf16[2,128,1280]{2,1,0:T(8,128)(2,1)S(1)}, bf16[2,128,1280]{2,1,0:T(8,128)(2,1)S(1)}, u32[]{:S(2)}, u32[]{:S(2)}) collective-permute-start(bf16[2,128,1280]{2,1,0:T(8,128)(2,1)S(1)} %broadcast_select_fusion.2), channel_id=1, source_target_pairs={{0,8},{4,12},{8,0},{12,4},{16,24},{20,28},{24,16},{28,20},{32,40},... | collective-permute-start | bytes 1966088 | tf_op jit(solution)/shard_map/ppermute | solution.py:178
  112.3 99.8 %collective-permute-start = (bf16[1280,1920]{1,0:T(8,128)(2,1)}, bf16[1280,1920]{1,0:T(8,128)(2,1)}, u32[]{:S(2)}, u32[]{:S(2)}) collective-permute-start(bf16[1280,1920]{1,0:T(8,128)(2,1)} %all-gather.6.cloned.1.call-done), channel_id=1, source_target_pairs={{0,4},{4,0},{8,12},{12,8},{16,20},{20,16},{24,28},{28,24},{32,36},... | collective-permute-start | bytes 14745608 | tf_op jit(solution)/shard_map/ppermute | solution.py:30
  114.2 7.6 %collective-permute-start.7 = (s32[3]{0:T(128)S(1)}, s32[3]{0:T(128)S(1)}, u32[]{:S(2)}, u32[]{:S(2)}) collective-permute-start(s32[3]{0:T(128)S(1)} %pad_add_fusion.5), channel_id=1, source_target_pairs={{0,8},{4,12},{8,16},{12,20},{16,24},{20,28},{24,32},{28,36},{32,40... | collective-permute-start | bytes 44 | tf_op jit(solution)/shard_map/ppermute | solution.py:20
  117.8 24.6 %collective-permute-start.11 = (bf16[2,128,1280]{2,1,0:T(8,128)(2,1)S(1)}, bf16[2,128,1280]{2,1,0:T(8,128)(2,1)S(1)}, u32[]{:S(2)}, u32[]{:S(2)}) collective-permute-start(bf16[2,128,1280]{2,1,0:T(8,128)(2,1)S(1)} %broadcast_select_fusion.3), channel_id=1, source_target_pairs={{0,16},{4,20},{8,24},{12,28},{16,0},{20,4},{24,8},{28,12},{32,48},... | collective-permute-start | bytes 1966088 | tf_op jit(solution)/shard_map/ppermute | solution.py:178
  124.2 48.4 %collective-permute-start.2 = (bf16[3,128,1280]{2,1,0:T(8,128)(2,1)S(1)}, bf16[3,128,1280]{2,1,0:T(8,128)(2,1)S(1)}, u32[]{:S(2)}, u32[]{:S(2)}) collective-permute-start(bf16[3,128,1280]{2,1,0:T(8,128)(2,1)S(1)} %gather_fusion.3), channel_id=1, source_target_pairs={{0,8},{4,12},{8,16},{12,20},{16,24},{20,28},{24,32},{28,36},{32,40... | collective-permute-start | bytes 2949128 | tf_op jit(solution)/shard_map/ppermute | solution.py:20
  142.4 0.9 copy-start.7
  144.5 30.1 %collective-permute-start.12 = (bf16[2,128,1280]{2,1,0:T(8,128)(2,1)S(1)}, bf16[2,128,1280]{2,1,0:T(8,128)(2,1)S(1)}, u32[]{:S(2)}, u32[]{:S(2)}) collective-permute-start(bf16[2,128,1280]{2,1,0:T(8,128)(2,1)S(1)} %broadcast_select_fusion.4), channel_id=1, source_target_pairs={{0,64},{4,68},{8,72},{12,76},{16,80},{20,84},{24,88},{28,92},{32,9... | collective-permute-start | bytes 1966088 | tf_op jit(solution)/shard_map/ppermute | solution.py:178
  148.0 33.9 %collective-permute-start.4 = (bf16[3,128,1280]{2,1,0:T(8,128)(2,1)}, bf16[3,128,1280]{2,1,0:T(8,128)(2,1)}, u32[]{:S(2)}, u32[]{:S(2)}) collective-permute-start(bf16[3,128,1280]{2,1,0:T(8,128)(2,1)} %gather_fusion.4), channel_id=1, source_target_pairs={{0,4},{4,8},{8,12},{12,16},{16,20},{20,24},{24,28},{28,32},{32,36}... | collective-permute-start | bytes 2949128 | tf_op jit(solution)/shard_map/ppermute | solution.py:20
  153.3 29.9 %collective-permute-start.6 = (bf16[3,128,1280]{2,1,0:T(8,128)(2,1)}, bf16[3,128,1280]{2,1,0:T(8,128)(2,1)}, u32[]{:S(2)}, u32[]{:S(2)}) collective-permute-start(bf16[3,128,1280]{2,1,0:T(8,128)(2,1)} %gather_fusion.5), channel_id=1, source_target_pairs={{4,0},{8,4},{12,8},{16,12},{20,16},{24,20},{28,24},{32,28},{36,32}... | collective-permute-start | bytes 2949128 | tf_op jit(solution)/shard_map/ppermute | solution.py:20
  162.3 49.8 %slice-start = ((s8[4915200]{0:T(1024)(128)(4,1)}), s8[4194304]{0:T(1024)(128)(4,1)S(1)}, s32[]{:S(2)}) async-start(s8[4915200]{0:T(1024)(128)(4,1)} %bitcast.116), calls=%async_computation.3 | async-start | bytes 8388608
  172.6 19.4 %collective-permute-start.8 = (bf16[3,128,1280]{2,1,0:T(8,128)(2,1)}, bf16[3,128,1280]{2,1,0:T(8,128)(2,1)S(1)}, u32[]{:S(2)}, u32[]{:S(2)}) collective-permute-start(bf16[3,128,1280]{2,1,0:T(8,128)(2,1)} %gather_fusion.6), channel_id=1, source_target_pairs={{8,0},{12,4},{16,8},{20,12},{24,16},{28,20},{32,24},{36,28},{40,32... | collective-permute-start | bytes 2949128 | tf_op jit(solution)/shard_map/ppermute | solution.py:20
  174.6 0.8 copy-start.6
  175.4 36.7 %slice-start.1 = ((s8[4915200]{0:T(1024)(128)(4,1)}), s8[720896]{0:T(1024)(128)(4,1)S(1)}, s32[]{:S(2)}) async-start(s8[4915200]{0:T(1024)(128)(4,1)} %bitcast.116), calls=%async_computation.4 | async-start | bytes 1441792
  176.7 32.2 %collective-permute-start.13 = (bf16[2,128,1280]{2,1,0:T(8,128)(2,1)S(1)}, bf16[2,128,1280]{2,1,0:T(8,128)(2,1)S(1)}, u32[]{:S(2)}, u32[]{:S(2)}) collective-permute-start(bf16[2,128,1280]{2,1,0:T(8,128)(2,1)S(1)} %broadcast_select_fusion.5), channel_id=1, source_target_pairs={{0,32},{4,36},{8,40},{12,44},{16,48},{20,52},{24,56},{28,60},{32,0... | collective-permute-start | bytes 1966088 | tf_op jit(solution)/shard_map/ppermute | solution.py:178
  209.2 2.9 copy-start.5
  212.1 7.2 %copy-start.4 = (bf16[256,1280]{1,0:T(8,128)(2,1)S(1)}, bf16[256,1280]{1,0:T(8,128)(2,1)}, u32[]{:S(2)}) copy-start(bf16[256,1280]{1,0:T(8,128)(2,1)} %fusion.11) | copy-start | bytes 1966084
  219.3 3.9 %copy-start.3 = (bf16[1280,1920]{1,0:T(8,128)(2,1)S(1)}, bf16[1280,1920]{1,0:T(8,128)(2,1)}, u32[]{:S(2)}) copy-start(bf16[1280,1920]{1,0:T(8,128)(2,1)} %get-tuple-element.31) | copy-start | bytes 14745604
  246.9 53.4 %copy-start.1 = (bf16[320,3840]{1,0:T(8,128)(2,1)S(1)}, bf16[320,3840]{1,0:T(8,128)(2,1)}, u32[]{:S(2)}) copy-start(bf16[320,3840]{1,0:T(8,128)(2,1)} %param.20) | copy-start | bytes 7372804
Sparse Core Ops, SparseCore 0:
  18.5 37.6 all-gather.3
  57.9 54.3 all-gather.5
  114.0 41.0 all-gather.7

commit v17 on v16

--- a/solution.py
+++ b/solution.py
@@ -168,7 +168,7 @@
     global_rows = group_rows[global_ids % group_tiles]
     owners = global_ids // group_tiles
     seq_bits = seq_size.bit_length() - 1
-    bit_order = [b for b in (0, 1, 2) if b < seq_bits]
+    bit_order = [b for b in (2, 1) if b < seq_bits]
     bit_order += [b for b in range(seq_bits - 1, -1, -1) if b not in bit_order]
     done_bits = 0
     for bit in bit_order:

time: 313 us -> 292 us (0.933)
  the two profiles are of different devices: /device:TPU:4 before, /device:TPU:24 now
where the time goes in v17:
time: 292 us; the launch traced here: 289 us
  waiting for transfers between devices  101 us (35%)
  Pallas kernels  52.5 us (18%)
  local copies, waits for them, and re-layouts  32.5 us (11%)
  matrix products  31.5 us (11%)
  starting transfers between devices  30.6 us (10%)
  other arithmetic  27.6 us (9%)
  between operations  13.5 us (5%)
    pallas_call x1, Pallas kernels, attend(): pl.pallas_call(attention_kernel, grid_spec=grid_spec, out_shape=jax.Shape...  52.5 us
    all_gather x1, waiting for transfers between devices, local(): lax.all_gather(normed, 'fsdp', axis=0, tiled=True)  37.5 us
    ppermute x5, waiting for transfers between devices, local(): lax.ppermute(global_rows, 'seq', [(i, i ^ step) for i in range(seq_size)])  35.3 us
    dot_general x1, matrix products, local(): jnp.dot(window_rows.reshape(-1, feat_width), w_full[:, feat_width:], pref...  23.6 us
    ppermute x8, starting transfers between devices, passed_along(): return lax.ppermute(block, axis, route)  23.1 us
    all_gather x1, waiting for transfers between devices, gathered_weight(): lax.all_gather(lax.dynamic_slice_in_dim(shard, core * half, half, 1), 'fs...  15.2 us
    gather x4, local copies, waits for them, and re-layouts, local(): near_blocks.append(passed_along(group_rows[asked], 'seq', -reach))  12.5 us
    ppermute x8, waiting for transfers between devices, passed_along(): return lax.ppermute(block, axis, route)  12.4 us
  transfers between devices with their start and end apart: 17, of which 6 were waited for; matrix products, arithmetic and copies ran while one was open for 24% of the time, Pallas kernels for 18%

profile of v17, /device:TPU:24, one launch (start us, length us, event | category | flops | bytes accessed | tf_op | source)
XLA Modules:
  0.0 288.9 jit_solution(9488438923117109247)
XLA Ops:
  6.5 0.8 compare_select_fusion.1
  7.4 0.8 convert_element_type.99
  8.9 4.1 %gather_fusion.2 = bf16[256,1280]{1,0:T(8,128)(2,1)} fusion(bf16[512,1280]{1,0:T(8,128)(2,1)} %param.17, s32[1024]{0:T(1024)S(1)} %get-tuple-element.43), kind=kCustom, calls=%fused_computation.2 | custom fusion | bytes 1311744 | tf_op jit(solution)/shard_map/gather | solution.py:51
  13.0 2.1 gather_fusion.1
  15.0 1.9 convert_reduce_fusion
  17.2 1.2 fusion.11
  18.5 37.5 %all-gather.4.cloned.1.call-done = bf16[1024,1280]{1,0:T(8,128)(2,1)} async-done(((bf16[256,1280]{1,0:T(8,128)(2,1)}), bf16[1024,1280]{1,0:T(8,128)(2,1)}) %all-gather.4.cloned.1.call-update) | async-done | bytes 2621456 | tf_op jit(solution)/shard_map/all_gather | solution.py:161
  56.0 1.2 constant_dynamic-slice_fusion
  58.5 1.8 pad_add_fusion.2
  60.3 2.7 collective-permute-start.1
  63.9 1.8 pad_add_fusion.3
  65.7 1.9 collective-permute-start.3
  68.5 1.8 pad_add_fusion.4
  70.4 2.4 collective-permute-start.5
  73.8 0.8 gather_fusion
  74.8 2.3 gather_fusion.7
  77.1 1.2 collective-permute-start.9
  79.0 15.4 %collective-permute-done.9 = bf16[2,128,1280]{2,1,0:T(8,128)(2,1)S(1)} collective-permute-done((bf16[2,128,1280]{2,1,0:T(8,128)(2,1)S(1)}, bf16[2,128,1280]{2,1,0:T(8,128)(2,1)S(1)}, u32[]{:S(2)}, u32[]{:S(2)}) %collective-permute-start.9) | collective-permute-done | bytes 655392 | tf_op jit(solution)/shard_map/ppermute | solution.py:178
  94.5 2.4 collective-permute-start.10
  96.9 15.2 %all-gather.6.cloned.1.call-done = bf16[1280,1920]{1,0:T(8,128)(2,1)} async-done(((bf16[320,1920]{1,0:T(8,128)(2,1)}), bf16[1280,1920]{1,0:T(8,128)(2,1)}) %all-gather.6.cloned.1.call-update) | async-done | bytes 4915216 | tf_op jit(solution)/shard_map/all_gather | solution.py:26
  112.1 1.9 pad_add_fusion.5
  114.0 3.3 %collective-permute-start.7 = (s32[3]{0:T(128)S(1)}, s32[3]{0:T(128)S(1)}, u32[]{:S(2)}, u32[]{:S(2)}) collective-permute-start(s32[3]{0:T(128)S(1)} %pad_add_fusion.5), channel_id=1, source_target_pairs={{0,8},{4,12},{8,16},{12,20},{16,24},{20,28},{24,32},{28,36},{32,40... | collective-permute-start | bytes 44 | tf_op jit(solution)/shard_map/ppermute | solution.py:20
  117.5 2.8 collective-permute-start.11
  120.3 2.4 gather_fusion.3
  122.6 4.7 %collective-permute-start.2 = (bf16[3,128,1280]{2,1,0:T(8,128)(2,1)S(1)}, bf16[3,128,1280]{2,1,0:T(8,128)(2,1)S(1)}, u32[]{:S(2)}, u32[]{:S(2)}) collective-permute-start(bf16[3,128,1280]{2,1,0:T(8,128)(2,1)S(1)} %gather_fusion.3), channel_id=1, source_target_pairs={{0,8},{4,12},{8,16},{12,20},{16,24},{20,28},{24,32},{28,36},{32,40... | collective-permute-start | bytes 2949128 | tf_op jit(solution)/shard_map/ppermute | solution.py:20
  127.3 9.3 %collective-permute-done.11 = bf16[2,128,1280]{2,1,0:T(8,128)(2,1)S(1)} collective-permute-done((bf16[2,128,1280]{2,1,0:T(8,128)(2,1)S(1)}, bf16[2,128,1280]{2,1,0:T(8,128)(2,1)S(1)}, u32[]{:S(2)}, u32[]{:S(2)}) %collective-permute-start.11) | collective-permute-done | bytes 655392 | tf_op jit(solution)/shard_map/ppermute | solution.py:178
  136.6 0.9 copy-done.7
  137.5 1.2 broadcast_select_fusion.4
  138.7 0.8 collective-permute-start.12
  139.5 3.4 %gather_fusion.4 = bf16[3,128,1280]{2,1,0:T(8,128)(2,1)} fusion(bf16[8,128,1280]{2,1,0:T(8,128)(2,1)} %bitcast.111, s32[1024]{0:T(1024)S(1)} %pad_clamp_fusion.3), kind=kCustom, calls=%fused_computation.4 | custom fusion | bytes 1966092 | tf_op jit(solution)/shard_map/gather | solution.py:185
  143.0 1.9 collective-permute-start.4
  144.9 3.4 %gather_fusion.5 = bf16[3,128,1280]{2,1,0:T(8,128)(2,1)} fusion(bf16[8,128,1280]{2,1,0:T(8,128)(2,1)} %bitcast.112, s32[1024]{0:T(1024)S(1)} %pad_clamp_fusion.2), kind=kCustom, calls=%fused_computation.5 | custom fusion | bytes 1966092 | tf_op jit(solution)/shard_map/gather | solution.py:185
  148.2 3.6 %collective-permute-start.6 = (bf16[3,128,1280]{2,1,0:T(8,128)(2,1)}, bf16[3,128,1280]{2,1,0:T(8,128)(2,1)}, u32[]{:S(2)}, u32[]{:S(2)}) collective-permute-start(bf16[3,128,1280]{2,1,0:T(8,128)(2,1)} %gather_fusion.5), channel_id=1, source_target_pairs={{4,0},{8,4},{12,8},{16,12},{20,16},{24,20},{28,24},{32,28},{36,32}... | collective-permute-start | bytes 2949128 | tf_op jit(solution)/shard_map/ppermute | solution.py:20
  151.9 3.3 %gather_fusion.6 = bf16[3,128,1280]{2,1,0:T(8,128)(2,1)} fusion(bf16[8,128,1280]{2,1,0:T(8,128)(2,1)} %bitcast.113, s32[1024]{0:T(1024)S(1)} %pad_clamp_fusion.1), kind=kCustom, calls=%fused_computation.6 | custom fusion | bytes 1966092 | tf_op jit(solution)/shard_map/gather | solution.py:185
  155.2 2.1 constant_dynamic-update-slice_fusion.4
  157.3 2.5 collective-permute-start.8
  159.9 10.6 %collective-permute-done.12 = bf16[2,128,1280]{2,1,0:T(8,128)(2,1)S(1)} collective-permute-done((bf16[2,128,1280]{2,1,0:T(8,128)(2,1)S(1)}, bf16[2,128,1280]{2,1,0:T(8,128)(2,1)S(1)}, u32[]{:S(2)}, u32[]{:S(2)}) %collective-permute-start.12) | collective-permute-done | bytes 655392 | tf_op jit(solution)/shard_map/ppermute | solution.py:178
  170.5 0.8 copy-done.6
  171.3 1.3 broadcast_select_fusion.5
  172.9 1.3 constant_dynamic-update-slice_fusion.2
  174.2 1.3 constant_dynamic-update-slice_fusion.1
  175.5 12.4 %collective-permute-done.8 = bf16[3,128,1280]{2,1,0:T(8,128)(2,1)S(1)} collective-permute-done((bf16[3,128,1280]{2,1,0:T(8,128)(2,1)}, bf16[3,128,1280]{2,1,0:T(8,128)(2,1)S(1)}, u32[]{:S(2)}, u32[]{:S(2)}) %collective-permute-start.8) | collective-permute-done | bytes 983072 | tf_op jit(solution)/shard_map/ppermute | solution.py:20
  188.3 2.9 copy-done.5
  191.1 7.1 %broadcast_select_fusion = (bf16[1280,1920]{1,0:T(8,128)(2,1)}, bf16[1280,1920]{1,0:T(8,128)(2,1)}) fusion(bf16[1280,1920]{1,0:T(8,128)(2,1)} %collective-permute-done, bf16[1280,1920]{1,0:T(8,128)(2,1)S(1)} %bitcast.117, pred[]{:T(512)S(6)} %eq.161), kind=kLoop, calls=%fused_computation.11 | loop fusion | flops 4915200 | bytes 19660800 | tf_op jit(solution)/shard_map/jit(_where)/select_n | solution.py:32
  198.3 3.9 %fusion.3 = bf16[256,1280]{1,0:T(8,128)(2,1)} fusion(bf16[256,1280]{1,0:T(8,128)(2,1)S(1)} %copy-done.4, bf16[1280,1920]{1,0:T(8,128)(2,1)} %get-tuple-element.32), kind=kOutput, calls=%fused_computation.15 | convolution fusion | flops 839188480 | bytes 4587520 | tf_op jit(solution)/shard_map/dot_general | solution.py:194
  202.2 23.6 %convolution_convert_fusion = bf16[2816,2560]{1,0:T(8,128)(2,1)} fusion(bf16[2816,1280]{1,0:T(8,128)(2,1)} %bitcast.118, bf16[1280,1920]{1,0:T(8,128)(2,1)S(1)} %copy-done.3, bf16[1280,1920]{1,0:T(8,128)(2,1)} %get-tuple-element.32), kind=kOutput, calls=%fused_computation.8 | convolution fusion | flops 18475253760 | bytes 31457280 | tf_op jit(solution)/shard_map/dot_general | solution.py:190
  225.8 52.5 %shard_map.109 = bf16[2,128,1280]{2,1,0:T(8,128)(2,1)} custom-call(s32[2,18]{1,0:T(2,128)} %pad_add_fusion.1.slots_ref, s32[2]{0:T(128)} %counts_ref.1, bf16[2,128,1280]{2,1,0:T(8,128)(2,1)} %bitcast.119, bf16[22,128,2560]{2,1,0:T(8,128)(2,1)} %bitcast.115), custom_call_target="tpu_custom_call" | custom-call | tf_op jit(solution)/shard_map/pallas_call | solution.py:127
  278.4 4.0 %convolution_convert_fusion.1 = bf16[256,1280]{1,0:T(8,128)(2,1)} fusion(bf16[256,1280]{1,0:T(8,128)(2,1)} %bitcast.120, bf16[1280,1280]{1,0:T(8,128)(2,1)} %all-gather.8.cloned.1.call-done), kind=kOutput, calls=%fused_computation.16 | convolution fusion | flops 839188480 | bytes 4587520 | tf_op jit(solution)/shard_map/dot_general | solution.py:215
  (92 shorter events, 7.0 us)
Async XLA Ops:
  6.5 49.5 %copy-start = (bf16[320,3840]{1,0:T(8,128)(2,1)S(1)}, bf16[320,3840]{1,0:T(8,128)(2,1)}, u32[]{:S(2)}) copy-start(bf16[320,3840]{1,0:T(8,128)(2,1)} %param.20) | copy-start | bytes 7372804
  6.5 6.4 %copy-start.2 = (bf16[256,1280]{1,0:T(8,128)(2,1)S(1)}, bf16[256,1280]{1,0:T(8,128)(2,1)}, u32[]{:S(2)}) copy-start(bf16[256,1280]{1,0:T(8,128)(2,1)} %param.16) | copy-start | bytes 1966084
  6.5 49.5 %all-gather.4.cloned.1.call-start = ((), (), s32[]{:S(2)}) async-start(), calls=%async_computation | async-start | bytes 3276800 | tf_op jit(solution)/shard_map/all_gather | solution.py:161
  15.0 42.2 %copy-start.8 = (s32[2,16]{1,0:T(2,128)S(1)}, s32[2,16]{1,0:T(2,128)}, u32[]{:S(2)}) copy-start(s32[2,16]{1,0:T(2,128)} %param.13) | copy-start | bytes 388
  15.0 59.7 %copy-start.9 = (s32[2]{0:T(128)S(1)}, s32[2]{0:T(128)}, u32[]{:S(2)}) copy-start(s32[2]{0:T(128)} %param.15) | copy-start | bytes 28
  18.4 93.7 %all-gather.6.cloned.1.call-start = ((), (), s32[]{:S(2)}) async-start(), calls=%async_computation.1 | async-start | bytes 6144000 | tf_op jit(solution)/shard_map/all_gather | solution.py:26
  57.2 221.2 %all-gather.8.cloned.1.call-start = ((), (), s32[]{:S(2)}) async-start(), calls=%async_computation.2 | async-start | bytes 4096000 | tf_op jit(solution)/shard_map/all_gather | solution.py:217
  60.3 53.6 %collective-permute-start.1 = (s32[3]{0:T(128)S(1)}, s32[3]{0:T(128)S(1)}, u32[]{:S(2)}, u32[]{:S(2)}) collective-permute-start(s32[3]{0:T(128)S(1)} %pad_add_fusion.2), channel_id=1, source_target_pairs={{8,0},{12,4},{16,8},{20,12},{24,16},{28,20},{32,24},{36,28},{40,32... | collective-permute-start | bytes 44 | tf_op jit(solution)/shard_map/ppermute | solution.py:20
  65.7 51.5 %collective-permute-start.3 = (s32[3]{0:T(128)S(1)}, s32[3]{0:T(128)S(1)}, u32[]{:S(2)}, u32[]{:S(2)}) collective-permute-start(s32[3]{0:T(128)S(1)} %pad_add_fusion.3), channel_id=1, source_target_pairs={{4,0},{8,4},{12,8},{16,12},{20,16},{24,20},{28,24},{32,28},{36,32}... | collective-permute-start | bytes 44 | tf_op jit(solution)/shard_map/ppermute | solution.py:20
  70.4 49.9 %collective-permute-start.5 = (s32[3]{0:T(128)S(1)}, s32[3]{0:T(128)S(1)}, u32[]{:S(2)}, u32[]{:S(2)}) collective-permute-start(s32[3]{0:T(128)S(1)} %pad_add_fusion.4), channel_id=1, source_target_pairs={{0,4},{4,8},{8,12},{12,16},{16,20},{20,24},{24,28},{28,32},{32,36}... | collective-permute-start | bytes 44 | tf_op jit(solution)/shard_map/ppermute | solution.py:20
  77.1 17.2 %collective-permute-start.9 = (bf16[2,128,1280]{2,1,0:T(8,128)(2,1)S(1)}, bf16[2,128,1280]{2,1,0:T(8,128)(2,1)S(1)}, u32[]{:S(2)}, u32[]{:S(2)}) collective-permute-start(bf16[2,128,1280]{2,1,0:T(8,128)(2,1)S(1)} %gather_fusion.7), channel_id=1, source_target_pairs={{0,16},{4,20},{8,24},{12,28},{16,0},{20,4},{24,8},{28,12},{32,48},... | collective-permute-start | bytes 1966088 | tf_op jit(solution)/shard_map/ppermute | solution.py:178
  94.5 22.8 %collective-permute-start.10 = (bf16[2,128,1280]{2,1,0:T(8,128)(2,1)S(1)}, bf16[2,128,1280]{2,1,0:T(8,128)(2,1)S(1)}, u32[]{:S(2)}, u32[]{:S(2)}) collective-permute-start(bf16[2,128,1280]{2,1,0:T(8,128)(2,1)S(1)} %broadcast_select_fusion.2), channel_id=1, source_target_pairs={{0,8},{4,12},{8,0},{12,4},{16,24},{20,28},{24,16},{28,20},{32,40},... | collective-permute-start | bytes 1966088 | tf_op jit(solution)/shard_map/ppermute | solution.py:178
  112.1 79.0 %collective-permute-start = (bf16[1280,1920]{1,0:T(8,128)(2,1)}, bf16[1280,1920]{1,0:T(8,128)(2,1)}, u32[]{:S(2)}, u32[]{:S(2)}) collective-permute-start(bf16[1280,1920]{1,0:T(8,128)(2,1)} %all-gather.6.cloned.1.call-done), channel_id=1, source_target_pairs={{0,4},{4,0},{8,12},{12,8},{16,20},{20,16},{24,28},{28,24},{32,36},... | collective-permute-start | bytes 14745608 | tf_op jit(solution)/shard_map/ppermute | solution.py:30
  114.0 6.3 %collective-permute-start.7 = (s32[3]{0:T(128)S(1)}, s32[3]{0:T(128)S(1)}, u32[]{:S(2)}, u32[]{:S(2)}) collective-permute-start(s32[3]{0:T(128)S(1)} %pad_add_fusion.5), channel_id=1, source_target_pairs={{0,8},{4,12},{8,16},{12,20},{16,24},{20,28},{24,32},{28,36},{32,40... | collective-permute-start | bytes 44 | tf_op jit(solution)/shard_map/ppermute | solution.py:20
  117.5 19.2 %collective-permute-start.11 = (bf16[2,128,1280]{2,1,0:T(8,128)(2,1)S(1)}, bf16[2,128,1280]{2,1,0:T(8,128)(2,1)S(1)}, u32[]{:S(2)}, u32[]{:S(2)}) collective-permute-start(bf16[2,128,1280]{2,1,0:T(8,128)(2,1)S(1)} %broadcast_select_fusion.3), channel_id=1, source_target_pairs={{0,64},{4,68},{8,72},{12,76},{16,80},{20,84},{24,88},{28,92},{32,9... | collective-permute-start | bytes 1966088 | tf_op jit(solution)/shard_map/ppermute | solution.py:178
  122.6 34.7 %collective-permute-start.2 = (bf16[3,128,1280]{2,1,0:T(8,128)(2,1)S(1)}, bf16[3,128,1280]{2,1,0:T(8,128)(2,1)S(1)}, u32[]{:S(2)}, u32[]{:S(2)}) collective-permute-start(bf16[3,128,1280]{2,1,0:T(8,128)(2,1)S(1)} %gather_fusion.3), channel_id=1, source_target_pairs={{0,8},{4,12},{8,16},{12,20},{16,24},{20,28},{24,32},{28,36},{32,40... | collective-permute-start | bytes 2949128 | tf_op jit(solution)/shard_map/ppermute | solution.py:20
  136.6 0.9 copy-start.7
  138.7 31.8 %collective-permute-start.12 = (bf16[2,128,1280]{2,1,0:T(8,128)(2,1)S(1)}, bf16[2,128,1280]{2,1,0:T(8,128)(2,1)S(1)}, u32[]{:S(2)}, u32[]{:S(2)}) collective-permute-start(bf16[2,128,1280]{2,1,0:T(8,128)(2,1)S(1)} %broadcast_select_fusion.4), channel_id=1, source_target_pairs={{0,32},{4,36},{8,40},{12,44},{16,48},{20,52},{24,56},{28,60},{32,0... | collective-permute-start | bytes 1966088 | tf_op jit(solution)/shard_map/ppermute | solution.py:178
  143.0 29.9 %collective-permute-start.4 = (bf16[3,128,1280]{2,1,0:T(8,128)(2,1)}, bf16[3,128,1280]{2,1,0:T(8,128)(2,1)}, u32[]{:S(2)}, u32[]{:S(2)}) collective-permute-start(bf16[3,128,1280]{2,1,0:T(8,128)(2,1)} %gather_fusion.4), channel_id=1, source_target_pairs={{0,4},{4,8},{8,12},{12,16},{16,20},{20,24},{24,28},{28,32},{32,36}... | collective-permute-start | bytes 2949128 | tf_op jit(solution)/shard_map/ppermute | solution.py:20
  148.2 25.9 %collective-permute-start.6 = (bf16[3,128,1280]{2,1,0:T(8,128)(2,1)}, bf16[3,128,1280]{2,1,0:T(8,128)(2,1)}, u32[]{:S(2)}, u32[]{:S(2)}) collective-permute-start(bf16[3,128,1280]{2,1,0:T(8,128)(2,1)} %gather_fusion.5), channel_id=1, source_target_pairs={{4,0},{8,4},{12,8},{16,12},{20,16},{24,20},{28,24},{32,28},{36,32}... | collective-permute-start | bytes 2949128 | tf_op jit(solution)/shard_map/ppermute | solution.py:20
  155.2 35.9 %slice-start = ((s8[4915200]{0:T(1024)(128)(4,1)}), s8[4194304]{0:T(1024)(128)(4,1)S(1)}, s32[]{:S(2)}) async-start(s8[4915200]{0:T(1024)(128)(4,1)} %bitcast.116), calls=%async_computation.3 | async-start | bytes 8388608
  157.3 30.6 %collective-permute-start.8 = (bf16[3,128,1280]{2,1,0:T(8,128)(2,1)}, bf16[3,128,1280]{2,1,0:T(8,128)(2,1)S(1)}, u32[]{:S(2)}, u32[]{:S(2)}) collective-permute-start(bf16[3,128,1280]{2,1,0:T(8,128)(2,1)} %gather_fusion.6), channel_id=1, source_target_pairs={{8,0},{12,4},{16,8},{20,12},{24,16},{28,20},{32,24},{36,28},{40,32... | collective-permute-start | bytes 2949128 | tf_op jit(solution)/shard_map/ppermute | solution.py:20
  170.5 0.8 copy-start.6
  171.3 19.8 %slice-start.1 = ((s8[4915200]{0:T(1024)(128)(4,1)}), s8[720896]{0:T(1024)(128)(4,1)S(1)}, s32[]{:S(2)}) async-start(s8[4915200]{0:T(1024)(128)(4,1)} %bitcast.116), calls=%async_computation.4 | async-start | bytes 1441792
  172.6 15.3 %collective-permute-start.13 = (bf16[2,128,1280]{2,1,0:T(8,128)(2,1)S(1)}, bf16[2,128,1280]{2,1,0:T(8,128)(2,1)S(1)}, u32[]{:S(2)}, u32[]{:S(2)}) collective-permute-start(bf16[2,128,1280]{2,1,0:T(8,128)(2,1)S(1)} %broadcast_select_fusion.5), channel_id=1, source_target_pairs={{0,4},{4,0},{8,12},{12,8},{16,20},{20,16},{24,28},{28,24},{32,36},... | collective-permute-start | bytes 1966088 | tf_op jit(solution)/shard_map/ppermute | solution.py:178
  188.2 2.9 copy-start.5
  191.1 7.2 %copy-start.4 = (bf16[256,1280]{1,0:T(8,128)(2,1)S(1)}, bf16[256,1280]{1,0:T(8,128)(2,1)}, u32[]{:S(2)}) copy-start(bf16[256,1280]{1,0:T(8,128)(2,1)} %fusion.11) | copy-start | bytes 1966084
  198.3 3.9 %copy-start.3 = (bf16[1280,1920]{1,0:T(8,128)(2,1)S(1)}, bf16[1280,1920]{1,0:T(8,128)(2,1)}, u32[]{:S(2)}) copy-start(bf16[1280,1920]{1,0:T(8,128)(2,1)} %get-tuple-element.31) | copy-start | bytes 14745604
  225.8 56.5 %copy-start.1 = (bf16[320,3840]{1,0:T(8,128)(2,1)S(1)}, bf16[320,3840]{1,0:T(8,128)(2,1)}, u32[]{:S(2)}) copy-start(bf16[320,3840]{1,0:T(8,128)(2,1)} %param.20) | copy-start | bytes 7372804
Sparse Core Ops, SparseCore 0:
  18.6 37.4 all-gather.3
  57.7 54.3 all-gather.5
  113.8 41.0 all-gather.7
